TPU v7x, 32 devices: a whole 2x2x4 slice. The times are simulated.
32 devices in a mesh: dp: 8 (over z, x), vocab: 4 (over y, core).
Axes of the slice: x: 2, y: 2, z: 4, core: 2. Of those that a mesh axis runs over, the one named last changes fastest.
Arguments:
- hidden: bfloat16 [256, 16384], P('dp', 'vocab'), may hold values from -10 to 10
- head_weight: bfloat16 [16384, 16384], P('vocab', 'dp'), may hold values from -0.1171875 to 0.1171875
- lengths: int32 [8], replicated, may hold values from 1 to 32, 160 in all
- targets: int32 [256], replicated, may hold values from 0 to 16383
- policy_logprobs: float32 [256], P('dp'), may hold values from -18 to -6
Outputs:
- ref_logprob: float32 [256], P('dp')
- token_kl: float32 [256], P('dp')
Inputs may be any that keep to these rules, and one draw needn't show every extreme that they name: The 8 lengths sum to exactly 160, and the longest is exactly 32.
All inputs are finite; a program needn't handle non-finite values.
Results may differ from a plain program's by a relative error of at most 0.0003.
Values may be sent and summed in bfloat16 or wider, within the bound.
No kernel may reach another device: no remote copies, remote signals or barrier semaphores. Data moves between devices by JAX's collectives and lax.ppermute only.
A program may use at most 64 MiB of HBM per device.

v0:
```python
import jax
import jax.numpy as jnp
from jax import lax
from jax.sharding import PartitionSpec as P

MB = 8


def tile_stats(logits, row_targets, col_start):
    highest = jnp.max(logits, axis=1)
    exp_total = jnp.sum(jnp.exp(logits - highest[:, None]), axis=1)
    columns = col_start + lax.broadcasted_iota(jnp.int32, logits.shape, 1)
    picked = jnp.sum(jnp.where(columns == row_targets[:, None], logits, 0.0), axis=1)
    return (highest, exp_total, picked)


def term_maker(work_rows, weight):
    return jnp.dot(work_rows, weight, preferred_element_type=jnp.float32)


def combine_rows(maxima, totals, picked):
    highest = lax.pmax(maxima, "dp")
    summed, target_logit = lax.psum((totals * jnp.exp(maxima - highest), picked), "dp")
    return target_logit - (highest + jnp.log(summed))


def on_device(hidden, head_weight, lengths, targets, policy_logprobs):
    row_count = hidden.shape[0]
    dp_size = lax.axis_size("dp")
    vocab_size = lax.axis_size("vocab")
    all_rows = row_count * dp_size
    slot_count = all_rows // MB
    tile_width = head_weight.shape[1]
    col_start = lax.axis_index("dp") * tile_width
    batches = jnp.arange(MB, dtype=jnp.int32)
    global_rows = lax.axis_index("dp") * row_count + jnp.arange(row_count, dtype=jnp.int32)
    member = (global_rows // slot_count)[:, None] == batches[None, :]
    in_batch = global_rows % slot_count
    is_live = in_batch < jnp.sum(jnp.where(member, lengths[None, :], 0), axis=1)
    full_rows = lax.all_gather(hidden, "dp", axis=0, tiled=True)
    share_rows = all_rows // vocab_size
    logits = lax.psum_scatter(
        term_maker(full_rows, head_weight), "vocab", scatter_dimension=0, tiled=True
    )
    first_row = lax.axis_index("vocab") * share_rows
    row_targets = lax.dynamic_slice_in_dim(targets, first_row, share_rows)
    maxima, totals, picked = tile_stats(logits, row_targets, col_start)
    logprob_block = combine_rows(maxima, totals, picked)
    all_values = lax.all_gather(logprob_block, "vocab", axis=0, tiled=True)
    own_values = lax.dynamic_slice_in_dim(all_values, lax.axis_index("dp") * row_count, row_count)
    ref_logprob = jnp.where(is_live, own_values, 0.0)
    ratio_log = jnp.clip(ref_logprob - policy_logprobs, -20.0, 20.0)
    kl_value = jnp.where(is_live, jnp.minimum(jnp.exp(ratio_log) - ratio_log - 1.0, 10.0), 0.0)
    return (ref_logprob, kl_value)


def solution(mesh):
    return jax.shard_map(
        on_device,
        mesh=mesh,
        in_specs=(P("dp", "vocab"), P("vocab", "dp"), P(), P(), P("dp")),
        out_specs=(P("dp"), P("dp")),
        check_vma=False,
    )
```

profile of v0, /device:TPU:0, one launch (start us, length us, event | category | flops | bytes accessed | tf_op | source)
XLA Modules:
  0.0 158.5 jit_solution(4165267616832723637)
XLA Ops:
  7.2 0.0 all-gather.2.cloned.1.call-start
  7.2 0.7 all-gather.2.cloned.1.call-update
  7.9 0.0 reduce-scatter.2.cloned.1.call-start
  7.9 54.0 %all-gather.2.cloned.1.call-done = bf16[256,4096]{1,0:T(8,128)(2,1)} async-done(((bf16[32,4096]{1,0:T(8,128)(2,1)}), bf16[256,4096]{1,0:T(8,128)(2,1)}) %all-gather.2.cloned.1.call-update) | async-done | bytes 2097168 | tf_op jit(solution)/shard_map/all_gather | solution.py:40
  61.9 12.2 %fusion.4 = f32[256,2048]{1,0:T(8,128)} fusion(bf16[256,4096]{1,0:T(8,128)(2,1)} %all-gather.2.cloned.1.call-done, bf16[4096,2048]{1,0:T(8,128)(2,1)} %param.6), kind=kOutput, calls=%fused_computation.19 | convolution fusion | flops 4294967296 | bytes 20971520 | tf_op jit(solution)/shard_map/dot_general | solution.py:18
  74.2 0.0 copy-start.1
  74.2 0.0 copy-start.3
  74.2 0.0 copy-start.2
  74.2 0.0 reduce-scatter.2.cloned.1.call-update
  74.2 0.6 copy-done.1
  74.9 0.1 dynamic_slice.6
  74.9 0.0 copy-done.3
  74.9 0.6 dynamic-slice
  76.2 0.0 copy-done.2
  76.2 0.1 select_reduce_fusion.1
  76.3 27.8 %reduce-scatter.2.cloned.1.call-done = f32[64,2048]{1,0:T(8,128)} async-done(((f32[256,2048]{1,0:T(8,128)}), f32[64,2048]{1,0:T(8,128)}) %reduce-scatter.2.cloned.1.call-update) | async-done | bytes 524304 | tf_op jit(solution)/shard_map/reduce_scatter | solution.py:42
  104.1 1.2 reduce_max.9
  105.2 21.4 %pmax.7 = f32[64]{0:T(128)S(1)} all-reduce(f32[64]{0:T(128)S(1)} %reduce_max.9), channel_id=1, replica_groups=mesh['dp'=8,'vocab'=4] {'dp'}, use_global_device_ids=true, to_apply=%region_5.6 | all-reduce | flops 64 | bytes 512 | tf_op jit(solution)/shard_map/pmax | solution.py:22
  126.6 1.3 exponential_reduce_fusion
  128.0 17.1 %all-reduce.1 = (f32[64]{0:T(128)S(1)}, f32[64]{0:T(128)S(1)}) all-reduce(f32[64]{0:T(128)S(1)} %get-tuple-element.3, f32[64]{0:T(128)S(1)} %exponential_multiply_fusion), channel_id=1, replica_groups=mesh['dp'=8,'vocab'=4] {'dp'}, use_global_device_ids=true, to_apply=%region_3.4 | all-reduce | flops 128 | bytes 1024 | tf_op jit(solution)/shard_map/psum | solution.py:23
  145.1 0.1 subtract_dynamic-update-slice_fusion
  145.2 5.9 %all-reduce = f32[256]{0:T(256)S(1)} all-reduce(f32[256]{0:T(256)S(1)} %subtract_dynamic-update-slice_fusion), channel_id=1, replica_groups=mesh['dp'=8,'vocab'=4] {'vocab'}, use_global_device_ids=true, to_apply=%add | all-reduce | flops 256 | bytes 2048
  151.1 0.0 copy-done
  151.1 0.6 fusion.3
  (5 shorter events, 0.0 us)
Async XLA Ops:
  7.2 54.8 %all-gather.2.cloned.1.call-start = ((), (), s32[]{:S(2)}) async-start(), calls=%async_computation.1 | async-start | bytes 2359296 | tf_op jit(solution)/shard_map/all_gather | solution.py:40
  7.9 96.2 %reduce-scatter.2.cloned.1.call-start = ((), (), s32[]{:S(2)}) async-start(), calls=%async_computation.2 | async-start | bytes 2621440 | tf_op jit(solution)/shard_map/reduce_scatter | solution.py:42
  74.2 0.7 copy-start.1
  74.2 0.8 copy-start.3
  74.2 2.0 %copy-start.2 = (s32[8]{0:T(128)S(1)}, s32[8]{0:T(128)}, u32[]{:S(2)}) copy-start(s32[8]{0:T(128)} %param.7) | copy-start | bytes 100
  74.2 76.9 %copy-start = (f32[32]{0:T(128)S(1)}, f32[32]{0:T(128)}, u32[]{:S(2)}) copy-start(f32[32]{0:T(128)} %param.9) | copy-start | bytes 388
Sparse Core Ops, SparseCore 0:
  10.1 51.7 all-gather.1
  74.3 29.6 reduce-scatter.1
where the time goes:
time: 159 us
  waiting for transfers between devices  82.5 us (52%)
  blocking collectives  44.4 us (28%)
  between operations  14.7 us (9%)
  matrix products  12.2 us (8%)
  other arithmetic  3.31 us (2%)
    all_gather x1, waiting for transfers between devices, on_device(): full_rows = lax.all_gather(hidden, 'dp', axis=0, tiled=True)  54 us
    reduce_scatter x1, waiting for transfers between devices, on_device(): lax.psum_scatter(term_maker(full_rows, head_weight), 'vocab', scatter_dim...  27.8 us
    pmax x1, blocking collectives, combine_rows(): highest = lax.pmax(maxima, 'dp')  21.4 us
    psum x1, blocking collectives, combine_rows(): lax.psum((totals * jnp.exp(maxima - highest), picked), 'dp')  17.1 us
    dot_general x1, matrix products, term_maker(): return jnp.dot(work_rows, weight, preferred_element_type=jnp.float32)  12.2 us
    unnamed x1, blocking collectives  5.9 us
  transfers between devices with their start and end apart: 2, of which 2 were waited for; matrix products, arithmetic and copies ran while one was open for 0% of the time, Pallas kernels for 0%

commit v1 on v0

v1 whole, which is shorter than its diff:
```python
import numpy as np
import jax
import jax.numpy as jnp
from jax import lax
from jax.sharding import PartitionSpec as P

MB = 8


def dp_ring(mesh):
    size = mesh.shape["dp"]
    try:
        coords = [tuple(dev.coords) for dev in mesh.devices[:, 0]]
        xs = sorted({c[0] for c in coords})
        zs = sorted({c[2] for c in coords})
        if len(xs) * len(zs) != size or len(zs) % 2:
            raise ValueError
        where = {(c[0], c[2]): i for i, c in enumerate(coords)}
        order = [where[(xs[0], z)] for z in zs]
        for row, z in enumerate(reversed(zs)):
            cols = xs[1:] if row % 2 == 0 else list(reversed(xs[1:]))
            order += [where[(x, z)] for x in cols]
        if sorted(order) != list(range(size)):
            raise ValueError
        return order
    except Exception:
        return list(range(size))


def ring_gather(block, ring):
    size = len(ring)
    pos_of = np.argsort(np.asarray(ring))
    fwd = [(ring[i], ring[(i + 1) % size]) for i in range(size)]
    bwd = [(ring[(i + 1) % size], ring[i]) for i in range(size)]
    slots = [None] * size
    slots[0] = block
    ahead, behind = block, block
    for step in range(1, size // 2 + 1):
        ahead = lax.ppermute(ahead, "dp", fwd)
        slots[step] = ahead
        if step < size - step:
            behind = lax.ppermute(behind, "dp", bwd)
            slots[size - step] = behind
    stacked = jnp.stack(slots)
    me = jnp.asarray(pos_of, jnp.int32)[lax.axis_index("dp")]
    pick = (me - jnp.asarray(pos_of, jnp.int32)) % size
    return jnp.take(stacked, pick, axis=0).reshape(-1, block.shape[1])


def halving_scatter(partial, size):
    me = lax.axis_index("vocab")
    first = jnp.int32(0)
    bit = 1
    while bit < size:
        half = partial.shape[0] // 2
        pairs = partial.reshape(2, half, partial.shape[1])
        side = (me // bit) % 2
        keep = jnp.take(pairs, side, axis=0)
        send = jnp.take(pairs, 1 - side, axis=0)
        got = lax.ppermute(send, "vocab", [(i, i ^ bit) for i in range(size)])
        partial = keep + got
        first = first + side * half
        bit *= 2
    return partial, first


def merge_stats(stats, size):
    bit = 1
    while bit < size:
        other = lax.ppermute(stats, "dp", [(i, i ^ bit) for i in range(size)])
        top = jnp.maximum(stats[0], other[0])
        total = stats[1] * jnp.exp(stats[0] - top) + other[1] * jnp.exp(other[0] - top)
        stats = jnp.stack([top, total, stats[2] + other[2]])
        bit *= 2
    return stats


def doubling_gather(values, first, size):
    me = lax.axis_index("vocab")
    total = values.shape[0] * size
    out = jnp.zeros((total,), values.dtype)
    out = lax.dynamic_update_slice(out, values, (first,))
    bit = 1
    while bit < size:
        other = lax.ppermute(out, "vocab", [(i, i ^ bit) for i in range(size)])
        out = out + other
        bit *= 2
    return out


def make_body(ring):
    def on_device(hidden, head_weight, lengths, targets, policy_logprobs):
        row_count = hidden.shape[0]
        dp_size = lax.axis_size("dp")
        vocab_size = lax.axis_size("vocab")
        all_rows = row_count * dp_size
        slot_count = all_rows // MB
        tile_width = head_weight.shape[1]
        col_start = lax.axis_index("dp") * tile_width
        full_rows = ring_gather(hidden, ring)
        partial = jnp.dot(full_rows, head_weight, preferred_element_type=jnp.float32)
        logits, first = halving_scatter(partial, vocab_size)
        share = logits.shape[0]
        row_targets = lax.dynamic_slice_in_dim(targets, first, share)
        highest = jnp.max(logits, axis=1)
        exp_total = jnp.sum(jnp.exp(logits - highest[:, None]), axis=1)
        columns = col_start + lax.broadcasted_iota(jnp.int32, logits.shape, 1)
        picked = jnp.sum(jnp.where(columns == row_targets[:, None], logits, 0.0), axis=1)
        stats = merge_stats(jnp.stack([highest, exp_total, picked]), dp_size)
        logprob = stats[2] - (stats[0] + jnp.log(stats[1]))
        all_values = doubling_gather(logprob, first, vocab_size)
        own_values = lax.dynamic_slice_in_dim(all_values, lax.axis_index("dp") * row_count, row_count)
        global_rows = lax.axis_index("dp") * row_count + jnp.arange(row_count, dtype=jnp.int32)
        batches = jnp.arange(MB, dtype=jnp.int32)
        member = (global_rows // slot_count)[:, None] == batches[None, :]
        in_batch = global_rows % slot_count
        is_live = in_batch < jnp.sum(jnp.where(member, lengths[None, :], 0), axis=1)
        ref_logprob = jnp.where(is_live, own_values, 0.0)
        ratio_log = jnp.clip(ref_logprob - policy_logprobs, -20.0, 20.0)
        kl_value = jnp.where(is_live, jnp.minimum(jnp.exp(ratio_log) - ratio_log - 1.0, 10.0), 0.0)
        return (ref_logprob, kl_value)

    return on_device


def solution(mesh):
    return jax.shard_map(
        make_body(dp_ring(mesh)),
        mesh=mesh,
        in_specs=(P("dp", "vocab"), P("vocab", "dp"), P(), P(), P("dp")),
        out_specs=(P("dp"), P("dp")),
        check_vma=False,
    )
```

time: 159 us -> 81 us (0.51)
  waiting for transfers between devices: 82.5 us -> 37.8 us
  blocking collectives: 44.4 us -> 0 us
  starting transfers between devices: 0.08 us -> 18.7 us
  between operations: 14.7 us -> 0.81 us
  local copies, waits for them, and re-layouts: 1.3 us -> 10.7 us
  matrix products: 12.2 us -> 8.19 us
    all_gather x1 -> x0, waiting for transfers between devices: 54 us -> none  [on_device(): full_rows = lax.all_gather(hidden, 'dp', axis=0, tiled=True)]
    ppermute x0 -> x14, waiting for transfers between devices: none -> 37.8 us  [the longest x2 14.9 us: halving_scatter(): got = lax.ppermute(send, 'vocab', [(i, i ^ bit) for i in range(size)])]
    reduce_scatter x1 -> x0, waiting for transfers between devices: 27.8 us -> none  [on_device(): lax.psum_scatter(term_maker(full_rows, head_weight), 'vocab', scatter_dim...]
    pmax x1 -> x0, blocking collectives: 21.4 us -> none  [combine_rows(): highest = lax.pmax(maxima, 'dp')]
    ppermute x0 -> x14, starting transfers between devices: none -> 18.7 us  [the longest x4 8.21 us: ring_gather(): ahead = lax.ppermute(ahead, 'dp', fwd)]
    psum x1 -> x0, blocking collectives: 17.1 us -> none  [combine_rows(): lax.psum((totals * jnp.exp(maxima - highest), picked), 'dp')]
    unnamed x1 -> x0, blocking collectives: 5.9 us -> none
    unnamed x10 -> x13, local copies, waits for them, and re-layouts: 1.23 us -> 6.11 us
  transfers between devices with their start and end apart: 2 -> 14, of which waited for: 2 -> 11; matrix products, arithmetic and copies ran while one was open for 0% -> 9% of each run, Pallas kernels for 0% -> 0%
where the time goes in v1:
time: 81 us; the launch traced here: 80.7 us
  waiting for transfers between devices  37.8 us (47%)
  starting transfers between devices  18.7 us (23%)
  local copies, waits for them, and re-layouts  10.7 us (13%)
  matrix products  8.19 us (10%)
  other arithmetic  4.52 us (6%)
  between operations  0.81 us (1%)
    ppermute x2, waiting for transfers between devices, halving_scatter(): got = lax.ppermute(send, 'vocab', [(i, i ^ bit) for i in range(size)])  14.9 us
    ppermute x4, waiting for transfers between devices, ring_gather(): ahead = lax.ppermute(ahead, 'dp', fwd)  14.4 us
    ppermute x4, starting transfers between devices, ring_gather(): ahead = lax.ppermute(ahead, 'dp', fwd)  8.21 us
    dot_general x1, matrix products, on_device(): jnp.dot(full_rows, head_weight, preferred_element_type=jnp.float32)  8.19 us
    ppermute x3, starting transfers between devices, merge_stats(): other = lax.ppermute(stats, 'dp', [(i, i ^ bit) for i in range(size)])  6.33 us
    unnamed x13, local copies, waits for them, and re-layouts  6.11 us
    ppermute x3, waiting for transfers between devices, merge_stats(): other = lax.ppermute(stats, 'dp', [(i, i ^ bit) for i in range(size)])  5.52 us
    ppermute x2, waiting for transfers between devices, doubling_gather(): other = lax.ppermute(out, 'vocab', [(i, i ^ bit) for i in range(size)])  2.95 us
  transfers between devices with their start and end apart: 14, of which 11 were waited for; matrix products, arithmetic and copies ran while one was open for 9% of the time, Pallas kernels for 0%

profile of v1, /device:TPU:0, one launch (start us, length us, event | category | flops | bytes accessed | tf_op | source)
XLA Modules:
  0.0 80.7 jit_solution(8050593297009170532)
XLA Ops:
  0.6 3.1 %collective-permute-start = (bf16[32,4096]{1,0:T(8,128)(2,1)}, bf16[32,4096]{1,0:T(8,128)(2,1)S(1)}, u32[]{:S(2)}, u32[]{:S(2)}) collective-permute-start(bf16[32,4096]{1,0:T(8,128)(2,1)} %param.11), channel_id=1, source_target_pairs={{0,8},{8,16},{16,24},{24,28},{28,20},{20,12},{12,4},{4,0},{1,9},{9... | collective-permute-start | bytes 786440 | tf_op jit(solution)/shard_map/ppermute | solution.py:39
  3.7 1.7 %bitcast_dynamic-update-slice_fusion.7 = bf16[8,32,4096]{2,1,0:T(8,128)(2,1)} fusion(bf16[32,4096]{1,0:T(8,128)(2,1)} %param.11), kind=kLoop, calls=%fused_computation.17 | loop fusion | bytes 524288
  6.7 1.3 %compare_and_fusion = (pred[8]{0:T(512)(128)(4,1)S(1)}, s32[8]{0:T(128)S(1)}) fusion(s32[8]{0:T(128)} %constant.184, s32[]{:T(128)} %bitcast), kind=kLoop, calls=%fused_computation.28 | loop fusion | flops 144 | bytes 76 | tf_op jit(solution)/shard_map/jit(_take)/and | solution.py:47
  8.3 1.9 %collective-permute-done = bf16[32,4096]{1,0:T(8,128)(2,1)S(1)} collective-permute-done((bf16[32,4096]{1,0:T(8,128)(2,1)}, bf16[32,4096]{1,0:T(8,128)(2,1)S(1)}, u32[]{:S(2)}, u32[]{:S(2)}) %collective-permute-start) | collective-permute-done | bytes 262176 | tf_op jit(solution)/shard_map/ppermute | solution.py:39
  10.2 1.8 %collective-permute-start.1 = (bf16[32,4096]{1,0:T(8,128)(2,1)S(1)}, bf16[32,4096]{1,0:T(8,128)(2,1)S(1)}, u32[]{:S(2)}, u32[]{:S(2)}) collective-permute-start(bf16[32,4096]{1,0:T(8,128)(2,1)S(1)} %collective-permute-done), channel_id=1, source_target_pairs={{0,8},{8,16},{16,24},{24,28},{28,20},{20,12},{12,4},{4,0},{1,9},{9... | collective-permute-start | bytes 786440 | tf_op jit(solution)/shard_map/ppermute | solution.py:39
  12.9 4.7 %collective-permute-done.1 = bf16[32,4096]{1,0:T(8,128)(2,1)S(1)} collective-permute-done((bf16[32,4096]{1,0:T(8,128)(2,1)S(1)}, bf16[32,4096]{1,0:T(8,128)(2,1)S(1)}, u32[]{:S(2)}, u32[]{:S(2)}) %collective-permute-start.1) | collective-permute-done | bytes 262176 | tf_op jit(solution)/shard_map/ppermute | solution.py:39
  17.6 1.5 %collective-permute-start.2 = (bf16[32,4096]{1,0:T(8,128)(2,1)S(1)}, bf16[32,4096]{1,0:T(8,128)(2,1)S(1)}, u32[]{:S(2)}, u32[]{:S(2)}) collective-permute-start(bf16[32,4096]{1,0:T(8,128)(2,1)S(1)} %collective-permute-done.1), channel_id=1, source_target_pairs={{0,8},{8,16},{16,24},{24,28},{28,20},{20,12},{12,4},{4,0},{1,9},{9... | collective-permute-start | bytes 786440 | tf_op jit(solution)/shard_map/ppermute | solution.py:39
  20.4 3.9 %collective-permute-done.2 = bf16[32,4096]{1,0:T(8,128)(2,1)S(1)} collective-permute-done((bf16[32,4096]{1,0:T(8,128)(2,1)S(1)}, bf16[32,4096]{1,0:T(8,128)(2,1)S(1)}, u32[]{:S(2)}, u32[]{:S(2)}) %collective-permute-start.2) | collective-permute-done | bytes 262176 | tf_op jit(solution)/shard_map/ppermute | solution.py:39
  24.2 1.7 %collective-permute-start.3 = (bf16[32,4096]{1,0:T(8,128)(2,1)S(1)}, bf16[32,4096]{1,0:T(8,128)(2,1)S(1)}, u32[]{:S(2)}, u32[]{:S(2)}) collective-permute-start(bf16[32,4096]{1,0:T(8,128)(2,1)S(1)} %collective-permute-done.2), channel_id=1, source_target_pairs={{0,8},{8,16},{16,24},{24,28},{28,20},{20,12},{12,4},{4,0},{1,9},{9... | collective-permute-start | bytes 786440 | tf_op jit(solution)/shard_map/ppermute | solution.py:39
  26.7 3.9 %collective-permute-done.3 = bf16[32,4096]{1,0:T(8,128)(2,1)S(1)} collective-permute-done((bf16[32,4096]{1,0:T(8,128)(2,1)S(1)}, bf16[32,4096]{1,0:T(8,128)(2,1)S(1)}, u32[]{:S(2)}, u32[]{:S(2)}) %collective-permute-start.3) | collective-permute-done | bytes 262176 | tf_op jit(solution)/shard_map/ppermute | solution.py:39
  33.6 2.3 %gather_fusion = bf16[8,32,4096]{2,1,0:T(8,128)(2,1)S(1)} fusion(bf16[8,32,4096]{2,1,0:T(8,128)(2,1)} %bitcast_dynamic-update-slice_fusion, s32[1024]{0:T(1024)S(1)} %pad_clamp_fusion), kind=kCustom, calls=%fused_computation | custom fusion | bytes 4194336 | tf_op jit(solution)/shard_map/jit(_take)/gather | solution.py:47
  36.1 8.2 %fusion = f32[2,128,2048]{2,1,0:T(8,128)S(1)} fusion(bf16[2,128,4096]{2,1,0:T(8,128)(2,1)S(1)} %bitcast_select_fusion, bf16[4096,2048]{1,0:T(8,128)(2,1)} %param.12), kind=kOutput, calls=%fused_computation.1 | convolution fusion | flops 4294967296 | bytes 20971520 | tf_op jit(solution)/shard_map/dot_general | solution.py:101
  44.6 2.7 %collective-permute-done.7 = f32[128,2048]{1,0:T(8,128)} collective-permute-done((f32[128,2048]{1,0:T(8,128)S(1)}, f32[128,2048]{1,0:T(8,128)}, u32[]{:S(2)}, u32[]{:S(2)}) %collective-permute-start.7) | collective-permute-done | bytes 1048608 | tf_op jit(solution)/shard_map/ppermute | solution.py:60
  47.3 1.3 %bitcast_add_fusion = f32[128,2048]{1,0:T(8,128)S(1)} fusion(f32[128,2048]{1,0:T(8,128)} %collective-permute-done.7, f32[2,128,2048]{2,1,0:T(8,128)S(1)} %fusion, s32[]{:T(128)S(6)} %select_n.108, pred[]{:T(512)S(6)} %and.65), kind=kLoop, calls=%fused_computation.4 | loop fusion | flops 524288 | bytes 3145733 | tf_op jit(solution)/shard_map/add | solution.py:61
  48.7 1.7 %collective-permute-start.8 = (f32[64,2048]{1,0:T(8,128)S(1)}, f32[64,2048]{1,0:T(8,128)S(1)}, u32[]{:S(2)}, u32[]{:S(2)}) collective-permute-start(f32[64,2048]{1,0:T(8,128)S(1)} %select_bitcast_fusion.1), channel_id=1, source_target_pairs={{0,2},{1,3},{2,0},{3,1},{4,6},{5,7},{6,4},{7,5},{8,10},{9,11},{10,... | collective-permute-start | bytes 1572872 | tf_op jit(solution)/shard_map/ppermute | solution.py:60
  50.5 12.2 %collective-permute-done.8 = f32[64,2048]{1,0:T(8,128)S(1)} collective-permute-done((f32[64,2048]{1,0:T(8,128)S(1)}, f32[64,2048]{1,0:T(8,128)S(1)}, u32[]{:S(2)}, u32[]{:S(2)}) %collective-permute-start.8) | collective-permute-done | bytes 524320 | tf_op jit(solution)/shard_map/ppermute | solution.py:60
  63.2 1.7 %collective-permute-start.9 = (f32[3,64]{1,0:T(4,128)S(1)}, f32[3,64]{1,0:T(4,128)S(1)}, u32[]{:S(2)}, u32[]{:S(2)}) collective-permute-start(f32[3,64]{1,0:T(4,128)S(1)} %pad_maximum_fusion), channel_id=1, source_target_pairs={{0,4},{4,0},{8,12},{12,8},{16,20},{20,16},{24,28},{28,24},{1,5},{5... | collective-permute-start | bytes 2312 | tf_op jit(solution)/shard_map/ppermute | solution.py:70
  64.9 1.9 %collective-permute-done.9 = f32[3,64]{1,0:T(4,128)S(1)} collective-permute-done((f32[3,64]{1,0:T(4,128)S(1)}, f32[3,64]{1,0:T(4,128)S(1)}, u32[]{:S(2)}, u32[]{:S(2)}) %collective-permute-start.9) | collective-permute-done | bytes 800 | tf_op jit(solution)/shard_map/ppermute | solution.py:70
  66.9 1.8 %collective-permute-start.10 = (f32[3,64]{1,0:T(4,128)S(1)}, f32[3,64]{1,0:T(4,128)S(1)}, u32[]{:S(2)}, u32[]{:S(2)}) collective-permute-start(f32[3,64]{1,0:T(4,128)S(1)} %pad_maximum_fusion.1), channel_id=1, source_target_pairs={{0,8},{4,12},{8,0},{12,4},{16,24},{20,28},{24,16},{28,20},{1,9},{5... | collective-permute-start | bytes 2312 | tf_op jit(solution)/shard_map/ppermute | solution.py:70
  68.7 1.9 %collective-permute-done.10 = f32[3,64]{1,0:T(4,128)S(1)} collective-permute-done((f32[3,64]{1,0:T(4,128)S(1)}, f32[3,64]{1,0:T(4,128)S(1)}, u32[]{:S(2)}, u32[]{:S(2)}) %collective-permute-start.10) | collective-permute-done | bytes 800 | tf_op jit(solution)/shard_map/ppermute | solution.py:70
  70.5 2.8 %collective-permute-start.11 = (f32[3,64]{1,0:T(4,128)S(1)}, f32[3,64]{1,0:T(4,128)S(1)}, u32[]{:S(2)}, u32[]{:S(2)}) collective-permute-start(f32[3,64]{1,0:T(4,128)S(1)} %pad_maximum_fusion.2), channel_id=1, source_target_pairs={{0,16},{4,20},{8,24},{12,28},{16,0},{20,4},{24,8},{28,12},{1,17},{... | collective-permute-start | bytes 2312 | tf_op jit(solution)/shard_map/ppermute | solution.py:70
  73.4 1.7 %collective-permute-done.11 = f32[3,64]{1,0:T(4,128)S(1)} collective-permute-done((f32[3,64]{1,0:T(4,128)S(1)}, f32[3,64]{1,0:T(4,128)S(1)}, u32[]{:S(2)}, u32[]{:S(2)}) %collective-permute-start.11) | collective-permute-done | bytes 800 | tf_op jit(solution)/shard_map/ppermute | solution.py:70
  76.5 1.7 %collective-permute-start.13 = (f32[256]{0:T(256)S(1)}, f32[256]{0:T(256)S(1)}, u32[]{:S(2)}, u32[]{:S(2)}) collective-permute-start(f32[256]{0:T(256)S(1)} %add_dynamic-update-slice_fusion), channel_id=1, source_target_pairs={{0,2},{1,3},{2,0},{3,1},{4,6},{5,7},{6,4},{7,5},{8,10},{9,11},{10,... | collective-permute-start | bytes 3080 | tf_op jit(solution)/shard_map/ppermute | solution.py:85
  78.3 1.8 %collective-permute-done.13 = f32[256]{0:T(256)S(1)} collective-permute-done((f32[256]{0:T(256)S(1)}, f32[256]{0:T(256)S(1)}, u32[]{:S(2)}, u32[]{:S(2)}) %collective-permute-start.13) | collective-permute-done | bytes 1056 | tf_op jit(solution)/shard_map/ppermute | solution.py:85
  (46 shorter events, 10.5 us)
Async XLA Ops:
  0.6 9.5 %collective-permute-start = (bf16[32,4096]{1,0:T(8,128)(2,1)}, bf16[32,4096]{1,0:T(8,128)(2,1)S(1)}, u32[]{:S(2)}, u32[]{:S(2)}) collective-permute-start(bf16[32,4096]{1,0:T(8,128)(2,1)} %param.11), channel_id=1, source_target_pairs={{0,8},{8,16},{16,24},{24,28},{28,20},{20,12},{12,4},{4,0},{1,9},{9... | collective-permute-start | bytes 786440 | tf_op jit(solution)/shard_map/ppermute | solution.py:39
  3.7 9.0 %collective-permute-start.4 = (bf16[32,4096]{1,0:T(8,128)(2,1)}, bf16[32,4096]{1,0:T(8,128)(2,1)S(1)}, u32[]{:S(2)}, u32[]{:S(2)}) collective-permute-start(bf16[32,4096]{1,0:T(8,128)(2,1)} %param.11), channel_id=1, source_target_pairs={{8,0},{16,8},{24,16},{28,24},{20,28},{12,20},{4,12},{0,4},{9,1},{1... | collective-permute-start | bytes 786440 | tf_op jit(solution)/shard_map/ppermute | solution.py:42
  10.2 7.5 %collective-permute-start.1 = (bf16[32,4096]{1,0:T(8,128)(2,1)S(1)}, bf16[32,4096]{1,0:T(8,128)(2,1)S(1)}, u32[]{:S(2)}, u32[]{:S(2)}) collective-permute-start(bf16[32,4096]{1,0:T(8,128)(2,1)S(1)} %collective-permute-done), channel_id=1, source_target_pairs={{0,8},{8,16},{16,24},{24,28},{28,20},{20,12},{12,4},{4,0},{1,9},{9... | collective-permute-start | bytes 786440 | tf_op jit(solution)/shard_map/ppermute | solution.py:39
  12.7 7.2 %collective-permute-start.5 = (bf16[32,4096]{1,0:T(8,128)(2,1)S(1)}, bf16[32,4096]{1,0:T(8,128)(2,1)S(1)}, u32[]{:S(2)}, u32[]{:S(2)}) collective-permute-start(bf16[32,4096]{1,0:T(8,128)(2,1)S(1)} %collective-permute-done.4), channel_id=1, source_target_pairs={{8,0},{16,8},{24,16},{28,24},{20,28},{12,20},{4,12},{0,4},{9,1},{1... | collective-permute-start | bytes 786440 | tf_op jit(solution)/shard_map/ppermute | solution.py:42
  17.6 6.6 %collective-permute-start.2 = (bf16[32,4096]{1,0:T(8,128)(2,1)S(1)}, bf16[32,4096]{1,0:T(8,128)(2,1)S(1)}, u32[]{:S(2)}, u32[]{:S(2)}) collective-permute-start(bf16[32,4096]{1,0:T(8,128)(2,1)S(1)} %collective-permute-done.1), channel_id=1, source_target_pairs={{0,8},{8,16},{16,24},{24,28},{28,20},{20,12},{12,4},{4,0},{1,9},{9... | collective-permute-start | bytes 786440 | tf_op jit(solution)/shard_map/ppermute | solution.py:39
  19.9 11.5 %collective-permute-start.6 = (bf16[32,4096]{1,0:T(8,128)(2,1)S(1)}, bf16[32,4096]{1,0:T(8,128)(2,1)S(1)}, u32[]{:S(2)}, u32[]{:S(2)}) collective-permute-start(bf16[32,4096]{1,0:T(8,128)(2,1)S(1)} %collective-permute-done.5), channel_id=1, source_target_pairs={{8,0},{16,8},{24,16},{28,24},{20,28},{12,20},{4,12},{0,4},{9,1},{1... | collective-permute-start | bytes 786440 | tf_op jit(solution)/shard_map/ppermute | solution.py:42
  24.2 6.4 %collective-permute-start.3 = (bf16[32,4096]{1,0:T(8,128)(2,1)S(1)}, bf16[32,4096]{1,0:T(8,128)(2,1)S(1)}, u32[]{:S(2)}, u32[]{:S(2)}) collective-permute-start(bf16[32,4096]{1,0:T(8,128)(2,1)S(1)} %collective-permute-done.2), channel_id=1, source_target_pairs={{0,8},{8,16},{16,24},{24,28},{28,20},{20,12},{12,4},{4,0},{1,9},{9... | collective-permute-start | bytes 786440 | tf_op jit(solution)/shard_map/ppermute | solution.py:39
  44.4 2.9 %collective-permute-start.7 = (f32[128,2048]{1,0:T(8,128)S(1)}, f32[128,2048]{1,0:T(8,128)}, u32[]{:S(2)}, u32[]{:S(2)}) collective-permute-start(f32[128,2048]{1,0:T(8,128)S(1)} %select_bitcast_fusion), channel_id=1, source_target_pairs={{0,1},{1,0},{2,3},{3,2},{4,5},{5,4},{6,7},{7,6},{8,9},{9,8},{10,11... | collective-permute-start | bytes 3145736 | tf_op jit(solution)/shard_map/ppermute | solution.py:60
  44.5 5.9 %copy-start.1 = (s32[256]{0:T(256)S(1)}, s32[256]{0:T(256)}, u32[]{:S(2)}) copy-start(s32[256]{0:T(256)} %param.14) | copy-start | bytes 3076
  48.6 29.6 %copy-start.2 = (s32[8]{0:T(128)S(1)}, s32[8]{0:T(128)}, u32[]{:S(2)}) copy-start(s32[8]{0:T(128)} %param.13) | copy-start | bytes 100
  48.6 31.5 %copy-start = (f32[32]{0:T(128)S(1)}, f32[32]{0:T(128)}, u32[]{:S(2)}) copy-start(f32[32]{0:T(128)} %param.15) | copy-start | bytes 388
  48.7 14.0 %collective-permute-start.8 = (f32[64,2048]{1,0:T(8,128)S(1)}, f32[64,2048]{1,0:T(8,128)S(1)}, u32[]{:S(2)}, u32[]{:S(2)}) collective-permute-start(f32[64,2048]{1,0:T(8,128)S(1)} %select_bitcast_fusion.1), channel_id=1, source_target_pairs={{0,2},{1,3},{2,0},{3,1},{4,6},{5,7},{6,4},{7,5},{8,10},{9,11},{10,... | collective-permute-start | bytes 1572872 | tf_op jit(solution)/shard_map/ppermute | solution.py:60
  63.2 3.7 %collective-permute-start.9 = (f32[3,64]{1,0:T(4,128)S(1)}, f32[3,64]{1,0:T(4,128)S(1)}, u32[]{:S(2)}, u32[]{:S(2)}) collective-permute-start(f32[3,64]{1,0:T(4,128)S(1)} %pad_maximum_fusion), channel_id=1, source_target_pairs={{0,4},{4,0},{8,12},{12,8},{16,20},{20,16},{24,28},{28,24},{1,5},{5... | collective-permute-start | bytes 2312 | tf_op jit(solution)/shard_map/ppermute | solution.py:70
  66.9 3.7 %collective-permute-start.10 = (f32[3,64]{1,0:T(4,128)S(1)}, f32[3,64]{1,0:T(4,128)S(1)}, u32[]{:S(2)}, u32[]{:S(2)}) collective-permute-start(f32[3,64]{1,0:T(4,128)S(1)} %pad_maximum_fusion.1), channel_id=1, source_target_pairs={{0,8},{4,12},{8,0},{12,4},{16,24},{20,28},{24,16},{28,20},{1,9},{5... | collective-permute-start | bytes 2312 | tf_op jit(solution)/shard_map/ppermute | solution.py:70
  70.5 4.5 %collective-permute-start.11 = (f32[3,64]{1,0:T(4,128)S(1)}, f32[3,64]{1,0:T(4,128)S(1)}, u32[]{:S(2)}, u32[]{:S(2)}) collective-permute-start(f32[3,64]{1,0:T(4,128)S(1)} %pad_maximum_fusion.2), channel_id=1, source_target_pairs={{0,16},{4,20},{8,24},{12,28},{16,0},{20,4},{24,8},{28,12},{1,17},{... | collective-permute-start | bytes 2312 | tf_op jit(solution)/shard_map/ppermute | solution.py:70
  75.2 1.2 %collective-permute-start.12 = (f32[256]{0:T(256)S(1)}, f32[256]{0:T(256)S(1)}, u32[]{:S(2)}, u32[]{:S(2)}) collective-permute-start(f32[256]{0:T(256)S(1)} %get-tuple-element.30), channel_id=1, source_target_pairs={{0,1},{1,0},{2,3},{3,2},{4,5},{5,4},{6,7},{7,6},{8,9},{9,8},{10,11... | collective-permute-start | bytes 3080 | tf_op jit(solution)/shard_map/ppermute | solution.py:85
  76.5 3.6 %collective-permute-start.13 = (f32[256]{0:T(256)S(1)}, f32[256]{0:T(256)S(1)}, u32[]{:S(2)}, u32[]{:S(2)}) collective-permute-start(f32[256]{0:T(256)S(1)} %add_dynamic-update-slice_fusion), channel_id=1, source_target_pairs={{0,2},{1,3},{2,0},{3,1},{4,6},{5,7},{6,4},{7,5},{8,10},{9,11},{10,... | collective-permute-start | bytes 3080 | tf_op jit(solution)/shard_map/ppermute | solution.py:85

commit v2 on v1

--- a/solution.py
+++ b/solution.py
@@ -27,7 +27,7 @@
         return list(range(size))
 
 
-def ring_gather(block, ring):
+def ring_gather(block, ring, rows):
     size = len(ring)
     pos_of = np.argsort(np.asarray(ring))
     fwd = [(ring[i], ring[(i + 1) % size]) for i in range(size)]
@@ -41,10 +41,12 @@
         if step < size - step:
             behind = lax.ppermute(behind, "dp", bwd)
             slots[size - step] = behind
-    stacked = jnp.stack(slots)
+    count = block.shape[0]
+    stacked = jnp.stack(slots).reshape(-1, block.shape[1])
     me = jnp.asarray(pos_of, jnp.int32)[lax.axis_index("dp")]
-    pick = (me - jnp.asarray(pos_of, jnp.int32)) % size
-    return jnp.take(stacked, pick, axis=0).reshape(-1, block.shape[1])
+    slot_of = (me - jnp.asarray(pos_of, jnp.int32)) % size
+    where = slot_of[rows // count] * count + rows % count
+    return jnp.take(stacked, where, axis=0)
 
 
 def halving_scatter(partial, size):
@@ -97,11 +99,18 @@
         slot_count = all_rows // MB
         tile_width = head_weight.shape[1]
         col_start = lax.axis_index("dp") * tile_width
-        full_rows = ring_gather(hidden, ring)
+        global_ids = jnp.arange(all_rows, dtype=jnp.int32)
+        lives = jnp.take(lengths, global_ids // slot_count)
+        live_all = (global_ids % slot_count) < lives
+        live_count = all_rows * 5 // 8
+        upto = jnp.cumsum(live_all.astype(jnp.int32))
+        packed = jnp.arange(live_count, dtype=jnp.int32)
+        live_rows = jnp.sum((upto[None, :] <= packed[:, None]).astype(jnp.int32), axis=1)
+        full_rows = ring_gather(hidden, ring, live_rows)
         partial = jnp.dot(full_rows, head_weight, preferred_element_type=jnp.float32)
         logits, first = halving_scatter(partial, vocab_size)
         share = logits.shape[0]
-        row_targets = lax.dynamic_slice_in_dim(targets, first, share)
+        row_targets = jnp.take(targets, lax.dynamic_slice_in_dim(live_rows, first, share))
         highest = jnp.max(logits, axis=1)
         exp_total = jnp.sum(jnp.exp(logits - highest[:, None]), axis=1)
         columns = col_start + lax.broadcasted_iota(jnp.int32, logits.shape, 1)
@@ -109,12 +118,9 @@
         stats = merge_stats(jnp.stack([highest, exp_total, picked]), dp_size)
         logprob = stats[2] - (stats[0] + jnp.log(stats[1]))
         all_values = doubling_gather(logprob, first, vocab_size)
-        own_values = lax.dynamic_slice_in_dim(all_values, lax.axis_index("dp") * row_count, row_count)
-        global_rows = lax.axis_index("dp") * row_count + jnp.arange(row_count, dtype=jnp.int32)
-        batches = jnp.arange(MB, dtype=jnp.int32)
-        member = (global_rows // slot_count)[:, None] == batches[None, :]
-        in_batch = global_rows % slot_count
-        is_live = in_batch < jnp.sum(jnp.where(member, lengths[None, :], 0), axis=1)
+        is_live = lax.dynamic_slice_in_dim(live_all, lax.axis_index("dp") * row_count, row_count)
+        own_slot = jnp.clip(lax.dynamic_slice_in_dim(upto, lax.axis_index("dp") * row_count, row_count) - 1, 0, live_count - 1)
+        own_values = jnp.take(all_values, own_slot)
         ref_logprob = jnp.where(is_live, own_values, 0.0)
         ratio_log = jnp.clip(ref_logprob - policy_logprobs, -20.0, 20.0)
         kl_value = jnp.where(is_live, jnp.minimum(jnp.exp(ratio_log) - ratio_log - 1.0, 10.0), 0.0)

time: 81 us -> 81.7 us (level)
  other arithmetic: 4.52 us -> 14.4 us
  waiting for transfers between devices: 37.8 us -> 33.7 us
  local copies, waits for them, and re-layouts: 10.7 us -> 7.75 us
  starting transfers between devices: 18.7 us -> 17.2 us
    gather x1 -> x7, other arithmetic: 0.01 us -> 8.78 us  [the longest x2 4.43 us: on_device(): lives = jnp.take(lengths, global_ids // slot_count)]
    ppermute x2, waiting for transfers between devices: 14.9 us -> 9.4 us  [halving_scatter(): got = lax.ppermute(send, 'vocab', [(i, i ^ bit) for i in range(size)])]
    unnamed x13 -> x11, local copies, waits for them, and re-layouts: 6.11 us -> 1.12 us
    gather x1 -> x5, local copies, waits for them, and re-layouts: 2.27 us -> 5.17 us  [the longest x1 1.64 us: on_device(): lives = jnp.take(lengths, global_ids // slot_count)]
    select_n x2 -> x5, other arithmetic: 0.26 us -> 1.56 us  [the longest x1 1.31 us: ring_gather(): slot_of = (me - jnp.asarray(pos_of, jnp.int32)) % size]
    add x1, other arithmetic: 1.34 us -> 0.07 us  [halving_scatter(): partial = keep + got]
    ppermute x4, waiting for transfers between devices: 14.4 us -> 15.3 us  [ring_gather(): ahead = lax.ppermute(ahead, 'dp', fwd)]
  transfers between devices with their start and end apart: 14 -> 14, of which waited for: 11 -> 10; matrix products, arithmetic and copies ran while one was open for 9% -> 23% of each run, Pallas kernels for 0% -> 0%
where the time goes in v2:
time: 81.7 us; the launch traced here: 81.3 us
  waiting for transfers between devices  33.7 us (41%)
  starting transfers between devices  17.2 us (21%)
  other arithmetic  14.4 us (18%)
  local copies, waits for them, and re-layouts  7.75 us (9%)
  matrix products  7.4 us (9%)
  between operations  0.95 us (1%)
    ppermute x4, waiting for transfers between devices, ring_gather(): ahead = lax.ppermute(ahead, 'dp', fwd)  15.3 us
    ppermute x2, waiting for transfers between devices, halving_scatter(): got = lax.ppermute(send, 'vocab', [(i, i ^ bit) for i in range(size)])  9.4 us
    ppermute x4, starting transfers between devices, ring_gather(): ahead = lax.ppermute(ahead, 'dp', fwd)  8.4 us
    dot_general x1, matrix products, on_device(): jnp.dot(full_rows, head_weight, preferred_element_type=jnp.float32)  7.4 us
    ppermute x3, waiting for transfers between devices, merge_stats(): other = lax.ppermute(stats, 'dp', [(i, i ^ bit) for i in range(size)])  5.68 us
    ppermute x3, starting transfers between devices, merge_stats(): other = lax.ppermute(stats, 'dp', [(i, i ^ bit) for i in range(size)])  5.51 us
    gather x2, other arithmetic, on_device(): lives = jnp.take(lengths, global_ids // slot_count)  4.43 us
    gather x2, other arithmetic, ring_gather(): where = slot_of[rows // count] * count + rows % count  4.33 us
  transfers between devices with their start and end apart: 14, of which 10 were waited for; matrix products, arithmetic and copies ran while one was open for 23% of the time, Pallas kernels for 0%

profile of v2, /device:TPU:0, one launch (start us, length us, event | category | flops | bytes accessed | tf_op | source)
XLA Modules:
  0.0 81.3 jit_solution(10462141597895369256)
XLA Ops:
  0.6 3.1 %collective-permute-start = (bf16[32,4096]{1,0:T(8,128)(2,1)}, bf16[32,4096]{1,0:T(8,128)(2,1)S(1)}, u32[]{:S(2)}, u32[]{:S(2)}) collective-permute-start(bf16[32,4096]{1,0:T(8,128)(2,1)} %param.11), channel_id=1, source_target_pairs={{0,8},{8,16},{16,24},{24,28},{28,20},{20,12},{12,4},{4,0},{1,9},{9... | collective-permute-start | bytes 786440 | tf_op jit(solution)/shard_map/ppermute | solution.py:39
  4.8 1.6 %fusion.37 = (s32[1]{0:T(128)}, s32[1]{0:T(128)}, s32[1]{0:T(128)}, s32[1]{0:T(128)}, s32[1]{0:T(128)}, /*index=5*/s32[1]{0:T(128)}, s32[1]{0:T(128)}, s32[1]{0:T(128)}) fusion(s32[8]{0:T(128)} %param.13), kind=kLoop, calls=%fused_computation.136 | loop fusion | bytes 64 | tf_op jit(solution)/shard_map/jit(_take)/gather | solution.py:103
  6.4 4.4 %compare_select_fusion.9 = s32[256,1]{0,1:T(1,128)S(1)} fusion(s32[]{:T(128)} %bitcast.1, s32[]{:T(128)} %bitcast.2, s32[]{:T(128)} %bitcast.3, s32[]{:T(128)} %bitcast.4, s32[]{:T(128)} %bitcast.5, s32[]{:T(128)} %bitcast.7, s32[]{:T(128)} %bitcast.6), kind=kLoop, calls=%fused_computation.38 | loop fusion | flops 5888 | bytes 1052 | tf_op jit(solution)/shard_map/jit(_take)/gather | solution.py:103
  12.2 1.2 %dynamic_slice.15 = s32[1]{0:T(128)} dynamic-slice(s32[8]{0:T(128)} %constant.231.clone, s32[]{:T(128)S(6)} %select_n.205), dynamic_slice_sizes={1} | dynamic-slice | bytes 12 | tf_op jit(solution)/shard_map/dynamic_slice | solution.py:46
  13.5 1.3 %and_select_fusion.4 = s32[8]{0:T(128)S(1)} fusion(s32[8]{0:T(128)} %constant.270, s32[]{:T(128)} %bitcast.12), kind=kLoop, calls=%fused_computation.67 | loop fusion | flops 96 | bytes 68 | tf_op jit(solution)/shard_map/jit(remainder)/select_n | solution.py:47
  15.5 4.3 %compare_select_fusion.3 = (s32[160,1]{0,1:T(1,128)S(1)}, s32[160,1]{0,1:T(1,128)S(1)}) fusion(s32[]{:T(128)} %bitcast.14, s32[]{:T(128)} %bitcast.15, s32[]{:T(128)} %bitcast.16, s32[]{:T(128)} %bitcast.17, s32[]{:T(128)} %bitcast.18, s32[]{:T(128)} %bitcast.20, s32[]{:T(128)} %bitcast.19, s32[160,1]{0,1:T(1,128)S(1)} %bitcast.172), kind=kLoop, calls=%fused_computation.31 | loop fusion | flops 4800 | bytes 1948 | tf_op jit(solution)/shard_map/gather | solution.py:48
  20.5 2.1 %collective-permute-start.1 = (bf16[32,4096]{1,0:T(8,128)(2,1)S(1)}, bf16[32,4096]{1,0:T(8,128)(2,1)S(1)}, u32[]{:S(2)}, u32[]{:S(2)}) collective-permute-start(bf16[32,4096]{1,0:T(8,128)(2,1)S(1)} %collective-permute-done), channel_id=1, source_target_pairs={{0,8},{8,16},{16,24},{24,28},{28,20},{20,12},{12,4},{4,0},{1,9},{9... | collective-permute-start | bytes 786440 | tf_op jit(solution)/shard_map/ppermute | solution.py:39
  22.7 5.6 %collective-permute-done.1 = bf16[32,4096]{1,0:T(8,128)(2,1)S(1)} collective-permute-done((bf16[32,4096]{1,0:T(8,128)(2,1)S(1)}, bf16[32,4096]{1,0:T(8,128)(2,1)S(1)}, u32[]{:S(2)}, u32[]{:S(2)}) %collective-permute-start.1) | collective-permute-done | bytes 262176 | tf_op jit(solution)/shard_map/ppermute | solution.py:39
  28.3 1.7 %collective-permute-start.2 = (bf16[32,4096]{1,0:T(8,128)(2,1)S(1)}, bf16[32,4096]{1,0:T(8,128)(2,1)S(1)}, u32[]{:S(2)}, u32[]{:S(2)}) collective-permute-start(bf16[32,4096]{1,0:T(8,128)(2,1)S(1)} %collective-permute-done.1), channel_id=1, source_target_pairs={{0,8},{8,16},{16,24},{24,28},{28,20},{20,12},{12,4},{4,0},{1,9},{9... | collective-permute-start | bytes 786440 | tf_op jit(solution)/shard_map/ppermute | solution.py:39
  30.5 4.8 %collective-permute-done.2 = bf16[32,4096]{1,0:T(8,128)(2,1)S(1)} collective-permute-done((bf16[32,4096]{1,0:T(8,128)(2,1)S(1)}, bf16[32,4096]{1,0:T(8,128)(2,1)S(1)}, u32[]{:S(2)}, u32[]{:S(2)}) %collective-permute-start.2) | collective-permute-done | bytes 262176 | tf_op jit(solution)/shard_map/ppermute | solution.py:39
  35.3 1.5 %collective-permute-start.3 = (bf16[32,4096]{1,0:T(8,128)(2,1)S(1)}, bf16[32,4096]{1,0:T(8,128)(2,1)S(1)}, u32[]{:S(2)}, u32[]{:S(2)}) collective-permute-start(bf16[32,4096]{1,0:T(8,128)(2,1)S(1)} %collective-permute-done.2), channel_id=1, source_target_pairs={{0,8},{8,16},{16,24},{24,28},{28,20},{20,12},{12,4},{4,0},{1,9},{9... | collective-permute-start | bytes 786440 | tf_op jit(solution)/shard_map/ppermute | solution.py:39
  36.7 4.9 %collective-permute-done.3 = bf16[32,4096]{1,0:T(8,128)(2,1)S(1)} collective-permute-done((bf16[32,4096]{1,0:T(8,128)(2,1)S(1)}, bf16[32,4096]{1,0:T(8,128)(2,1)S(1)}, u32[]{:S(2)}, u32[]{:S(2)}) %collective-permute-start.3) | collective-permute-done | bytes 262176 | tf_op jit(solution)/shard_map/ppermute | solution.py:39
  41.7 1.4 %gather_fusion.1 = bf16[160,4096]{1,0:T(8,128)(2,1)S(1)} fusion(bf16[256,4096]{1,0:T(8,128)(2,1)S(1)} %bitcast.167, s32[1024]{0:T(1024)S(1)} %pad_clamp_fusion.1), kind=kCustom, calls=%fused_computation.1 | custom fusion | bytes 2622080 | tf_op jit(solution)/shard_map/jit(_take)/gather | solution.py:49
  43.1 7.4 %fusion = f32[160,2048]{1,0:T(8,128)S(1)} fusion(bf16[4096,2048]{1,0:T(8,128)(2,1)} %param.12, bf16[160,4096]{1,0:T(8,128)(2,1)S(1)} %gather_fusion.1, pred[160]{0:T(512)(128)(4,1)S(1)} %get-tuple-element.36), kind=kOutput, calls=%fused_computation.3 | convolution fusion | flops 2685009920 | bytes 19398816 | tf_op jit(solution)/shard_map/dot_general | solution.py:110
  52.9 1.5 %collective-permute-start.8 = (f32[40,2048]{1,0:T(8,128)S(1)}, f32[40,2048]{1,0:T(8,128)S(1)}, u32[]{:S(2)}, u32[]{:S(2)}) collective-permute-start(f32[40,2048]{1,0:T(8,128)S(1)} %select_bitcast_fusion.1), channel_id=1, source_target_pairs={{0,2},{1,3},{2,0},{3,1},{4,6},{5,7},{6,4},{7,5},{8,10},{9,11},{10,... | collective-permute-start | bytes 983048 | tf_op jit(solution)/shard_map/ppermute | solution.py:62
  54.4 8.3 %collective-permute-done.8 = f32[40,2048]{1,0:T(8,128)S(1)} collective-permute-done((f32[40,2048]{1,0:T(8,128)S(1)}, f32[40,2048]{1,0:T(8,128)S(1)}, u32[]{:S(2)}, u32[]{:S(2)}) %collective-permute-start.8) | collective-permute-done | bytes 327712 | tf_op jit(solution)/shard_map/ppermute | solution.py:62
  63.1 1.4 %collective-permute-start.9 = (f32[3,40]{1,0:T(4,128)S(1)}, f32[3,40]{1,0:T(4,128)S(1)}, u32[]{:S(2)}, u32[]{:S(2)}) collective-permute-start(f32[3,40]{1,0:T(4,128)S(1)} %pad_maximum_fusion), channel_id=1, source_target_pairs={{0,4},{4,0},{8,12},{12,8},{16,20},{20,16},{24,28},{28,24},{1,5},{5... | collective-permute-start | bytes 1448 | tf_op jit(solution)/shard_map/ppermute | solution.py:72
  64.5 2.2 %collective-permute-done.9 = f32[3,40]{1,0:T(4,128)S(1)} collective-permute-done((f32[3,40]{1,0:T(4,128)S(1)}, f32[3,40]{1,0:T(4,128)S(1)}, u32[]{:S(2)}, u32[]{:S(2)}) %collective-permute-start.9) | collective-permute-done | bytes 512 | tf_op jit(solution)/shard_map/ppermute | solution.py:72
  66.8 1.5 %collective-permute-start.10 = (f32[3,40]{1,0:T(4,128)S(1)}, f32[3,40]{1,0:T(4,128)S(1)}, u32[]{:S(2)}, u32[]{:S(2)}) collective-permute-start(f32[3,40]{1,0:T(4,128)S(1)} %pad_maximum_fusion.1), channel_id=1, source_target_pairs={{0,8},{4,12},{8,0},{12,4},{16,24},{20,28},{24,16},{28,20},{1,9},{5... | collective-permute-start | bytes 1448 | tf_op jit(solution)/shard_map/ppermute | solution.py:72
  68.3 2.1 %collective-permute-done.10 = f32[3,40]{1,0:T(4,128)S(1)} collective-permute-done((f32[3,40]{1,0:T(4,128)S(1)}, f32[3,40]{1,0:T(4,128)S(1)}, u32[]{:S(2)}, u32[]{:S(2)}) %collective-permute-start.10) | collective-permute-done | bytes 512 | tf_op jit(solution)/shard_map/ppermute | solution.py:72
  70.5 2.5 %collective-permute-start.11 = (f32[3,40]{1,0:T(4,128)S(1)}, f32[3,40]{1,0:T(4,128)S(1)}, u32[]{:S(2)}, u32[]{:S(2)}) collective-permute-start(f32[3,40]{1,0:T(4,128)S(1)} %pad_maximum_fusion.2), channel_id=1, source_target_pairs={{0,16},{4,20},{8,24},{12,28},{16,0},{20,4},{24,8},{28,12},{1,17},{... | collective-permute-start | bytes 1448 | tf_op jit(solution)/shard_map/ppermute | solution.py:72
  73.7 1.3 %collective-permute-done.11 = f32[3,40]{1,0:T(4,128)S(1)} collective-permute-done((f32[3,40]{1,0:T(4,128)S(1)}, f32[3,40]{1,0:T(4,128)S(1)}, u32[]{:S(2)}, u32[]{:S(2)}) %collective-permute-start.11) | collective-permute-done | bytes 512 | tf_op jit(solution)/shard_map/ppermute | solution.py:72
  76.5 1.4 %collective-permute-start.13 = (f32[160]{0:T(256)S(1)}, f32[160]{0:T(256)S(1)}, u32[]{:S(2)}, u32[]{:S(2)}) collective-permute-start(f32[160]{0:T(256)S(1)} %add_dynamic-update-slice_fusion), channel_id=1, source_target_pairs={{0,2},{1,3},{2,0},{3,1},{4,6},{5,7},{6,4},{7,5},{8,10},{9,11},{10,... | collective-permute-start | bytes 1928 | tf_op jit(solution)/shard_map/ppermute | solution.py:87
  77.9 2.2 %collective-permute-done.13 = f32[160]{0:T(256)S(1)} collective-permute-done((f32[160]{0:T(256)S(1)}, f32[160]{0:T(256)S(1)}, u32[]{:S(2)}, u32[]{:S(2)}) %collective-permute-start.13) | collective-permute-done | bytes 672 | tf_op jit(solution)/shard_map/ppermute | solution.py:87
  (60 shorter events, 10.5 us)
Async XLA Ops:
  0.6 50.2 %copy-start = (s32[256]{0:T(256)S(1)}, s32[256]{0:T(256)}, u32[]{:S(2)}) copy-start(s32[256]{0:T(256)} %param.14) | copy-start | bytes 3076
  0.6 19.9 %collective-permute-start = (bf16[32,4096]{1,0:T(8,128)(2,1)}, bf16[32,4096]{1,0:T(8,128)(2,1)S(1)}, u32[]{:S(2)}, u32[]{:S(2)}) collective-permute-start(bf16[32,4096]{1,0:T(8,128)(2,1)} %param.11), channel_id=1, source_target_pairs={{0,8},{8,16},{16,24},{24,28},{28,20},{20,12},{12,4},{4,0},{1,9},{9... | collective-permute-start | bytes 786440 | tf_op jit(solution)/shard_map/ppermute | solution.py:39
  3.7 18.9 %collective-permute-start.4 = (bf16[32,4096]{1,0:T(8,128)(2,1)}, bf16[32,4096]{1,0:T(8,128)(2,1)S(1)}, u32[]{:S(2)}, u32[]{:S(2)}) collective-permute-start(bf16[32,4096]{1,0:T(8,128)(2,1)} %param.11), channel_id=1, source_target_pairs={{8,0},{16,8},{24,16},{28,24},{20,28},{12,20},{4,12},{0,4},{9,1},{1... | collective-permute-start | bytes 786440 | tf_op jit(solution)/shard_map/ppermute | solution.py:42
  20.5 7.8 %collective-permute-start.1 = (bf16[32,4096]{1,0:T(8,128)(2,1)S(1)}, bf16[32,4096]{1,0:T(8,128)(2,1)S(1)}, u32[]{:S(2)}, u32[]{:S(2)}) collective-permute-start(bf16[32,4096]{1,0:T(8,128)(2,1)S(1)} %collective-permute-done), channel_id=1, source_target_pairs={{0,8},{8,16},{16,24},{24,28},{28,20},{20,12},{12,4},{4,0},{1,9},{9... | collective-permute-start | bytes 786440 | tf_op jit(solution)/shard_map/ppermute | solution.py:39
  22.6 7.5 %collective-permute-start.5 = (bf16[32,4096]{1,0:T(8,128)(2,1)S(1)}, bf16[32,4096]{1,0:T(8,128)(2,1)S(1)}, u32[]{:S(2)}, u32[]{:S(2)}) collective-permute-start(bf16[32,4096]{1,0:T(8,128)(2,1)S(1)} %collective-permute-done.4), channel_id=1, source_target_pairs={{8,0},{16,8},{24,16},{28,24},{20,28},{12,20},{4,12},{0,4},{9,1},{1... | collective-permute-start | bytes 786440 | tf_op jit(solution)/shard_map/ppermute | solution.py:42
  28.3 6.9 %collective-permute-start.2 = (bf16[32,4096]{1,0:T(8,128)(2,1)S(1)}, bf16[32,4096]{1,0:T(8,128)(2,1)S(1)}, u32[]{:S(2)}, u32[]{:S(2)}) collective-permute-start(bf16[32,4096]{1,0:T(8,128)(2,1)S(1)} %collective-permute-done.1), channel_id=1, source_target_pairs={{0,8},{8,16},{16,24},{24,28},{28,20},{20,12},{12,4},{4,0},{1,9},{9... | collective-permute-start | bytes 786440 | tf_op jit(solution)/shard_map/ppermute | solution.py:39
  30.1 11.5 %collective-permute-start.6 = (bf16[32,4096]{1,0:T(8,128)(2,1)S(1)}, bf16[32,4096]{1,0:T(8,128)(2,1)S(1)}, u32[]{:S(2)}, u32[]{:S(2)}) collective-permute-start(bf16[32,4096]{1,0:T(8,128)(2,1)S(1)} %collective-permute-done.5), channel_id=1, source_target_pairs={{8,0},{16,8},{24,16},{28,24},{20,28},{12,20},{4,12},{0,4},{9,1},{1... | collective-permute-start | bytes 786440 | tf_op jit(solution)/shard_map/ppermute | solution.py:42
  35.3 6.4 %collective-permute-start.3 = (bf16[32,4096]{1,0:T(8,128)(2,1)S(1)}, bf16[32,4096]{1,0:T(8,128)(2,1)S(1)}, u32[]{:S(2)}, u32[]{:S(2)}) collective-permute-start(bf16[32,4096]{1,0:T(8,128)(2,1)S(1)} %collective-permute-done.2), channel_id=1, source_target_pairs={{0,8},{8,16},{16,24},{24,28},{28,20},{20,12},{12,4},{4,0},{1,9},{9... | collective-permute-start | bytes 786440 | tf_op jit(solution)/shard_map/ppermute | solution.py:39
  50.6 2.2 %collective-permute-start.7 = (f32[80,2048]{1,0:T(8,128)S(1)}, f32[80,2048]{1,0:T(8,128)S(1)}, u32[]{:S(2)}, u32[]{:S(2)}) collective-permute-start(f32[80,2048]{1,0:T(8,128)S(1)} %select_bitcast_fusion), channel_id=1, source_target_pairs={{0,1},{1,0},{2,3},{3,2},{4,5},{5,4},{6,7},{7,6},{8,9},{9,8},{10,11... | collective-permute-start | bytes 1966088 | tf_op jit(solution)/shard_map/ppermute | solution.py:62
  51.6 29.1 %copy-start.1 = (f32[32]{0:T(128)S(1)}, f32[32]{0:T(128)}, u32[]{:S(2)}) copy-start(f32[32]{0:T(128)} %param.15) | copy-start | bytes 388
  52.9 9.8 %collective-permute-start.8 = (f32[40,2048]{1,0:T(8,128)S(1)}, f32[40,2048]{1,0:T(8,128)S(1)}, u32[]{:S(2)}, u32[]{:S(2)}) collective-permute-start(f32[40,2048]{1,0:T(8,128)S(1)} %select_bitcast_fusion.1), channel_id=1, source_target_pairs={{0,2},{1,3},{2,0},{3,1},{4,6},{5,7},{6,4},{7,5},{8,10},{9,11},{10,... | collective-permute-start | bytes 983048 | tf_op jit(solution)/shard_map/ppermute | solution.py:62
  63.1 3.7 %collective-permute-start.9 = (f32[3,40]{1,0:T(4,128)S(1)}, f32[3,40]{1,0:T(4,128)S(1)}, u32[]{:S(2)}, u32[]{:S(2)}) collective-permute-start(f32[3,40]{1,0:T(4,128)S(1)} %pad_maximum_fusion), channel_id=1, source_target_pairs={{0,4},{4,0},{8,12},{12,8},{16,20},{20,16},{24,28},{28,24},{1,5},{5... | collective-permute-start | bytes 1448 | tf_op jit(solution)/shard_map/ppermute | solution.py:72
  66.8 3.7 %collective-permute-start.10 = (f32[3,40]{1,0:T(4,128)S(1)}, f32[3,40]{1,0:T(4,128)S(1)}, u32[]{:S(2)}, u32[]{:S(2)}) collective-permute-start(f32[3,40]{1,0:T(4,128)S(1)} %pad_maximum_fusion.1), channel_id=1, source_target_pairs={{0,8},{4,12},{8,0},{12,4},{16,24},{20,28},{24,16},{28,20},{1,9},{5... | collective-permute-start | bytes 1448 | tf_op jit(solution)/shard_map/ppermute | solution.py:72
  70.5 4.5 %collective-permute-start.11 = (f32[3,40]{1,0:T(4,128)S(1)}, f32[3,40]{1,0:T(4,128)S(1)}, u32[]{:S(2)}, u32[]{:S(2)}) collective-permute-start(f32[3,40]{1,0:T(4,128)S(1)} %pad_maximum_fusion.2), channel_id=1, source_target_pairs={{0,16},{4,20},{8,24},{12,28},{16,0},{20,4},{24,8},{28,12},{1,17},{... | collective-permute-start | bytes 1448 | tf_op jit(solution)/shard_map/ppermute | solution.py:72
  75.1 1.2 %collective-permute-start.12 = (f32[160]{0:T(256)S(1)}, f32[160]{0:T(256)S(1)}, u32[]{:S(2)}, u32[]{:S(2)}) collective-permute-start(f32[160]{0:T(256)S(1)} %get-tuple-element.30), channel_id=1, source_target_pairs={{0,1},{1,0},{2,3},{3,2},{4,5},{5,4},{6,7},{7,6},{8,9},{9,8},{10,11... | collective-permute-start | bytes 1928 | tf_op jit(solution)/shard_map/ppermute | solution.py:87
  76.5 3.6 %collective-permute-start.13 = (f32[160]{0:T(256)S(1)}, f32[160]{0:T(256)S(1)}, u32[]{:S(2)}, u32[]{:S(2)}) collective-permute-start(f32[160]{0:T(256)S(1)} %add_dynamic-update-slice_fusion), channel_id=1, source_target_pairs={{0,2},{1,3},{2,0},{3,1},{4,6},{5,7},{6,4},{7,5},{8,10},{9,11},{10,... | collective-permute-start | bytes 1928 | tf_op jit(solution)/shard_map/ppermute | solution.py:87

commit v3 on v2

--- a/solution.py
+++ b/solution.py
@@ -99,13 +99,12 @@
         slot_count = all_rows // MB
         tile_width = head_weight.shape[1]
         col_start = lax.axis_index("dp") * tile_width
-        global_ids = jnp.arange(all_rows, dtype=jnp.int32)
-        lives = jnp.take(lengths, global_ids // slot_count)
-        live_all = (global_ids % slot_count) < lives
         live_count = all_rows * 5 // 8
-        upto = jnp.cumsum(live_all.astype(jnp.int32))
+        ends = jnp.cumsum(lengths)
+        starts = ends - lengths
         packed = jnp.arange(live_count, dtype=jnp.int32)
-        live_rows = jnp.sum((upto[None, :] <= packed[:, None]).astype(jnp.int32), axis=1)
+        batch_of = jnp.sum((ends[None, :] <= packed[:, None]).astype(jnp.int32), axis=1)
+        live_rows = batch_of * slot_count + packed - jnp.take(starts, batch_of)
         full_rows = ring_gather(hidden, ring, live_rows)
         partial = jnp.dot(full_rows, head_weight, preferred_element_type=jnp.float32)
         logits, first = halving_scatter(partial, vocab_size)
@@ -118,8 +117,10 @@
         stats = merge_stats(jnp.stack([highest, exp_total, picked]), dp_size)
         logprob = stats[2] - (stats[0] + jnp.log(stats[1]))
         all_values = doubling_gather(logprob, first, vocab_size)
-        is_live = lax.dynamic_slice_in_dim(live_all, lax.axis_index("dp") * row_count, row_count)
-        own_slot = jnp.clip(lax.dynamic_slice_in_dim(upto, lax.axis_index("dp") * row_count, row_count) - 1, 0, live_count - 1)
+        own_rows = lax.axis_index("dp") * row_count + jnp.arange(row_count, dtype=jnp.int32)
+        own_batch = own_rows // slot_count
+        is_live = own_rows % slot_count < jnp.take(lengths, own_batch)
+        own_slot = jnp.clip(jnp.take(starts, own_batch) + own_rows % slot_count, 0, live_count - 1)
         own_values = jnp.take(all_values, own_slot)
         ref_logprob = jnp.where(is_live, own_values, 0.0)
         ratio_log = jnp.clip(ref_logprob - policy_logprobs, -20.0, 20.0)

time: 81.7 us -> 81.7 us (level)
    gather x2 -> x4, other arithmetic: 4.43 us -> 5.14 us  [the longest x3 5.13 us: on_device(): live_rows = batch_of * slot_count + packed - jnp.take(starts, batch_of)]
    gather x1 -> x3, local copies, waits for them, and re-layouts: 1.64 us -> 2.08 us  [the longest x1 0.7 us: on_device(): is_live = own_rows % slot_count < jnp.take(lengths, own_batch)]
  transfers between devices with their start and end apart: 14 -> 14, of which waited for: 10 -> 10; matrix products, arithmetic and copies ran while one was open for 23% -> 24% of each run, Pallas kernels for 0% -> 0%
where the time goes in v3:
time: 81.7 us; the launch traced here: 81.4 us
  waiting for transfers between devices  33.2 us (41%)
  starting transfers between devices  17 us (21%)
  other arithmetic  14.7 us (18%)
  local copies, waits for them, and re-layouts  8.08 us (10%)
  matrix products  7.44 us (9%)
  between operations  0.96 us (1%)
    ppermute x4, waiting for transfers between devices, ring_gather(): ahead = lax.ppermute(ahead, 'dp', fwd)  15.4 us
    ppermute x2, waiting for transfers between devices, halving_scatter(): got = lax.ppermute(send, 'vocab', [(i, i ^ bit) for i in range(size)])  9.43 us
    ppermute x4, starting transfers between devices, ring_gather(): ahead = lax.ppermute(ahead, 'dp', fwd)  8.28 us
    dot_general x1, matrix products, on_device(): jnp.dot(full_rows, head_weight, preferred_element_type=jnp.float32)  7.44 us
    ppermute x3, waiting for transfers between devices, merge_stats(): other = lax.ppermute(stats, 'dp', [(i, i ^ bit) for i in range(size)])  5.73 us
    ppermute x3, starting transfers between devices, merge_stats(): other = lax.ppermute(stats, 'dp', [(i, i ^ bit) for i in range(size)])  5.4 us
    gather x3, other arithmetic, on_device(): live_rows = batch_of * slot_count + packed - jnp.take(starts, batch_of)  5.13 us
    gather x2, other arithmetic, ring_gather(): where = slot_of[rows // count] * count + rows % count  4.4 us
  transfers between devices with their start and end apart: 14, of which 10 were waited for; matrix products, arithmetic and copies ran while one was open for 24% of the time, Pallas kernels for 0%

profile of v3, /device:TPU:0, one launch (start us, length us, event | category | flops | bytes accessed | tf_op | source)
XLA Modules:
  0.0 81.4 jit_solution(10420511953778576664)
XLA Ops:
  0.6 3.1 %collective-permute-start = (bf16[32,4096]{1,0:T(8,128)(2,1)}, bf16[32,4096]{1,0:T(8,128)(2,1)S(1)}, u32[]{:S(2)}, u32[]{:S(2)}) collective-permute-start(bf16[32,4096]{1,0:T(8,128)(2,1)} %param.13), channel_id=1, source_target_pairs={{0,8},{8,16},{16,24},{24,28},{28,20},{20,12},{12,4},{4,0},{1,9},{9... | collective-permute-start | bytes 786440 | tf_op jit(solution)/shard_map/ppermute | solution.py:39
  7.1 1.3 %dynamic_slice.7 = s32[1]{0:T(128)} dynamic-slice(s32[8]{0:T(128)} %constant.225.clone, s32[]{:T(128)S(6)} %select_n.204), dynamic_slice_sizes={1} | dynamic-slice | bytes 12 | tf_op jit(solution)/shard_map/dynamic_slice | solution.py:46
  8.4 1.3 %and_select_fusion.4 = s32[8]{0:T(128)S(1)} fusion(s32[8]{0:T(128)} %constant.264, s32[]{:T(128)} %bitcast.13), kind=kLoop, calls=%fused_computation.68 | loop fusion | flops 96 | bytes 68 | tf_op jit(solution)/shard_map/jit(remainder)/select_n | solution.py:47
  10.4 4.5 %compare_select_fusion.9 = s32[160,1]{0,1:T(1,128)S(1)} fusion(s32[]{:T(128)} %bitcast.4, s32[]{:T(128)} %bitcast.5, s32[]{:T(128)} %bitcast.6, s32[]{:T(128)} %bitcast.7, s32[]{:T(128)} %bitcast.8, s32[]{:T(128)} %bitcast.10, s32[]{:T(128)} %bitcast.9, s32[160,1]{0,1:T(1,128)S(1)} %bitcast.176), kind=kLoop, calls=%fused_computation.41 | loop fusion | flops 2400 | bytes 1308 | tf_op jit(solution)/shard_map/jit(_take)/gather | solution.py:107
  15.5 4.4 %compare_select_fusion.3 = (s32[160,1]{0,1:T(1,128)S(1)}, s32[160,1]{0,1:T(1,128)S(1)}, s32[160,1]{0,1:T(1,128)S(1)}) fusion(s32[]{:T(128)} %bitcast.15, s32[]{:T(128)} %bitcast.16, s32[]{:T(128)} %bitcast.17, s32[]{:T(128)} %bitcast.18, s32[]{:T(128)} %bitcast.19, s32[]{:T(128)} %bitcast.21, s32[]{:T(128)} %bitcast.20, s32[160,1]{0,1:T(1,128)S(1)} %bitcast.174, ...), kind=kLoop, calls=%fused_computation.34 | loop fusion | flops 6400 | bytes 3228 | tf_op jit(solution)/shard_map/gather | solution.py:48
  20.6 2.0 %collective-permute-start.1 = (bf16[32,4096]{1,0:T(8,128)(2,1)S(1)}, bf16[32,4096]{1,0:T(8,128)(2,1)S(1)}, u32[]{:S(2)}, u32[]{:S(2)}) collective-permute-start(bf16[32,4096]{1,0:T(8,128)(2,1)S(1)} %collective-permute-done), channel_id=1, source_target_pairs={{0,8},{8,16},{16,24},{24,28},{28,20},{20,12},{12,4},{4,0},{1,9},{9... | collective-permute-start | bytes 786440 | tf_op jit(solution)/shard_map/ppermute | solution.py:39
  22.8 5.7 %collective-permute-done.1 = bf16[32,4096]{1,0:T(8,128)(2,1)S(1)} collective-permute-done((bf16[32,4096]{1,0:T(8,128)(2,1)S(1)}, bf16[32,4096]{1,0:T(8,128)(2,1)S(1)}, u32[]{:S(2)}, u32[]{:S(2)}) %collective-permute-start.1) | collective-permute-done | bytes 262176 | tf_op jit(solution)/shard_map/ppermute | solution.py:39
  28.4 1.7 %collective-permute-start.2 = (bf16[32,4096]{1,0:T(8,128)(2,1)S(1)}, bf16[32,4096]{1,0:T(8,128)(2,1)S(1)}, u32[]{:S(2)}, u32[]{:S(2)}) collective-permute-start(bf16[32,4096]{1,0:T(8,128)(2,1)S(1)} %collective-permute-done.1), channel_id=1, source_target_pairs={{0,8},{8,16},{16,24},{24,28},{28,20},{20,12},{12,4},{4,0},{1,9},{9... | collective-permute-start | bytes 786440 | tf_op jit(solution)/shard_map/ppermute | solution.py:39
  30.5 4.8 %collective-permute-done.2 = bf16[32,4096]{1,0:T(8,128)(2,1)S(1)} collective-permute-done((bf16[32,4096]{1,0:T(8,128)(2,1)S(1)}, bf16[32,4096]{1,0:T(8,128)(2,1)S(1)}, u32[]{:S(2)}, u32[]{:S(2)}) %collective-permute-start.2) | collective-permute-done | bytes 262176 | tf_op jit(solution)/shard_map/ppermute | solution.py:39
  35.3 1.4 %collective-permute-start.3 = (bf16[32,4096]{1,0:T(8,128)(2,1)S(1)}, bf16[32,4096]{1,0:T(8,128)(2,1)S(1)}, u32[]{:S(2)}, u32[]{:S(2)}) collective-permute-start(bf16[32,4096]{1,0:T(8,128)(2,1)S(1)} %collective-permute-done.2), channel_id=1, source_target_pairs={{0,8},{8,16},{16,24},{24,28},{28,20},{20,12},{12,4},{4,0},{1,9},{9... | collective-permute-start | bytes 786440 | tf_op jit(solution)/shard_map/ppermute | solution.py:39
  36.8 4.9 %collective-permute-done.3 = bf16[32,4096]{1,0:T(8,128)(2,1)S(1)} collective-permute-done((bf16[32,4096]{1,0:T(8,128)(2,1)S(1)}, bf16[32,4096]{1,0:T(8,128)(2,1)S(1)}, u32[]{:S(2)}, u32[]{:S(2)}) %collective-permute-start.3) | collective-permute-done | bytes 262176 | tf_op jit(solution)/shard_map/ppermute | solution.py:39
  41.8 1.4 %gather_fusion.1 = bf16[160,4096]{1,0:T(8,128)(2,1)S(1)} fusion(bf16[256,4096]{1,0:T(8,128)(2,1)S(1)} %bitcast.168, s32[1024]{0:T(1024)S(1)} %pad_clamp_fusion.1), kind=kCustom, calls=%fused_computation.3 | custom fusion | bytes 2622080 | tf_op jit(solution)/shard_map/jit(_take)/gather | solution.py:49
  43.2 7.4 %fusion = f32[160,2048]{1,0:T(8,128)S(1)} fusion(bf16[4096,2048]{1,0:T(8,128)(2,1)} %param.14, bf16[160,4096]{1,0:T(8,128)(2,1)S(1)} %gather_fusion.1, pred[160]{0:T(512)(128)(4,1)S(1)} %get-tuple-element.37), kind=kOutput, calls=%fused_computation.5 | convolution fusion | flops 2685009920 | bytes 19398816 | tf_op jit(solution)/shard_map/dot_general | solution.py:109
  51.7 1.1 %collective-permute-done.7 = f32[80,2048]{1,0:T(8,128)S(1)} collective-permute-done((f32[80,2048]{1,0:T(8,128)S(1)}, f32[80,2048]{1,0:T(8,128)S(1)}, u32[]{:S(2)}, u32[]{:S(2)}) %collective-permute-start.7) | collective-permute-done | bytes 655392 | tf_op jit(solution)/shard_map/ppermute | solution.py:62
  53.0 1.4 %collective-permute-start.8 = (f32[40,2048]{1,0:T(8,128)S(1)}, f32[40,2048]{1,0:T(8,128)S(1)}, u32[]{:S(2)}, u32[]{:S(2)}) collective-permute-start(f32[40,2048]{1,0:T(8,128)S(1)} %select_bitcast_fusion.1), channel_id=1, source_target_pairs={{0,2},{1,3},{2,0},{3,1},{4,6},{5,7},{6,4},{7,5},{8,10},{9,11},{10,... | collective-permute-start | bytes 983048 | tf_op jit(solution)/shard_map/ppermute | solution.py:62
  54.5 8.3 %collective-permute-done.8 = f32[40,2048]{1,0:T(8,128)S(1)} collective-permute-done((f32[40,2048]{1,0:T(8,128)S(1)}, f32[40,2048]{1,0:T(8,128)S(1)}, u32[]{:S(2)}, u32[]{:S(2)}) %collective-permute-start.8) | collective-permute-done | bytes 327712 | tf_op jit(solution)/shard_map/ppermute | solution.py:62
  63.2 1.4 %collective-permute-start.9 = (f32[3,40]{1,0:T(4,128)S(1)}, f32[3,40]{1,0:T(4,128)S(1)}, u32[]{:S(2)}, u32[]{:S(2)}) collective-permute-start(f32[3,40]{1,0:T(4,128)S(1)} %pad_maximum_fusion), channel_id=1, source_target_pairs={{0,4},{4,0},{8,12},{12,8},{16,20},{20,16},{24,28},{28,24},{1,5},{5... | collective-permute-start | bytes 1448 | tf_op jit(solution)/shard_map/ppermute | solution.py:72
  64.6 2.2 %collective-permute-done.9 = f32[3,40]{1,0:T(4,128)S(1)} collective-permute-done((f32[3,40]{1,0:T(4,128)S(1)}, f32[3,40]{1,0:T(4,128)S(1)}, u32[]{:S(2)}, u32[]{:S(2)}) %collective-permute-start.9) | collective-permute-done | bytes 512 | tf_op jit(solution)/shard_map/ppermute | solution.py:72
  66.9 1.5 %collective-permute-start.10 = (f32[3,40]{1,0:T(4,128)S(1)}, f32[3,40]{1,0:T(4,128)S(1)}, u32[]{:S(2)}, u32[]{:S(2)}) collective-permute-start(f32[3,40]{1,0:T(4,128)S(1)} %pad_maximum_fusion.1), channel_id=1, source_target_pairs={{0,8},{4,12},{8,0},{12,4},{16,24},{20,28},{24,16},{28,20},{1,9},{5... | collective-permute-start | bytes 1448 | tf_op jit(solution)/shard_map/ppermute | solution.py:72
  68.4 2.1 %collective-permute-done.10 = f32[3,40]{1,0:T(4,128)S(1)} collective-permute-done((f32[3,40]{1,0:T(4,128)S(1)}, f32[3,40]{1,0:T(4,128)S(1)}, u32[]{:S(2)}, u32[]{:S(2)}) %collective-permute-start.10) | collective-permute-done | bytes 512 | tf_op jit(solution)/shard_map/ppermute | solution.py:72
  70.6 2.5 %collective-permute-start.11 = (f32[3,40]{1,0:T(4,128)S(1)}, f32[3,40]{1,0:T(4,128)S(1)}, u32[]{:S(2)}, u32[]{:S(2)}) collective-permute-start(f32[3,40]{1,0:T(4,128)S(1)} %pad_maximum_fusion.2), channel_id=1, source_target_pairs={{0,16},{4,20},{8,24},{12,28},{16,0},{20,4},{24,8},{28,12},{1,17},{... | collective-permute-start | bytes 1448 | tf_op jit(solution)/shard_map/ppermute | solution.py:72
  73.8 1.3 %collective-permute-done.11 = f32[3,40]{1,0:T(4,128)S(1)} collective-permute-done((f32[3,40]{1,0:T(4,128)S(1)}, f32[3,40]{1,0:T(4,128)S(1)}, u32[]{:S(2)}, u32[]{:S(2)}) %collective-permute-start.11) | collective-permute-done | bytes 512 | tf_op jit(solution)/shard_map/ppermute | solution.py:72
  76.6 1.4 %collective-permute-start.13 = (f32[160]{0:T(256)S(1)}, f32[160]{0:T(256)S(1)}, u32[]{:S(2)}, u32[]{:S(2)}) collective-permute-start(f32[160]{0:T(256)S(1)} %add_dynamic-update-slice_fusion), channel_id=1, source_target_pairs={{0,2},{1,3},{2,0},{3,1},{4,6},{5,7},{6,4},{7,5},{8,10},{9,11},{10,... | collective-permute-start | bytes 1928 | tf_op jit(solution)/shard_map/ppermute | solution.py:87
  78.6 1.5 %collective-permute-done.13 = f32[160]{0:T(256)S(1)} collective-permute-done((f32[160]{0:T(256)S(1)}, f32[160]{0:T(256)S(1)}, u32[]{:S(2)}, u32[]{:S(2)}) %collective-permute-start.13) | collective-permute-done | bytes 672 | tf_op jit(solution)/shard_map/ppermute | solution.py:87
  (62 shorter events, 11.7 us)
Async XLA Ops:
  0.6 50.3 %copy-start = (s32[256]{0:T(256)S(1)}, s32[256]{0:T(256)}, u32[]{:S(2)}) copy-start(s32[256]{0:T(256)} %param.16) | copy-start | bytes 3076
  0.6 19.9 %collective-permute-start = (bf16[32,4096]{1,0:T(8,128)(2,1)}, bf16[32,4096]{1,0:T(8,128)(2,1)S(1)}, u32[]{:S(2)}, u32[]{:S(2)}) collective-permute-start(bf16[32,4096]{1,0:T(8,128)(2,1)} %param.13), channel_id=1, source_target_pairs={{0,8},{8,16},{16,24},{24,28},{28,20},{20,12},{12,4},{4,0},{1,9},{9... | collective-permute-start | bytes 786440 | tf_op jit(solution)/shard_map/ppermute | solution.py:39
  3.7 18.9 %collective-permute-start.4 = (bf16[32,4096]{1,0:T(8,128)(2,1)}, bf16[32,4096]{1,0:T(8,128)(2,1)S(1)}, u32[]{:S(2)}, u32[]{:S(2)}) collective-permute-start(bf16[32,4096]{1,0:T(8,128)(2,1)} %param.13), channel_id=1, source_target_pairs={{8,0},{16,8},{24,16},{28,24},{20,28},{12,20},{4,12},{0,4},{9,1},{1... | collective-permute-start | bytes 786440 | tf_op jit(solution)/shard_map/ppermute | solution.py:42
  20.6 7.8 %collective-permute-start.1 = (bf16[32,4096]{1,0:T(8,128)(2,1)S(1)}, bf16[32,4096]{1,0:T(8,128)(2,1)S(1)}, u32[]{:S(2)}, u32[]{:S(2)}) collective-permute-start(bf16[32,4096]{1,0:T(8,128)(2,1)S(1)} %collective-permute-done), channel_id=1, source_target_pairs={{0,8},{8,16},{16,24},{24,28},{28,20},{20,12},{12,4},{4,0},{1,9},{9... | collective-permute-start | bytes 786440 | tf_op jit(solution)/shard_map/ppermute | solution.py:39
  22.7 7.5 %collective-permute-start.5 = (bf16[32,4096]{1,0:T(8,128)(2,1)S(1)}, bf16[32,4096]{1,0:T(8,128)(2,1)S(1)}, u32[]{:S(2)}, u32[]{:S(2)}) collective-permute-start(bf16[32,4096]{1,0:T(8,128)(2,1)S(1)} %collective-permute-done.4), channel_id=1, source_target_pairs={{8,0},{16,8},{24,16},{28,24},{20,28},{12,20},{4,12},{0,4},{9,1},{1... | collective-permute-start | bytes 786440 | tf_op jit(solution)/shard_map/ppermute | solution.py:42
  28.4 6.9 %collective-permute-start.2 = (bf16[32,4096]{1,0:T(8,128)(2,1)S(1)}, bf16[32,4096]{1,0:T(8,128)(2,1)S(1)}, u32[]{:S(2)}, u32[]{:S(2)}) collective-permute-start(bf16[32,4096]{1,0:T(8,128)(2,1)S(1)} %collective-permute-done.1), channel_id=1, source_target_pairs={{0,8},{8,16},{16,24},{24,28},{28,20},{20,12},{12,4},{4,0},{1,9},{9... | collective-permute-start | bytes 786440 | tf_op jit(solution)/shard_map/ppermute | solution.py:39
  30.2 11.6 %collective-permute-start.6 = (bf16[32,4096]{1,0:T(8,128)(2,1)S(1)}, bf16[32,4096]{1,0:T(8,128)(2,1)S(1)}, u32[]{:S(2)}, u32[]{:S(2)}) collective-permute-start(bf16[32,4096]{1,0:T(8,128)(2,1)S(1)} %collective-permute-done.5), channel_id=1, source_target_pairs={{8,0},{16,8},{24,16},{28,24},{20,28},{12,20},{4,12},{0,4},{9,1},{1... | collective-permute-start | bytes 786440 | tf_op jit(solution)/shard_map/ppermute | solution.py:42
  35.3 6.4 %collective-permute-start.3 = (bf16[32,4096]{1,0:T(8,128)(2,1)S(1)}, bf16[32,4096]{1,0:T(8,128)(2,1)S(1)}, u32[]{:S(2)}, u32[]{:S(2)}) collective-permute-start(bf16[32,4096]{1,0:T(8,128)(2,1)S(1)} %collective-permute-done.2), channel_id=1, source_target_pairs={{0,8},{8,16},{16,24},{24,28},{28,20},{20,12},{12,4},{4,0},{1,9},{9... | collective-permute-start | bytes 786440 | tf_op jit(solution)/shard_map/ppermute | solution.py:39
  50.7 2.2 %collective-permute-start.7 = (f32[80,2048]{1,0:T(8,128)S(1)}, f32[80,2048]{1,0:T(8,128)S(1)}, u32[]{:S(2)}, u32[]{:S(2)}) collective-permute-start(f32[80,2048]{1,0:T(8,128)S(1)} %select_bitcast_fusion), channel_id=1, source_target_pairs={{0,1},{1,0},{2,3},{3,2},{4,5},{5,4},{6,7},{7,6},{8,9},{9,8},{10,11... | collective-permute-start | bytes 1966088 | tf_op jit(solution)/shard_map/ppermute | solution.py:62
  51.7 26.2 %copy-start.1 = (s32[8]{0:T(128)S(1)}, s32[8]{0:T(128)}, u32[]{:S(2)}) copy-start(s32[8]{0:T(128)} %param.15) | copy-start | bytes 100
  52.9 27.9 %copy-start.2 = (f32[32]{0:T(128)S(1)}, f32[32]{0:T(128)}, u32[]{:S(2)}) copy-start(f32[32]{0:T(128)} %param.17) | copy-start | bytes 388
  53.0 9.8 %collective-permute-start.8 = (f32[40,2048]{1,0:T(8,128)S(1)}, f32[40,2048]{1,0:T(8,128)S(1)}, u32[]{:S(2)}, u32[]{:S(2)}) collective-permute-start(f32[40,2048]{1,0:T(8,128)S(1)} %select_bitcast_fusion.1), channel_id=1, source_target_pairs={{0,2},{1,3},{2,0},{3,1},{4,6},{5,7},{6,4},{7,5},{8,10},{9,11},{10,... | collective-permute-start | bytes 983048 | tf_op jit(solution)/shard_map/ppermute | solution.py:62
  63.2 3.7 %collective-permute-start.9 = (f32[3,40]{1,0:T(4,128)S(1)}, f32[3,40]{1,0:T(4,128)S(1)}, u32[]{:S(2)}, u32[]{:S(2)}) collective-permute-start(f32[3,40]{1,0:T(4,128)S(1)} %pad_maximum_fusion), channel_id=1, source_target_pairs={{0,4},{4,0},{8,12},{12,8},{16,20},{20,16},{24,28},{28,24},{1,5},{5... | collective-permute-start | bytes 1448 | tf_op jit(solution)/shard_map/ppermute | solution.py:72
  66.9 3.7 %collective-permute-start.10 = (f32[3,40]{1,0:T(4,128)S(1)}, f32[3,40]{1,0:T(4,128)S(1)}, u32[]{:S(2)}, u32[]{:S(2)}) collective-permute-start(f32[3,40]{1,0:T(4,128)S(1)} %pad_maximum_fusion.1), channel_id=1, source_target_pairs={{0,8},{4,12},{8,0},{12,4},{16,24},{20,28},{24,16},{28,20},{1,9},{5... | collective-permute-start | bytes 1448 | tf_op jit(solution)/shard_map/ppermute | solution.py:72
  70.6 4.5 %collective-permute-start.11 = (f32[3,40]{1,0:T(4,128)S(1)}, f32[3,40]{1,0:T(4,128)S(1)}, u32[]{:S(2)}, u32[]{:S(2)}) collective-permute-start(f32[3,40]{1,0:T(4,128)S(1)} %pad_maximum_fusion.2), channel_id=1, source_target_pairs={{0,16},{4,20},{8,24},{12,28},{16,0},{20,4},{24,8},{28,12},{1,17},{... | collective-permute-start | bytes 1448 | tf_op jit(solution)/shard_map/ppermute | solution.py:72
  75.2 1.2 %collective-permute-start.12 = (f32[160]{0:T(256)S(1)}, f32[160]{0:T(256)S(1)}, u32[]{:S(2)}, u32[]{:S(2)}) collective-permute-start(f32[160]{0:T(256)S(1)} %get-tuple-element.31), channel_id=1, source_target_pairs={{0,1},{1,0},{2,3},{3,2},{4,5},{5,4},{6,7},{7,6},{8,9},{9,8},{10,11... | collective-permute-start | bytes 1928 | tf_op jit(solution)/shard_map/ppermute | solution.py:87
  76.6 3.6 %collective-permute-start.13 = (f32[160]{0:T(256)S(1)}, f32[160]{0:T(256)S(1)}, u32[]{:S(2)}, u32[]{:S(2)}) collective-permute-start(f32[160]{0:T(256)S(1)} %add_dynamic-update-slice_fusion), channel_id=1, source_target_pairs={{0,2},{1,3},{2,0},{3,1},{4,6},{5,7},{6,4},{7,5},{8,10},{9,11},{10,... | collective-permute-start | bytes 1928 | tf_op jit(solution)/shard_map/ppermute | solution.py:87

commit v4 on v3

--- a/solution.py
+++ b/solution.py
@@ -45,8 +45,12 @@
     stacked = jnp.stack(slots).reshape(-1, block.shape[1])
     me = jnp.asarray(pos_of, jnp.int32)[lax.axis_index("dp")]
     slot_of = (me - jnp.asarray(pos_of, jnp.int32)) % size
-    where = slot_of[rows // count] * count + rows % count
-    return jnp.take(stacked, where, axis=0)
+    owner = rows // count
+    hit = owner[None, :] == jnp.arange(size, dtype=jnp.int32)[:, None]
+    where = jnp.sum(jnp.where(hit, slot_of[:, None], 0), axis=0) * count + rows % count
+    choose = lax.broadcasted_iota(jnp.int32, (stacked.shape[0], where.shape[0]), 0) == where[None, :]
+    picked = lax.dot_general(choose.astype(stacked.dtype), stacked, (((0,), (0,)), ((), ())), preferred_element_type=jnp.float32)
+    return picked.astype(stacked.dtype)
 
 
 def halving_scatter(partial, size):
@@ -103,8 +107,10 @@
         ends = jnp.cumsum(lengths)
         starts = ends - lengths
         packed = jnp.arange(live_count, dtype=jnp.int32)
-        batch_of = jnp.sum((ends[None, :] <= packed[:, None]).astype(jnp.int32), axis=1)
-        live_rows = batch_of * slot_count + packed - jnp.take(starts, batch_of)
+        batch_hit = ends[:, None] <= packed[None, :]
+        batch_of = jnp.sum(batch_hit.astype(jnp.int32), axis=0)
+        in_batch = packed - jnp.sum(jnp.where(batch_of[None, :] == jnp.arange(MB, dtype=jnp.int32)[:, None], starts[:, None], 0), axis=0)
+        live_rows = batch_of * slot_count + in_batch
         full_rows = ring_gather(hidden, ring, live_rows)
         partial = jnp.dot(full_rows, head_weight, preferred_element_type=jnp.float32)
         logits, first = halving_scatter(partial, vocab_size)

time: 81.7 us -> 69.4 us (0.85)
  other arithmetic: 14.7 us -> 4.72 us
  local copies, waits for them, and re-layouts: 8.08 us -> 5.32 us
  starting transfers between devices: 17 us -> 18.8 us
  waiting for transfers between devices: 33.2 us -> 31.8 us
    gather x7 -> x1, other arithmetic: 9.55 us -> 0.01 us  [the longest x3 5.13 us: on_device(): live_rows = batch_of * slot_count + packed - jnp.take(starts, batch_of)]
    gather x3 -> x0, local copies, waits for them, and re-layouts: 2.74 us -> none  [the longest x1 1.36 us: ring_gather(): return jnp.take(stacked, where, axis=0)]
    ppermute x3, waiting for transfers between devices: 5.73 us -> 4.82 us  [merge_stats(): other = lax.ppermute(stats, 'dp', [(i, i ^ bit) for i in range(size)])]
    ppermute x3, starting transfers between devices: 5.4 us -> 6.32 us  [merge_stats(): other = lax.ppermute(stats, 'dp', [(i, i ^ bit) for i in range(size)])]
  transfers between devices with their start and end apart: 14 -> 14, of which waited for: 10 -> 11; matrix products, arithmetic and copies ran while one was open for 24% -> 11% of each run, Pallas kernels for 0% -> 0%
where the time goes in v4:
time: 69.4 us; the launch traced here: 69.2 us
  waiting for transfers between devices  31.8 us (46%)
  starting transfers between devices  18.8 us (27%)
  matrix products  7.71 us (11%)
  local copies, waits for them, and re-layouts  5.32 us (8%)
  other arithmetic  4.72 us (7%)
  between operations  0.91 us (1%)
    ppermute x4, waiting for transfers between devices, ring_gather(): ahead = lax.ppermute(ahead, 'dp', fwd)  15.5 us
    ppermute x2, waiting for transfers between devices, halving_scatter(): got = lax.ppermute(send, 'vocab', [(i, i ^ bit) for i in range(size)])  9.12 us
    ppermute x4, starting transfers between devices, ring_gather(): ahead = lax.ppermute(ahead, 'dp', fwd)  8.21 us
    dot_general x1, matrix products, on_device(): jnp.dot(full_rows, head_weight, preferred_element_type=jnp.float32)  7.71 us
    ppermute x3, starting transfers between devices, merge_stats(): other = lax.ppermute(stats, 'dp', [(i, i ^ bit) for i in range(size)])  6.32 us
    ppermute x3, waiting for transfers between devices, merge_stats(): other = lax.ppermute(stats, 'dp', [(i, i ^ bit) for i in range(size)])  4.82 us
    ppermute x2, waiting for transfers between devices, doubling_gather(): other = lax.ppermute(out, 'vocab', [(i, i ^ bit) for i in range(size)])  2.32 us
    ppermute x2, starting transfers between devices, halving_scatter(): got = lax.ppermute(send, 'vocab', [(i, i ^ bit) for i in range(size)])  1.81 us
  transfers between devices with their start and end apart: 14, of which 11 were waited for; matrix products, arithmetic and copies ran while one was open for 11% of the time, Pallas kernels for 0%

profile of v4, /device:TPU:0, one launch (start us, length us, event | category | flops | bytes accessed | tf_op | source)
XLA Modules:
  0.0 69.2 jit_solution(1905964468807112302)
XLA Ops:
  0.6 3.1 %collective-permute-start = (bf16[32,4096]{1,0:T(8,128)(2,1)}, bf16[32,4096]{1,0:T(8,128)(2,1)S(1)}, u32[]{:S(2)}, u32[]{:S(2)}) collective-permute-start(bf16[32,4096]{1,0:T(8,128)(2,1)} %param.13), channel_id=1, source_target_pairs={{0,8},{8,16},{16,24},{24,28},{28,20},{20,12},{12,4},{4,0},{1,9},{9... | collective-permute-start | bytes 786440 | tf_op jit(solution)/shard_map/ppermute | solution.py:39
  3.8 1.0 %bitcast_dynamic-update-slice_fusion.7 = bf16[8,32,4096]{2,1,0:T(8,128)(2,1)S(1)} fusion(bf16[32,4096]{1,0:T(8,128)(2,1)} %param.13), kind=kLoop, calls=%fused_computation.19 | loop fusion | bytes 524288
  6.5 1.2 %dynamic_slice.7 = s32[1]{0:T(128)} dynamic-slice(s32[8]{0:T(128)} %constant.196.clone, s32[]{:T(128)S(6)} %select_n.127), dynamic_slice_sizes={1} | dynamic-slice | bytes 12 | tf_op jit(solution)/shard_map/dynamic_slice | solution.py:46
  7.7 1.3 %and_select_fusion.1 = s32[8]{0:T(128)S(1)} fusion(s32[8]{0:T(128)} %constant.235, s32[]{:T(128)} %bitcast.2), kind=kLoop, calls=%fused_computation.42 | loop fusion | flops 96 | bytes 68 | tf_op jit(solution)/shard_map/jit(remainder)/select_n | solution.py:47
  9.2 1.0 %collective-permute-done = bf16[32,4096]{1,0:T(8,128)(2,1)S(1)} collective-permute-done((bf16[32,4096]{1,0:T(8,128)(2,1)}, bf16[32,4096]{1,0:T(8,128)(2,1)S(1)}, u32[]{:S(2)}, u32[]{:S(2)}) %collective-permute-start) | collective-permute-done | bytes 262176 | tf_op jit(solution)/shard_map/ppermute | solution.py:39
  10.2 1.8 %collective-permute-start.1 = (bf16[32,4096]{1,0:T(8,128)(2,1)S(1)}, bf16[32,4096]{1,0:T(8,128)(2,1)S(1)}, u32[]{:S(2)}, u32[]{:S(2)}) collective-permute-start(bf16[32,4096]{1,0:T(8,128)(2,1)S(1)} %collective-permute-done), channel_id=1, source_target_pairs={{0,8},{8,16},{16,24},{24,28},{28,20},{20,12},{12,4},{4,0},{1,9},{9... | collective-permute-start | bytes 786440 | tf_op jit(solution)/shard_map/ppermute | solution.py:39
  12.3 5.4 %collective-permute-done.1 = bf16[32,4096]{1,0:T(8,128)(2,1)S(1)} collective-permute-done((bf16[32,4096]{1,0:T(8,128)(2,1)S(1)}, bf16[32,4096]{1,0:T(8,128)(2,1)S(1)}, u32[]{:S(2)}, u32[]{:S(2)}) %collective-permute-start.1) | collective-permute-done | bytes 262176 | tf_op jit(solution)/shard_map/ppermute | solution.py:39
  17.7 1.5 %collective-permute-start.2 = (bf16[32,4096]{1,0:T(8,128)(2,1)S(1)}, bf16[32,4096]{1,0:T(8,128)(2,1)S(1)}, u32[]{:S(2)}, u32[]{:S(2)}) collective-permute-start(bf16[32,4096]{1,0:T(8,128)(2,1)S(1)} %collective-permute-done.1), channel_id=1, source_target_pairs={{0,8},{8,16},{16,24},{24,28},{28,20},{20,12},{12,4},{4,0},{1,9},{9... | collective-permute-start | bytes 786440 | tf_op jit(solution)/shard_map/ppermute | solution.py:39
  19.8 4.5 %collective-permute-done.2 = bf16[32,4096]{1,0:T(8,128)(2,1)S(1)} collective-permute-done((bf16[32,4096]{1,0:T(8,128)(2,1)S(1)}, bf16[32,4096]{1,0:T(8,128)(2,1)S(1)}, u32[]{:S(2)}, u32[]{:S(2)}) %collective-permute-start.2) | collective-permute-done | bytes 262176 | tf_op jit(solution)/shard_map/ppermute | solution.py:39
  24.3 1.7 %collective-permute-start.3 = (bf16[32,4096]{1,0:T(8,128)(2,1)S(1)}, bf16[32,4096]{1,0:T(8,128)(2,1)S(1)}, u32[]{:S(2)}, u32[]{:S(2)}) collective-permute-start(bf16[32,4096]{1,0:T(8,128)(2,1)S(1)} %collective-permute-done.2), channel_id=1, source_target_pairs={{0,8},{8,16},{16,24},{24,28},{28,20},{20,12},{12,4},{4,0},{1,9},{9... | collective-permute-start | bytes 786440 | tf_op jit(solution)/shard_map/ppermute | solution.py:39
  26.0 4.6 %collective-permute-done.3 = bf16[32,4096]{1,0:T(8,128)(2,1)S(1)} collective-permute-done((bf16[32,4096]{1,0:T(8,128)(2,1)S(1)}, bf16[32,4096]{1,0:T(8,128)(2,1)S(1)}, u32[]{:S(2)}, u32[]{:S(2)}) %collective-permute-start.3) | collective-permute-done | bytes 262176 | tf_op jit(solution)/shard_map/ppermute | solution.py:39
  30.8 7.7 %fusion = f32[160,2048]{1,0:T(8,128)S(1)} fusion(bf16[4096,2048]{1,0:T(8,128)(2,1)} %param.14, bf16[256,4096]{1,0:T(8,128)(2,1)S(1)} %bitcast.151, s32[160]{0:T(256)S(1)} %fusion.3), kind=kOutput, calls=%fused_computation.5 | convolution fusion | flops 3020595200 | bytes 20185728 | tf_op jit(solution)/shard_map/dot_general | solution.py:115
  39.6 1.1 %collective-permute-done.7 = f32[80,2048]{1,0:T(8,128)S(1)} collective-permute-done((f32[80,2048]{1,0:T(8,128)S(1)}, f32[80,2048]{1,0:T(8,128)S(1)}, u32[]{:S(2)}, u32[]{:S(2)}) %collective-permute-start.7) | collective-permute-done | bytes 655392 | tf_op jit(solution)/shard_map/ppermute | solution.py:66
  40.8 1.7 %collective-permute-start.8 = (f32[40,2048]{1,0:T(8,128)S(1)}, f32[40,2048]{1,0:T(8,128)S(1)}, u32[]{:S(2)}, u32[]{:S(2)}) collective-permute-start(f32[40,2048]{1,0:T(8,128)S(1)} %select_bitcast_fusion.1), channel_id=1, source_target_pairs={{0,2},{1,3},{2,0},{3,1},{4,6},{5,7},{6,4},{7,5},{8,10},{9,11},{10,... | collective-permute-start | bytes 983048 | tf_op jit(solution)/shard_map/ppermute | solution.py:66
  42.6 8.0 %collective-permute-done.8 = f32[40,2048]{1,0:T(8,128)S(1)} collective-permute-done((f32[40,2048]{1,0:T(8,128)S(1)}, f32[40,2048]{1,0:T(8,128)S(1)}, u32[]{:S(2)}, u32[]{:S(2)}) %collective-permute-start.8) | collective-permute-done | bytes 327712 | tf_op jit(solution)/shard_map/ppermute | solution.py:66
  51.1 1.7 %collective-permute-start.9 = (f32[3,40]{1,0:T(4,128)S(1)}, f32[3,40]{1,0:T(4,128)S(1)}, u32[]{:S(2)}, u32[]{:S(2)}) collective-permute-start(f32[3,40]{1,0:T(4,128)S(1)} %pad_maximum_fusion), channel_id=1, source_target_pairs={{0,4},{4,0},{8,12},{12,8},{16,20},{20,16},{24,28},{28,24},{1,5},{5... | collective-permute-start | bytes 1448 | tf_op jit(solution)/shard_map/ppermute | solution.py:76
  52.8 1.9 %collective-permute-done.9 = f32[3,40]{1,0:T(4,128)S(1)} collective-permute-done((f32[3,40]{1,0:T(4,128)S(1)}, f32[3,40]{1,0:T(4,128)S(1)}, u32[]{:S(2)}, u32[]{:S(2)}) %collective-permute-start.9) | collective-permute-done | bytes 512 | tf_op jit(solution)/shard_map/ppermute | solution.py:76
  54.7 1.8 %collective-permute-start.10 = (f32[3,40]{1,0:T(4,128)S(1)}, f32[3,40]{1,0:T(4,128)S(1)}, u32[]{:S(2)}, u32[]{:S(2)}) collective-permute-start(f32[3,40]{1,0:T(4,128)S(1)} %pad_maximum_fusion.1), channel_id=1, source_target_pairs={{0,8},{4,12},{8,0},{12,4},{16,24},{20,28},{24,16},{28,20},{1,9},{5... | collective-permute-start | bytes 1448 | tf_op jit(solution)/shard_map/ppermute | solution.py:76
  56.6 1.8 %collective-permute-done.10 = f32[3,40]{1,0:T(4,128)S(1)} collective-permute-done((f32[3,40]{1,0:T(4,128)S(1)}, f32[3,40]{1,0:T(4,128)S(1)}, u32[]{:S(2)}, u32[]{:S(2)}) %collective-permute-start.10) | collective-permute-done | bytes 512 | tf_op jit(solution)/shard_map/ppermute | solution.py:76
  58.4 2.8 %collective-permute-start.11 = (f32[3,40]{1,0:T(4,128)S(1)}, f32[3,40]{1,0:T(4,128)S(1)}, u32[]{:S(2)}, u32[]{:S(2)}) collective-permute-start(f32[3,40]{1,0:T(4,128)S(1)} %pad_maximum_fusion.2), channel_id=1, source_target_pairs={{0,16},{4,20},{8,24},{12,28},{16,0},{20,4},{24,8},{28,12},{1,17},{... | collective-permute-start | bytes 1448 | tf_op jit(solution)/shard_map/ppermute | solution.py:76
  61.9 1.0 %collective-permute-done.11 = f32[3,40]{1,0:T(4,128)S(1)} collective-permute-done((f32[3,40]{1,0:T(4,128)S(1)}, f32[3,40]{1,0:T(4,128)S(1)}, u32[]{:S(2)}, u32[]{:S(2)}) %collective-permute-start.11) | collective-permute-done | bytes 512 | tf_op jit(solution)/shard_map/ppermute | solution.py:76
  63.1 1.1 %collective-permute-done.12 = f32[160]{0:T(256)S(1)} collective-permute-done((f32[160]{0:T(256)S(1)}, f32[160]{0:T(256)S(1)}, u32[]{:S(2)}, u32[]{:S(2)}) %collective-permute-start.12) | collective-permute-done | bytes 672 | tf_op jit(solution)/shard_map/ppermute | solution.py:91
  64.4 1.7 %collective-permute-start.13 = (f32[160]{0:T(256)S(1)}, f32[160]{0:T(256)S(1)}, u32[]{:S(2)}, u32[]{:S(2)}) collective-permute-start(f32[160]{0:T(256)S(1)} %add_dynamic-update-slice_fusion), channel_id=1, source_target_pairs={{0,2},{1,3},{2,0},{3,1},{4,6},{5,7},{6,4},{7,5},{8,10},{9,11},{10,... | collective-permute-start | bytes 1928 | tf_op jit(solution)/shard_map/ppermute | solution.py:91
  66.8 1.2 %collective-permute-done.13 = f32[160]{0:T(256)S(1)} collective-permute-done((f32[160]{0:T(256)S(1)}, f32[160]{0:T(256)S(1)}, u32[]{:S(2)}, u32[]{:S(2)}) %collective-permute-start.13) | collective-permute-done | bytes 672 | tf_op jit(solution)/shard_map/ppermute | solution.py:91
  (55 shorter events, 7.3 us)
Async XLA Ops:
  0.6 38.1 %copy-start = (s32[256]{0:T(256)S(1)}, s32[256]{0:T(256)}, u32[]{:S(2)}) copy-start(s32[256]{0:T(256)} %param.16) | copy-start | bytes 3076
  0.6 9.5 %collective-permute-start = (bf16[32,4096]{1,0:T(8,128)(2,1)}, bf16[32,4096]{1,0:T(8,128)(2,1)S(1)}, u32[]{:S(2)}, u32[]{:S(2)}) collective-permute-start(bf16[32,4096]{1,0:T(8,128)(2,1)} %param.13), channel_id=1, source_target_pairs={{0,8},{8,16},{16,24},{24,28},{28,20},{20,12},{12,4},{4,0},{1,9},{9... | collective-permute-start | bytes 786440 | tf_op jit(solution)/shard_map/ppermute | solution.py:39
  3.7 8.3 %collective-permute-start.4 = (bf16[32,4096]{1,0:T(8,128)(2,1)}, bf16[32,4096]{1,0:T(8,128)(2,1)S(1)}, u32[]{:S(2)}, u32[]{:S(2)}) collective-permute-start(bf16[32,4096]{1,0:T(8,128)(2,1)} %param.13), channel_id=1, source_target_pairs={{8,0},{16,8},{24,16},{28,24},{20,28},{12,20},{4,12},{0,4},{9,1},{1... | collective-permute-start | bytes 786440 | tf_op jit(solution)/shard_map/ppermute | solution.py:42
  10.2 7.5 %collective-permute-start.1 = (bf16[32,4096]{1,0:T(8,128)(2,1)S(1)}, bf16[32,4096]{1,0:T(8,128)(2,1)S(1)}, u32[]{:S(2)}, u32[]{:S(2)}) collective-permute-start(bf16[32,4096]{1,0:T(8,128)(2,1)S(1)} %collective-permute-done), channel_id=1, source_target_pairs={{0,8},{8,16},{16,24},{24,28},{28,20},{20,12},{12,4},{4,0},{1,9},{9... | collective-permute-start | bytes 786440 | tf_op jit(solution)/shard_map/ppermute | solution.py:39
  12.0 7.2 %collective-permute-start.5 = (bf16[32,4096]{1,0:T(8,128)(2,1)S(1)}, bf16[32,4096]{1,0:T(8,128)(2,1)S(1)}, u32[]{:S(2)}, u32[]{:S(2)}) collective-permute-start(bf16[32,4096]{1,0:T(8,128)(2,1)S(1)} %collective-permute-done.4), channel_id=1, source_target_pairs={{8,0},{16,8},{24,16},{28,24},{20,28},{12,20},{4,12},{0,4},{9,1},{1... | collective-permute-start | bytes 786440 | tf_op jit(solution)/shard_map/ppermute | solution.py:42
  17.7 6.6 %collective-permute-start.2 = (bf16[32,4096]{1,0:T(8,128)(2,1)S(1)}, bf16[32,4096]{1,0:T(8,128)(2,1)S(1)}, u32[]{:S(2)}, u32[]{:S(2)}) collective-permute-start(bf16[32,4096]{1,0:T(8,128)(2,1)S(1)} %collective-permute-done.1), channel_id=1, source_target_pairs={{0,8},{8,16},{16,24},{24,28},{28,20},{20,12},{12,4},{4,0},{1,9},{9... | collective-permute-start | bytes 786440 | tf_op jit(solution)/shard_map/ppermute | solution.py:39
  19.2 11.4 %collective-permute-start.6 = (bf16[32,4096]{1,0:T(8,128)(2,1)S(1)}, bf16[32,4096]{1,0:T(8,128)(2,1)S(1)}, u32[]{:S(2)}, u32[]{:S(2)}) collective-permute-start(bf16[32,4096]{1,0:T(8,128)(2,1)S(1)} %collective-permute-done.5), channel_id=1, source_target_pairs={{8,0},{16,8},{24,16},{28,24},{20,28},{12,20},{4,12},{0,4},{9,1},{1... | collective-permute-start | bytes 786440 | tf_op jit(solution)/shard_map/ppermute | solution.py:42
  24.3 6.4 %collective-permute-start.3 = (bf16[32,4096]{1,0:T(8,128)(2,1)S(1)}, bf16[32,4096]{1,0:T(8,128)(2,1)S(1)}, u32[]{:S(2)}, u32[]{:S(2)}) collective-permute-start(bf16[32,4096]{1,0:T(8,128)(2,1)S(1)} %collective-permute-done.2), channel_id=1, source_target_pairs={{0,8},{8,16},{16,24},{24,28},{28,20},{20,12},{12,4},{4,0},{1,9},{9... | collective-permute-start | bytes 786440 | tf_op jit(solution)/shard_map/ppermute | solution.py:39
  38.5 2.2 %collective-permute-start.7 = (f32[80,2048]{1,0:T(8,128)S(1)}, f32[80,2048]{1,0:T(8,128)S(1)}, u32[]{:S(2)}, u32[]{:S(2)}) collective-permute-start(f32[80,2048]{1,0:T(8,128)S(1)} %select_bitcast_fusion), channel_id=1, source_target_pairs={{0,1},{1,0},{2,3},{3,2},{4,5},{5,4},{6,7},{7,6},{8,9},{9,8},{10,11... | collective-permute-start | bytes 1966088 | tf_op jit(solution)/shard_map/ppermute | solution.py:66
  39.6 26.5 %copy-start.1 = (s32[8]{0:T(128)S(1)}, s32[8]{0:T(128)}, u32[]{:S(2)}) copy-start(s32[8]{0:T(128)} %param.15) | copy-start | bytes 100
  40.8 27.9 %copy-start.2 = (f32[32]{0:T(128)S(1)}, f32[32]{0:T(128)}, u32[]{:S(2)}) copy-start(f32[32]{0:T(128)} %param.17) | copy-start | bytes 388
  40.8 9.8 %collective-permute-start.8 = (f32[40,2048]{1,0:T(8,128)S(1)}, f32[40,2048]{1,0:T(8,128)S(1)}, u32[]{:S(2)}, u32[]{:S(2)}) collective-permute-start(f32[40,2048]{1,0:T(8,128)S(1)} %select_bitcast_fusion.1), channel_id=1, source_target_pairs={{0,2},{1,3},{2,0},{3,1},{4,6},{5,7},{6,4},{7,5},{8,10},{9,11},{10,... | collective-permute-start | bytes 983048 | tf_op jit(solution)/shard_map/ppermute | solution.py:66
  51.1 3.7 %collective-permute-start.9 = (f32[3,40]{1,0:T(4,128)S(1)}, f32[3,40]{1,0:T(4,128)S(1)}, u32[]{:S(2)}, u32[]{:S(2)}) collective-permute-start(f32[3,40]{1,0:T(4,128)S(1)} %pad_maximum_fusion), channel_id=1, source_target_pairs={{0,4},{4,0},{8,12},{12,8},{16,20},{20,16},{24,28},{28,24},{1,5},{5... | collective-permute-start | bytes 1448 | tf_op jit(solution)/shard_map/ppermute | solution.py:76
  54.7 3.7 %collective-permute-start.10 = (f32[3,40]{1,0:T(4,128)S(1)}, f32[3,40]{1,0:T(4,128)S(1)}, u32[]{:S(2)}, u32[]{:S(2)}) collective-permute-start(f32[3,40]{1,0:T(4,128)S(1)} %pad_maximum_fusion.1), channel_id=1, source_target_pairs={{0,8},{4,12},{8,0},{12,4},{16,24},{20,28},{24,16},{28,20},{1,9},{5... | collective-permute-start | bytes 1448 | tf_op jit(solution)/shard_map/ppermute | solution.py:76
  58.4 4.5 %collective-permute-start.11 = (f32[3,40]{1,0:T(4,128)S(1)}, f32[3,40]{1,0:T(4,128)S(1)}, u32[]{:S(2)}, u32[]{:S(2)}) collective-permute-start(f32[3,40]{1,0:T(4,128)S(1)} %pad_maximum_fusion.2), channel_id=1, source_target_pairs={{0,16},{4,20},{8,24},{12,28},{16,0},{20,4},{24,8},{28,12},{1,17},{... | collective-permute-start | bytes 1448 | tf_op jit(solution)/shard_map/ppermute | solution.py:76
  63.1 1.2 %collective-permute-start.12 = (f32[160]{0:T(256)S(1)}, f32[160]{0:T(256)S(1)}, u32[]{:S(2)}, u32[]{:S(2)}) collective-permute-start(f32[160]{0:T(256)S(1)} %get-tuple-element.31), channel_id=1, source_target_pairs={{0,1},{1,0},{2,3},{3,2},{4,5},{5,4},{6,7},{7,6},{8,9},{9,8},{10,11... | collective-permute-start | bytes 1928 | tf_op jit(solution)/shard_map/ppermute | solution.py:91
  64.4 3.6 %collective-permute-start.13 = (f32[160]{0:T(256)S(1)}, f32[160]{0:T(256)S(1)}, u32[]{:S(2)}, u32[]{:S(2)}) collective-permute-start(f32[160]{0:T(256)S(1)} %add_dynamic-update-slice_fusion), channel_id=1, source_target_pairs={{0,2},{1,3},{2,0},{3,1},{4,6},{5,7},{6,4},{7,5},{8,10},{9,11},{10,... | collective-permute-start | bytes 1928 | tf_op jit(solution)/shard_map/ppermute | solution.py:91

commit v5 on v4

--- a/solution.py
+++ b/solution.py
@@ -54,20 +54,30 @@
 
 
 def halving_scatter(partial, size):
-    me = lax.axis_index("vocab")
-    first = jnp.int32(0)
     bit = 1
     while bit < size:
         half = partial.shape[0] // 2
-        pairs = partial.reshape(2, half, partial.shape[1])
+        got = lax.ppermute(partial[:half], "vocab", [(i, i ^ bit) for i in range(size)])
+        partial = partial[half:] + got
+        bit *= 2
+    return partial
+
+
+def send_first_order(count, size):
+    me = lax.axis_index("vocab")
+    place = jnp.arange(count, dtype=jnp.int32)
+    canon = jnp.zeros((count,), jnp.int32)
+    first = jnp.int32(0)
+    span, bit, level = count, 1, 0
+    while bit < size:
+        span //= 2
         side = (me // bit) % 2
-        keep = jnp.take(pairs, side, axis=0)
-        send = jnp.take(pairs, 1 - side, axis=0)
-        got = lax.ppermute(send, "vocab", [(i, i ^ bit) for i in range(size)])
-        partial = keep + got
-        first = first + side * half
+        digit = (place // span) % 2
+        canon = canon + ((1 - side) ^ digit) * span
+        first = first + side * span
         bit *= 2
-    return partial, first
+        level += 1
+    return canon + place % span, first
 
 
 def merge_stats(stats, size):
@@ -106,20 +116,31 @@
         live_count = all_rows * 5 // 8
         ends = jnp.cumsum(lengths)
         starts = ends - lengths
-        packed = jnp.arange(live_count, dtype=jnp.int32)
+        packed, first = send_first_order(live_count, vocab_size)
         batch_hit = ends[:, None] <= packed[None, :]
         batch_of = jnp.sum(batch_hit.astype(jnp.int32), axis=0)
         in_batch = packed - jnp.sum(jnp.where(batch_of[None, :] == jnp.arange(MB, dtype=jnp.int32)[:, None], starts[:, None], 0), axis=0)
         live_rows = batch_of * slot_count + in_batch
         full_rows = ring_gather(hidden, ring, live_rows)
-        partial = jnp.dot(full_rows, head_weight, preferred_element_type=jnp.float32)
-        logits, first = halving_scatter(partial, vocab_size)
-        share = logits.shape[0]
-        row_targets = jnp.take(targets, lax.dynamic_slice_in_dim(live_rows, first, share))
-        highest = jnp.max(logits, axis=1)
-        exp_total = jnp.sum(jnp.exp(logits - highest[:, None]), axis=1)
-        columns = col_start + lax.broadcasted_iota(jnp.int32, logits.shape, 1)
-        picked = jnp.sum(jnp.where(columns == row_targets[:, None], logits, 0.0), axis=1)
+        share = live_count // vocab_size
+        row_targets = lax.dynamic_slice_in_dim(live_rows, live_count - share, share)
+        row_targets = jnp.take(targets, row_targets)
+        pieces = 2 if tile_width % 256 == 0 else 1
+        width = tile_width // pieces
+        parts = []
+        for piece in range(pieces):
+            partial = jnp.dot(full_rows, head_weight[:, piece * width:(piece + 1) * width], preferred_element_type=jnp.float32)
+            logits = halving_scatter(partial, vocab_size)
+            highest = jnp.max(logits, axis=1)
+            exp_total = jnp.sum(jnp.exp(logits - highest[:, None]), axis=1)
+            columns = col_start + piece * width + lax.broadcasted_iota(jnp.int32, logits.shape, 1)
+            picked = jnp.sum(jnp.where(columns == row_targets[:, None], logits, 0.0), axis=1)
+            parts.append((highest, exp_total, picked))
+        highest = parts[0][0]
+        for part in parts[1:]:
+            highest = jnp.maximum(highest, part[0])
+        exp_total = sum(part[1] * jnp.exp(part[0] - highest) for part in parts)
+        picked = sum(part[2] for part in parts)
         stats = merge_stats(jnp.stack([highest, exp_total, picked]), dp_size)
         logprob = stats[2] - (stats[0] + jnp.log(stats[1]))
         all_values = doubling_gather(logprob, first, vocab_size)

time: 69.4 us -> 70.2 us (1.012)
  local copies, waits for them, and re-layouts: 5.32 us -> 7.65 us
  waiting for transfers between devices: 31.8 us -> 30.5 us
    unnamed x13 -> x15, local copies, waits for them, and re-layouts: 1.16 us -> 3.43 us
    ppermute x2 -> x4, waiting for transfers between devices: 9.12 us -> 7.03 us  [halving_scatter(): lax.ppermute(partial[:half], 'vocab', [(i, i ^ bit) for i in range(size)])]
    ppermute x2 -> x4, starting transfers between devices: 1.81 us -> 3.09 us  [halving_scatter(): lax.ppermute(partial[:half], 'vocab', [(i, i ^ bit) for i in range(size)])]
    ppermute x3, waiting for transfers between devices: 4.82 us -> 5.55 us  [merge_stats(): other = lax.ppermute(stats, 'dp', [(i, i ^ bit) for i in range(size)])]
    ppermute x3, starting transfers between devices: 6.32 us -> 5.59 us  [merge_stats(): other = lax.ppermute(stats, 'dp', [(i, i ^ bit) for i in range(size)])]
    dot_general x1 -> x3, matrix products: 7.71 us -> 7.3 us  [the longest x2 6.75 us: on_device(): jnp.dot(full_rows, head_weight[:, piece * width:(piece + 1) * width], pre...]
  transfers between devices with their start and end apart: 14 -> 16, of which waited for: 11 -> 11; matrix products, arithmetic and copies ran while one was open for 11% -> 14% of each run, Pallas kernels for 0% -> 0%
where the time goes in v5:
time: 70.2 us; the launch traced here: 70 us
  waiting for transfers between devices  30.5 us (43%)
  starting transfers between devices  18.9 us (27%)
  local copies, waits for them, and re-layouts  7.65 us (11%)
  matrix products  7.3 us (10%)
  other arithmetic  4.79 us (7%)
  between operations  0.91 us (1%)
    ppermute x4, waiting for transfers between devices, ring_gather(): ahead = lax.ppermute(ahead, 'dp', fwd)  15.3 us
    ppermute x4, starting transfers between devices, ring_gather(): ahead = lax.ppermute(ahead, 'dp', fwd)  8.24 us
    ppermute x4, waiting for transfers between devices, halving_scatter(): lax.ppermute(partial[:half], 'vocab', [(i, i ^ bit) for i in range(size)])  7.03 us
    dot_general x2, matrix products, on_device(): jnp.dot(full_rows, head_weight[:, piece * width:(piece + 1) * width], pre...  6.75 us
    ppermute x3, starting transfers between devices, merge_stats(): other = lax.ppermute(stats, 'dp', [(i, i ^ bit) for i in range(size)])  5.59 us
    ppermute x3, waiting for transfers between devices, merge_stats(): other = lax.ppermute(stats, 'dp', [(i, i ^ bit) for i in range(size)])  5.55 us
    unnamed x15, local copies, waits for them, and re-layouts  3.43 us
    ppermute x4, starting transfers between devices, halving_scatter(): lax.ppermute(partial[:half], 'vocab', [(i, i ^ bit) for i in range(size)])  3.09 us
  transfers between devices with their start and end apart: 16, of which 11 were waited for; matrix products, arithmetic and copies ran while one was open for 14% of the time, Pallas kernels for 0%

profile of v5, /device:TPU:0, one launch (start us, length us, event | category | flops | bytes accessed | tf_op | source)
XLA Modules:
  0.0 70.0 jit_solution(6439805000225727740)
XLA Ops:
  0.6 3.1 %collective-permute-start = (bf16[32,4096]{1,0:T(8,128)(2,1)}, bf16[32,4096]{1,0:T(8,128)(2,1)S(1)}, u32[]{:S(2)}, u32[]{:S(2)}) collective-permute-start(bf16[32,4096]{1,0:T(8,128)(2,1)} %param.9), channel_id=1, source_target_pairs={{0,8},{8,16},{16,24},{24,28},{28,20},{20,12},{12,4},{4,0},{1,9},{9... | collective-permute-start | bytes 786440 | tf_op jit(solution)/shard_map/ppermute | solution.py:39
  6.6 1.2 %dynamic_slice.7 = s32[1]{0:T(128)} dynamic-slice(s32[8]{0:T(128)} %constant.206.clone, s32[]{:T(128)S(6)} %select_n.189), dynamic_slice_sizes={1} | dynamic-slice | bytes 12 | tf_op jit(solution)/shard_map/dynamic_slice | solution.py:46
  7.8 1.3 %and_select_fusion.1 = s32[8]{0:T(128)S(1)} fusion(s32[8]{0:T(128)} %constant.207, s32[]{:T(128)} %bitcast.2), kind=kLoop, calls=%fused_computation.54 | loop fusion | flops 96 | bytes 68 | tf_op jit(solution)/shard_map/jit(remainder)/select_n | solution.py:47
  10.2 1.9 %collective-permute-start.1 = (bf16[32,4096]{1,0:T(8,128)(2,1)S(1)}, bf16[32,4096]{1,0:T(8,128)(2,1)S(1)}, u32[]{:S(2)}, u32[]{:S(2)}) collective-permute-start(bf16[32,4096]{1,0:T(8,128)(2,1)S(1)} %collective-permute-done), channel_id=1, source_target_pairs={{0,8},{8,16},{16,24},{24,28},{28,20},{20,12},{12,4},{4,0},{1,9},{9... | collective-permute-start | bytes 786440 | tf_op jit(solution)/shard_map/ppermute | solution.py:39
  12.3 5.6 %collective-permute-done.1 = bf16[32,4096]{1,0:T(8,128)(2,1)S(1)} collective-permute-done((bf16[32,4096]{1,0:T(8,128)(2,1)S(1)}, bf16[32,4096]{1,0:T(8,128)(2,1)S(1)}, u32[]{:S(2)}, u32[]{:S(2)}) %collective-permute-start.1) | collective-permute-done | bytes 262176 | tf_op jit(solution)/shard_map/ppermute | solution.py:39
  17.9 1.7 %collective-permute-start.2 = (bf16[32,4096]{1,0:T(8,128)(2,1)S(1)}, bf16[32,4096]{1,0:T(8,128)(2,1)S(1)}, u32[]{:S(2)}, u32[]{:S(2)}) collective-permute-start(bf16[32,4096]{1,0:T(8,128)(2,1)S(1)} %collective-permute-done.1), channel_id=1, source_target_pairs={{0,8},{8,16},{16,24},{24,28},{28,20},{20,12},{12,4},{4,0},{1,9},{9... | collective-permute-start | bytes 786440 | tf_op jit(solution)/shard_map/ppermute | solution.py:39
  20.0 4.7 %collective-permute-done.2 = bf16[32,4096]{1,0:T(8,128)(2,1)S(1)} collective-permute-done((bf16[32,4096]{1,0:T(8,128)(2,1)S(1)}, bf16[32,4096]{1,0:T(8,128)(2,1)S(1)}, u32[]{:S(2)}, u32[]{:S(2)}) %collective-permute-start.2) | collective-permute-done | bytes 262176 | tf_op jit(solution)/shard_map/ppermute | solution.py:39
  24.7 1.5 %collective-permute-start.3 = (bf16[32,4096]{1,0:T(8,128)(2,1)S(1)}, bf16[32,4096]{1,0:T(8,128)(2,1)S(1)}, u32[]{:S(2)}, u32[]{:S(2)}) collective-permute-start(bf16[32,4096]{1,0:T(8,128)(2,1)S(1)} %collective-permute-done.2), channel_id=1, source_target_pairs={{0,8},{8,16},{16,24},{24,28},{28,20},{20,12},{12,4},{4,0},{1,9},{9... | collective-permute-start | bytes 786440 | tf_op jit(solution)/shard_map/ppermute | solution.py:39
  26.2 4.9 %collective-permute-done.3 = bf16[32,4096]{1,0:T(8,128)(2,1)S(1)} collective-permute-done((bf16[32,4096]{1,0:T(8,128)(2,1)S(1)}, bf16[32,4096]{1,0:T(8,128)(2,1)S(1)}, u32[]{:S(2)}, u32[]{:S(2)}) %collective-permute-start.3) | collective-permute-done | bytes 262176 | tf_op jit(solution)/shard_map/ppermute | solution.py:39
  31.8 5.2 %fusion.2 = f32[160,1024]{1,0:T(8,128)S(1)} fusion(bf16[160,4096]{1,0:T(8,128)(2,1)S(1)} %convolution_convert_fusion, bf16[4096,2048]{1,0:T(8,128)(2,1)} %param.10), kind=kOutput, calls=%fused_computation.6 | convolution fusion | flops 1342177280 | bytes 10354688 | tf_op jit(solution)/shard_map/dot_general | solution.py:132
  37.1 2.3 %copy-done.3 = bf16[4096,2048]{1,0:T(8,128)(2,1)S(1)} copy-done((bf16[4096,2048]{1,0:T(8,128)(2,1)S(1)}, bf16[4096,2048]{1,0:T(8,128)(2,1)}, u32[]{:S(2)}) %copy-start.3) | copy-done | bytes 16777240
  39.4 1.5 %fusion = f32[160,1024]{1,0:T(8,128)S(1)} fusion(bf16[160,4096]{1,0:T(8,128)(2,1)S(1)} %convolution_convert_fusion, bf16[4096,2048]{1,0:T(8,128)(2,1)S(1)} %copy-done.3), kind=kOutput, calls=%fused_computation.4 | convolution fusion | flops 1342177280 | bytes 10354688 | tf_op jit(solution)/shard_map/dot_general | solution.py:132
  41.2 1.5 %collective-permute-start.8 = (f32[40,1024]{1,0:T(8,128)S(1)}, f32[40,1024]{1,0:T(8,128)S(1)}, u32[]{:S(2)}, u32[]{:S(2)}) collective-permute-start(f32[40,1024]{1,0:T(8,128)S(1)} %slice.90), channel_id=1, source_target_pairs={{0,2},{1,3},{2,0},{3,1},{4,6},{5,7},{6,4},{7,5},{8,10},{9,11},{10,... | collective-permute-start | bytes 491528 | tf_op jit(solution)/shard_map/ppermute | solution.py:60
  42.8 1.5 %collective-permute-start.10 = (f32[40,1024]{1,0:T(8,128)S(1)}, f32[40,1024]{1,0:T(8,128)S(1)}, u32[]{:S(2)}, u32[]{:S(2)}) collective-permute-start(f32[40,1024]{1,0:T(8,128)S(1)} %slice.94), channel_id=1, source_target_pairs={{0,2},{1,3},{2,0},{3,1},{4,6},{5,7},{6,4},{7,5},{8,10},{9,11},{10,... | collective-permute-start | bytes 491528 | tf_op jit(solution)/shard_map/ppermute | solution.py:60
  44.2 4.1 %collective-permute-done.8 = f32[40,1024]{1,0:T(8,128)S(1)} collective-permute-done((f32[40,1024]{1,0:T(8,128)S(1)}, f32[40,1024]{1,0:T(8,128)S(1)}, u32[]{:S(2)}, u32[]{:S(2)}) %collective-permute-start.8) | collective-permute-done | bytes 163872 | tf_op jit(solution)/shard_map/ppermute | solution.py:60
  48.5 2.9 %collective-permute-done.10 = f32[40,1024]{1,0:T(8,128)S(1)} collective-permute-done((f32[40,1024]{1,0:T(8,128)S(1)}, f32[40,1024]{1,0:T(8,128)S(1)}, u32[]{:S(2)}, u32[]{:S(2)}) %collective-permute-start.10) | collective-permute-done | bytes 163872 | tf_op jit(solution)/shard_map/ppermute | solution.py:60
  51.8 1.5 %collective-permute-start.11 = (f32[3,40]{1,0:T(4,128)S(1)}, f32[3,40]{1,0:T(4,128)S(1)}, u32[]{:S(2)}, u32[]{:S(2)}) collective-permute-start(f32[3,40]{1,0:T(4,128)S(1)} %pad_maximum_fusion), channel_id=1, source_target_pairs={{0,4},{4,0},{8,12},{12,8},{16,20},{20,16},{24,28},{28,24},{1,5},{5... | collective-permute-start | bytes 1448 | tf_op jit(solution)/shard_map/ppermute | solution.py:86
  53.3 2.2 %collective-permute-done.11 = f32[3,40]{1,0:T(4,128)S(1)} collective-permute-done((f32[3,40]{1,0:T(4,128)S(1)}, f32[3,40]{1,0:T(4,128)S(1)}, u32[]{:S(2)}, u32[]{:S(2)}) %collective-permute-start.11) | collective-permute-done | bytes 512 | tf_op jit(solution)/shard_map/ppermute | solution.py:86
  55.5 1.6 %collective-permute-start.12 = (f32[3,40]{1,0:T(4,128)S(1)}, f32[3,40]{1,0:T(4,128)S(1)}, u32[]{:S(2)}, u32[]{:S(2)}) collective-permute-start(f32[3,40]{1,0:T(4,128)S(1)} %pad_maximum_fusion.1), channel_id=1, source_target_pairs={{0,8},{4,12},{8,0},{12,4},{16,24},{20,28},{24,16},{28,20},{1,9},{5... | collective-permute-start | bytes 1448 | tf_op jit(solution)/shard_map/ppermute | solution.py:86
  57.0 2.1 %collective-permute-done.12 = f32[3,40]{1,0:T(4,128)S(1)} collective-permute-done((f32[3,40]{1,0:T(4,128)S(1)}, f32[3,40]{1,0:T(4,128)S(1)}, u32[]{:S(2)}, u32[]{:S(2)}) %collective-permute-start.12) | collective-permute-done | bytes 512 | tf_op jit(solution)/shard_map/ppermute | solution.py:86
  59.2 2.6 %collective-permute-start.13 = (f32[3,40]{1,0:T(4,128)S(1)}, f32[3,40]{1,0:T(4,128)S(1)}, u32[]{:S(2)}, u32[]{:S(2)}) collective-permute-start(f32[3,40]{1,0:T(4,128)S(1)} %pad_maximum_fusion.2), channel_id=1, source_target_pairs={{0,16},{4,20},{8,24},{12,28},{16,0},{20,4},{24,8},{28,12},{1,17},{... | collective-permute-start | bytes 1448 | tf_op jit(solution)/shard_map/ppermute | solution.py:86
  62.4 1.3 %collective-permute-done.13 = f32[3,40]{1,0:T(4,128)S(1)} collective-permute-done((f32[3,40]{1,0:T(4,128)S(1)}, f32[3,40]{1,0:T(4,128)S(1)}, u32[]{:S(2)}, u32[]{:S(2)}) %collective-permute-start.13) | collective-permute-done | bytes 512 | tf_op jit(solution)/shard_map/ppermute | solution.py:86
  65.1 1.4 %collective-permute-start.15 = (f32[160]{0:T(256)S(1)}, f32[160]{0:T(256)S(1)}, u32[]{:S(2)}, u32[]{:S(2)}) collective-permute-start(f32[160]{0:T(256)S(1)} %add_dynamic-update-slice_fusion), channel_id=1, source_target_pairs={{0,2},{1,3},{2,0},{3,1},{4,6},{5,7},{6,4},{7,5},{8,10},{9,11},{10,... | collective-permute-start | bytes 1928 | tf_op jit(solution)/shard_map/ppermute | solution.py:101
  67.3 1.4 %collective-permute-done.15 = f32[160]{0:T(256)S(1)} collective-permute-done((f32[160]{0:T(256)S(1)}, f32[160]{0:T(256)S(1)}, u32[]{:S(2)}, u32[]{:S(2)}) %collective-permute-start.15) | collective-permute-done | bytes 672 | tf_op jit(solution)/shard_map/ppermute | solution.py:101
  (70 shorter events, 10.1 us)
Async XLA Ops:
  0.6 8.6 %copy-start = (s32[256]{0:T(256)S(1)}, s32[256]{0:T(256)}, u32[]{:S(2)}) copy-start(s32[256]{0:T(256)} %param.12) | copy-start | bytes 3076
  0.6 9.5 %collective-permute-start = (bf16[32,4096]{1,0:T(8,128)(2,1)}, bf16[32,4096]{1,0:T(8,128)(2,1)S(1)}, u32[]{:S(2)}, u32[]{:S(2)}) collective-permute-start(bf16[32,4096]{1,0:T(8,128)(2,1)} %param.9), channel_id=1, source_target_pairs={{0,8},{8,16},{16,24},{24,28},{28,20},{20,12},{12,4},{4,0},{1,9},{9... | collective-permute-start | bytes 786440 | tf_op jit(solution)/shard_map/ppermute | solution.py:39
  3.7 8.4 %collective-permute-start.4 = (bf16[32,4096]{1,0:T(8,128)(2,1)}, bf16[32,4096]{1,0:T(8,128)(2,1)S(1)}, u32[]{:S(2)}, u32[]{:S(2)}) collective-permute-start(bf16[32,4096]{1,0:T(8,128)(2,1)} %param.9), channel_id=1, source_target_pairs={{8,0},{16,8},{24,16},{28,24},{20,28},{12,20},{4,12},{0,4},{9,1},{1... | collective-permute-start | bytes 786440 | tf_op jit(solution)/shard_map/ppermute | solution.py:42
  10.2 7.7 %collective-permute-start.1 = (bf16[32,4096]{1,0:T(8,128)(2,1)S(1)}, bf16[32,4096]{1,0:T(8,128)(2,1)S(1)}, u32[]{:S(2)}, u32[]{:S(2)}) collective-permute-start(bf16[32,4096]{1,0:T(8,128)(2,1)S(1)} %collective-permute-done), channel_id=1, source_target_pairs={{0,8},{8,16},{16,24},{24,28},{28,20},{20,12},{12,4},{4,0},{1,9},{9... | collective-permute-start | bytes 786440 | tf_op jit(solution)/shard_map/ppermute | solution.py:39
  12.1 7.5 %collective-permute-start.5 = (bf16[32,4096]{1,0:T(8,128)(2,1)S(1)}, bf16[32,4096]{1,0:T(8,128)(2,1)S(1)}, u32[]{:S(2)}, u32[]{:S(2)}) collective-permute-start(bf16[32,4096]{1,0:T(8,128)(2,1)S(1)} %collective-permute-done.4), channel_id=1, source_target_pairs={{8,0},{16,8},{24,16},{28,24},{20,28},{12,20},{4,12},{0,4},{9,1},{1... | collective-permute-start | bytes 786440 | tf_op jit(solution)/shard_map/ppermute | solution.py:42
  17.9 6.9 %collective-permute-start.2 = (bf16[32,4096]{1,0:T(8,128)(2,1)S(1)}, bf16[32,4096]{1,0:T(8,128)(2,1)S(1)}, u32[]{:S(2)}, u32[]{:S(2)}) collective-permute-start(bf16[32,4096]{1,0:T(8,128)(2,1)S(1)} %collective-permute-done.1), channel_id=1, source_target_pairs={{0,8},{8,16},{16,24},{24,28},{28,20},{20,12},{12,4},{4,0},{1,9},{9... | collective-permute-start | bytes 786440 | tf_op jit(solution)/shard_map/ppermute | solution.py:39
  19.6 11.5 %collective-permute-start.6 = (bf16[32,4096]{1,0:T(8,128)(2,1)S(1)}, bf16[32,4096]{1,0:T(8,128)(2,1)S(1)}, u32[]{:S(2)}, u32[]{:S(2)}) collective-permute-start(bf16[32,4096]{1,0:T(8,128)(2,1)S(1)} %collective-permute-done.5), channel_id=1, source_target_pairs={{8,0},{16,8},{24,16},{28,24},{20,28},{12,20},{4,12},{0,4},{9,1},{1... | collective-permute-start | bytes 786440 | tf_op jit(solution)/shard_map/ppermute | solution.py:42
  24.7 6.4 %collective-permute-start.3 = (bf16[32,4096]{1,0:T(8,128)(2,1)S(1)}, bf16[32,4096]{1,0:T(8,128)(2,1)S(1)}, u32[]{:S(2)}, u32[]{:S(2)}) collective-permute-start(bf16[32,4096]{1,0:T(8,128)(2,1)S(1)} %collective-permute-done.2), channel_id=1, source_target_pairs={{0,8},{8,16},{16,24},{24,28},{28,20},{20,12},{12,4},{4,0},{1,9},{9... | collective-permute-start | bytes 786440 | tf_op jit(solution)/shard_map/ppermute | solution.py:39
  31.2 8.2 %copy-start.3 = (bf16[4096,2048]{1,0:T(8,128)(2,1)S(1)}, bf16[4096,2048]{1,0:T(8,128)(2,1)}, u32[]{:S(2)}) copy-start(bf16[4096,2048]{1,0:T(8,128)(2,1)} %param.10) | copy-start | bytes 50331652
  37.0 4.1 %collective-permute-start.7 = (f32[80,1024]{1,0:T(8,128)S(1)}, f32[80,1024]{1,0:T(8,128)S(1)}, u32[]{:S(2)}, u32[]{:S(2)}) collective-permute-start(f32[80,1024]{1,0:T(8,128)S(1)} %slice.88), channel_id=1, source_target_pairs={{0,1},{1,0},{2,3},{3,2},{4,5},{5,4},{6,7},{7,6},{8,9},{9,8},{10,11... | collective-permute-start | bytes 983048 | tf_op jit(solution)/shard_map/ppermute | solution.py:60
  41.0 1.7 %collective-permute-start.9 = (f32[80,1024]{1,0:T(8,128)S(1)}, f32[80,1024]{1,0:T(8,128)S(1)}, u32[]{:S(2)}, u32[]{:S(2)}) collective-permute-start(f32[80,1024]{1,0:T(8,128)S(1)} %slice.92), channel_id=1, source_target_pairs={{0,1},{1,0},{2,3},{3,2},{4,5},{5,4},{6,7},{7,6},{8,9},{9,8},{10,11... | collective-permute-start | bytes 983048 | tf_op jit(solution)/shard_map/ppermute | solution.py:60
  41.1 25.5 %copy-start.1 = (s32[8]{0:T(128)S(1)}, s32[8]{0:T(128)}, u32[]{:S(2)}) copy-start(s32[8]{0:T(128)} %param.11) | copy-start | bytes 100
  41.2 28.2 %copy-start.2 = (f32[32]{0:T(128)S(1)}, f32[32]{0:T(128)}, u32[]{:S(2)}) copy-start(f32[32]{0:T(128)} %param.13) | copy-start | bytes 388
  41.2 7.1 %collective-permute-start.8 = (f32[40,1024]{1,0:T(8,128)S(1)}, f32[40,1024]{1,0:T(8,128)S(1)}, u32[]{:S(2)}, u32[]{:S(2)}) collective-permute-start(f32[40,1024]{1,0:T(8,128)S(1)} %slice.90), channel_id=1, source_target_pairs={{0,2},{1,3},{2,0},{3,1},{4,6},{5,7},{6,4},{7,5},{8,10},{9,11},{10,... | collective-permute-start | bytes 491528 | tf_op jit(solution)/shard_map/ppermute | solution.py:60
  42.8 8.6 %collective-permute-start.10 = (f32[40,1024]{1,0:T(8,128)S(1)}, f32[40,1024]{1,0:T(8,128)S(1)}, u32[]{:S(2)}, u32[]{:S(2)}) collective-permute-start(f32[40,1024]{1,0:T(8,128)S(1)} %slice.94), channel_id=1, source_target_pairs={{0,2},{1,3},{2,0},{3,1},{4,6},{5,7},{6,4},{7,5},{8,10},{9,11},{10,... | collective-permute-start | bytes 491528 | tf_op jit(solution)/shard_map/ppermute | solution.py:60
  51.8 3.7 %collective-permute-start.11 = (f32[3,40]{1,0:T(4,128)S(1)}, f32[3,40]{1,0:T(4,128)S(1)}, u32[]{:S(2)}, u32[]{:S(2)}) collective-permute-start(f32[3,40]{1,0:T(4,128)S(1)} %pad_maximum_fusion), channel_id=1, source_target_pairs={{0,4},{4,0},{8,12},{12,8},{16,20},{20,16},{24,28},{28,24},{1,5},{5... | collective-permute-start | bytes 1448 | tf_op jit(solution)/shard_map/ppermute | solution.py:86
  55.5 3.7 %collective-permute-start.12 = (f32[3,40]{1,0:T(4,128)S(1)}, f32[3,40]{1,0:T(4,128)S(1)}, u32[]{:S(2)}, u32[]{:S(2)}) collective-permute-start(f32[3,40]{1,0:T(4,128)S(1)} %pad_maximum_fusion.1), channel_id=1, source_target_pairs={{0,8},{4,12},{8,0},{12,4},{16,24},{20,28},{24,16},{28,20},{1,9},{5... | collective-permute-start | bytes 1448 | tf_op jit(solution)/shard_map/ppermute | solution.py:86
  59.2 4.5 %collective-permute-start.13 = (f32[3,40]{1,0:T(4,128)S(1)}, f32[3,40]{1,0:T(4,128)S(1)}, u32[]{:S(2)}, u32[]{:S(2)}) collective-permute-start(f32[3,40]{1,0:T(4,128)S(1)} %pad_maximum_fusion.2), channel_id=1, source_target_pairs={{0,16},{4,20},{8,24},{12,28},{16,0},{20,4},{24,8},{28,12},{1,17},{... | collective-permute-start | bytes 1448 | tf_op jit(solution)/shard_map/ppermute | solution.py:86
  63.8 1.2 %collective-permute-start.14 = (f32[160]{0:T(256)S(1)}, f32[160]{0:T(256)S(1)}, u32[]{:S(2)}, u32[]{:S(2)}) collective-permute-start(f32[160]{0:T(256)S(1)} %get-tuple-element.9), channel_id=1, source_target_pairs={{0,1},{1,0},{2,3},{3,2},{4,5},{5,4},{6,7},{7,6},{8,9},{9,8},{10,11... | collective-permute-start | bytes 1928 | tf_op jit(solution)/shard_map/ppermute | solution.py:101
  65.1 3.6 %collective-permute-start.15 = (f32[160]{0:T(256)S(1)}, f32[160]{0:T(256)S(1)}, u32[]{:S(2)}, u32[]{:S(2)}) collective-permute-start(f32[160]{0:T(256)S(1)} %add_dynamic-update-slice_fusion), channel_id=1, source_target_pairs={{0,2},{1,3},{2,0},{3,1},{4,6},{5,7},{6,4},{7,5},{8,10},{9,11},{10,... | collective-permute-start | bytes 1928 | tf_op jit(solution)/shard_map/ppermute | solution.py:101

commit v6 on v5

--- a/solution.py
+++ b/solution.py
@@ -125,23 +125,22 @@
         share = live_count // vocab_size
         row_targets = lax.dynamic_slice_in_dim(live_rows, live_count - share, share)
         row_targets = jnp.take(targets, row_targets)
-        pieces = 2 if tile_width % 256 == 0 else 1
-        width = tile_width // pieces
-        parts = []
-        for piece in range(pieces):
-            partial = jnp.dot(full_rows, head_weight[:, piece * width:(piece + 1) * width], preferred_element_type=jnp.float32)
+        tail = tile_width // 4 if tile_width % 512 == 0 else 0
+        bounds = [(0, tile_width - tail), (tile_width - tail, tile_width)] if tail else [(0, tile_width)]
+        merged = []
+        for low, high in bounds:
+            partial = jnp.dot(full_rows, head_weight[:, low:high], preferred_element_type=jnp.float32)
+            partial, full_rows = lax.optimization_barrier((partial, full_rows))
             logits = halving_scatter(partial, vocab_size)
             highest = jnp.max(logits, axis=1)
             exp_total = jnp.sum(jnp.exp(logits - highest[:, None]), axis=1)
-            columns = col_start + piece * width + lax.broadcasted_iota(jnp.int32, logits.shape, 1)
+            columns = col_start + low + lax.broadcasted_iota(jnp.int32, logits.shape, 1)
             picked = jnp.sum(jnp.where(columns == row_targets[:, None], logits, 0.0), axis=1)
-            parts.append((highest, exp_total, picked))
-        highest = parts[0][0]
-        for part in parts[1:]:
-            highest = jnp.maximum(highest, part[0])
-        exp_total = sum(part[1] * jnp.exp(part[0] - highest) for part in parts)
-        picked = sum(part[2] for part in parts)
-        stats = merge_stats(jnp.stack([highest, exp_total, picked]), dp_size)
+            merged.append(merge_stats(jnp.stack([highest, exp_total, picked]), dp_size))
+        top = merged[0][0]
+        for part in merged[1:]:
+            top = jnp.maximum(top, part[0])
+        stats = jnp.stack([top, sum(part[1] * jnp.exp(part[0] - top) for part in merged), sum(part[2] for part in merged)])
         logprob = stats[2] - (stats[0] + jnp.log(stats[1]))
         all_values = doubling_gather(logprob, first, vocab_size)
         own_rows = lax.axis_index("dp") * row_count + jnp.arange(row_count, dtype=jnp.int32)

time: 70.2 us -> 75.2 us (1.071)
  starting transfers between devices: 18.9 us -> 23.8 us
  local copies, waits for them, and re-layouts: 7.65 us -> 5.39 us
  matrix products: 7.3 us -> 9.47 us
    ppermute x3 -> x6, starting transfers between devices: 5.59 us -> 9.94 us  [merge_stats(): other = lax.ppermute(stats, 'dp', [(i, i ^ bit) for i in range(size)])]
    unnamed x15 -> x13, local copies, waits for them, and re-layouts: 3.43 us -> 1.17 us
    dot_general x2, matrix products: 6.75 us -> 8.92 us  [on_device(): jnp.dot(full_rows, head_weight[:, low:high], preferred_element_type=jnp.f...]
    ppermute x3 -> x6, waiting for transfers between devices: 5.55 us -> 5.3 us  [merge_stats(): other = lax.ppermute(stats, 'dp', [(i, i ^ bit) for i in range(size)])]
  transfers between devices with their start and end apart: 16 -> 19, of which waited for: 11 -> 11; matrix products, arithmetic and copies ran while one was open for 14% -> 12% of each run, Pallas kernels for 0% -> 0%
where the time goes in v6:
time: 75.2 us; the launch traced here: 75 us
  waiting for transfers between devices  30.3 us (40%)
  starting transfers between devices  23.8 us (32%)
  matrix products  9.47 us (13%)
  local copies, waits for them, and re-layouts  5.39 us (7%)
  other arithmetic  5.02 us (7%)
  between operations  0.93 us (1%)
    ppermute x4, waiting for transfers between devices, ring_gather(): ahead = lax.ppermute(ahead, 'dp', fwd)  15.4 us
    ppermute x6, starting transfers between devices, merge_stats(): other = lax.ppermute(stats, 'dp', [(i, i ^ bit) for i in range(size)])  9.94 us
    dot_general x2, matrix products, on_device(): jnp.dot(full_rows, head_weight[:, low:high], preferred_element_type=jnp.f...  8.92 us
    ppermute x4, starting transfers between devices, ring_gather(): ahead = lax.ppermute(ahead, 'dp', fwd)  8.27 us
    ppermute x4, waiting for transfers between devices, halving_scatter(): lax.ppermute(partial[:half], 'vocab', [(i, i ^ bit) for i in range(size)])  7.15 us
    ppermute x6, waiting for transfers between devices, merge_stats(): other = lax.ppermute(stats, 'dp', [(i, i ^ bit) for i in range(size)])  5.3 us
    ppermute x4, starting transfers between devices, halving_scatter(): lax.ppermute(partial[:half], 'vocab', [(i, i ^ bit) for i in range(size)])  3.63 us
    ppermute x2, waiting for transfers between devices, doubling_gather(): other = lax.ppermute(out, 'vocab', [(i, i ^ bit) for i in range(size)])  2.47 us
  transfers between devices with their start and end apart: 19, of which 11 were waited for; matrix products, arithmetic and copies ran while one was open for 12% of the time, Pallas kernels for 0%

profile of v6, /device:TPU:0, one launch (start us, length us, event | category | flops | bytes accessed | tf_op | source)
XLA Modules:
  0.0 75.0 jit_solution(11410543372164123563)
XLA Ops:
  0.6 3.1 %collective-permute-start = (bf16[32,4096]{1,0:T(8,128)(2,1)}, bf16[32,4096]{1,0:T(8,128)(2,1)S(1)}, u32[]{:S(2)}, u32[]{:S(2)}) collective-permute-start(bf16[32,4096]{1,0:T(8,128)(2,1)} %param.9), channel_id=1, source_target_pairs={{0,8},{8,16},{16,24},{24,28},{28,20},{20,12},{12,4},{4,0},{1,9},{9... | collective-permute-start | bytes 786440 | tf_op jit(solution)/shard_map/ppermute | solution.py:39
  7.5 1.2 %dynamic_slice.7 = s32[1]{0:T(128)} dynamic-slice(s32[8]{0:T(128)} %constant.206.clone, s32[]{:T(128)S(6)} %select_n.190), dynamic_slice_sizes={1} | dynamic-slice | bytes 12 | tf_op jit(solution)/shard_map/dynamic_slice | solution.py:46
  8.7 1.3 %and_select_fusion.1 = s32[8]{0:T(128)S(1)} fusion(s32[8]{0:T(128)} %constant.207, s32[]{:T(128)} %bitcast.2), kind=kLoop, calls=%fused_computation.57 | loop fusion | flops 96 | bytes 68 | tf_op jit(solution)/shard_map/jit(remainder)/select_n | solution.py:47
  10.2 2.0 %collective-permute-start.1 = (bf16[32,4096]{1,0:T(8,128)(2,1)S(1)}, bf16[32,4096]{1,0:T(8,128)(2,1)S(1)}, u32[]{:S(2)}, u32[]{:S(2)}) collective-permute-start(bf16[32,4096]{1,0:T(8,128)(2,1)S(1)} %collective-permute-done), channel_id=1, source_target_pairs={{0,8},{8,16},{16,24},{24,28},{28,20},{20,12},{12,4},{4,0},{1,9},{9... | collective-permute-start | bytes 786440 | tf_op jit(solution)/shard_map/ppermute | solution.py:39
  12.3 5.7 %collective-permute-done.1 = bf16[32,4096]{1,0:T(8,128)(2,1)S(1)} collective-permute-done((bf16[32,4096]{1,0:T(8,128)(2,1)S(1)}, bf16[32,4096]{1,0:T(8,128)(2,1)S(1)}, u32[]{:S(2)}, u32[]{:S(2)}) %collective-permute-start.1) | collective-permute-done | bytes 262176 | tf_op jit(solution)/shard_map/ppermute | solution.py:39
  18.0 1.7 %collective-permute-start.2 = (bf16[32,4096]{1,0:T(8,128)(2,1)S(1)}, bf16[32,4096]{1,0:T(8,128)(2,1)S(1)}, u32[]{:S(2)}, u32[]{:S(2)}) collective-permute-start(bf16[32,4096]{1,0:T(8,128)(2,1)S(1)} %collective-permute-done.1), channel_id=1, source_target_pairs={{0,8},{8,16},{16,24},{24,28},{28,20},{20,12},{12,4},{4,0},{1,9},{9... | collective-permute-start | bytes 786440 | tf_op jit(solution)/shard_map/ppermute | solution.py:39
  20.1 4.8 %collective-permute-done.2 = bf16[32,4096]{1,0:T(8,128)(2,1)S(1)} collective-permute-done((bf16[32,4096]{1,0:T(8,128)(2,1)S(1)}, bf16[32,4096]{1,0:T(8,128)(2,1)S(1)}, u32[]{:S(2)}, u32[]{:S(2)}) %collective-permute-start.2) | collective-permute-done | bytes 262176 | tf_op jit(solution)/shard_map/ppermute | solution.py:39
  24.9 1.4 %collective-permute-start.3 = (bf16[32,4096]{1,0:T(8,128)(2,1)S(1)}, bf16[32,4096]{1,0:T(8,128)(2,1)S(1)}, u32[]{:S(2)}, u32[]{:S(2)}) collective-permute-start(bf16[32,4096]{1,0:T(8,128)(2,1)S(1)} %collective-permute-done.2), channel_id=1, source_target_pairs={{0,8},{8,16},{16,24},{24,28},{28,20},{20,12},{12,4},{4,0},{1,9},{9... | collective-permute-start | bytes 786440 | tf_op jit(solution)/shard_map/ppermute | solution.py:39
  26.3 4.9 %collective-permute-done.3 = bf16[32,4096]{1,0:T(8,128)(2,1)S(1)} collective-permute-done((bf16[32,4096]{1,0:T(8,128)(2,1)S(1)}, bf16[32,4096]{1,0:T(8,128)(2,1)S(1)}, u32[]{:S(2)}, u32[]{:S(2)}) %collective-permute-start.3) | collective-permute-done | bytes 262176 | tf_op jit(solution)/shard_map/ppermute | solution.py:39
  31.9 5.9 %fusion = f32[160,1536]{1,0:T(8,128)S(1)} fusion(bf16[160,4096]{1,0:T(8,128)(2,1)S(1)} %convolution_convert_fusion, bf16[4096,2048]{1,0:T(8,128)(2,1)} %param.10), kind=kOutput, calls=%fused_computation.4 | convolution fusion | flops 2013265920 | bytes 14876672 | tf_op jit(solution)/shard_map/dot_general | solution.py:132
  37.8 3.1 %fusion.2 = f32[160,512]{1,0:T(8,128)S(1)} fusion(bf16[160,4096]{1,0:T(8,128)(2,1)S(1)} %convolution_convert_fusion, bf16[4096,2048]{1,0:T(8,128)(2,1)} %param.10), kind=kOutput, calls=%fused_computation.7 | convolution fusion | flops 671088640 | bytes 5832704 | tf_op jit(solution)/shard_map/dot_general | solution.py:132
  42.4 1.4 %collective-permute-start.13 = (f32[40,512]{1,0:T(8,128)S(1)}, f32[40,512]{1,0:T(8,128)S(1)}, u32[]{:S(2)}, u32[]{:S(2)}) collective-permute-start(f32[40,512]{1,0:T(8,128)S(1)} %slice.129), channel_id=1, source_target_pairs={{0,2},{1,3},{2,0},{3,1},{4,6},{5,7},{6,4},{7,5},{8,10},{9,11},{10,... | collective-permute-start | bytes 245768 | tf_op jit(solution)/shard_map/ppermute | solution.py:60
  43.8 3.1 %collective-permute-done.13 = f32[40,512]{1,0:T(8,128)S(1)} collective-permute-done((f32[40,512]{1,0:T(8,128)S(1)}, f32[40,512]{1,0:T(8,128)S(1)}, u32[]{:S(2)}, u32[]{:S(2)}) %collective-permute-start.13) | collective-permute-done | bytes 81952 | tf_op jit(solution)/shard_map/ppermute | solution.py:60
  47.3 1.4 %collective-permute-start.14 = (f32[3,40]{1,0:T(4,128)S(1)}, f32[3,40]{1,0:T(4,128)S(1)}, u32[]{:S(2)}, u32[]{:S(2)}) collective-permute-start(f32[3,40]{1,0:T(4,128)S(1)} %pad_maximum_fusion.3), channel_id=1, source_target_pairs={{0,4},{4,0},{8,12},{12,8},{16,20},{20,16},{24,28},{28,24},{1,5},{5... | collective-permute-start | bytes 1448 | tf_op jit(solution)/shard_map/ppermute | solution.py:86
  48.8 1.6 %collective-permute-start.8 = (f32[40,1536]{1,0:T(8,128)S(1)}, f32[40,1536]{1,0:T(8,128)S(1)}, u32[]{:S(2)}, u32[]{:S(2)}) collective-permute-start(f32[40,1536]{1,0:T(8,128)S(1)} %slice.127), channel_id=1, source_target_pairs={{0,2},{1,3},{2,0},{3,1},{4,6},{5,7},{6,4},{7,5},{8,10},{9,11},{10,... | collective-permute-start | bytes 737288 | tf_op jit(solution)/shard_map/ppermute | solution.py:60
  51.0 1.5 %collective-permute-start.15 = (f32[3,40]{1,0:T(4,128)S(1)}, f32[3,40]{1,0:T(4,128)S(1)}, u32[]{:S(2)}, u32[]{:S(2)}) collective-permute-start(f32[3,40]{1,0:T(4,128)S(1)} %pad_maximum_fusion.4), channel_id=1, source_target_pairs={{0,8},{4,12},{8,0},{12,4},{16,24},{20,28},{24,16},{28,20},{1,9},{5... | collective-permute-start | bytes 1448 | tf_op jit(solution)/shard_map/ppermute | solution.py:86
  52.5 3.3 %collective-permute-done.8 = f32[40,1536]{1,0:T(8,128)S(1)} collective-permute-done((f32[40,1536]{1,0:T(8,128)S(1)}, f32[40,1536]{1,0:T(8,128)S(1)}, u32[]{:S(2)}, u32[]{:S(2)}) %collective-permute-start.8) | collective-permute-done | bytes 245792 | tf_op jit(solution)/shard_map/ppermute | solution.py:60
  56.9 2.9 %collective-permute-done.9 = f32[3,40]{1,0:T(4,128)S(1)} collective-permute-done((f32[3,40]{1,0:T(4,128)S(1)}, f32[3,40]{1,0:T(4,128)S(1)}, u32[]{:S(2)}, u32[]{:S(2)}) %collective-permute-start.9) | collective-permute-done | bytes 512 | tf_op jit(solution)/shard_map/ppermute | solution.py:86
  59.8 1.6 %collective-permute-start.10 = (f32[3,40]{1,0:T(4,128)S(1)}, f32[3,40]{1,0:T(4,128)S(1)}, u32[]{:S(2)}, u32[]{:S(2)}) collective-permute-start(f32[3,40]{1,0:T(4,128)S(1)} %pad_maximum_fusion.1), channel_id=1, source_target_pairs={{0,8},{4,12},{8,0},{12,4},{16,24},{20,28},{24,16},{28,20},{1,9},{5... | collective-permute-start | bytes 1448 | tf_op jit(solution)/shard_map/ppermute | solution.py:86
  61.5 2.7 %collective-permute-start.16 = (f32[3,40]{1,0:T(4,128)S(1)}, f32[3,40]{1,0:T(4,128)S(1)}, u32[]{:S(2)}, u32[]{:S(2)}) collective-permute-start(f32[3,40]{1,0:T(4,128)S(1)} %pad_maximum_fusion.5), channel_id=1, source_target_pairs={{0,16},{4,20},{8,24},{12,28},{16,0},{20,4},{24,8},{28,12},{1,17},{... | collective-permute-start | bytes 1448 | tf_op jit(solution)/shard_map/ppermute | solution.py:86
  64.2 2.0 %collective-permute-start.11 = (f32[3,40]{1,0:T(4,128)S(1)}, f32[3,40]{1,0:T(4,128)S(1)}, u32[]{:S(2)}, u32[]{:S(2)}) collective-permute-start(f32[3,40]{1,0:T(4,128)S(1)} %pad_maximum_fusion.2), channel_id=1, source_target_pairs={{0,16},{4,20},{8,24},{12,28},{16,0},{20,4},{24,8},{28,12},{1,17},{... | collective-permute-start | bytes 1448 | tf_op jit(solution)/shard_map/ppermute | solution.py:86
  66.9 1.8 %collective-permute-done.11 = f32[3,40]{1,0:T(4,128)S(1)} collective-permute-done((f32[3,40]{1,0:T(4,128)S(1)}, f32[3,40]{1,0:T(4,128)S(1)}, u32[]{:S(2)}, u32[]{:S(2)}) %collective-permute-start.11) | collective-permute-done | bytes 512 | tf_op jit(solution)/shard_map/ppermute | solution.py:86
  70.1 1.5 %collective-permute-start.18 = (f32[160]{0:T(256)S(1)}, f32[160]{0:T(256)S(1)}, u32[]{:S(2)}, u32[]{:S(2)}) collective-permute-start(f32[160]{0:T(256)S(1)} %add_dynamic-update-slice_fusion), channel_id=1, source_target_pairs={{0,2},{1,3},{2,0},{3,1},{4,6},{5,7},{6,4},{7,5},{8,10},{9,11},{10,... | collective-permute-start | bytes 1928 | tf_op jit(solution)/shard_map/ppermute | solution.py:101
  72.4 1.3 %collective-permute-done.18 = f32[160]{0:T(256)S(1)} collective-permute-done((f32[160]{0:T(256)S(1)}, f32[160]{0:T(256)S(1)}, u32[]{:S(2)}, u32[]{:S(2)}) %collective-permute-start.18) | collective-permute-done | bytes 672 | tf_op jit(solution)/shard_map/ppermute | solution.py:101
  (79 shorter events, 12.7 us)
Async XLA Ops:
  0.6 6.0 %copy-start = (s32[256]{0:T(256)S(1)}, s32[256]{0:T(256)}, u32[]{:S(2)}) copy-start(s32[256]{0:T(256)} %param.12) | copy-start | bytes 3076
  0.6 9.5 %collective-permute-start = (bf16[32,4096]{1,0:T(8,128)(2,1)}, bf16[32,4096]{1,0:T(8,128)(2,1)S(1)}, u32[]{:S(2)}, u32[]{:S(2)}) collective-permute-start(bf16[32,4096]{1,0:T(8,128)(2,1)} %param.9), channel_id=1, source_target_pairs={{0,8},{8,16},{16,24},{24,28},{28,20},{20,12},{12,4},{4,0},{1,9},{9... | collective-permute-start | bytes 786440 | tf_op jit(solution)/shard_map/ppermute | solution.py:39
  3.7 8.5 %collective-permute-start.4 = (bf16[32,4096]{1,0:T(8,128)(2,1)}, bf16[32,4096]{1,0:T(8,128)(2,1)S(1)}, u32[]{:S(2)}, u32[]{:S(2)}) collective-permute-start(bf16[32,4096]{1,0:T(8,128)(2,1)} %param.9), channel_id=1, source_target_pairs={{8,0},{16,8},{24,16},{28,24},{20,28},{12,20},{4,12},{0,4},{9,1},{1... | collective-permute-start | bytes 786440 | tf_op jit(solution)/shard_map/ppermute | solution.py:42
  10.2 7.8 %collective-permute-start.1 = (bf16[32,4096]{1,0:T(8,128)(2,1)S(1)}, bf16[32,4096]{1,0:T(8,128)(2,1)S(1)}, u32[]{:S(2)}, u32[]{:S(2)}) collective-permute-start(bf16[32,4096]{1,0:T(8,128)(2,1)S(1)} %collective-permute-done), channel_id=1, source_target_pairs={{0,8},{8,16},{16,24},{24,28},{28,20},{20,12},{12,4},{4,0},{1,9},{9... | collective-permute-start | bytes 786440 | tf_op jit(solution)/shard_map/ppermute | solution.py:39
  12.2 7.5 %collective-permute-start.5 = (bf16[32,4096]{1,0:T(8,128)(2,1)S(1)}, bf16[32,4096]{1,0:T(8,128)(2,1)S(1)}, u32[]{:S(2)}, u32[]{:S(2)}) collective-permute-start(bf16[32,4096]{1,0:T(8,128)(2,1)S(1)} %collective-permute-done.4), channel_id=1, source_target_pairs={{8,0},{16,8},{24,16},{28,24},{20,28},{12,20},{4,12},{0,4},{9,1},{1... | collective-permute-start | bytes 786440 | tf_op jit(solution)/shard_map/ppermute | solution.py:42
  18.0 6.9 %collective-permute-start.2 = (bf16[32,4096]{1,0:T(8,128)(2,1)S(1)}, bf16[32,4096]{1,0:T(8,128)(2,1)S(1)}, u32[]{:S(2)}, u32[]{:S(2)}) collective-permute-start(bf16[32,4096]{1,0:T(8,128)(2,1)S(1)} %collective-permute-done.1), channel_id=1, source_target_pairs={{0,8},{8,16},{16,24},{24,28},{28,20},{20,12},{12,4},{4,0},{1,9},{9... | collective-permute-start | bytes 786440 | tf_op jit(solution)/shard_map/ppermute | solution.py:39
  19.7 11.6 %collective-permute-start.6 = (bf16[32,4096]{1,0:T(8,128)(2,1)S(1)}, bf16[32,4096]{1,0:T(8,128)(2,1)S(1)}, u32[]{:S(2)}, u32[]{:S(2)}) collective-permute-start(bf16[32,4096]{1,0:T(8,128)(2,1)S(1)} %collective-permute-done.5), channel_id=1, source_target_pairs={{8,0},{16,8},{24,16},{28,24},{20,28},{12,20},{4,12},{0,4},{9,1},{1... | collective-permute-start | bytes 786440 | tf_op jit(solution)/shard_map/ppermute | solution.py:42
  24.9 6.4 %collective-permute-start.3 = (bf16[32,4096]{1,0:T(8,128)(2,1)S(1)}, bf16[32,4096]{1,0:T(8,128)(2,1)S(1)}, u32[]{:S(2)}, u32[]{:S(2)}) collective-permute-start(bf16[32,4096]{1,0:T(8,128)(2,1)S(1)} %collective-permute-done.2), channel_id=1, source_target_pairs={{0,8},{8,16},{16,24},{24,28},{28,20},{20,12},{12,4},{4,0},{1,9},{9... | collective-permute-start | bytes 786440 | tf_op jit(solution)/shard_map/ppermute | solution.py:39
  40.9 1.5 %collective-permute-start.12 = (f32[80,512]{1,0:T(8,128)S(1)}, f32[80,512]{1,0:T(8,128)S(1)}, u32[]{:S(2)}, u32[]{:S(2)}) collective-permute-start(f32[80,512]{1,0:T(8,128)S(1)} %slice.104), channel_id=1, source_target_pairs={{0,1},{1,0},{2,3},{3,2},{4,5},{5,4},{6,7},{7,6},{8,9},{9,8},{10,11... | collective-permute-start | bytes 491528 | tf_op jit(solution)/shard_map/ppermute | solution.py:60
  41.0 7.7 %collective-permute-start.7 = (f32[80,1536]{1,0:T(8,128)S(1)}, f32[80,1536]{1,0:T(8,128)S(1)}, u32[]{:S(2)}, u32[]{:S(2)}) collective-permute-start(f32[80,1536]{1,0:T(8,128)S(1)} %slice.92), channel_id=1, source_target_pairs={{0,1},{1,0},{2,3},{3,2},{4,5},{5,4},{6,7},{7,6},{8,9},{9,8},{10,11... | collective-permute-start | bytes 1474568 | tf_op jit(solution)/shard_map/ppermute | solution.py:60
  42.4 29.3 %copy-start.1 = (s32[8]{0:T(128)S(1)}, s32[8]{0:T(128)}, u32[]{:S(2)}) copy-start(s32[8]{0:T(128)} %param.11) | copy-start | bytes 100
  42.4 4.6 %collective-permute-start.13 = (f32[40,512]{1,0:T(8,128)S(1)}, f32[40,512]{1,0:T(8,128)S(1)}, u32[]{:S(2)}, u32[]{:S(2)}) collective-permute-start(f32[40,512]{1,0:T(8,128)S(1)} %slice.129), channel_id=1, source_target_pairs={{0,2},{1,3},{2,0},{3,1},{4,6},{5,7},{6,4},{7,5},{8,10},{9,11},{10,... | collective-permute-start | bytes 245768 | tf_op jit(solution)/shard_map/ppermute | solution.py:60
  47.3 27.1 %copy-start.2 = (f32[32]{0:T(128)S(1)}, f32[32]{0:T(128)}, u32[]{:S(2)}) copy-start(f32[32]{0:T(128)} %param.13) | copy-start | bytes 388
  47.3 3.7 %collective-permute-start.14 = (f32[3,40]{1,0:T(4,128)S(1)}, f32[3,40]{1,0:T(4,128)S(1)}, u32[]{:S(2)}, u32[]{:S(2)}) collective-permute-start(f32[3,40]{1,0:T(4,128)S(1)} %pad_maximum_fusion.3), channel_id=1, source_target_pairs={{0,4},{4,0},{8,12},{12,8},{16,20},{20,16},{24,28},{28,24},{1,5},{5... | collective-permute-start | bytes 1448 | tf_op jit(solution)/shard_map/ppermute | solution.py:86
  48.8 6.9 %collective-permute-start.8 = (f32[40,1536]{1,0:T(8,128)S(1)}, f32[40,1536]{1,0:T(8,128)S(1)}, u32[]{:S(2)}, u32[]{:S(2)}) collective-permute-start(f32[40,1536]{1,0:T(8,128)S(1)} %slice.127), channel_id=1, source_target_pairs={{0,2},{1,3},{2,0},{3,1},{4,6},{5,7},{6,4},{7,5},{8,10},{9,11},{10,... | collective-permute-start | bytes 737288 | tf_op jit(solution)/shard_map/ppermute | solution.py:60
  51.0 5.9 %collective-permute-start.15 = (f32[3,40]{1,0:T(4,128)S(1)}, f32[3,40]{1,0:T(4,128)S(1)}, u32[]{:S(2)}, u32[]{:S(2)}) collective-permute-start(f32[3,40]{1,0:T(4,128)S(1)} %pad_maximum_fusion.4), channel_id=1, source_target_pairs={{0,8},{4,12},{8,0},{12,4},{16,24},{20,28},{24,16},{28,20},{1,9},{5... | collective-permute-start | bytes 1448 | tf_op jit(solution)/shard_map/ppermute | solution.py:86
  56.1 3.7 %collective-permute-start.9 = (f32[3,40]{1,0:T(4,128)S(1)}, f32[3,40]{1,0:T(4,128)S(1)}, u32[]{:S(2)}, u32[]{:S(2)}) collective-permute-start(f32[3,40]{1,0:T(4,128)S(1)} %pad_maximum_fusion), channel_id=1, source_target_pairs={{0,4},{4,0},{8,12},{12,8},{16,20},{20,16},{24,28},{28,24},{1,5},{5... | collective-permute-start | bytes 1448 | tf_op jit(solution)/shard_map/ppermute | solution.py:86
  59.8 4.3 %collective-permute-start.10 = (f32[3,40]{1,0:T(4,128)S(1)}, f32[3,40]{1,0:T(4,128)S(1)}, u32[]{:S(2)}, u32[]{:S(2)}) collective-permute-start(f32[3,40]{1,0:T(4,128)S(1)} %pad_maximum_fusion.1), channel_id=1, source_target_pairs={{0,8},{4,12},{8,0},{12,4},{16,24},{20,28},{24,16},{28,20},{1,9},{5... | collective-permute-start | bytes 1448 | tf_op jit(solution)/shard_map/ppermute | solution.py:86
  61.5 5.4 %collective-permute-start.16 = (f32[3,40]{1,0:T(4,128)S(1)}, f32[3,40]{1,0:T(4,128)S(1)}, u32[]{:S(2)}, u32[]{:S(2)}) collective-permute-start(f32[3,40]{1,0:T(4,128)S(1)} %pad_maximum_fusion.5), channel_id=1, source_target_pairs={{0,16},{4,20},{8,24},{12,28},{16,0},{20,4},{24,8},{28,12},{1,17},{... | collective-permute-start | bytes 1448 | tf_op jit(solution)/shard_map/ppermute | solution.py:86
  64.2 4.5 %collective-permute-start.11 = (f32[3,40]{1,0:T(4,128)S(1)}, f32[3,40]{1,0:T(4,128)S(1)}, u32[]{:S(2)}, u32[]{:S(2)}) collective-permute-start(f32[3,40]{1,0:T(4,128)S(1)} %pad_maximum_fusion.2), channel_id=1, source_target_pairs={{0,16},{4,20},{8,24},{12,28},{16,0},{20,4},{24,8},{28,12},{1,17},{... | collective-permute-start | bytes 1448 | tf_op jit(solution)/shard_map/ppermute | solution.py:86
  68.8 1.2 %collective-permute-start.17 = (f32[160]{0:T(256)S(1)}, f32[160]{0:T(256)S(1)}, u32[]{:S(2)}, u32[]{:S(2)}) collective-permute-start(f32[160]{0:T(256)S(1)} %get-tuple-element.15), channel_id=1, source_target_pairs={{0,1},{1,0},{2,3},{3,2},{4,5},{5,4},{6,7},{7,6},{8,9},{9,8},{10,11... | collective-permute-start | bytes 1928 | tf_op jit(solution)/shard_map/ppermute | solution.py:101
  70.1 3.6 %collective-permute-start.18 = (f32[160]{0:T(256)S(1)}, f32[160]{0:T(256)S(1)}, u32[]{:S(2)}, u32[]{:S(2)}) collective-permute-start(f32[160]{0:T(256)S(1)} %add_dynamic-update-slice_fusion), channel_id=1, source_target_pairs={{0,2},{1,3},{2,0},{3,1},{4,6},{5,7},{6,4},{7,5},{8,10},{9,11},{10,... | collective-permute-start | bytes 1928 | tf_op jit(solution)/shard_map/ppermute | solution.py:101

commit v7 on v4

--- a/solution.py
+++ b/solution.py
@@ -50,7 +50,7 @@
     where = jnp.sum(jnp.where(hit, slot_of[:, None], 0), axis=0) * count + rows % count
     choose = lax.broadcasted_iota(jnp.int32, (stacked.shape[0], where.shape[0]), 0) == where[None, :]
     picked = lax.dot_general(choose.astype(stacked.dtype), stacked, (((0,), (0,)), ((), ())), preferred_element_type=jnp.float32)
-    return picked.astype(stacked.dtype)
+    return lax.optimization_barrier(picked.astype(stacked.dtype))
 
 
 def halving_scatter(partial, size):
@@ -70,14 +70,22 @@
     return partial, first
 
 
+def merge_pair(stats, other):
+    top = jnp.maximum(stats[0], other[0])
+    total = stats[1] * jnp.exp(stats[0] - top) + other[1] * jnp.exp(other[0] - top)
+    return jnp.stack([top, total, stats[2] + other[2]])
+
+
 def merge_stats(stats, size):
     bit = 1
     while bit < size:
-        other = lax.ppermute(stats, "dp", [(i, i ^ bit) for i in range(size)])
-        top = jnp.maximum(stats[0], other[0])
-        total = stats[1] * jnp.exp(stats[0] - top) + other[1] * jnp.exp(other[0] - top)
-        stats = jnp.stack([top, total, stats[2] + other[2]])
-        bit *= 2
+        if bit * 4 <= size:
+            got = [lax.ppermute(stats, "dp", [(i, i ^ (bit * k)) for i in range(size)]) for k in (1, 2, 3)]
+            stats = merge_pair(merge_pair(stats, got[0]), merge_pair(got[1], got[2]))
+            bit *= 4
+        else:
+            stats = merge_pair(stats, lax.ppermute(stats, "dp", [(i, i ^ bit) for i in range(size)]))
+            bit *= 2
     return stats
 
 

time: 69.4 us -> 69.1 us (level)
    ppermute x3 -> x4, waiting for transfers between devices: 4.82 us -> 4.39 us  [the longest x3 3.19 us: merge_stats(): lax.ppermute(stats, 'dp', [(i, i ^ bit * k) for i in range(size)])]
    ppermute x3 -> x4, starting transfers between devices: 6.32 us -> 6.2 us  [the longest x3 3.55 us: merge_stats(): lax.ppermute(stats, 'dp', [(i, i ^ bit * k) for i in range(size)])]
  transfers between devices with their start and end apart: 14 -> 15, of which waited for: 11 -> 12; matrix products, arithmetic and copies ran while one was open for 11% -> 11% of each run, Pallas kernels for 0% -> 0%
where the time goes in v7:
time: 69.1 us; the launch traced here: 68.9 us
  waiting for transfers between devices  31.5 us (46%)
  starting transfers between devices  18.5 us (27%)
  matrix products  7.93 us (11%)
  local copies, waits for them, and re-layouts  5.32 us (8%)
  other arithmetic  4.72 us (7%)
  between operations  0.92 us (1%)
    ppermute x4, waiting for transfers between devices, ring_gather(): ahead = lax.ppermute(ahead, 'dp', fwd)  15.5 us
    ppermute x2, waiting for transfers between devices, halving_scatter(): got = lax.ppermute(send, 'vocab', [(i, i ^ bit) for i in range(size)])  9.12 us
    ppermute x4, starting transfers between devices, ring_gather(): ahead = lax.ppermute(ahead, 'dp', fwd)  8.21 us
    dot_general x1, matrix products, on_device(): jnp.dot(full_rows, head_weight, preferred_element_type=jnp.float32)  7.37 us
    ppermute x3, starting transfers between devices, merge_stats(): lax.ppermute(stats, 'dp', [(i, i ^ bit * k) for i in range(size)])  3.55 us
    ppermute x3, waiting for transfers between devices, merge_stats(): lax.ppermute(stats, 'dp', [(i, i ^ bit * k) for i in range(size)])  3.19 us
    ppermute x1, starting transfers between devices, merge_stats(): lax.ppermute(stats, 'dp', [(i, i ^ bit) for i in range(size)])  2.65 us
    ppermute x2, waiting for transfers between devices, doubling_gather(): other = lax.ppermute(out, 'vocab', [(i, i ^ bit) for i in range(size)])  2.47 us
  transfers between devices with their start and end apart: 15, of which 12 were waited for; matrix products, arithmetic and copies ran while one was open for 11% of the time, Pallas kernels for 0%

profile of v7, /device:TPU:0, one launch (start us, length us, event | category | flops | bytes accessed | tf_op | source)
XLA Modules:
  0.0 68.9 jit_solution(13587643618241293349)
XLA Ops:
  0.6 3.1 %collective-permute-start = (bf16[32,4096]{1,0:T(8,128)(2,1)}, bf16[32,4096]{1,0:T(8,128)(2,1)S(1)}, u32[]{:S(2)}, u32[]{:S(2)}) collective-permute-start(bf16[32,4096]{1,0:T(8,128)(2,1)} %param.13), channel_id=1, source_target_pairs={{0,8},{8,16},{16,24},{24,28},{28,20},{20,12},{12,4},{4,0},{1,9},{9... | collective-permute-start | bytes 786440 | tf_op jit(solution)/shard_map/ppermute | solution.py:39
  3.8 1.0 %bitcast_dynamic-update-slice_fusion.7 = bf16[8,32,4096]{2,1,0:T(8,128)(2,1)S(1)} fusion(bf16[32,4096]{1,0:T(8,128)(2,1)} %param.13), kind=kLoop, calls=%fused_computation.18 | loop fusion | bytes 524288
  4.8 0.8 %reduce-window.8 = s32[8,1]{0,1:T(1,128)S(1)} reduce-window(s32[8,1]{0,1:T(1,128)} %bitcast.166, s32[]{:T(128)} %constant.172.clone.1), window={size=8x1 pad=7_0x0_0}, to_apply=%region_0.2 | reduce-window | flops 56 | bytes 68 | tf_op jit(solution)/shard_map/reduce-window.3
  6.5 1.2 %dynamic_slice.7 = s32[1]{0:T(128)} dynamic-slice(s32[8]{0:T(128)} %constant.196.clone, s32[]{:T(128)S(6)} %select_n.127), dynamic_slice_sizes={1} | dynamic-slice | bytes 12 | tf_op jit(solution)/shard_map/dynamic_slice | solution.py:46
  7.7 1.3 %and_select_fusion.1 = s32[8]{0:T(128)S(1)} fusion(s32[8]{0:T(128)} %constant.235, s32[]{:T(128)} %bitcast.2), kind=kLoop, calls=%fused_computation.40 | loop fusion | flops 96 | bytes 68 | tf_op jit(solution)/shard_map/jit(remainder)/select_n | solution.py:47
  9.2 1.0 %collective-permute-done = bf16[32,4096]{1,0:T(8,128)(2,1)S(1)} collective-permute-done((bf16[32,4096]{1,0:T(8,128)(2,1)}, bf16[32,4096]{1,0:T(8,128)(2,1)S(1)}, u32[]{:S(2)}, u32[]{:S(2)}) %collective-permute-start) | collective-permute-done | bytes 262176 | tf_op jit(solution)/shard_map/ppermute | solution.py:39
  10.2 1.8 %collective-permute-start.1 = (bf16[32,4096]{1,0:T(8,128)(2,1)S(1)}, bf16[32,4096]{1,0:T(8,128)(2,1)S(1)}, u32[]{:S(2)}, u32[]{:S(2)}) collective-permute-start(bf16[32,4096]{1,0:T(8,128)(2,1)S(1)} %collective-permute-done), channel_id=1, source_target_pairs={{0,8},{8,16},{16,24},{24,28},{28,20},{20,12},{12,4},{4,0},{1,9},{9... | collective-permute-start | bytes 786440 | tf_op jit(solution)/shard_map/ppermute | solution.py:39
  12.3 5.4 %collective-permute-done.1 = bf16[32,4096]{1,0:T(8,128)(2,1)S(1)} collective-permute-done((bf16[32,4096]{1,0:T(8,128)(2,1)S(1)}, bf16[32,4096]{1,0:T(8,128)(2,1)S(1)}, u32[]{:S(2)}, u32[]{:S(2)}) %collective-permute-start.1) | collective-permute-done | bytes 262176 | tf_op jit(solution)/shard_map/ppermute | solution.py:39
  17.7 1.5 %collective-permute-start.2 = (bf16[32,4096]{1,0:T(8,128)(2,1)S(1)}, bf16[32,4096]{1,0:T(8,128)(2,1)S(1)}, u32[]{:S(2)}, u32[]{:S(2)}) collective-permute-start(bf16[32,4096]{1,0:T(8,128)(2,1)S(1)} %collective-permute-done.1), channel_id=1, source_target_pairs={{0,8},{8,16},{16,24},{24,28},{28,20},{20,12},{12,4},{4,0},{1,9},{9... | collective-permute-start | bytes 786440 | tf_op jit(solution)/shard_map/ppermute | solution.py:39
  19.8 4.5 %collective-permute-done.2 = bf16[32,4096]{1,0:T(8,128)(2,1)S(1)} collective-permute-done((bf16[32,4096]{1,0:T(8,128)(2,1)S(1)}, bf16[32,4096]{1,0:T(8,128)(2,1)S(1)}, u32[]{:S(2)}, u32[]{:S(2)}) %collective-permute-start.2) | collective-permute-done | bytes 262176 | tf_op jit(solution)/shard_map/ppermute | solution.py:39
  24.3 1.7 %collective-permute-start.3 = (bf16[32,4096]{1,0:T(8,128)(2,1)S(1)}, bf16[32,4096]{1,0:T(8,128)(2,1)S(1)}, u32[]{:S(2)}, u32[]{:S(2)}) collective-permute-start(bf16[32,4096]{1,0:T(8,128)(2,1)S(1)} %collective-permute-done.2), channel_id=1, source_target_pairs={{0,8},{8,16},{16,24},{24,28},{28,20},{20,12},{12,4},{4,0},{1,9},{9... | collective-permute-start | bytes 786440 | tf_op jit(solution)/shard_map/ppermute | solution.py:39
  26.0 4.6 %collective-permute-done.3 = bf16[32,4096]{1,0:T(8,128)(2,1)S(1)} collective-permute-done((bf16[32,4096]{1,0:T(8,128)(2,1)S(1)}, bf16[32,4096]{1,0:T(8,128)(2,1)S(1)}, u32[]{:S(2)}, u32[]{:S(2)}) %collective-permute-start.3) | collective-permute-done | bytes 262176 | tf_op jit(solution)/shard_map/ppermute | solution.py:39
  31.3 7.4 %fusion.30 = f32[160,2048]{1,0:T(8,128)S(1)} fusion(bf16[160,4096]{1,0:T(8,128)(2,1)S(1)} %convolution_convert_fusion, bf16[4096,2048]{1,0:T(8,128)(2,1)} %param.14), kind=kOutput, calls=%fused_computation.107 | convolution fusion | flops 2684354560 | bytes 19398656 | tf_op jit(solution)/shard_map/dot_general | solution.py:123
  39.8 1.1 %collective-permute-done.7 = f32[80,2048]{1,0:T(8,128)S(1)} collective-permute-done((f32[80,2048]{1,0:T(8,128)S(1)}, f32[80,2048]{1,0:T(8,128)S(1)}, u32[]{:S(2)}, u32[]{:S(2)}) %collective-permute-start.7) | collective-permute-done | bytes 655392 | tf_op jit(solution)/shard_map/ppermute | solution.py:66
  41.1 1.7 %collective-permute-start.8 = (f32[40,2048]{1,0:T(8,128)S(1)}, f32[40,2048]{1,0:T(8,128)S(1)}, u32[]{:S(2)}, u32[]{:S(2)}) collective-permute-start(f32[40,2048]{1,0:T(8,128)S(1)} %select_bitcast_fusion.1), channel_id=1, source_target_pairs={{0,2},{1,3},{2,0},{3,1},{4,6},{5,7},{6,4},{7,5},{8,10},{9,11},{10,... | collective-permute-start | bytes 983048 | tf_op jit(solution)/shard_map/ppermute | solution.py:66
  42.9 8.0 %collective-permute-done.8 = f32[40,2048]{1,0:T(8,128)S(1)} collective-permute-done((f32[40,2048]{1,0:T(8,128)S(1)}, f32[40,2048]{1,0:T(8,128)S(1)}, u32[]{:S(2)}, u32[]{:S(2)}) %collective-permute-start.8) | collective-permute-done | bytes 327712 | tf_op jit(solution)/shard_map/ppermute | solution.py:66
  51.3 1.8 %collective-permute-start.10 = (f32[3,40]{1,0:T(4,128)S(1)}, f32[3,40]{1,0:T(4,128)S(1)}, u32[]{:S(2)}, u32[]{:S(2)}) collective-permute-start(f32[3,40]{1,0:T(4,128)S(1)} %pad_maximum_fusion), channel_id=1, source_target_pairs={{0,8},{4,12},{8,0},{12,4},{16,24},{20,28},{24,16},{28,20},{1,9},{5... | collective-permute-start | bytes 1448 | tf_op jit(solution)/shard_map/ppermute | solution.py:83
  53.1 1.4 %collective-permute-start.11 = (f32[3,40]{1,0:T(4,128)S(1)}, f32[3,40]{1,0:T(4,128)S(1)}, u32[]{:S(2)}, u32[]{:S(2)}) collective-permute-start(f32[3,40]{1,0:T(4,128)S(1)} %pad_maximum_fusion), channel_id=1, source_target_pairs={{0,12},{4,8},{8,4},{12,0},{16,28},{20,24},{24,20},{28,16},{1,13},{... | collective-permute-start | bytes 1448 | tf_op jit(solution)/shard_map/ppermute | solution.py:83
  54.9 2.6 %collective-permute-done.11 = f32[3,40]{1,0:T(4,128)S(1)} collective-permute-done((f32[3,40]{1,0:T(4,128)S(1)}, f32[3,40]{1,0:T(4,128)S(1)}, u32[]{:S(2)}, u32[]{:S(2)}) %collective-permute-start.11) | collective-permute-done | bytes 512 | tf_op jit(solution)/shard_map/ppermute | solution.py:83
  58.1 2.6 %collective-permute-start.12 = (f32[3,40]{1,0:T(4,128)S(1)}, f32[3,40]{1,0:T(4,128)S(1)}, u32[]{:S(2)}, u32[]{:S(2)}) collective-permute-start(f32[3,40]{1,0:T(4,128)S(1)} %pad_maximum_fusion.1), channel_id=1, source_target_pairs={{0,16},{4,20},{8,24},{12,28},{16,0},{20,4},{24,8},{28,12},{1,17},{... | collective-permute-start | bytes 1448 | tf_op jit(solution)/shard_map/ppermute | solution.py:87
  61.4 1.2 %collective-permute-done.12 = f32[3,40]{1,0:T(4,128)S(1)} collective-permute-done((f32[3,40]{1,0:T(4,128)S(1)}, f32[3,40]{1,0:T(4,128)S(1)}, u32[]{:S(2)}, u32[]{:S(2)}) %collective-permute-start.12) | collective-permute-done | bytes 512 | tf_op jit(solution)/shard_map/ppermute | solution.py:87
  62.8 1.1 %collective-permute-done.13 = f32[160]{0:T(256)S(1)} collective-permute-done((f32[160]{0:T(256)S(1)}, f32[160]{0:T(256)S(1)}, u32[]{:S(2)}, u32[]{:S(2)}) %collective-permute-start.13) | collective-permute-done | bytes 672 | tf_op jit(solution)/shard_map/ppermute | solution.py:99
  64.1 1.5 %collective-permute-start.14 = (f32[160]{0:T(256)S(1)}, f32[160]{0:T(256)S(1)}, u32[]{:S(2)}, u32[]{:S(2)}) collective-permute-start(f32[160]{0:T(256)S(1)} %add_dynamic-update-slice_fusion), channel_id=1, source_target_pairs={{0,2},{1,3},{2,0},{3,1},{4,6},{5,7},{6,4},{7,5},{8,10},{9,11},{10,... | collective-permute-start | bytes 1928 | tf_op jit(solution)/shard_map/ppermute | solution.py:99
  66.3 1.3 %collective-permute-done.14 = f32[160]{0:T(256)S(1)} collective-permute-done((f32[160]{0:T(256)S(1)}, f32[160]{0:T(256)S(1)}, u32[]{:S(2)}, u32[]{:S(2)}) %collective-permute-start.14) | collective-permute-done | bytes 672 | tf_op jit(solution)/shard_map/ppermute | solution.py:99
  (56 shorter events, 8.0 us)
Async XLA Ops:
  0.6 38.4 %copy-start = (s32[256]{0:T(256)S(1)}, s32[256]{0:T(256)}, u32[]{:S(2)}) copy-start(s32[256]{0:T(256)} %param.16) | copy-start | bytes 3076
  0.6 9.5 %collective-permute-start = (bf16[32,4096]{1,0:T(8,128)(2,1)}, bf16[32,4096]{1,0:T(8,128)(2,1)S(1)}, u32[]{:S(2)}, u32[]{:S(2)}) collective-permute-start(bf16[32,4096]{1,0:T(8,128)(2,1)} %param.13), channel_id=1, source_target_pairs={{0,8},{8,16},{16,24},{24,28},{28,20},{20,12},{12,4},{4,0},{1,9},{9... | collective-permute-start | bytes 786440 | tf_op jit(solution)/shard_map/ppermute | solution.py:39
  3.7 8.3 %collective-permute-start.4 = (bf16[32,4096]{1,0:T(8,128)(2,1)}, bf16[32,4096]{1,0:T(8,128)(2,1)S(1)}, u32[]{:S(2)}, u32[]{:S(2)}) collective-permute-start(bf16[32,4096]{1,0:T(8,128)(2,1)} %param.13), channel_id=1, source_target_pairs={{8,0},{16,8},{24,16},{28,24},{20,28},{12,20},{4,12},{0,4},{9,1},{1... | collective-permute-start | bytes 786440 | tf_op jit(solution)/shard_map/ppermute | solution.py:42
  10.2 7.5 %collective-permute-start.1 = (bf16[32,4096]{1,0:T(8,128)(2,1)S(1)}, bf16[32,4096]{1,0:T(8,128)(2,1)S(1)}, u32[]{:S(2)}, u32[]{:S(2)}) collective-permute-start(bf16[32,4096]{1,0:T(8,128)(2,1)S(1)} %collective-permute-done), channel_id=1, source_target_pairs={{0,8},{8,16},{16,24},{24,28},{28,20},{20,12},{12,4},{4,0},{1,9},{9... | collective-permute-start | bytes 786440 | tf_op jit(solution)/shard_map/ppermute | solution.py:39
  12.0 7.2 %collective-permute-start.5 = (bf16[32,4096]{1,0:T(8,128)(2,1)S(1)}, bf16[32,4096]{1,0:T(8,128)(2,1)S(1)}, u32[]{:S(2)}, u32[]{:S(2)}) collective-permute-start(bf16[32,4096]{1,0:T(8,128)(2,1)S(1)} %collective-permute-done.4), channel_id=1, source_target_pairs={{8,0},{16,8},{24,16},{28,24},{20,28},{12,20},{4,12},{0,4},{9,1},{1... | collective-permute-start | bytes 786440 | tf_op jit(solution)/shard_map/ppermute | solution.py:42
  17.7 6.6 %collective-permute-start.2 = (bf16[32,4096]{1,0:T(8,128)(2,1)S(1)}, bf16[32,4096]{1,0:T(8,128)(2,1)S(1)}, u32[]{:S(2)}, u32[]{:S(2)}) collective-permute-start(bf16[32,4096]{1,0:T(8,128)(2,1)S(1)} %collective-permute-done.1), channel_id=1, source_target_pairs={{0,8},{8,16},{16,24},{24,28},{28,20},{20,12},{12,4},{4,0},{1,9},{9... | collective-permute-start | bytes 786440 | tf_op jit(solution)/shard_map/ppermute | solution.py:39
  19.2 11.4 %collective-permute-start.6 = (bf16[32,4096]{1,0:T(8,128)(2,1)S(1)}, bf16[32,4096]{1,0:T(8,128)(2,1)S(1)}, u32[]{:S(2)}, u32[]{:S(2)}) collective-permute-start(bf16[32,4096]{1,0:T(8,128)(2,1)S(1)} %collective-permute-done.5), channel_id=1, source_target_pairs={{8,0},{16,8},{24,16},{28,24},{20,28},{12,20},{4,12},{0,4},{9,1},{1... | collective-permute-start | bytes 786440 | tf_op jit(solution)/shard_map/ppermute | solution.py:42
  24.3 6.4 %collective-permute-start.3 = (bf16[32,4096]{1,0:T(8,128)(2,1)S(1)}, bf16[32,4096]{1,0:T(8,128)(2,1)S(1)}, u32[]{:S(2)}, u32[]{:S(2)}) collective-permute-start(bf16[32,4096]{1,0:T(8,128)(2,1)S(1)} %collective-permute-done.2), channel_id=1, source_target_pairs={{0,8},{8,16},{16,24},{24,28},{28,20},{20,12},{12,4},{4,0},{1,9},{9... | collective-permute-start | bytes 786440 | tf_op jit(solution)/shard_map/ppermute | solution.py:39
  38.8 2.2 %collective-permute-start.7 = (f32[80,2048]{1,0:T(8,128)S(1)}, f32[80,2048]{1,0:T(8,128)S(1)}, u32[]{:S(2)}, u32[]{:S(2)}) collective-permute-start(f32[80,2048]{1,0:T(8,128)S(1)} %select_bitcast_fusion), channel_id=1, source_target_pairs={{0,1},{1,0},{2,3},{3,2},{4,5},{5,4},{6,7},{7,6},{8,9},{9,8},{10,11... | collective-permute-start | bytes 1966088 | tf_op jit(solution)/shard_map/ppermute | solution.py:66
  39.8 25.8 %copy-start.1 = (s32[8]{0:T(128)S(1)}, s32[8]{0:T(128)}, u32[]{:S(2)}) copy-start(s32[8]{0:T(128)} %param.15) | copy-start | bytes 100
  41.0 27.4 %copy-start.2 = (f32[32]{0:T(128)S(1)}, f32[32]{0:T(128)}, u32[]{:S(2)}) copy-start(f32[32]{0:T(128)} %param.17) | copy-start | bytes 388
  41.1 9.8 %collective-permute-start.8 = (f32[40,2048]{1,0:T(8,128)S(1)}, f32[40,2048]{1,0:T(8,128)S(1)}, u32[]{:S(2)}, u32[]{:S(2)}) collective-permute-start(f32[40,2048]{1,0:T(8,128)S(1)} %select_bitcast_fusion.1), channel_id=1, source_target_pairs={{0,2},{1,3},{2,0},{3,1},{4,6},{5,7},{6,4},{7,5},{8,10},{9,11},{10,... | collective-permute-start | bytes 983048 | tf_op jit(solution)/shard_map/ppermute | solution.py:66
  51.3 3.7 %collective-permute-start.10 = (f32[3,40]{1,0:T(4,128)S(1)}, f32[3,40]{1,0:T(4,128)S(1)}, u32[]{:S(2)}, u32[]{:S(2)}) collective-permute-start(f32[3,40]{1,0:T(4,128)S(1)} %pad_maximum_fusion), channel_id=1, source_target_pairs={{0,8},{4,12},{8,0},{12,4},{16,24},{20,28},{24,16},{28,20},{1,9},{5... | collective-permute-start | bytes 1448 | tf_op jit(solution)/shard_map/ppermute | solution.py:83
  53.1 4.5 %collective-permute-start.11 = (f32[3,40]{1,0:T(4,128)S(1)}, f32[3,40]{1,0:T(4,128)S(1)}, u32[]{:S(2)}, u32[]{:S(2)}) collective-permute-start(f32[3,40]{1,0:T(4,128)S(1)} %pad_maximum_fusion), channel_id=1, source_target_pairs={{0,12},{4,8},{8,4},{12,0},{16,28},{20,24},{24,20},{28,16},{1,13},{... | collective-permute-start | bytes 1448 | tf_op jit(solution)/shard_map/ppermute | solution.py:83
  54.5 3.6 %collective-permute-start.9 = (f32[3,40]{1,0:T(4,128)S(1)}, f32[3,40]{1,0:T(4,128)S(1)}, u32[]{:S(2)}, u32[]{:S(2)}) collective-permute-start(f32[3,40]{1,0:T(4,128)S(1)} %pad_maximum_fusion), channel_id=1, source_target_pairs={{0,4},{4,0},{8,12},{12,8},{16,20},{20,16},{24,28},{28,24},{1,5},{5... | collective-permute-start | bytes 1448 | tf_op jit(solution)/shard_map/ppermute | solution.py:83
  58.1 4.5 %collective-permute-start.12 = (f32[3,40]{1,0:T(4,128)S(1)}, f32[3,40]{1,0:T(4,128)S(1)}, u32[]{:S(2)}, u32[]{:S(2)}) collective-permute-start(f32[3,40]{1,0:T(4,128)S(1)} %pad_maximum_fusion.1), channel_id=1, source_target_pairs={{0,16},{4,20},{8,24},{12,28},{16,0},{20,4},{24,8},{28,12},{1,17},{... | collective-permute-start | bytes 1448 | tf_op jit(solution)/shard_map/ppermute | solution.py:87
  62.8 1.2 %collective-permute-start.13 = (f32[160]{0:T(256)S(1)}, f32[160]{0:T(256)S(1)}, u32[]{:S(2)}, u32[]{:S(2)}) collective-permute-start(f32[160]{0:T(256)S(1)} %get-tuple-element.31), channel_id=1, source_target_pairs={{0,1},{1,0},{2,3},{3,2},{4,5},{5,4},{6,7},{7,6},{8,9},{9,8},{10,11... | collective-permute-start | bytes 1928 | tf_op jit(solution)/shard_map/ppermute | solution.py:99
  64.1 3.6 %collective-permute-start.14 = (f32[160]{0:T(256)S(1)}, f32[160]{0:T(256)S(1)}, u32[]{:S(2)}, u32[]{:S(2)}) collective-permute-start(f32[160]{0:T(256)S(1)} %add_dynamic-update-slice_fusion), channel_id=1, source_target_pairs={{0,2},{1,3},{2,0},{3,1},{4,6},{5,7},{6,4},{7,5},{8,10},{9,11},{10,... | collective-permute-start | bytes 1928 | tf_op jit(solution)/shard_map/ppermute | solution.py:99

commit v8 on v7

--- a/solution.py
+++ b/solution.py
@@ -35,7 +35,13 @@
     slots = [None] * size
     slots[0] = block
     ahead, behind = block, block
+    count = block.shape[0]
     for step in range(1, size // 2 + 1):
+        if step == size - step and count % 32 == 0:
+            front = lax.ppermute(ahead[:count // 2], "dp", fwd)
+            back = lax.ppermute(behind[count // 2:], "dp", bwd)
+            slots[step] = jnp.concatenate([front, back])
+            continue
         ahead = lax.ppermute(ahead, "dp", fwd)
         slots[step] = ahead
         if step < size - step:
@@ -43,7 +49,7 @@
             slots[size - step] = behind
     count = block.shape[0]
     stacked = jnp.stack(slots).reshape(-1, block.shape[1])
-    me = jnp.asarray(pos_of, jnp.int32)[lax.axis_index("dp")]
+    me = jnp.sum(jnp.where(jnp.arange(size) == lax.axis_index("dp"), jnp.asarray(pos_of, jnp.int32), 0))
     slot_of = (me - jnp.asarray(pos_of, jnp.int32)) % size
     owner = rows // count
     hit = owner[None, :] == jnp.arange(size, dtype=jnp.int32)[:, None]
@@ -112,7 +118,7 @@
         tile_width = head_weight.shape[1]
         col_start = lax.axis_index("dp") * tile_width
         live_count = all_rows * 5 // 8
-        ends = jnp.cumsum(lengths)
+        ends = jnp.sum(jnp.where(jnp.arange(MB)[None, :] <= jnp.arange(MB)[:, None], lengths[None, :], 0), axis=1)
         starts = ends - lengths
         packed = jnp.arange(live_count, dtype=jnp.int32)
         batch_hit = ends[:, None] <= packed[None, :]
@@ -132,10 +138,20 @@
         logprob = stats[2] - (stats[0] + jnp.log(stats[1]))
         all_values = doubling_gather(logprob, first, vocab_size)
         own_rows = lax.axis_index("dp") * row_count + jnp.arange(row_count, dtype=jnp.int32)
-        own_batch = own_rows // slot_count
-        is_live = own_rows % slot_count < jnp.take(lengths, own_batch)
-        own_slot = jnp.clip(jnp.take(starts, own_batch) + own_rows % slot_count, 0, live_count - 1)
-        own_values = jnp.take(all_values, own_slot)
+        if slot_count % row_count == 0:
+            own_batch = lax.axis_index("dp") * row_count // slot_count
+            hit = jnp.arange(MB) == own_batch
+            own_length = jnp.sum(jnp.where(hit, lengths, 0))
+            own_start = jnp.sum(jnp.where(hit, starts, 0))
+            offset = lax.axis_index("dp") * row_count % slot_count
+            is_live = offset + jnp.arange(row_count, dtype=jnp.int32) < own_length
+            padded = jnp.concatenate([all_values, jnp.zeros((row_count,), all_values.dtype)])
+            own_values = lax.dynamic_slice_in_dim(padded, jnp.clip(own_start + offset, 0, live_count), row_count)
+        else:
+            own_batch = own_rows // slot_count
+            is_live = own_rows % slot_count < jnp.take(lengths, own_batch)
+            own_slot = jnp.clip(jnp.take(starts, own_batch) + own_rows % slot_count, 0, live_count - 1)
+            own_values = jnp.take(all_values, own_slot)
         ref_logprob = jnp.where(is_live, own_values, 0.0)
         ratio_log = jnp.clip(ref_logprob - policy_logprobs, -20.0, 20.0)
         kl_value = jnp.where(is_live, jnp.minimum(jnp.exp(ratio_log) - ratio_log - 1.0, 10.0), 0.0)

time: 69.1 us -> 69.3 us (level)
  local copies, waits for them, and re-layouts: 5.32 us -> 1.97 us
  other arithmetic: 4.72 us -> 6.74 us
  waiting for transfers between devices: 31.5 us -> 32.2 us
    ppermute x0 -> x2, waiting for transfers between devices: none -> 4.59 us  [the longest x1 2.85 us: ring_gather(): front = lax.ppermute(ahead[:count // 2], 'dp', fwd)]
    ppermute x4 -> x3, waiting for transfers between devices: 15.5 us -> 10.9 us  [ring_gather(): ahead = lax.ppermute(ahead, 'dp', fwd)]
    reduce_sum x0 -> x3, other arithmetic: none -> 4.11 us  [the longest x1 2.04 us: on_device(): own_start = jnp.sum(jnp.where(hit, starts, 0))]
    ppermute x0 -> x2, starting transfers between devices: none -> 2.13 us  [the longest x1 1.72 us: ring_gather(): front = lax.ppermute(ahead[:count // 2], 'dp', fwd)]
    gather x3 -> x0, local copies, waits for them, and re-layouts: 2.1 us -> none  [the longest x1 0.71 us: on_device(): own_values = jnp.take(all_values, own_slot)]
    ppermute x4 -> x3, starting transfers between devices: 8.21 us -> 6.48 us  [ring_gather(): ahead = lax.ppermute(ahead, 'dp', fwd)]
    select_n x3 -> x0, other arithmetic: 1.34 us -> none  [the longest x1 1.31 us: ring_gather(): slot_of = (me - jnp.asarray(pos_of, jnp.int32)) % size]
    dynamic_slice x1 -> x0, local copies, waits for them, and re-layouts: 1.24 us -> none  [ring_gather(): me = jnp.asarray(pos_of, jnp.int32)[lax.axis_index('dp')]]
  transfers between devices with their start and end apart: 15 -> 16, of which waited for: 12 -> 13; matrix products, arithmetic and copies ran while one was open for 11% -> 9% of each run, Pallas kernels for 0% -> 0%
where the time goes in v8:
time: 69.3 us; the launch traced here: 69 us
  waiting for transfers between devices  32.2 us (46%)
  starting transfers between devices  18.7 us (27%)
  matrix products  7.93 us (11%)
  other arithmetic  6.74 us (10%)
  local copies, waits for them, and re-layouts  1.97 us (3%)
  between operations  1.55 us (2%)
    ppermute x3, waiting for transfers between devices, ring_gather(): ahead = lax.ppermute(ahead, 'dp', fwd)  10.9 us
    ppermute x2, waiting for transfers between devices, halving_scatter(): got = lax.ppermute(send, 'vocab', [(i, i ^ bit) for i in range(size)])  9.28 us
    dot_general x1, matrix products, on_device(): jnp.dot(full_rows, head_weight, preferred_element_type=jnp.float32)  7.37 us
    ppermute x3, starting transfers between devices, ring_gather(): ahead = lax.ppermute(ahead, 'dp', fwd)  6.48 us
    ppermute x3, starting transfers between devices, merge_stats(): lax.ppermute(stats, 'dp', [(i, i ^ bit * k) for i in range(size)])  3.55 us
    ppermute x3, waiting for transfers between devices, merge_stats(): lax.ppermute(stats, 'dp', [(i, i ^ bit * k) for i in range(size)])  2.93 us
    ppermute x1, waiting for transfers between devices, ring_gather(): front = lax.ppermute(ahead[:count // 2], 'dp', fwd)  2.85 us
    ppermute x1, starting transfers between devices, merge_stats(): lax.ppermute(stats, 'dp', [(i, i ^ bit) for i in range(size)])  2.66 us
  transfers between devices with their start and end apart: 16, of which 13 were waited for; matrix products, arithmetic and copies ran while one was open for 9% of the time, Pallas kernels for 0%

profile of v8, /device:TPU:0, one launch (start us, length us, event | category | flops | bytes accessed | tf_op | source)
XLA Modules:
  0.0 69.0 jit_solution(15524693810114519206)
XLA Ops:
  0.6 3.1 %collective-permute-start = (bf16[32,4096]{1,0:T(8,128)(2,1)}, bf16[32,4096]{1,0:T(8,128)(2,1)S(1)}, u32[]{:S(2)}, u32[]{:S(2)}) collective-permute-start(bf16[32,4096]{1,0:T(8,128)(2,1)} %param.11), channel_id=1, source_target_pairs={{0,8},{8,16},{16,24},{24,28},{28,20},{20,12},{12,4},{4,0},{1,9},{9... | collective-permute-start | bytes 786440 | tf_op jit(solution)/shard_map/ppermute | solution.py:45
  3.8 1.0 %bitcast_dynamic-update-slice_fusion.6 = bf16[8,32,4096]{2,1,0:T(8,128)(2,1)S(1)} fusion(bf16[32,4096]{1,0:T(8,128)(2,1)} %param.11), kind=kLoop, calls=%fused_computation.16 | loop fusion | bytes 524288
  4.8 1.3 %fusion.8 = s32[]{:T(128)} fusion(s32[8]{0:T(128)} %constant.162.clone, s32[]{:T(128)S(6)} %axis_index.15), kind=kLoop, calls=%fused_computation.55 | loop fusion | flops 23 | bytes 40 | tf_op jit(solution)/shard_map/reduce_sum | solution.py:52
  7.0 2.0 %fusion.7 = (s32[]{:T(128)}, s32[8]{0:T(128)S(1)}, s32[]{:T(128)}, s32[8]{0:T(128)S(1)}) fusion(s32[]{:T(128)S(6)} %select_n.110, s32[8]{0:T(128)S(1)} %select_reduce_fusion.3, s32[8]{0:T(128)} %param.13, s32[8]{0:T(128)} %constant.203, s32[]{:T(128)} %fusion.8), kind=kLoop, calls=%fused_computation.54 | loop fusion | flops 142 | bytes 176 | tf_op jit(solution)/shard_map/reduce_sum | solution.py:145
  10.2 1.8 %collective-permute-start.1 = (bf16[32,4096]{1,0:T(8,128)(2,1)S(1)}, bf16[32,4096]{1,0:T(8,128)(2,1)S(1)}, u32[]{:S(2)}, u32[]{:S(2)}) collective-permute-start(bf16[32,4096]{1,0:T(8,128)(2,1)S(1)} %collective-permute-done), channel_id=1, source_target_pairs={{0,8},{8,16},{16,24},{24,28},{28,20},{20,12},{12,4},{4,0},{1,9},{9... | collective-permute-start | bytes 786440 | tf_op jit(solution)/shard_map/ppermute | solution.py:45
  12.2 5.4 %collective-permute-done.1 = bf16[32,4096]{1,0:T(8,128)(2,1)S(1)} collective-permute-done((bf16[32,4096]{1,0:T(8,128)(2,1)S(1)}, bf16[32,4096]{1,0:T(8,128)(2,1)S(1)}, u32[]{:S(2)}, u32[]{:S(2)}) %collective-permute-start.1) | collective-permute-done | bytes 262176 | tf_op jit(solution)/shard_map/ppermute | solution.py:45
  17.7 1.5 %collective-permute-start.2 = (bf16[32,4096]{1,0:T(8,128)(2,1)S(1)}, bf16[32,4096]{1,0:T(8,128)(2,1)S(1)}, u32[]{:S(2)}, u32[]{:S(2)}) collective-permute-start(bf16[32,4096]{1,0:T(8,128)(2,1)S(1)} %collective-permute-done.1), channel_id=1, source_target_pairs={{0,8},{8,16},{16,24},{24,28},{28,20},{20,12},{12,4},{4,0},{1,9},{9... | collective-permute-start | bytes 786440 | tf_op jit(solution)/shard_map/ppermute | solution.py:45
  19.7 4.6 %collective-permute-done.2 = bf16[32,4096]{1,0:T(8,128)(2,1)S(1)} collective-permute-done((bf16[32,4096]{1,0:T(8,128)(2,1)S(1)}, bf16[32,4096]{1,0:T(8,128)(2,1)S(1)}, u32[]{:S(2)}, u32[]{:S(2)}) %collective-permute-start.2) | collective-permute-done | bytes 262176 | tf_op jit(solution)/shard_map/ppermute | solution.py:45
  24.3 1.7 %collective-permute-start.3 = (bf16[16,4096]{1,0:T(8,128)(2,1)S(1)}, bf16[16,4096]{1,0:T(8,128)(2,1)S(1)}, u32[]{:S(2)}, u32[]{:S(2)}) collective-permute-start(bf16[16,4096]{1,0:T(8,128)(2,1)S(1)} %slice.80), channel_id=1, source_target_pairs={{0,8},{8,16},{16,24},{24,28},{28,20},{20,12},{12,4},{4,0},{1,9},{9... | collective-permute-start | bytes 393224 | tf_op jit(solution)/shard_map/ppermute | solution.py:41
  26.4 2.9 %collective-permute-done.3 = bf16[16,4096]{1,0:T(8,128)(2,1)S(1)} collective-permute-done((bf16[16,4096]{1,0:T(8,128)(2,1)S(1)}, bf16[16,4096]{1,0:T(8,128)(2,1)S(1)}, u32[]{:S(2)}, u32[]{:S(2)}) %collective-permute-start.3) | collective-permute-done | bytes 131104 | tf_op jit(solution)/shard_map/ppermute | solution.py:41
  29.3 1.7 %collective-permute-done.7 = bf16[16,4096]{1,0:T(8,128)(2,1)S(1)} collective-permute-done((bf16[16,4096]{1,0:T(8,128)(2,1)S(1)}, bf16[16,4096]{1,0:T(8,128)(2,1)S(1)}, u32[]{:S(2)}, u32[]{:S(2)}) %collective-permute-start.7) | collective-permute-done | bytes 131104 | tf_op jit(solution)/shard_map/ppermute | solution.py:42
  31.7 7.4 %fusion.30 = f32[160,2048]{1,0:T(8,128)S(1)} fusion(bf16[160,4096]{1,0:T(8,128)(2,1)S(1)} %convolution_convert_fusion, bf16[4096,2048]{1,0:T(8,128)(2,1)} %param.12), kind=kOutput, calls=%fused_computation.99 | convolution fusion | flops 2684354560 | bytes 19398656 | tf_op jit(solution)/shard_map/dot_general | solution.py:129
  40.2 1.1 %collective-permute-done.8 = f32[80,2048]{1,0:T(8,128)S(1)} collective-permute-done((f32[80,2048]{1,0:T(8,128)S(1)}, f32[80,2048]{1,0:T(8,128)S(1)}, u32[]{:S(2)}, u32[]{:S(2)}) %collective-permute-start.8) | collective-permute-done | bytes 655392 | tf_op jit(solution)/shard_map/ppermute | solution.py:72
  41.4 1.6 %collective-permute-start.9 = (f32[40,2048]{1,0:T(8,128)S(1)}, f32[40,2048]{1,0:T(8,128)S(1)}, u32[]{:S(2)}, u32[]{:S(2)}) collective-permute-start(f32[40,2048]{1,0:T(8,128)S(1)} %select_bitcast_fusion.1), channel_id=1, source_target_pairs={{0,2},{1,3},{2,0},{3,1},{4,6},{5,7},{6,4},{7,5},{8,10},{9,11},{10,... | collective-permute-start | bytes 983048 | tf_op jit(solution)/shard_map/ppermute | solution.py:72
  43.1 8.2 %collective-permute-done.9 = f32[40,2048]{1,0:T(8,128)S(1)} collective-permute-done((f32[40,2048]{1,0:T(8,128)S(1)}, f32[40,2048]{1,0:T(8,128)S(1)}, u32[]{:S(2)}, u32[]{:S(2)}) %collective-permute-start.9) | collective-permute-done | bytes 327712 | tf_op jit(solution)/shard_map/ppermute | solution.py:72
  52.1 1.6 %collective-permute-start.11 = (f32[3,40]{1,0:T(4,128)S(1)}, f32[3,40]{1,0:T(4,128)S(1)}, u32[]{:S(2)}, u32[]{:S(2)}) collective-permute-start(f32[3,40]{1,0:T(4,128)S(1)} %pad_maximum_fusion), channel_id=1, source_target_pairs={{0,8},{4,12},{8,0},{12,4},{16,24},{20,28},{24,16},{28,20},{1,9},{5... | collective-permute-start | bytes 1448 | tf_op jit(solution)/shard_map/ppermute | solution.py:89
  53.7 1.5 %collective-permute-start.12 = (f32[3,40]{1,0:T(4,128)S(1)}, f32[3,40]{1,0:T(4,128)S(1)}, u32[]{:S(2)}, u32[]{:S(2)}) collective-permute-start(f32[3,40]{1,0:T(4,128)S(1)} %pad_maximum_fusion), channel_id=1, source_target_pairs={{0,12},{4,8},{8,4},{12,0},{16,28},{20,24},{24,20},{28,16},{1,13},{... | collective-permute-start | bytes 1448 | tf_op jit(solution)/shard_map/ppermute | solution.py:89
  55.7 2.5 %collective-permute-done.12 = f32[3,40]{1,0:T(4,128)S(1)} collective-permute-done((f32[3,40]{1,0:T(4,128)S(1)}, f32[3,40]{1,0:T(4,128)S(1)}, u32[]{:S(2)}, u32[]{:S(2)}) %collective-permute-start.12) | collective-permute-done | bytes 512 | tf_op jit(solution)/shard_map/ppermute | solution.py:89
  58.2 2.7 %collective-permute-start.13 = (f32[3,40]{1,0:T(4,128)S(1)}, f32[3,40]{1,0:T(4,128)S(1)}, u32[]{:S(2)}, u32[]{:S(2)}) collective-permute-start(f32[3,40]{1,0:T(4,128)S(1)} %pad_maximum_fusion.1), channel_id=1, source_target_pairs={{0,16},{4,20},{8,24},{12,28},{16,0},{20,4},{24,8},{28,12},{1,17},{... | collective-permute-start | bytes 1448 | tf_op jit(solution)/shard_map/ppermute | solution.py:93
  60.8 1.9 %collective-permute-done.13 = f32[3,40]{1,0:T(4,128)S(1)} collective-permute-done((f32[3,40]{1,0:T(4,128)S(1)}, f32[3,40]{1,0:T(4,128)S(1)}, u32[]{:S(2)}, u32[]{:S(2)}) %collective-permute-start.13) | collective-permute-done | bytes 512 | tf_op jit(solution)/shard_map/ppermute | solution.py:93
  62.9 1.2 %collective-permute-done.14 = f32[160]{0:T(256)S(1)} collective-permute-done((f32[160]{0:T(256)S(1)}, f32[160]{0:T(256)S(1)}, u32[]{:S(2)}, u32[]{:S(2)}) %collective-permute-start.14) | collective-permute-done | bytes 672 | tf_op jit(solution)/shard_map/ppermute | solution.py:105
  64.2 1.5 %collective-permute-start.15 = (f32[160]{0:T(256)S(1)}, f32[160]{0:T(256)S(1)}, u32[]{:S(2)}, u32[]{:S(2)}) collective-permute-start(f32[160]{0:T(256)S(1)} %add_dynamic-update-slice_fusion), channel_id=1, source_target_pairs={{0,2},{1,3},{2,0},{3,1},{4,6},{5,7},{6,4},{7,5},{8,10},{9,11},{10,... | collective-permute-start | bytes 1928 | tf_op jit(solution)/shard_map/ppermute | solution.py:105
  66.3 1.4 %collective-permute-done.15 = f32[160]{0:T(256)S(1)} collective-permute-done((f32[160]{0:T(256)S(1)}, f32[160]{0:T(256)S(1)}, u32[]{:S(2)}, u32[]{:S(2)}) %collective-permute-start.15) | collective-permute-done | bytes 672 | tf_op jit(solution)/shard_map/ppermute | solution.py:105
  67.8 1.3 %compare_select_fusion.4 = (f32[32]{0:T(128)}, f32[32]{0:T(128)}) fusion(f32[32]{0:T(128)S(1)} %copy-done.1, s32[]{:T(128)} %get-tuple-element.41, s32[]{:T(128)S(6)} %select_n.109, s32[]{:T(128)S(6)} %min.18, f32[160]{0:T(256)S(1)} %add.184), kind=kLoop, calls=%fused_computation.42 | loop fusion | flops 288 | bytes 1036 | tf_op jit(solution)/shard_map/jit(_where)/select_n | solution.py:157
  (50 shorter events, 6.6 us)
Async XLA Ops:
  0.6 38.7 %copy-start = (s32[256]{0:T(256)S(1)}, s32[256]{0:T(256)}, u32[]{:S(2)}) copy-start(s32[256]{0:T(256)} %param.14) | copy-start | bytes 3076
  0.6 9.5 %collective-permute-start = (bf16[32,4096]{1,0:T(8,128)(2,1)}, bf16[32,4096]{1,0:T(8,128)(2,1)S(1)}, u32[]{:S(2)}, u32[]{:S(2)}) collective-permute-start(bf16[32,4096]{1,0:T(8,128)(2,1)} %param.11), channel_id=1, source_target_pairs={{0,8},{8,16},{16,24},{24,28},{28,20},{20,12},{12,4},{4,0},{1,9},{9... | collective-permute-start | bytes 786440 | tf_op jit(solution)/shard_map/ppermute | solution.py:45
  3.7 8.3 %collective-permute-start.4 = (bf16[32,4096]{1,0:T(8,128)(2,1)}, bf16[32,4096]{1,0:T(8,128)(2,1)S(1)}, u32[]{:S(2)}, u32[]{:S(2)}) collective-permute-start(bf16[32,4096]{1,0:T(8,128)(2,1)} %param.11), channel_id=1, source_target_pairs={{8,0},{16,8},{24,16},{28,24},{20,28},{12,20},{4,12},{0,4},{9,1},{1... | collective-permute-start | bytes 786440 | tf_op jit(solution)/shard_map/ppermute | solution.py:48
  10.2 7.5 %collective-permute-start.1 = (bf16[32,4096]{1,0:T(8,128)(2,1)S(1)}, bf16[32,4096]{1,0:T(8,128)(2,1)S(1)}, u32[]{:S(2)}, u32[]{:S(2)}) collective-permute-start(bf16[32,4096]{1,0:T(8,128)(2,1)S(1)} %collective-permute-done), channel_id=1, source_target_pairs={{0,8},{8,16},{16,24},{24,28},{28,20},{20,12},{12,4},{4,0},{1,9},{9... | collective-permute-start | bytes 786440 | tf_op jit(solution)/shard_map/ppermute | solution.py:45
  12.0 7.2 %collective-permute-start.5 = (bf16[32,4096]{1,0:T(8,128)(2,1)S(1)}, bf16[32,4096]{1,0:T(8,128)(2,1)S(1)}, u32[]{:S(2)}, u32[]{:S(2)}) collective-permute-start(bf16[32,4096]{1,0:T(8,128)(2,1)S(1)} %collective-permute-done.4), channel_id=1, source_target_pairs={{8,0},{16,8},{24,16},{28,24},{20,28},{12,20},{4,12},{0,4},{9,1},{1... | collective-permute-start | bytes 786440 | tf_op jit(solution)/shard_map/ppermute | solution.py:48
  17.7 6.6 %collective-permute-start.2 = (bf16[32,4096]{1,0:T(8,128)(2,1)S(1)}, bf16[32,4096]{1,0:T(8,128)(2,1)S(1)}, u32[]{:S(2)}, u32[]{:S(2)}) collective-permute-start(bf16[32,4096]{1,0:T(8,128)(2,1)S(1)} %collective-permute-done.1), channel_id=1, source_target_pairs={{0,8},{8,16},{16,24},{24,28},{28,20},{20,12},{12,4},{4,0},{1,9},{9... | collective-permute-start | bytes 786440 | tf_op jit(solution)/shard_map/ppermute | solution.py:45
  19.2 6.8 %collective-permute-start.6 = (bf16[32,4096]{1,0:T(8,128)(2,1)S(1)}, bf16[32,4096]{1,0:T(8,128)(2,1)S(1)}, u32[]{:S(2)}, u32[]{:S(2)}) collective-permute-start(bf16[32,4096]{1,0:T(8,128)(2,1)S(1)} %collective-permute-done.5), channel_id=1, source_target_pairs={{8,0},{16,8},{24,16},{28,24},{20,28},{12,20},{4,12},{0,4},{9,1},{1... | collective-permute-start | bytes 786440 | tf_op jit(solution)/shard_map/ppermute | solution.py:48
  24.3 5.0 %collective-permute-start.3 = (bf16[16,4096]{1,0:T(8,128)(2,1)S(1)}, bf16[16,4096]{1,0:T(8,128)(2,1)S(1)}, u32[]{:S(2)}, u32[]{:S(2)}) collective-permute-start(bf16[16,4096]{1,0:T(8,128)(2,1)S(1)} %slice.80), channel_id=1, source_target_pairs={{0,8},{8,16},{16,24},{24,28},{28,20},{20,12},{12,4},{4,0},{1,9},{9... | collective-permute-start | bytes 393224 | tf_op jit(solution)/shard_map/ppermute | solution.py:41
  26.0 5.0 %collective-permute-start.7 = (bf16[16,4096]{1,0:T(8,128)(2,1)S(1)}, bf16[16,4096]{1,0:T(8,128)(2,1)S(1)}, u32[]{:S(2)}, u32[]{:S(2)}) collective-permute-start(bf16[16,4096]{1,0:T(8,128)(2,1)S(1)} %slice.81), channel_id=1, source_target_pairs={{8,0},{16,8},{24,16},{28,24},{20,28},{12,20},{4,12},{0,4},{9,1},{1... | collective-permute-start | bytes 393224 | tf_op jit(solution)/shard_map/ppermute | solution.py:42
  39.1 2.2 %collective-permute-start.8 = (f32[80,2048]{1,0:T(8,128)S(1)}, f32[80,2048]{1,0:T(8,128)S(1)}, u32[]{:S(2)}, u32[]{:S(2)}) collective-permute-start(f32[80,2048]{1,0:T(8,128)S(1)} %select_bitcast_fusion), channel_id=1, source_target_pairs={{0,1},{1,0},{2,3},{3,2},{4,5},{5,4},{6,7},{7,6},{8,9},{9,8},{10,11... | collective-permute-start | bytes 1966088 | tf_op jit(solution)/shard_map/ppermute | solution.py:72
  40.2 27.6 %copy-start.1 = (f32[32]{0:T(128)S(1)}, f32[32]{0:T(128)}, u32[]{:S(2)}) copy-start(f32[32]{0:T(128)} %param.15) | copy-start | bytes 388
  41.4 9.8 %collective-permute-start.9 = (f32[40,2048]{1,0:T(8,128)S(1)}, f32[40,2048]{1,0:T(8,128)S(1)}, u32[]{:S(2)}, u32[]{:S(2)}) collective-permute-start(f32[40,2048]{1,0:T(8,128)S(1)} %select_bitcast_fusion.1), channel_id=1, source_target_pairs={{0,2},{1,3},{2,0},{3,1},{4,6},{5,7},{6,4},{7,5},{8,10},{9,11},{10,... | collective-permute-start | bytes 983048 | tf_op jit(solution)/shard_map/ppermute | solution.py:72
  51.7 3.7 %collective-permute-start.10 = (f32[3,40]{1,0:T(4,128)S(1)}, f32[3,40]{1,0:T(4,128)S(1)}, u32[]{:S(2)}, u32[]{:S(2)}) collective-permute-start(f32[3,40]{1,0:T(4,128)S(1)} %pad_maximum_fusion), channel_id=1, source_target_pairs={{0,4},{4,0},{8,12},{12,8},{16,20},{20,16},{24,28},{28,24},{1,5},{5... | collective-permute-start | bytes 1448 | tf_op jit(solution)/shard_map/ppermute | solution.py:89
  52.1 3.6 %collective-permute-start.11 = (f32[3,40]{1,0:T(4,128)S(1)}, f32[3,40]{1,0:T(4,128)S(1)}, u32[]{:S(2)}, u32[]{:S(2)}) collective-permute-start(f32[3,40]{1,0:T(4,128)S(1)} %pad_maximum_fusion), channel_id=1, source_target_pairs={{0,8},{4,12},{8,0},{12,4},{16,24},{20,28},{24,16},{28,20},{1,9},{5... | collective-permute-start | bytes 1448 | tf_op jit(solution)/shard_map/ppermute | solution.py:89
  53.7 4.5 %collective-permute-start.12 = (f32[3,40]{1,0:T(4,128)S(1)}, f32[3,40]{1,0:T(4,128)S(1)}, u32[]{:S(2)}, u32[]{:S(2)}) collective-permute-start(f32[3,40]{1,0:T(4,128)S(1)} %pad_maximum_fusion), channel_id=1, source_target_pairs={{0,12},{4,8},{8,4},{12,0},{16,28},{20,24},{24,20},{28,16},{1,13},{... | collective-permute-start | bytes 1448 | tf_op jit(solution)/shard_map/ppermute | solution.py:89
  58.2 4.5 %collective-permute-start.13 = (f32[3,40]{1,0:T(4,128)S(1)}, f32[3,40]{1,0:T(4,128)S(1)}, u32[]{:S(2)}, u32[]{:S(2)}) collective-permute-start(f32[3,40]{1,0:T(4,128)S(1)} %pad_maximum_fusion.1), channel_id=1, source_target_pairs={{0,16},{4,20},{8,24},{12,28},{16,0},{20,4},{24,8},{28,12},{1,17},{... | collective-permute-start | bytes 1448 | tf_op jit(solution)/shard_map/ppermute | solution.py:93
  62.9 1.2 %collective-permute-start.14 = (f32[160]{0:T(256)S(1)}, f32[160]{0:T(256)S(1)}, u32[]{:S(2)}, u32[]{:S(2)}) collective-permute-start(f32[160]{0:T(256)S(1)} %get-tuple-element.30), channel_id=1, source_target_pairs={{0,1},{1,0},{2,3},{3,2},{4,5},{5,4},{6,7},{7,6},{8,9},{9,8},{10,11... | collective-permute-start | bytes 1928 | tf_op jit(solution)/shard_map/ppermute | solution.py:105
  64.2 3.6 %collective-permute-start.15 = (f32[160]{0:T(256)S(1)}, f32[160]{0:T(256)S(1)}, u32[]{:S(2)}, u32[]{:S(2)}) collective-permute-start(f32[160]{0:T(256)S(1)} %add_dynamic-update-slice_fusion), channel_id=1, source_target_pairs={{0,2},{1,3},{2,0},{3,1},{4,6},{5,7},{6,4},{7,5},{8,10},{9,11},{10,... | collective-permute-start | bytes 1928 | tf_op jit(solution)/shard_map/ppermute | solution.py:105

commit v9 on v8

--- a/solution.py
+++ b/solution.py
@@ -27,7 +27,7 @@
         return list(range(size))
 
 
-def ring_gather(block, ring, rows):
+def ring_gather(block, ring, rows, weight):
     size = len(ring)
     pos_of = np.argsort(np.asarray(ring))
     fwd = [(ring[i], ring[(i + 1) % size]) for i in range(size)]
@@ -48,15 +48,13 @@
             behind = lax.ppermute(behind, "dp", bwd)
             slots[size - step] = behind
     count = block.shape[0]
-    stacked = jnp.stack(slots).reshape(-1, block.shape[1])
     me = jnp.sum(jnp.where(jnp.arange(size) == lax.axis_index("dp"), jnp.asarray(pos_of, jnp.int32), 0))
     slot_of = (me - jnp.asarray(pos_of, jnp.int32)) % size
     owner = rows // count
     hit = owner[None, :] == jnp.arange(size, dtype=jnp.int32)[:, None]
     where = jnp.sum(jnp.where(hit, slot_of[:, None], 0), axis=0) * count + rows % count
-    choose = lax.broadcasted_iota(jnp.int32, (stacked.shape[0], where.shape[0]), 0) == where[None, :]
-    picked = lax.dot_general(choose.astype(stacked.dtype), stacked, (((0,), (0,)), ((), ())), preferred_element_type=jnp.float32)
-    return lax.optimization_barrier(picked.astype(stacked.dtype))
+    products = [jnp.dot(part, weight, preferred_element_type=jnp.float32) for part in slots]
+    return jnp.take(jnp.concatenate(products), where, axis=0)
 
 
 def halving_scatter(partial, size):
@@ -125,8 +123,7 @@
         batch_of = jnp.sum(batch_hit.astype(jnp.int32), axis=0)
         in_batch = packed - jnp.sum(jnp.where(batch_of[None, :] == jnp.arange(MB, dtype=jnp.int32)[:, None], starts[:, None], 0), axis=0)
         live_rows = batch_of * slot_count + in_batch
-        full_rows = ring_gather(hidden, ring, live_rows)
-        partial = jnp.dot(full_rows, head_weight, preferred_element_type=jnp.float32)
+        partial = ring_gather(hidden, ring, live_rows, head_weight)
         logits, first = halving_scatter(partial, vocab_size)
         share = logits.shape[0]
         row_targets = jnp.take(targets, lax.dynamic_slice_in_dim(live_rows, first, share))

time: 69.3 us -> 86.2 us (1.24)
  matrix products: 7.93 us -> 36.3 us
  waiting for transfers between devices: 32.2 us -> 20.6 us
    dot_general x2 -> x8, matrix products: 7.93 us -> 36.3 us  [ring_gather(): jnp.dot(part, weight, preferred_element_type=jnp.float32)]
    ppermute x3, waiting for transfers between devices: 10.9 us -> 0.01 us  [ring_gather(): ahead = lax.ppermute(ahead, 'dp', fwd)]
    ppermute x3, waiting for transfers between devices: 0.01 us -> 3.54 us  [ring_gather(): behind = lax.ppermute(behind, 'dp', bwd)]
    ppermute x1, waiting for transfers between devices: 2.85 us -> 0.24 us  [ring_gather(): front = lax.ppermute(ahead[:count // 2], 'dp', fwd)]
    ppermute x1, waiting for transfers between devices: 1.73 us -> 0.01 us  [ring_gather(): back = lax.ppermute(behind[count // 2:], 'dp', bwd)]
    unnamed x10, local copies, waits for them, and re-layouts: 1.14 us -> 0.02 us
    gather x0 -> x1, local copies, waits for them, and re-layouts: none -> 1.11 us  [ring_gather(): return jnp.take(jnp.concatenate(products), where, axis=0)]
  transfers between devices with their start and end apart: 16 -> 16, of which waited for: 13 -> 10; matrix products, arithmetic and copies ran while one was open for 9% -> 34% of each run, Pallas kernels for 0% -> 0%
where the time goes in v9:
time: 86.2 us; the launch traced here: 86 us
  matrix products  36.3 us (42%)
  waiting for transfers between devices  20.6 us (24%)
  starting transfers between devices  19.1 us (22%)
  other arithmetic  6.23 us (7%)
  local copies, waits for them, and re-layouts  2.19 us (3%)
  between operations  1.56 us (2%)
    dot_general x8, matrix products, ring_gather(): jnp.dot(part, weight, preferred_element_type=jnp.float32)  36.3 us
    ppermute x2, waiting for transfers between devices, halving_scatter(): got = lax.ppermute(send, 'vocab', [(i, i ^ bit) for i in range(size)])  9.12 us
    ppermute x3, starting transfers between devices, ring_gather(): ahead = lax.ppermute(ahead, 'dp', fwd)  7.26 us
    ppermute x3, starting transfers between devices, merge_stats(): lax.ppermute(stats, 'dp', [(i, i ^ bit * k) for i in range(size)])  3.55 us
    ppermute x3, waiting for transfers between devices, ring_gather(): behind = lax.ppermute(behind, 'dp', bwd)  3.54 us
    ppermute x3, waiting for transfers between devices, merge_stats(): lax.ppermute(stats, 'dp', [(i, i ^ bit * k) for i in range(size)])  3.21 us
    ppermute x1, starting transfers between devices, merge_stats(): lax.ppermute(stats, 'dp', [(i, i ^ bit) for i in range(size)])  2.65 us
    ppermute x2, waiting for transfers between devices, doubling_gather(): other = lax.ppermute(out, 'vocab', [(i, i ^ bit) for i in range(size)])  2.55 us
  transfers between devices with their start and end apart: 16, of which 10 were waited for; matrix products, arithmetic and copies ran while one was open for 34% of the time, Pallas kernels for 0%

profile of v9, /device:TPU:0, one launch (start us, length us, event | category | flops | bytes accessed | tf_op | source)
XLA Modules:
  0.0 86.0 jit_solution(3169591649500062148)
XLA Ops:
  0.6 3.1 %collective-permute-start = (bf16[32,4096]{1,0:T(8,128)(2,1)}, bf16[32,4096]{1,0:T(8,128)(2,1)S(1)}, u32[]{:S(2)}, u32[]{:S(2)}) collective-permute-start(bf16[32,4096]{1,0:T(8,128)(2,1)} %param.11), channel_id=1, source_target_pairs={{0,8},{8,16},{16,24},{24,28},{28,20},{20,12},{12,4},{4,0},{1,9},{9... | collective-permute-start | bytes 786440 | tf_op jit(solution)/shard_map/ppermute | solution.py:45
  4.5 1.3 %fusion.12 = s32[]{:T(128)} fusion(s32[8]{0:T(128)} %constant.178.clone, s32[]{:T(128)S(6)} %axis_index.15), kind=kLoop, calls=%fused_computation.68 | loop fusion | flops 23 | bytes 40 | tf_op jit(solution)/shard_map/reduce_sum | solution.py:51
  5.8 8.9 %convolution_dynamic-update-slice_fusion.7 = f32[256,2048]{1,0:T(8,128)S(1)} fusion(bf16[32,4096]{1,0:T(8,128)(2,1)} %param.11, bf16[4096,2048]{1,0:T(8,128)(2,1)} %param.12), kind=kOutput, calls=%fused_computation.9 | convolution fusion | flops 536870912 | bytes 17301504 | tf_op jit(solution)/shard_map/dot_general | solution.py:56
  14.8 1.4 %fusion.11 = (s32[]{:T(128)}, s32[8]{0:T(128)S(1)}, s32[]{:T(128)}, s32[8]{0:T(128)S(1)}) fusion(s32[]{:T(128)S(6)} %select_n.139, s32[8]{0:T(128)S(1)} %select_reduce_fusion.3, s32[8]{0:T(128)S(1)} %copy-done.2, s32[8]{0:T(128)S(1)} %copy-done.3, s32[]{:T(128)} %fusion.12), kind=kLoop, calls=%fused_computation.67 | loop fusion | flops 142 | bytes 176 | tf_op jit(solution)/shard_map/reduce_sum | solution.py:142
  16.7 2.1 %collective-permute-start.1 = (bf16[32,4096]{1,0:T(8,128)(2,1)S(1)}, bf16[32,4096]{1,0:T(8,128)(2,1)S(1)}, u32[]{:S(2)}, u32[]{:S(2)}) collective-permute-start(bf16[32,4096]{1,0:T(8,128)(2,1)S(1)} %collective-permute-done), channel_id=1, source_target_pairs={{0,8},{8,16},{16,24},{24,28},{28,20},{20,12},{12,4},{4,0},{1,9},{9... | collective-permute-start | bytes 786440 | tf_op jit(solution)/shard_map/ppermute | solution.py:45
  18.8 9.5 %convolution_dynamic-update-slice_fusion.6 = f32[256,2048]{1,0:T(8,128)S(1)} fusion(f32[256,2048]{1,0:T(8,128)S(1)} %convolution_dynamic-update-slice_fusion.7, bf16[32,4096]{1,0:T(8,128)(2,1)S(1)} %collective-permute-done, bf16[4096,2048]{1,0:T(8,128)(2,1)} %param.12), kind=kOutput, calls=%fused_computation.8 | convolution fusion | flops 536870912 | bytes 17301504 | tf_op jit(solution)/shard_map/dot_general | solution.py:56
  28.3 2.1 %collective-permute-start.2 = (bf16[32,4096]{1,0:T(8,128)(2,1)S(1)}, bf16[32,4096]{1,0:T(8,128)(2,1)S(1)}, u32[]{:S(2)}, u32[]{:S(2)}) collective-permute-start(bf16[32,4096]{1,0:T(8,128)(2,1)S(1)} %collective-permute-done.1), channel_id=1, source_target_pairs={{0,8},{8,16},{16,24},{24,28},{28,20},{20,12},{12,4},{4,0},{1,9},{9... | collective-permute-start | bytes 786440 | tf_op jit(solution)/shard_map/ppermute | solution.py:45
  30.4 3.0 %convolution_dynamic-update-slice_fusion.5 = f32[256,2048]{1,0:T(8,128)S(1)} fusion(f32[256,2048]{1,0:T(8,128)S(1)} %convolution_dynamic-update-slice_fusion.6, bf16[32,4096]{1,0:T(8,128)(2,1)S(1)} %collective-permute-done.1, bf16[4096,2048]{1,0:T(8,128)(2,1)S(1)} %copy-done.1), kind=kOutput, calls=%fused_computation.7 | convolution fusion | flops 536870912 | bytes 17301504 | tf_op jit(solution)/shard_map/dot_general | solution.py:56
  33.4 3.5 %collective-permute-done.6 = bf16[32,4096]{1,0:T(8,128)(2,1)S(1)} collective-permute-done((bf16[32,4096]{1,0:T(8,128)(2,1)S(1)}, bf16[32,4096]{1,0:T(8,128)(2,1)S(1)}, u32[]{:S(2)}, u32[]{:S(2)}) %collective-permute-start.6) | collective-permute-done | bytes 262176 | tf_op jit(solution)/shard_map/ppermute | solution.py:48
  37.3 2.0 %collective-permute-start.3 = (bf16[16,4096]{1,0:T(8,128)(2,1)S(1)}, bf16[16,4096]{1,0:T(8,128)(2,1)S(1)}, u32[]{:S(2)}, u32[]{:S(2)}) collective-permute-start(bf16[16,4096]{1,0:T(8,128)(2,1)S(1)} %slice.82), channel_id=1, source_target_pairs={{0,8},{8,16},{16,24},{24,28},{28,20},{20,12},{12,4},{4,0},{1,9},{9... | collective-permute-start | bytes 393224 | tf_op jit(solution)/shard_map/ppermute | solution.py:41
  39.3 3.0 %convolution_dynamic-update-slice_fusion.4 = f32[256,2048]{1,0:T(8,128)S(1)} fusion(f32[256,2048]{1,0:T(8,128)S(1)} %convolution_dynamic-update-slice_fusion.5, bf16[32,4096]{1,0:T(8,128)(2,1)S(1)} %collective-permute-done.2, bf16[4096,2048]{1,0:T(8,128)(2,1)S(1)} %copy-done.1), kind=kOutput, calls=%fused_computation.6 | convolution fusion | flops 536870912 | bytes 17301504 | tf_op jit(solution)/shard_map/dot_general | solution.py:56
  42.5 3.0 %convolution_dynamic-update-slice_fusion.3 = f32[256,2048]{1,0:T(8,128)S(1)} fusion(f32[256,2048]{1,0:T(8,128)S(1)} %convolution_dynamic-update-slice_fusion.4, bf16[4096,2048]{1,0:T(8,128)(2,1)S(1)} %copy-done.1, bf16[16,4096]{1,0:T(8,128)(2,1)S(1)} %collective-permute-done.7, bf16[16,4096]{1,0:T(8,128)(2,1)S(1)} %collective-permute-done.3), kind=kOutput, calls=%fused_computation.5 | convolution fusion | flops 537395200 | bytes 17301504 | tf_op jit(solution)/shard_map/dot_general | solution.py:56
  45.5 3.0 %convolution_dynamic-update-slice_fusion.2 = f32[256,2048]{1,0:T(8,128)S(1)} fusion(f32[256,2048]{1,0:T(8,128)S(1)} %convolution_dynamic-update-slice_fusion.3, bf16[32,4096]{1,0:T(8,128)(2,1)S(1)} %collective-permute-done.6, bf16[4096,2048]{1,0:T(8,128)(2,1)S(1)} %copy-done.1), kind=kOutput, calls=%fused_computation.4 | convolution fusion | flops 536870912 | bytes 17301504 | tf_op jit(solution)/shard_map/dot_general | solution.py:56
  48.5 3.0 %convolution_dynamic-update-slice_fusion.1 = f32[256,2048]{1,0:T(8,128)S(1)} fusion(f32[256,2048]{1,0:T(8,128)S(1)} %convolution_dynamic-update-slice_fusion.2, bf16[32,4096]{1,0:T(8,128)(2,1)S(1)} %collective-permute-done.5, bf16[4096,2048]{1,0:T(8,128)(2,1)S(1)} %copy-done.1), kind=kOutput, calls=%fused_computation.3 | convolution fusion | flops 536870912 | bytes 17301504 | tf_op jit(solution)/shard_map/dot_general | solution.py:56
  51.4 3.0 %convolution_dynamic-update-slice_fusion = f32[256,2048]{1,0:T(8,128)S(1)} fusion(f32[256,2048]{1,0:T(8,128)S(1)} %convolution_dynamic-update-slice_fusion.1, bf16[32,4096]{1,0:T(8,128)(2,1)S(1)} %collective-permute-done.4, bf16[4096,2048]{1,0:T(8,128)(2,1)S(1)} %copy-done.1), kind=kOutput, calls=%fused_computation.2 | convolution fusion | flops 536870912 | bytes 17301504 | tf_op jit(solution)/shard_map/dot_general | solution.py:56
  58.1 1.7 %collective-permute-start.9 = (f32[40,2048]{1,0:T(8,128)S(1)}, f32[40,2048]{1,0:T(8,128)S(1)}, u32[]{:S(2)}, u32[]{:S(2)}) collective-permute-start(f32[40,2048]{1,0:T(8,128)S(1)} %select_bitcast_fusion.1), channel_id=1, source_target_pairs={{0,2},{1,3},{2,0},{3,1},{4,6},{5,7},{6,4},{7,5},{8,10},{9,11},{10,... | collective-permute-start | bytes 983048 | tf_op jit(solution)/shard_map/ppermute | solution.py:70
  59.9 8.0 %collective-permute-done.9 = f32[40,2048]{1,0:T(8,128)S(1)} collective-permute-done((f32[40,2048]{1,0:T(8,128)S(1)}, f32[40,2048]{1,0:T(8,128)S(1)}, u32[]{:S(2)}, u32[]{:S(2)}) %collective-permute-start.9) | collective-permute-done | bytes 327712 | tf_op jit(solution)/shard_map/ppermute | solution.py:70
  68.3 2.7 %collective-permute-start.12 = (f32[3,40]{1,0:T(4,128)S(1)}, f32[3,40]{1,0:T(4,128)S(1)}, u32[]{:S(2)}, u32[]{:S(2)}) collective-permute-start(f32[3,40]{1,0:T(4,128)S(1)} %pad_maximum_fusion), channel_id=1, source_target_pairs={{0,12},{4,8},{8,4},{12,0},{16,28},{20,24},{24,20},{28,16},{1,13},{... | collective-permute-start | bytes 1448 | tf_op jit(solution)/shard_map/ppermute | solution.py:87
  72.9 1.8 %collective-permute-done.11 = f32[3,40]{1,0:T(4,128)S(1)} collective-permute-done((f32[3,40]{1,0:T(4,128)S(1)}, f32[3,40]{1,0:T(4,128)S(1)}, u32[]{:S(2)}, u32[]{:S(2)}) %collective-permute-start.11) | collective-permute-done | bytes 512 | tf_op jit(solution)/shard_map/ppermute | solution.py:87
  75.1 2.7 %collective-permute-start.13 = (f32[3,40]{1,0:T(4,128)S(1)}, f32[3,40]{1,0:T(4,128)S(1)}, u32[]{:S(2)}, u32[]{:S(2)}) collective-permute-start(f32[3,40]{1,0:T(4,128)S(1)} %pad_maximum_fusion.1), channel_id=1, source_target_pairs={{0,16},{4,20},{8,24},{12,28},{16,0},{20,4},{24,8},{28,12},{1,17},{... | collective-permute-start | bytes 1448 | tf_op jit(solution)/shard_map/ppermute | solution.py:91
  77.8 1.9 %collective-permute-done.13 = f32[3,40]{1,0:T(4,128)S(1)} collective-permute-done((f32[3,40]{1,0:T(4,128)S(1)}, f32[3,40]{1,0:T(4,128)S(1)}, u32[]{:S(2)}, u32[]{:S(2)}) %collective-permute-start.13) | collective-permute-done | bytes 512 | tf_op jit(solution)/shard_map/ppermute | solution.py:91
  81.1 1.5 %collective-permute-start.15 = (f32[160]{0:T(256)S(1)}, f32[160]{0:T(256)S(1)}, u32[]{:S(2)}, u32[]{:S(2)}) collective-permute-start(f32[160]{0:T(256)S(1)} %add_dynamic-update-slice_fusion), channel_id=1, source_target_pairs={{0,2},{1,3},{2,0},{3,1},{4,6},{5,7},{6,4},{7,5},{8,10},{9,11},{10,... | collective-permute-start | bytes 1928 | tf_op jit(solution)/shard_map/ppermute | solution.py:103
  83.3 1.4 %collective-permute-done.15 = f32[160]{0:T(256)S(1)} collective-permute-done((f32[160]{0:T(256)S(1)}, f32[160]{0:T(256)S(1)}, u32[]{:S(2)}, u32[]{:S(2)}) %collective-permute-start.15) | collective-permute-done | bytes 672 | tf_op jit(solution)/shard_map/ppermute | solution.py:103
  84.7 1.3 %compare_select_fusion.10 = (f32[32]{0:T(128)}, f32[32]{0:T(128)}) fusion(f32[32]{0:T(128)S(1)} %copy-done.4, s32[]{:T(128)} %get-tuple-element.42, s32[]{:T(128)S(6)} %select_n.138, s32[]{:T(128)S(6)} %min.18, f32[160]{0:T(256)S(1)} %add.242), kind=kLoop, calls=%fused_computation.52 | loop fusion | flops 288 | bytes 1036 | tf_op jit(solution)/shard_map/jit(_where)/select_n | solution.py:154
  (62 shorter events, 9.7 us)
Async XLA Ops:
  0.6 55.4 %copy-start = (s32[256]{0:T(256)S(1)}, s32[256]{0:T(256)}, u32[]{:S(2)}) copy-start(s32[256]{0:T(256)} %param.14) | copy-start | bytes 3076
  0.6 16.1 %collective-permute-start = (bf16[32,4096]{1,0:T(8,128)(2,1)}, bf16[32,4096]{1,0:T(8,128)(2,1)S(1)}, u32[]{:S(2)}, u32[]{:S(2)}) collective-permute-start(bf16[32,4096]{1,0:T(8,128)(2,1)} %param.11), channel_id=1, source_target_pairs={{0,8},{8,16},{16,24},{24,28},{28,20},{20,12},{12,4},{4,0},{1,9},{9... | collective-permute-start | bytes 786440 | tf_op jit(solution)/shard_map/ppermute | solution.py:45
  3.7 15.0 %collective-permute-start.4 = (bf16[32,4096]{1,0:T(8,128)(2,1)}, bf16[32,4096]{1,0:T(8,128)(2,1)S(1)}, u32[]{:S(2)}, u32[]{:S(2)}) collective-permute-start(bf16[32,4096]{1,0:T(8,128)(2,1)} %param.11), channel_id=1, source_target_pairs={{8,0},{16,8},{24,16},{28,24},{20,28},{12,20},{4,12},{0,4},{9,1},{1... | collective-permute-start | bytes 786440 | tf_op jit(solution)/shard_map/ppermute | solution.py:48
  5.8 9.0 %copy-start.2 = (s32[8]{0:T(128)S(1)}, s32[8]{0:T(128)}, u32[]{:S(2)}) copy-start(s32[8]{0:T(128)} %param.13) | copy-start | bytes 100
  5.8 9.0 %copy-start.3 = (s32[8]{0:T(128)S(1)}, s32[8]{0:T(128)}, u32[]{:S(2)}) copy-start(s32[8]{0:T(128)} %constant.219) | copy-start | bytes 100
  16.7 13.7 %copy-start.1 = (bf16[4096,2048]{1,0:T(8,128)(2,1)S(1)}, bf16[4096,2048]{1,0:T(8,128)(2,1)}, u32[]{:S(2)}) copy-start(bf16[4096,2048]{1,0:T(8,128)(2,1)} %param.12) | copy-start | bytes 50331652
  16.7 11.6 %collective-permute-start.1 = (bf16[32,4096]{1,0:T(8,128)(2,1)S(1)}, bf16[32,4096]{1,0:T(8,128)(2,1)S(1)}, u32[]{:S(2)}, u32[]{:S(2)}) collective-permute-start(bf16[32,4096]{1,0:T(8,128)(2,1)S(1)} %collective-permute-done), channel_id=1, source_target_pairs={{0,8},{8,16},{16,24},{24,28},{28,20},{20,12},{12,4},{4,0},{1,9},{9... | collective-permute-start | bytes 786440 | tf_op jit(solution)/shard_map/ppermute | solution.py:45
  18.8 11.6 %collective-permute-start.5 = (bf16[32,4096]{1,0:T(8,128)(2,1)S(1)}, bf16[32,4096]{1,0:T(8,128)(2,1)S(1)}, u32[]{:S(2)}, u32[]{:S(2)}) collective-permute-start(bf16[32,4096]{1,0:T(8,128)(2,1)S(1)} %collective-permute-done.4), channel_id=1, source_target_pairs={{8,0},{16,8},{24,16},{28,24},{20,28},{12,20},{4,12},{0,4},{9,1},{1... | collective-permute-start | bytes 786440 | tf_op jit(solution)/shard_map/ppermute | solution.py:48
  28.3 9.0 %collective-permute-start.2 = (bf16[32,4096]{1,0:T(8,128)(2,1)S(1)}, bf16[32,4096]{1,0:T(8,128)(2,1)S(1)}, u32[]{:S(2)}, u32[]{:S(2)}) collective-permute-start(bf16[32,4096]{1,0:T(8,128)(2,1)S(1)} %collective-permute-done.1), channel_id=1, source_target_pairs={{0,8},{8,16},{16,24},{24,28},{28,20},{20,12},{12,4},{4,0},{1,9},{9... | collective-permute-start | bytes 786440 | tf_op jit(solution)/shard_map/ppermute | solution.py:45
  30.4 6.5 %collective-permute-start.6 = (bf16[32,4096]{1,0:T(8,128)(2,1)S(1)}, bf16[32,4096]{1,0:T(8,128)(2,1)S(1)}, u32[]{:S(2)}, u32[]{:S(2)}) collective-permute-start(bf16[32,4096]{1,0:T(8,128)(2,1)S(1)} %collective-permute-done.5), channel_id=1, source_target_pairs={{8,0},{16,8},{24,16},{28,24},{20,28},{12,20},{4,12},{0,4},{9,1},{1... | collective-permute-start | bytes 786440 | tf_op jit(solution)/shard_map/ppermute | solution.py:48
  36.9 5.3 %collective-permute-start.7 = (bf16[16,4096]{1,0:T(8,128)(2,1)S(1)}, bf16[16,4096]{1,0:T(8,128)(2,1)S(1)}, u32[]{:S(2)}, u32[]{:S(2)}) collective-permute-start(bf16[16,4096]{1,0:T(8,128)(2,1)S(1)} %slice.83), channel_id=1, source_target_pairs={{8,0},{16,8},{24,16},{28,24},{20,28},{12,20},{4,12},{0,4},{9,1},{1... | collective-permute-start | bytes 393224 | tf_op jit(solution)/shard_map/ppermute | solution.py:42
  37.3 5.2 %collective-permute-start.3 = (bf16[16,4096]{1,0:T(8,128)(2,1)S(1)}, bf16[16,4096]{1,0:T(8,128)(2,1)S(1)}, u32[]{:S(2)}, u32[]{:S(2)}) collective-permute-start(bf16[16,4096]{1,0:T(8,128)(2,1)S(1)} %slice.82), channel_id=1, source_target_pairs={{0,8},{8,16},{16,24},{24,28},{28,20},{20,12},{12,4},{4,0},{1,9},{9... | collective-permute-start | bytes 393224 | tf_op jit(solution)/shard_map/ppermute | solution.py:41
  55.8 2.2 %collective-permute-start.8 = (f32[80,2048]{1,0:T(8,128)S(1)}, f32[80,2048]{1,0:T(8,128)S(1)}, u32[]{:S(2)}, u32[]{:S(2)}) collective-permute-start(f32[80,2048]{1,0:T(8,128)S(1)} %select_bitcast_fusion), channel_id=1, source_target_pairs={{0,1},{1,0},{2,3},{3,2},{4,5},{5,4},{6,7},{7,6},{8,9},{9,8},{10,11... | collective-permute-start | bytes 1966088 | tf_op jit(solution)/shard_map/ppermute | solution.py:70
  56.8 27.9 %copy-start.4 = (f32[32]{0:T(128)S(1)}, f32[32]{0:T(128)}, u32[]{:S(2)}) copy-start(f32[32]{0:T(128)} %param.15) | copy-start | bytes 388
  58.1 9.8 %collective-permute-start.9 = (f32[40,2048]{1,0:T(8,128)S(1)}, f32[40,2048]{1,0:T(8,128)S(1)}, u32[]{:S(2)}, u32[]{:S(2)}) collective-permute-start(f32[40,2048]{1,0:T(8,128)S(1)} %select_bitcast_fusion.1), channel_id=1, source_target_pairs={{0,2},{1,3},{2,0},{3,1},{4,6},{5,7},{6,4},{7,5},{8,10},{9,11},{10,... | collective-permute-start | bytes 983048 | tf_op jit(solution)/shard_map/ppermute | solution.py:70
  68.3 4.5 %collective-permute-start.12 = (f32[3,40]{1,0:T(4,128)S(1)}, f32[3,40]{1,0:T(4,128)S(1)}, u32[]{:S(2)}, u32[]{:S(2)}) collective-permute-start(f32[3,40]{1,0:T(4,128)S(1)} %pad_maximum_fusion), channel_id=1, source_target_pairs={{0,12},{4,8},{8,4},{12,0},{16,28},{20,24},{24,20},{28,16},{1,13},{... | collective-permute-start | bytes 1448 | tf_op jit(solution)/shard_map/ppermute | solution.py:87
  71.0 3.6 %collective-permute-start.11 = (f32[3,40]{1,0:T(4,128)S(1)}, f32[3,40]{1,0:T(4,128)S(1)}, u32[]{:S(2)}, u32[]{:S(2)}) collective-permute-start(f32[3,40]{1,0:T(4,128)S(1)} %pad_maximum_fusion), channel_id=1, source_target_pairs={{0,8},{4,12},{8,0},{12,4},{16,24},{20,28},{24,16},{28,20},{1,9},{5... | collective-permute-start | bytes 1448 | tf_op jit(solution)/shard_map/ppermute | solution.py:87
  71.5 3.6 %collective-permute-start.10 = (f32[3,40]{1,0:T(4,128)S(1)}, f32[3,40]{1,0:T(4,128)S(1)}, u32[]{:S(2)}, u32[]{:S(2)}) collective-permute-start(f32[3,40]{1,0:T(4,128)S(1)} %pad_maximum_fusion), channel_id=1, source_target_pairs={{0,4},{4,0},{8,12},{12,8},{16,20},{20,16},{24,28},{28,24},{1,5},{5... | collective-permute-start | bytes 1448 | tf_op jit(solution)/shard_map/ppermute | solution.py:87
  75.1 4.5 %collective-permute-start.13 = (f32[3,40]{1,0:T(4,128)S(1)}, f32[3,40]{1,0:T(4,128)S(1)}, u32[]{:S(2)}, u32[]{:S(2)}) collective-permute-start(f32[3,40]{1,0:T(4,128)S(1)} %pad_maximum_fusion.1), channel_id=1, source_target_pairs={{0,16},{4,20},{8,24},{12,28},{16,0},{20,4},{24,8},{28,12},{1,17},{... | collective-permute-start | bytes 1448 | tf_op jit(solution)/shard_map/ppermute | solution.py:91
  79.8 1.2 %collective-permute-start.14 = (f32[160]{0:T(256)S(1)}, f32[160]{0:T(256)S(1)}, u32[]{:S(2)}, u32[]{:S(2)}) collective-permute-start(f32[160]{0:T(256)S(1)} %get-tuple-element.30), channel_id=1, source_target_pairs={{0,1},{1,0},{2,3},{3,2},{4,5},{5,4},{6,7},{7,6},{8,9},{9,8},{10,11... | collective-permute-start | bytes 1928 | tf_op jit(solution)/shard_map/ppermute | solution.py:103
  81.1 3.6 %collective-permute-start.15 = (f32[160]{0:T(256)S(1)}, f32[160]{0:T(256)S(1)}, u32[]{:S(2)}, u32[]{:S(2)}) collective-permute-start(f32[160]{0:T(256)S(1)} %add_dynamic-update-slice_fusion), channel_id=1, source_target_pairs={{0,2},{1,3},{2,0},{3,1},{4,6},{5,7},{6,4},{7,5},{8,10},{9,11},{10,... | collective-permute-start | bytes 1928 | tf_op jit(solution)/shard_map/ppermute | solution.py:103

commit v10 on v7

--- a/solution.py
+++ b/solution.py
@@ -32,15 +32,18 @@
     pos_of = np.argsort(np.asarray(ring))
     fwd = [(ring[i], ring[(i + 1) % size]) for i in range(size)]
     bwd = [(ring[(i + 1) % size], ring[i]) for i in range(size)]
+    count = block.shape[0]
+    lanes = 2 if count % 32 == 0 else 1
+    parts = [block[i * count // lanes:(i + 1) * count // lanes] for i in range(lanes)]
     slots = [None] * size
     slots[0] = block
-    ahead, behind = block, block
+    ahead, behind = list(parts), list(parts)
     for step in range(1, size // 2 + 1):
-        ahead = lax.ppermute(ahead, "dp", fwd)
-        slots[step] = ahead
+        ahead = [lax.ppermute(piece, "dp", fwd) for piece in ahead]
+        slots[step] = jnp.concatenate(ahead) if lanes > 1 else ahead[0]
         if step < size - step:
-            behind = lax.ppermute(behind, "dp", bwd)
-            slots[size - step] = behind
+            behind = [lax.ppermute(piece, "dp", bwd) for piece in behind]
+            slots[size - step] = jnp.concatenate(behind) if lanes > 1 else behind[0]
     count = block.shape[0]
     stacked = jnp.stack(slots).reshape(-1, block.shape[1])
     me = jnp.asarray(pos_of, jnp.int32)[lax.axis_index("dp")]

time: 69.1 us -> 72 us (1.042)
  starting transfers between devices: 18.5 us -> 26.5 us
  waiting for transfers between devices: 31.5 us -> 25.5 us
  local copies, waits for them, and re-layouts: 5.32 us -> 6.11 us
    ppermute x7 -> x14, starting transfers between devices: 8.99 us -> 17.1 us  [the longest x8 14.5 us: ring_gather(): ahead = [lax.ppermute(piece, 'dp', fwd) for piece in ahead]]
    ppermute x7 -> x14, waiting for transfers between devices: 15.5 us -> 8.49 us  [the longest x8 8.48 us: ring_gather(): ahead = [lax.ppermute(piece, 'dp', fwd) for piece in ahead]]
    slice x0 -> x1, local copies, waits for them, and re-layouts: none -> 0.99 us  [ring_gather(): block[i * count // lanes:(i + 1) * count // lanes]]
    ppermute x3, waiting for transfers between devices: 3.19 us -> 4.09 us  [merge_stats(): lax.ppermute(stats, 'dp', [(i, i ^ bit * k) for i in range(size)])]
  transfers between devices with their start and end apart: 15 -> 22, of which waited for: 12 -> 13; matrix products, arithmetic and copies ran while one was open for 11% -> 11% of each run, Pallas kernels for 0% -> 0%
where the time goes in v10:
time: 72 us; the launch traced here: 71.8 us
  starting transfers between devices  26.5 us (37%)
  waiting for transfers between devices  25.5 us (35%)
  matrix products  7.93 us (11%)
  local copies, waits for them, and re-layouts  6.11 us (8%)
  other arithmetic  4.85 us (7%)
  between operations  0.92 us (1%)
    ppermute x8, starting transfers between devices, ring_gather(): ahead = [lax.ppermute(piece, 'dp', fwd) for piece in ahead]  14.5 us
    ppermute x2, waiting for transfers between devices, halving_scatter(): got = lax.ppermute(send, 'vocab', [(i, i ^ bit) for i in range(size)])  9.24 us
    ppermute x8, waiting for transfers between devices, ring_gather(): ahead = [lax.ppermute(piece, 'dp', fwd) for piece in ahead]  8.48 us
    dot_general x1, matrix products, on_device(): jnp.dot(full_rows, head_weight, preferred_element_type=jnp.float32)  7.37 us
    ppermute x3, waiting for transfers between devices, merge_stats(): lax.ppermute(stats, 'dp', [(i, i ^ bit * k) for i in range(size)])  4.09 us
    ppermute x3, starting transfers between devices, merge_stats(): lax.ppermute(stats, 'dp', [(i, i ^ bit * k) for i in range(size)])  3.55 us
    ppermute x1, starting transfers between devices, merge_stats(): lax.ppermute(stats, 'dp', [(i, i ^ bit) for i in range(size)])  2.66 us
    ppermute x6, starting transfers between devices, ring_gather(): behind = [lax.ppermute(piece, 'dp', bwd) for piece in behind]  2.57 us
  transfers between devices with their start and end apart: 22, of which 13 were waited for; matrix products, arithmetic and copies ran while one was open for 11% of the time, Pallas kernels for 0%

profile of v10, /device:TPU:0, one launch (start us, length us, event | category | flops | bytes accessed | tf_op | source)
XLA Modules:
  0.0 71.8 jit_solution(6812923746860050369)
XLA Ops:
  1.6 3.1 %collective-permute-start = (bf16[16,4096]{1,0:T(8,128)(2,1)S(1)}, bf16[16,4096]{1,0:T(8,128)(2,1)S(1)}, u32[]{:S(2)}, u32[]{:S(2)}) collective-permute-start(bf16[16,4096]{1,0:T(8,128)(2,1)S(1)} %get-tuple-element.39), channel_id=1, source_target_pairs={{0,8},{8,16},{16,24},{24,28},{28,20},{20,12},{12,4},{4,0},{1,9},{9... | collective-permute-start | bytes 393224 | tf_op jit(solution)/shard_map/ppermute | solution.py:42
  4.7 2.0 %collective-permute-start.1 = (bf16[16,4096]{1,0:T(8,128)(2,1)S(1)}, bf16[16,4096]{1,0:T(8,128)(2,1)S(1)}, u32[]{:S(2)}, u32[]{:S(2)}) collective-permute-start(bf16[16,4096]{1,0:T(8,128)(2,1)S(1)} %get-tuple-element.40), channel_id=1, source_target_pairs={{0,8},{8,16},{16,24},{24,28},{28,20},{20,12},{12,4},{4,0},{1,9},{9... | collective-permute-start | bytes 393224 | tf_op jit(solution)/shard_map/ppermute | solution.py:42
  9.4 1.2 %dynamic_slice.7 = s32[1]{0:T(128)} dynamic-slice(s32[8]{0:T(128)} %constant.196.clone, s32[]{:T(128)S(6)} %select_n.127), dynamic_slice_sizes={1} | dynamic-slice | bytes 12 | tf_op jit(solution)/shard_map/dynamic_slice | solution.py:49
  10.7 1.3 %and_select_fusion.1 = s32[8]{0:T(128)S(1)} fusion(s32[8]{0:T(128)} %constant.235, s32[]{:T(128)} %bitcast.2), kind=kLoop, calls=%fused_computation.47 | loop fusion | flops 96 | bytes 68 | tf_op jit(solution)/shard_map/jit(remainder)/select_n | solution.py:50
  12.1 2.1 %collective-permute-start.2 = (bf16[16,4096]{1,0:T(8,128)(2,1)S(1)}, bf16[16,4096]{1,0:T(8,128)(2,1)S(1)}, u32[]{:S(2)}, u32[]{:S(2)}) collective-permute-start(bf16[16,4096]{1,0:T(8,128)(2,1)S(1)} %collective-permute-done), channel_id=1, source_target_pairs={{0,8},{8,16},{16,24},{24,28},{28,20},{20,12},{12,4},{4,0},{1,9},{9... | collective-permute-start | bytes 393224 | tf_op jit(solution)/shard_map/ppermute | solution.py:42
  14.2 1.6 %collective-permute-start.3 = (bf16[16,4096]{1,0:T(8,128)(2,1)S(1)}, bf16[16,4096]{1,0:T(8,128)(2,1)S(1)}, u32[]{:S(2)}, u32[]{:S(2)}) collective-permute-start(bf16[16,4096]{1,0:T(8,128)(2,1)S(1)} %collective-permute-done.1), channel_id=1, source_target_pairs={{0,8},{8,16},{16,24},{24,28},{28,20},{20,12},{12,4},{4,0},{1,9},{9... | collective-permute-start | bytes 393224 | tf_op jit(solution)/shard_map/ppermute | solution.py:42
  16.4 2.1 %collective-permute-done.2 = bf16[16,4096]{1,0:T(8,128)(2,1)S(1)} collective-permute-done((bf16[16,4096]{1,0:T(8,128)(2,1)S(1)}, bf16[16,4096]{1,0:T(8,128)(2,1)S(1)}, u32[]{:S(2)}, u32[]{:S(2)}) %collective-permute-start.2) | collective-permute-done | bytes 131104 | tf_op jit(solution)/shard_map/ppermute | solution.py:42
  18.5 1.6 %collective-permute-start.4 = (bf16[16,4096]{1,0:T(8,128)(2,1)S(1)}, bf16[16,4096]{1,0:T(8,128)(2,1)S(1)}, u32[]{:S(2)}, u32[]{:S(2)}) collective-permute-start(bf16[16,4096]{1,0:T(8,128)(2,1)S(1)} %collective-permute-done.2), channel_id=1, source_target_pairs={{0,8},{8,16},{16,24},{24,28},{28,20},{20,12},{12,4},{4,0},{1,9},{9... | collective-permute-start | bytes 393224 | tf_op jit(solution)/shard_map/ppermute | solution.py:42
  20.1 1.2 %collective-permute-done.3 = bf16[16,4096]{1,0:T(8,128)(2,1)S(1)} collective-permute-done((bf16[16,4096]{1,0:T(8,128)(2,1)S(1)}, bf16[16,4096]{1,0:T(8,128)(2,1)S(1)}, u32[]{:S(2)}, u32[]{:S(2)}) %collective-permute-start.3) | collective-permute-done | bytes 131104 | tf_op jit(solution)/shard_map/ppermute | solution.py:42
  21.3 1.6 %collective-permute-start.5 = (bf16[16,4096]{1,0:T(8,128)(2,1)S(1)}, bf16[16,4096]{1,0:T(8,128)(2,1)S(1)}, u32[]{:S(2)}, u32[]{:S(2)}) collective-permute-start(bf16[16,4096]{1,0:T(8,128)(2,1)S(1)} %collective-permute-done.3), channel_id=1, source_target_pairs={{0,8},{8,16},{16,24},{24,28},{28,20},{20,12},{12,4},{4,0},{1,9},{9... | collective-permute-start | bytes 393224 | tf_op jit(solution)/shard_map/ppermute | solution.py:42
  23.4 1.5 %collective-permute-start.13 = (bf16[16,4096]{1,0:T(8,128)(2,1)S(1)}, bf16[16,4096]{1,0:T(8,128)(2,1)S(1)}, u32[]{:S(2)}, u32[]{:S(2)}) collective-permute-start(bf16[16,4096]{1,0:T(8,128)(2,1)S(1)} %collective-permute-done.12), channel_id=1, source_target_pairs={{8,0},{16,8},{24,16},{28,24},{20,28},{12,20},{4,12},{0,4},{9,1},{1... | collective-permute-start | bytes 393224 | tf_op jit(solution)/shard_map/ppermute | solution.py:45
  25.8 1.8 %collective-permute-done.5 = bf16[16,4096]{1,0:T(8,128)(2,1)S(1)} collective-permute-done((bf16[16,4096]{1,0:T(8,128)(2,1)S(1)}, bf16[16,4096]{1,0:T(8,128)(2,1)S(1)}, u32[]{:S(2)}, u32[]{:S(2)}) %collective-permute-start.5) | collective-permute-done | bytes 131104 | tf_op jit(solution)/shard_map/ppermute | solution.py:42
  27.6 1.6 %collective-permute-start.7 = (bf16[16,4096]{1,0:T(8,128)(2,1)S(1)}, bf16[16,4096]{1,0:T(8,128)(2,1)S(1)}, u32[]{:S(2)}, u32[]{:S(2)}) collective-permute-start(bf16[16,4096]{1,0:T(8,128)(2,1)S(1)} %collective-permute-done.5), channel_id=1, source_target_pairs={{0,8},{8,16},{16,24},{24,28},{28,20},{20,12},{12,4},{4,0},{1,9},{9... | collective-permute-start | bytes 393224 | tf_op jit(solution)/shard_map/ppermute | solution.py:42
  29.9 2.7 %collective-permute-done.7 = bf16[16,4096]{1,0:T(8,128)(2,1)S(1)} collective-permute-done((bf16[16,4096]{1,0:T(8,128)(2,1)S(1)}, bf16[16,4096]{1,0:T(8,128)(2,1)S(1)}, u32[]{:S(2)}, u32[]{:S(2)}) %collective-permute-start.7) | collective-permute-done | bytes 131104 | tf_op jit(solution)/shard_map/ppermute | solution.py:42
  33.3 7.4 %fusion.38 = f32[160,2048]{1,0:T(8,128)S(1)} fusion(bf16[160,4096]{1,0:T(8,128)(2,1)S(1)} %convolution_convert_fusion, bf16[4096,2048]{1,0:T(8,128)(2,1)} %param.14), kind=kOutput, calls=%fused_computation.115 | convolution fusion | flops 2684354560 | bytes 19398656 | tf_op jit(solution)/shard_map/dot_general | solution.py:126
  43.0 1.6 %collective-permute-start.15 = (f32[40,2048]{1,0:T(8,128)S(1)}, f32[40,2048]{1,0:T(8,128)S(1)}, u32[]{:S(2)}, u32[]{:S(2)}) collective-permute-start(f32[40,2048]{1,0:T(8,128)S(1)} %select_bitcast_fusion.1), channel_id=1, source_target_pairs={{0,2},{1,3},{2,0},{3,1},{4,6},{5,7},{6,4},{7,5},{8,10},{9,11},{10,... | collective-permute-start | bytes 983048 | tf_op jit(solution)/shard_map/ppermute | solution.py:69
  44.7 8.1 %collective-permute-done.15 = f32[40,2048]{1,0:T(8,128)S(1)} collective-permute-done((f32[40,2048]{1,0:T(8,128)S(1)}, f32[40,2048]{1,0:T(8,128)S(1)}, u32[]{:S(2)}, u32[]{:S(2)}) %collective-permute-start.15) | collective-permute-done | bytes 327712 | tf_op jit(solution)/shard_map/ppermute | solution.py:69
  53.3 1.6 %collective-permute-start.16 = (f32[3,40]{1,0:T(4,128)S(1)}, f32[3,40]{1,0:T(4,128)S(1)}, u32[]{:S(2)}, u32[]{:S(2)}) collective-permute-start(f32[3,40]{1,0:T(4,128)S(1)} %pad_maximum_fusion), channel_id=1, source_target_pairs={{0,4},{4,0},{8,12},{12,8},{16,20},{20,16},{24,28},{28,24},{1,5},{5... | collective-permute-start | bytes 1448 | tf_op jit(solution)/shard_map/ppermute | solution.py:86
  54.9 1.6 %collective-permute-start.17 = (f32[3,40]{1,0:T(4,128)S(1)}, f32[3,40]{1,0:T(4,128)S(1)}, u32[]{:S(2)}, u32[]{:S(2)}) collective-permute-start(f32[3,40]{1,0:T(4,128)S(1)} %pad_maximum_fusion), channel_id=1, source_target_pairs={{0,8},{4,12},{8,0},{12,4},{16,24},{20,28},{24,16},{28,20},{1,9},{5... | collective-permute-start | bytes 1448 | tf_op jit(solution)/shard_map/ppermute | solution.py:86
  56.9 1.5 %collective-permute-done.17 = f32[3,40]{1,0:T(4,128)S(1)} collective-permute-done((f32[3,40]{1,0:T(4,128)S(1)}, f32[3,40]{1,0:T(4,128)S(1)}, u32[]{:S(2)}, u32[]{:S(2)}) %collective-permute-start.17) | collective-permute-done | bytes 512 | tf_op jit(solution)/shard_map/ppermute | solution.py:86
  58.5 2.5 %collective-permute-done.18 = f32[3,40]{1,0:T(4,128)S(1)} collective-permute-done((f32[3,40]{1,0:T(4,128)S(1)}, f32[3,40]{1,0:T(4,128)S(1)}, u32[]{:S(2)}, u32[]{:S(2)}) %collective-permute-start.18) | collective-permute-done | bytes 512 | tf_op jit(solution)/shard_map/ppermute | solution.py:86
  61.0 2.7 %collective-permute-start.19 = (f32[3,40]{1,0:T(4,128)S(1)}, f32[3,40]{1,0:T(4,128)S(1)}, u32[]{:S(2)}, u32[]{:S(2)}) collective-permute-start(f32[3,40]{1,0:T(4,128)S(1)} %pad_maximum_fusion.1), channel_id=1, source_target_pairs={{0,16},{4,20},{8,24},{12,28},{16,0},{20,4},{24,8},{28,12},{1,17},{... | collective-permute-start | bytes 1448 | tf_op jit(solution)/shard_map/ppermute | solution.py:90
  67.0 1.5 %collective-permute-start.21 = (f32[160]{0:T(256)S(1)}, f32[160]{0:T(256)S(1)}, u32[]{:S(2)}, u32[]{:S(2)}) collective-permute-start(f32[160]{0:T(256)S(1)} %add_dynamic-update-slice_fusion), channel_id=1, source_target_pairs={{0,2},{1,3},{2,0},{3,1},{4,6},{5,7},{6,4},{7,5},{8,10},{9,11},{10,... | collective-permute-start | bytes 1928 | tf_op jit(solution)/shard_map/ppermute | solution.py:102
  69.2 1.3 %collective-permute-done.21 = f32[160]{0:T(256)S(1)} collective-permute-done((f32[160]{0:T(256)S(1)}, f32[160]{0:T(256)S(1)}, u32[]{:S(2)}, u32[]{:S(2)}) %collective-permute-start.21) | collective-permute-done | bytes 672 | tf_op jit(solution)/shard_map/ppermute | solution.py:102
  (71 shorter events, 15.5 us)
Async XLA Ops:
  0.6 40.4 %copy-start = (s32[256]{0:T(256)S(1)}, s32[256]{0:T(256)}, u32[]{:S(2)}) copy-start(s32[256]{0:T(256)} %param.16) | copy-start | bytes 3076
  1.6 10.5 %collective-permute-start = (bf16[16,4096]{1,0:T(8,128)(2,1)S(1)}, bf16[16,4096]{1,0:T(8,128)(2,1)S(1)}, u32[]{:S(2)}, u32[]{:S(2)}) collective-permute-start(bf16[16,4096]{1,0:T(8,128)(2,1)S(1)} %get-tuple-element.39), channel_id=1, source_target_pairs={{0,8},{8,16},{16,24},{24,28},{28,20},{20,12},{12,4},{4,0},{1,9},{9... | collective-permute-start | bytes 393224 | tf_op jit(solution)/shard_map/ppermute | solution.py:42
  4.7 11.0 %collective-permute-start.8 = (bf16[16,4096]{1,0:T(8,128)(2,1)S(1)}, bf16[16,4096]{1,0:T(8,128)(2,1)S(1)}, u32[]{:S(2)}, u32[]{:S(2)}) collective-permute-start(bf16[16,4096]{1,0:T(8,128)(2,1)S(1)} %get-tuple-element.39), channel_id=1, source_target_pairs={{8,0},{16,8},{24,16},{28,24},{20,28},{12,20},{4,12},{0,4},{9,1},{1... | collective-permute-start | bytes 393224 | tf_op jit(solution)/shard_map/ppermute | solution.py:45
  4.7 9.4 %collective-permute-start.1 = (bf16[16,4096]{1,0:T(8,128)(2,1)S(1)}, bf16[16,4096]{1,0:T(8,128)(2,1)S(1)}, u32[]{:S(2)}, u32[]{:S(2)}) collective-permute-start(bf16[16,4096]{1,0:T(8,128)(2,1)S(1)} %get-tuple-element.40), channel_id=1, source_target_pairs={{0,8},{8,16},{16,24},{24,28},{28,20},{20,12},{12,4},{4,0},{1,9},{9... | collective-permute-start | bytes 393224 | tf_op jit(solution)/shard_map/ppermute | solution.py:42
  6.8 9.5 %collective-permute-start.11 = (bf16[16,4096]{1,0:T(8,128)(2,1)S(1)}, bf16[16,4096]{1,0:T(8,128)(2,1)S(1)}, u32[]{:S(2)}, u32[]{:S(2)}) collective-permute-start(bf16[16,4096]{1,0:T(8,128)(2,1)S(1)} %get-tuple-element.40), channel_id=1, source_target_pairs={{8,0},{16,8},{24,16},{28,24},{20,28},{12,20},{4,12},{0,4},{9,1},{1... | collective-permute-start | bytes 393224 | tf_op jit(solution)/shard_map/ppermute | solution.py:45
  12.1 6.4 %collective-permute-start.2 = (bf16[16,4096]{1,0:T(8,128)(2,1)S(1)}, bf16[16,4096]{1,0:T(8,128)(2,1)S(1)}, u32[]{:S(2)}, u32[]{:S(2)}) collective-permute-start(bf16[16,4096]{1,0:T(8,128)(2,1)S(1)} %collective-permute-done), channel_id=1, source_target_pairs={{0,8},{8,16},{16,24},{24,28},{28,20},{20,12},{12,4},{4,0},{1,9},{9... | collective-permute-start | bytes 393224 | tf_op jit(solution)/shard_map/ppermute | solution.py:42
  14.2 7.1 %collective-permute-start.3 = (bf16[16,4096]{1,0:T(8,128)(2,1)S(1)}, bf16[16,4096]{1,0:T(8,128)(2,1)S(1)}, u32[]{:S(2)}, u32[]{:S(2)}) collective-permute-start(bf16[16,4096]{1,0:T(8,128)(2,1)S(1)} %collective-permute-done.1), channel_id=1, source_target_pairs={{0,8},{8,16},{16,24},{24,28},{28,20},{20,12},{12,4},{4,0},{1,9},{9... | collective-permute-start | bytes 393224 | tf_op jit(solution)/shard_map/ppermute | solution.py:42
  15.8 7.1 %collective-permute-start.9 = (bf16[16,4096]{1,0:T(8,128)(2,1)S(1)}, bf16[16,4096]{1,0:T(8,128)(2,1)S(1)}, u32[]{:S(2)}, u32[]{:S(2)}) collective-permute-start(bf16[16,4096]{1,0:T(8,128)(2,1)S(1)} %collective-permute-done.8), channel_id=1, source_target_pairs={{8,0},{16,8},{24,16},{28,24},{20,28},{12,20},{4,12},{0,4},{9,1},{1... | collective-permute-start | bytes 393224 | tf_op jit(solution)/shard_map/ppermute | solution.py:45
  16.3 7.1 %collective-permute-start.12 = (bf16[16,4096]{1,0:T(8,128)(2,1)S(1)}, bf16[16,4096]{1,0:T(8,128)(2,1)S(1)}, u32[]{:S(2)}, u32[]{:S(2)}) collective-permute-start(bf16[16,4096]{1,0:T(8,128)(2,1)S(1)} %collective-permute-done.11), channel_id=1, source_target_pairs={{8,0},{16,8},{24,16},{28,24},{20,28},{12,20},{4,12},{0,4},{9,1},{1... | collective-permute-start | bytes 393224 | tf_op jit(solution)/shard_map/ppermute | solution.py:45
  18.5 6.5 %collective-permute-start.4 = (bf16[16,4096]{1,0:T(8,128)(2,1)S(1)}, bf16[16,4096]{1,0:T(8,128)(2,1)S(1)}, u32[]{:S(2)}, u32[]{:S(2)}) collective-permute-start(bf16[16,4096]{1,0:T(8,128)(2,1)S(1)} %collective-permute-done.2), channel_id=1, source_target_pairs={{0,8},{8,16},{16,24},{24,28},{28,20},{20,12},{12,4},{4,0},{1,9},{9... | collective-permute-start | bytes 393224 | tf_op jit(solution)/shard_map/ppermute | solution.py:42
  21.3 6.4 %collective-permute-start.5 = (bf16[16,4096]{1,0:T(8,128)(2,1)S(1)}, bf16[16,4096]{1,0:T(8,128)(2,1)S(1)}, u32[]{:S(2)}, u32[]{:S(2)}) collective-permute-start(bf16[16,4096]{1,0:T(8,128)(2,1)S(1)} %collective-permute-done.3), channel_id=1, source_target_pairs={{0,8},{8,16},{16,24},{24,28},{28,20},{20,12},{12,4},{4,0},{1,9},{9... | collective-permute-start | bytes 393224 | tf_op jit(solution)/shard_map/ppermute | solution.py:42
  22.9 9.7 %collective-permute-start.10 = (bf16[16,4096]{1,0:T(8,128)(2,1)S(1)}, bf16[16,4096]{1,0:T(8,128)(2,1)S(1)}, u32[]{:S(2)}, u32[]{:S(2)}) collective-permute-start(bf16[16,4096]{1,0:T(8,128)(2,1)S(1)} %collective-permute-done.9), channel_id=1, source_target_pairs={{8,0},{16,8},{24,16},{28,24},{20,28},{12,20},{4,12},{0,4},{9,1},{1... | collective-permute-start | bytes 393224 | tf_op jit(solution)/shard_map/ppermute | solution.py:45
  23.4 9.3 %collective-permute-start.13 = (bf16[16,4096]{1,0:T(8,128)(2,1)S(1)}, bf16[16,4096]{1,0:T(8,128)(2,1)S(1)}, u32[]{:S(2)}, u32[]{:S(2)}) collective-permute-start(bf16[16,4096]{1,0:T(8,128)(2,1)S(1)} %collective-permute-done.12), channel_id=1, source_target_pairs={{8,0},{16,8},{24,16},{28,24},{20,28},{12,20},{4,12},{0,4},{9,1},{1... | collective-permute-start | bytes 393224 | tf_op jit(solution)/shard_map/ppermute | solution.py:45
  24.9 5.0 %collective-permute-start.6 = (bf16[16,4096]{1,0:T(8,128)(2,1)S(1)}, bf16[16,4096]{1,0:T(8,128)(2,1)S(1)}, u32[]{:S(2)}, u32[]{:S(2)}) collective-permute-start(bf16[16,4096]{1,0:T(8,128)(2,1)S(1)} %collective-permute-done.4), channel_id=1, source_target_pairs={{0,8},{8,16},{16,24},{24,28},{28,20},{20,12},{12,4},{4,0},{1,9},{9... | collective-permute-start | bytes 393224 | tf_op jit(solution)/shard_map/ppermute | solution.py:42
  27.6 5.0 %collective-permute-start.7 = (bf16[16,4096]{1,0:T(8,128)(2,1)S(1)}, bf16[16,4096]{1,0:T(8,128)(2,1)S(1)}, u32[]{:S(2)}, u32[]{:S(2)}) collective-permute-start(bf16[16,4096]{1,0:T(8,128)(2,1)S(1)} %collective-permute-done.5), channel_id=1, source_target_pairs={{0,8},{8,16},{16,24},{24,28},{28,20},{20,12},{12,4},{4,0},{1,9},{9... | collective-permute-start | bytes 393224 | tf_op jit(solution)/shard_map/ppermute | solution.py:42
  40.7 2.2 %collective-permute-start.14 = (f32[80,2048]{1,0:T(8,128)S(1)}, f32[80,2048]{1,0:T(8,128)S(1)}, u32[]{:S(2)}, u32[]{:S(2)}) collective-permute-start(f32[80,2048]{1,0:T(8,128)S(1)} %select_bitcast_fusion), channel_id=1, source_target_pairs={{0,1},{1,0},{2,3},{3,2},{4,5},{5,4},{6,7},{7,6},{8,9},{9,8},{10,11... | collective-permute-start | bytes 1966088 | tf_op jit(solution)/shard_map/ppermute | solution.py:69
  43.0 28.3 %copy-start.2 = (f32[32]{0:T(128)S(1)}, f32[32]{0:T(128)}, u32[]{:S(2)}) copy-start(f32[32]{0:T(128)} %param.17) | copy-start | bytes 388
  43.0 9.8 %collective-permute-start.15 = (f32[40,2048]{1,0:T(8,128)S(1)}, f32[40,2048]{1,0:T(8,128)S(1)}, u32[]{:S(2)}, u32[]{:S(2)}) collective-permute-start(f32[40,2048]{1,0:T(8,128)S(1)} %select_bitcast_fusion.1), channel_id=1, source_target_pairs={{0,2},{1,3},{2,0},{3,1},{4,6},{5,7},{6,4},{7,5},{8,10},{9,11},{10,... | collective-permute-start | bytes 983048 | tf_op jit(solution)/shard_map/ppermute | solution.py:69
  53.3 3.7 %collective-permute-start.16 = (f32[3,40]{1,0:T(4,128)S(1)}, f32[3,40]{1,0:T(4,128)S(1)}, u32[]{:S(2)}, u32[]{:S(2)}) collective-permute-start(f32[3,40]{1,0:T(4,128)S(1)} %pad_maximum_fusion), channel_id=1, source_target_pairs={{0,4},{4,0},{8,12},{12,8},{16,20},{20,16},{24,28},{28,24},{1,5},{5... | collective-permute-start | bytes 1448 | tf_op jit(solution)/shard_map/ppermute | solution.py:86
  54.9 3.6 %collective-permute-start.17 = (f32[3,40]{1,0:T(4,128)S(1)}, f32[3,40]{1,0:T(4,128)S(1)}, u32[]{:S(2)}, u32[]{:S(2)}) collective-permute-start(f32[3,40]{1,0:T(4,128)S(1)} %pad_maximum_fusion), channel_id=1, source_target_pairs={{0,8},{4,12},{8,0},{12,4},{16,24},{20,28},{24,16},{28,20},{1,9},{5... | collective-permute-start | bytes 1448 | tf_op jit(solution)/shard_map/ppermute | solution.py:86
  56.5 4.5 %collective-permute-start.18 = (f32[3,40]{1,0:T(4,128)S(1)}, f32[3,40]{1,0:T(4,128)S(1)}, u32[]{:S(2)}, u32[]{:S(2)}) collective-permute-start(f32[3,40]{1,0:T(4,128)S(1)} %pad_maximum_fusion), channel_id=1, source_target_pairs={{0,12},{4,8},{8,4},{12,0},{16,28},{20,24},{24,20},{28,16},{1,13},{... | collective-permute-start | bytes 1448 | tf_op jit(solution)/shard_map/ppermute | solution.py:86
  61.0 4.5 %collective-permute-start.19 = (f32[3,40]{1,0:T(4,128)S(1)}, f32[3,40]{1,0:T(4,128)S(1)}, u32[]{:S(2)}, u32[]{:S(2)}) collective-permute-start(f32[3,40]{1,0:T(4,128)S(1)} %pad_maximum_fusion.1), channel_id=1, source_target_pairs={{0,16},{4,20},{8,24},{12,28},{16,0},{20,4},{24,8},{28,12},{1,17},{... | collective-permute-start | bytes 1448 | tf_op jit(solution)/shard_map/ppermute | solution.py:90
  65.6 1.2 %collective-permute-start.20 = (f32[160]{0:T(256)S(1)}, f32[160]{0:T(256)S(1)}, u32[]{:S(2)}, u32[]{:S(2)}) collective-permute-start(f32[160]{0:T(256)S(1)} %get-tuple-element.31), channel_id=1, source_target_pairs={{0,1},{1,0},{2,3},{3,2},{4,5},{5,4},{6,7},{7,6},{8,9},{9,8},{10,11... | collective-permute-start | bytes 1928 | tf_op jit(solution)/shard_map/ppermute | solution.py:102
  67.0 3.6 %collective-permute-start.21 = (f32[160]{0:T(256)S(1)}, f32[160]{0:T(256)S(1)}, u32[]{:S(2)}, u32[]{:S(2)}) collective-permute-start(f32[160]{0:T(256)S(1)} %add_dynamic-update-slice_fusion), channel_id=1, source_target_pairs={{0,2},{1,3},{2,0},{3,1},{4,6},{5,7},{6,4},{7,5},{8,10},{9,11},{10,... | collective-permute-start | bytes 1928 | tf_op jit(solution)/shard_map/ppermute | solution.py:102
  (1 other events, 26.7 us)

commit v11 on v7

--- a/solution.py
+++ b/solution.py
@@ -3,6 +3,8 @@
 import jax.numpy as jnp
 from jax import lax
 from jax.sharding import PartitionSpec as P
+from jax.experimental import pallas as pl
+from jax.experimental.pallas import tpu as pltpu
 
 MB = 8
 
@@ -51,6 +53,22 @@
     choose = lax.broadcasted_iota(jnp.int32, (stacked.shape[0], where.shape[0]), 0) == where[None, :]
     picked = lax.dot_general(choose.astype(stacked.dtype), stacked, (((0,), (0,)), ((), ())), preferred_element_type=jnp.float32)
     return lax.optimization_barrier(picked.astype(stacked.dtype))
+
+
+def product_kernel(rows_ref, weight_ref, out_ref):
+    out_ref[...] = jnp.dot(rows_ref[...], weight_ref[...], preferred_element_type=jnp.float32)
+
+
+def column_product(rows, weight, first, width, tile):
+    count, depth = rows.shape
+    base = first // tile
+    return pl.pallas_call(
+        product_kernel,
+        out_shape=jax.ShapeDtypeStruct((count, width), jnp.float32),
+        grid=(width // tile,),
+        in_specs=[pl.BlockSpec((count, depth), lambda j: (0, 0)), pl.BlockSpec((depth, tile), lambda j: (0, base + j))],
+        out_specs=pl.BlockSpec((count, tile), lambda j: (0, j)),
+    )(rows, weight)
 
 
 def halving_scatter(partial, size):
@@ -120,14 +138,24 @@
         in_batch = packed - jnp.sum(jnp.where(batch_of[None, :] == jnp.arange(MB, dtype=jnp.int32)[:, None], starts[:, None], 0), axis=0)
         live_rows = batch_of * slot_count + in_batch
         full_rows = ring_gather(hidden, ring, live_rows)
-        partial = jnp.dot(full_rows, head_weight, preferred_element_type=jnp.float32)
-        logits, first = halving_scatter(partial, vocab_size)
-        share = logits.shape[0]
-        row_targets = jnp.take(targets, lax.dynamic_slice_in_dim(live_rows, first, share))
-        highest = jnp.max(logits, axis=1)
-        exp_total = jnp.sum(jnp.exp(logits - highest[:, None]), axis=1)
-        columns = col_start + lax.broadcasted_iota(jnp.int32, logits.shape, 1)
-        picked = jnp.sum(jnp.where(columns == row_targets[:, None], logits, 0.0), axis=1)
+        pieces = 2 if tile_width % 1024 == 0 else 1
+        width = tile_width // pieces
+        parts = []
+        for piece in range(pieces):
+            partial = column_product(full_rows, head_weight, piece * width, width, 512 if width % 512 == 0 else width)
+            logits, first = halving_scatter(partial, vocab_size)
+            share = logits.shape[0]
+            row_targets = jnp.take(targets, lax.dynamic_slice_in_dim(live_rows, first, share))
+            highest = jnp.max(logits, axis=1)
+            exp_total = jnp.sum(jnp.exp(logits - highest[:, None]), axis=1)
+            columns = col_start + piece * width + lax.broadcasted_iota(jnp.int32, logits.shape, 1)
+            picked = jnp.sum(jnp.where(columns == row_targets[:, None], logits, 0.0), axis=1)
+            parts.append((highest, exp_total, picked))
+        highest = parts[0][0]
+        for part in parts[1:]:
+            highest = jnp.maximum(highest, part[0])
+        exp_total = sum(part[1] * jnp.exp(part[0] - highest) for part in parts)
+        picked = sum(part[2] for part in parts)
         stats = merge_stats(jnp.stack([highest, exp_total, picked]), dp_size)
         logprob = stats[2] - (stats[0] + jnp.log(stats[1]))
         all_values = doubling_gather(logprob, first, vocab_size)

time: 69.1 us -> 75.5 us (1.093)
  Pallas kernels: 0 us -> 11 us
  matrix products: 7.93 us -> 1.63 us
  other arithmetic: 4.72 us -> 6.86 us
  waiting for transfers between devices: 31.5 us -> 29.9 us
  starting transfers between devices: 18.5 us -> 19.7 us
    pallas_call x0 -> x2, Pallas kernels: none -> 11 us  [column_product(): pl.pallas_call(product_kernel, out_shape=jax.ShapeDtypeStruct((count, wid...]
    dot_general x1 -> x0, matrix products: 7.37 us -> none  [on_device(): jnp.dot(full_rows, head_weight, preferred_element_type=jnp.float32)]
    ppermute x2 -> x4, waiting for transfers between devices: 9.12 us -> 6.88 us  [halving_scatter(): got = lax.ppermute(send, 'vocab', [(i, i ^ bit) for i in range(size)])]
    select_n x2 -> x4, other arithmetic: 0.09 us -> 2.11 us  [halving_scatter(): send = jnp.take(pairs, 1 - side, axis=0)]
    ppermute x2 -> x4, starting transfers between devices: 1.81 us -> 3.26 us  [halving_scatter(): got = lax.ppermute(send, 'vocab', [(i, i ^ bit) for i in range(size)])]
    dot_general x1, matrix products: 0.56 us -> 1.63 us  [ring_gather(): lax.dot_general(choose.astype(stacked.dtype), stacked, (((0,), (0,)), (()...]
  transfers between devices with their start and end apart: 15 -> 17, of which waited for: 12 -> 12; matrix products, arithmetic and copies ran while one was open for 11% -> 12% of each run, Pallas kernels for 0% -> 7%
where the time goes in v11:
time: 75.5 us; the launch traced here: 75.3 us
  waiting for transfers between devices  29.9 us (40%)
  starting transfers between devices  19.7 us (26%)
  Pallas kernels  11 us (15%)
  other arithmetic  6.86 us (9%)
  local copies, waits for them, and re-layouts  5.33 us (7%)
  matrix products  1.63 us (2%)
  between operations  0.92 us (1%)
    ppermute x4, waiting for transfers between devices, ring_gather(): ahead = lax.ppermute(ahead, 'dp', fwd)  15.4 us
    pallas_call x2, Pallas kernels, column_product(): pl.pallas_call(product_kernel, out_shape=jax.ShapeDtypeStruct((count, wid...  11 us
    ppermute x4, starting transfers between devices, ring_gather(): ahead = lax.ppermute(ahead, 'dp', fwd)  8.23 us
    ppermute x4, waiting for transfers between devices, halving_scatter(): got = lax.ppermute(send, 'vocab', [(i, i ^ bit) for i in range(size)])  6.88 us
    ppermute x3, waiting for transfers between devices, merge_stats(): lax.ppermute(stats, 'dp', [(i, i ^ bit * k) for i in range(size)])  3.94 us
    ppermute x3, starting transfers between devices, merge_stats(): lax.ppermute(stats, 'dp', [(i, i ^ bit * k) for i in range(size)])  3.55 us
    ppermute x4, starting transfers between devices, halving_scatter(): got = lax.ppermute(send, 'vocab', [(i, i ^ bit) for i in range(size)])  3.26 us
    ppermute x1, starting transfers between devices, merge_stats(): lax.ppermute(stats, 'dp', [(i, i ^ bit) for i in range(size)])  2.66 us
  transfers between devices with their start and end apart: 17, of which 12 were waited for; matrix products, arithmetic and copies ran while one was open for 12% of the time, Pallas kernels for 7%

profile of v11, /device:TPU:0, one launch (start us, length us, event | category | flops | bytes accessed | tf_op | source)
XLA Modules:
  0.0 75.3 jit_solution(4324261469772060136)
XLA Ops:
  0.6 3.1 %collective-permute-start = (bf16[32,4096]{1,0:T(8,128)(2,1)}, bf16[32,4096]{1,0:T(8,128)(2,1)S(1)}, u32[]{:S(2)}, u32[]{:S(2)}) collective-permute-start(bf16[32,4096]{1,0:T(8,128)(2,1)} %param.15), channel_id=1, source_target_pairs={{0,8},{8,16},{16,24},{24,28},{28,20},{20,12},{12,4},{4,0},{1,9},{9... | collective-permute-start | bytes 786440 | tf_op jit(solution)/shard_map/ppermute | solution.py:41
  6.5 1.2 %dynamic_slice.8 = s32[1]{0:T(128)} dynamic-slice(s32[8]{0:T(128)} %constant.201.clone, s32[]{:T(128)S(6)} %select_n.131), dynamic_slice_sizes={1} | dynamic-slice | bytes 12 | tf_op jit(solution)/shard_map/dynamic_slice | solution.py:48
  7.8 1.3 %and_select_fusion.2 = s32[8]{0:T(128)S(1)} fusion(s32[8]{0:T(128)} %constant.240, s32[]{:T(128)} %bitcast.2), kind=kLoop, calls=%fused_computation.48 | loop fusion | flops 96 | bytes 68 | tf_op jit(solution)/shard_map/jit(remainder)/select_n | solution.py:49
  10.2 2.0 %collective-permute-start.1 = (bf16[32,4096]{1,0:T(8,128)(2,1)S(1)}, bf16[32,4096]{1,0:T(8,128)(2,1)S(1)}, u32[]{:S(2)}, u32[]{:S(2)}) collective-permute-start(bf16[32,4096]{1,0:T(8,128)(2,1)S(1)} %collective-permute-done), channel_id=1, source_target_pairs={{0,8},{8,16},{16,24},{24,28},{28,20},{20,12},{12,4},{4,0},{1,9},{9... | collective-permute-start | bytes 786440 | tf_op jit(solution)/shard_map/ppermute | solution.py:41
  12.3 5.6 %collective-permute-done.1 = bf16[32,4096]{1,0:T(8,128)(2,1)S(1)} collective-permute-done((bf16[32,4096]{1,0:T(8,128)(2,1)S(1)}, bf16[32,4096]{1,0:T(8,128)(2,1)S(1)}, u32[]{:S(2)}, u32[]{:S(2)}) %collective-permute-start.1) | collective-permute-done | bytes 262176 | tf_op jit(solution)/shard_map/ppermute | solution.py:41
  17.9 1.7 %collective-permute-start.2 = (bf16[32,4096]{1,0:T(8,128)(2,1)S(1)}, bf16[32,4096]{1,0:T(8,128)(2,1)S(1)}, u32[]{:S(2)}, u32[]{:S(2)}) collective-permute-start(bf16[32,4096]{1,0:T(8,128)(2,1)S(1)} %collective-permute-done.1), channel_id=1, source_target_pairs={{0,8},{8,16},{16,24},{24,28},{28,20},{20,12},{12,4},{4,0},{1,9},{9... | collective-permute-start | bytes 786440 | tf_op jit(solution)/shard_map/ppermute | solution.py:41
  20.0 4.8 %collective-permute-done.2 = bf16[32,4096]{1,0:T(8,128)(2,1)S(1)} collective-permute-done((bf16[32,4096]{1,0:T(8,128)(2,1)S(1)}, bf16[32,4096]{1,0:T(8,128)(2,1)S(1)}, u32[]{:S(2)}, u32[]{:S(2)}) %collective-permute-start.2) | collective-permute-done | bytes 262176 | tf_op jit(solution)/shard_map/ppermute | solution.py:41
  24.8 1.5 %collective-permute-start.3 = (bf16[32,4096]{1,0:T(8,128)(2,1)S(1)}, bf16[32,4096]{1,0:T(8,128)(2,1)S(1)}, u32[]{:S(2)}, u32[]{:S(2)}) collective-permute-start(bf16[32,4096]{1,0:T(8,128)(2,1)S(1)} %collective-permute-done.2), channel_id=1, source_target_pairs={{0,8},{8,16},{16,24},{24,28},{28,20},{20,12},{12,4},{4,0},{1,9},{9... | collective-permute-start | bytes 786440 | tf_op jit(solution)/shard_map/ppermute | solution.py:41
  26.3 4.9 %collective-permute-done.3 = bf16[32,4096]{1,0:T(8,128)(2,1)S(1)} collective-permute-done((bf16[32,4096]{1,0:T(8,128)(2,1)S(1)}, bf16[32,4096]{1,0:T(8,128)(2,1)S(1)}, u32[]{:S(2)}, u32[]{:S(2)}) %collective-permute-start.3) | collective-permute-done | bytes 262176 | tf_op jit(solution)/shard_map/ppermute | solution.py:41
  31.3 1.6 %convolution_convert_fusion.rows_ref = bf16[160,4096]{1,0:T(8,128)(2,1)} fusion(bf16[256,4096]{1,0:T(8,128)(2,1)S(1)} %bitcast.194, s32[160]{0:T(256)S(1)} %fusion.1), kind=kOutput, calls=%fused_computation.4 | convolution fusion | flops 336240640 | bytes 3408512 | tf_op jit(solution)/shard_map/dot_general | solution.py:54
  32.9 5.5 %shard_map.86 = f32[160,1024]{1,0:T(8,128)} custom-call(bf16[160,4096]{1,0:T(8,128)(2,1)} %convolution_convert_fusion.rows_ref, bf16[4096,2048]{1,0:T(8,128)(2,1)} %weight_ref.3), custom_call_target="tpu_custom_call" | custom-call | tf_op jit(solution)/shard_map/pallas_call | solution.py:65
  39.5 5.5 %shard_map.87 = f32[160,1024]{1,0:T(8,128)} custom-call(bf16[160,4096]{1,0:T(8,128)(2,1)} %convolution_convert_fusion.rows_ref, bf16[4096,2048]{1,0:T(8,128)(2,1)} %weight_ref.3), custom_call_target="tpu_custom_call" | custom-call | tf_op jit(solution)/shard_map/pallas_call | solution.py:65
  46.8 1.5 %collective-permute-start.8 = (f32[40,1024]{1,0:T(8,128)S(1)}, f32[40,1024]{1,0:T(8,128)S(1)}, u32[]{:S(2)}, u32[]{:S(2)}) collective-permute-start(f32[40,1024]{1,0:T(8,128)S(1)} %select_bitcast_fusion.3), channel_id=1, source_target_pairs={{0,2},{1,3},{2,0},{3,1},{4,6},{5,7},{6,4},{7,5},{8,10},{9,11},{10,... | collective-permute-start | bytes 491528 | tf_op jit(solution)/shard_map/ppermute | solution.py:84
  48.3 1.2 %collective-permute-start.10 = (f32[40,1024]{1,0:T(8,128)S(1)}, f32[40,1024]{1,0:T(8,128)S(1)}, u32[]{:S(2)}, u32[]{:S(2)}) collective-permute-start(f32[40,1024]{1,0:T(8,128)S(1)} %select_bitcast_fusion.2), channel_id=1, source_target_pairs={{0,2},{1,3},{2,0},{3,1},{4,6},{5,7},{6,4},{7,5},{8,10},{9,11},{10,... | collective-permute-start | bytes 491528 | tf_op jit(solution)/shard_map/ppermute | solution.py:84
  49.5 4.4 %collective-permute-done.8 = f32[40,1024]{1,0:T(8,128)S(1)} collective-permute-done((f32[40,1024]{1,0:T(8,128)S(1)}, f32[40,1024]{1,0:T(8,128)S(1)}, u32[]{:S(2)}, u32[]{:S(2)}) %collective-permute-start.8) | collective-permute-done | bytes 163872 | tf_op jit(solution)/shard_map/ppermute | solution.py:84
  54.0 2.5 %collective-permute-done.10 = f32[40,1024]{1,0:T(8,128)S(1)} collective-permute-done((f32[40,1024]{1,0:T(8,128)S(1)}, f32[40,1024]{1,0:T(8,128)S(1)}, u32[]{:S(2)}, u32[]{:S(2)}) %collective-permute-start.10) | collective-permute-done | bytes 163872 | tf_op jit(solution)/shard_map/ppermute | solution.py:84
  56.9 1.4 %collective-permute-start.11 = (f32[3,40]{1,0:T(4,128)S(1)}, f32[3,40]{1,0:T(4,128)S(1)}, u32[]{:S(2)}, u32[]{:S(2)}) collective-permute-start(f32[3,40]{1,0:T(4,128)S(1)} %pad_maximum_fusion), channel_id=1, source_target_pairs={{0,4},{4,0},{8,12},{12,8},{16,20},{20,16},{24,28},{28,24},{1,5},{5... | collective-permute-start | bytes 1448 | tf_op jit(solution)/shard_map/ppermute | solution.py:101
  58.3 1.6 %collective-permute-start.12 = (f32[3,40]{1,0:T(4,128)S(1)}, f32[3,40]{1,0:T(4,128)S(1)}, u32[]{:S(2)}, u32[]{:S(2)}) collective-permute-start(f32[3,40]{1,0:T(4,128)S(1)} %pad_maximum_fusion), channel_id=1, source_target_pairs={{0,8},{4,12},{8,0},{12,4},{16,24},{20,28},{24,16},{28,20},{1,9},{5... | collective-permute-start | bytes 1448 | tf_op jit(solution)/shard_map/ppermute | solution.py:101
  60.6 1.4 %collective-permute-done.12 = f32[3,40]{1,0:T(4,128)S(1)} collective-permute-done((f32[3,40]{1,0:T(4,128)S(1)}, f32[3,40]{1,0:T(4,128)S(1)}, u32[]{:S(2)}, u32[]{:S(2)}) %collective-permute-start.12) | collective-permute-done | bytes 512 | tf_op jit(solution)/shard_map/ppermute | solution.py:101
  61.9 2.5 %collective-permute-done.13 = f32[3,40]{1,0:T(4,128)S(1)} collective-permute-done((f32[3,40]{1,0:T(4,128)S(1)}, f32[3,40]{1,0:T(4,128)S(1)}, u32[]{:S(2)}, u32[]{:S(2)}) %collective-permute-start.13) | collective-permute-done | bytes 512 | tf_op jit(solution)/shard_map/ppermute | solution.py:101
  64.4 2.7 %collective-permute-start.14 = (f32[3,40]{1,0:T(4,128)S(1)}, f32[3,40]{1,0:T(4,128)S(1)}, u32[]{:S(2)}, u32[]{:S(2)}) collective-permute-start(f32[3,40]{1,0:T(4,128)S(1)} %pad_maximum_fusion.1), channel_id=1, source_target_pairs={{0,16},{4,20},{8,24},{12,28},{16,0},{20,4},{24,8},{28,12},{1,17},{... | collective-permute-start | bytes 1448 | tf_op jit(solution)/shard_map/ppermute | solution.py:105
  67.8 1.2 %collective-permute-done.14 = f32[3,40]{1,0:T(4,128)S(1)} collective-permute-done((f32[3,40]{1,0:T(4,128)S(1)}, f32[3,40]{1,0:T(4,128)S(1)}, u32[]{:S(2)}, u32[]{:S(2)}) %collective-permute-start.14) | collective-permute-done | bytes 512 | tf_op jit(solution)/shard_map/ppermute | solution.py:105
  70.4 1.5 %collective-permute-start.16 = (f32[160]{0:T(256)S(1)}, f32[160]{0:T(256)S(1)}, u32[]{:S(2)}, u32[]{:S(2)}) collective-permute-start(f32[160]{0:T(256)S(1)} %add_dynamic-update-slice_fusion), channel_id=1, source_target_pairs={{0,2},{1,3},{2,0},{3,1},{4,6},{5,7},{6,4},{7,5},{8,10},{9,11},{10,... | collective-permute-start | bytes 1928 | tf_op jit(solution)/shard_map/ppermute | solution.py:117
  72.7 1.3 %collective-permute-done.16 = f32[160]{0:T(256)S(1)} collective-permute-done((f32[160]{0:T(256)S(1)}, f32[160]{0:T(256)S(1)}, u32[]{:S(2)}, u32[]{:S(2)}) %collective-permute-start.16) | collective-permute-done | bytes 672 | tf_op jit(solution)/shard_map/ppermute | solution.py:117
  (71 shorter events, 12.6 us)
Async XLA Ops:
  0.6 8.6 %copy-start = (s32[256]{0:T(256)S(1)}, s32[256]{0:T(256)}, u32[]{:S(2)}) copy-start(s32[256]{0:T(256)} %param.18) | copy-start | bytes 3076
  0.6 9.5 %collective-permute-start = (bf16[32,4096]{1,0:T(8,128)(2,1)}, bf16[32,4096]{1,0:T(8,128)(2,1)S(1)}, u32[]{:S(2)}, u32[]{:S(2)}) collective-permute-start(bf16[32,4096]{1,0:T(8,128)(2,1)} %param.15), channel_id=1, source_target_pairs={{0,8},{8,16},{16,24},{24,28},{28,20},{20,12},{12,4},{4,0},{1,9},{9... | collective-permute-start | bytes 786440 | tf_op jit(solution)/shard_map/ppermute | solution.py:41
  3.7 8.4 %collective-permute-start.4 = (bf16[32,4096]{1,0:T(8,128)(2,1)}, bf16[32,4096]{1,0:T(8,128)(2,1)S(1)}, u32[]{:S(2)}, u32[]{:S(2)}) collective-permute-start(bf16[32,4096]{1,0:T(8,128)(2,1)} %param.15), channel_id=1, source_target_pairs={{8,0},{16,8},{24,16},{28,24},{20,28},{12,20},{4,12},{0,4},{9,1},{1... | collective-permute-start | bytes 786440 | tf_op jit(solution)/shard_map/ppermute | solution.py:44
  10.2 7.7 %collective-permute-start.1 = (bf16[32,4096]{1,0:T(8,128)(2,1)S(1)}, bf16[32,4096]{1,0:T(8,128)(2,1)S(1)}, u32[]{:S(2)}, u32[]{:S(2)}) collective-permute-start(bf16[32,4096]{1,0:T(8,128)(2,1)S(1)} %collective-permute-done), channel_id=1, source_target_pairs={{0,8},{8,16},{16,24},{24,28},{28,20},{20,12},{12,4},{4,0},{1,9},{9... | collective-permute-start | bytes 786440 | tf_op jit(solution)/shard_map/ppermute | solution.py:41
  12.2 7.5 %collective-permute-start.5 = (bf16[32,4096]{1,0:T(8,128)(2,1)S(1)}, bf16[32,4096]{1,0:T(8,128)(2,1)S(1)}, u32[]{:S(2)}, u32[]{:S(2)}) collective-permute-start(bf16[32,4096]{1,0:T(8,128)(2,1)S(1)} %collective-permute-done.4), channel_id=1, source_target_pairs={{8,0},{16,8},{24,16},{28,24},{20,28},{12,20},{4,12},{0,4},{9,1},{1... | collective-permute-start | bytes 786440 | tf_op jit(solution)/shard_map/ppermute | solution.py:44
  17.9 6.9 %collective-permute-start.2 = (bf16[32,4096]{1,0:T(8,128)(2,1)S(1)}, bf16[32,4096]{1,0:T(8,128)(2,1)S(1)}, u32[]{:S(2)}, u32[]{:S(2)}) collective-permute-start(bf16[32,4096]{1,0:T(8,128)(2,1)S(1)} %collective-permute-done.1), channel_id=1, source_target_pairs={{0,8},{8,16},{16,24},{24,28},{28,20},{20,12},{12,4},{4,0},{1,9},{9... | collective-permute-start | bytes 786440 | tf_op jit(solution)/shard_map/ppermute | solution.py:41
  19.7 11.5 %collective-permute-start.6 = (bf16[32,4096]{1,0:T(8,128)(2,1)S(1)}, bf16[32,4096]{1,0:T(8,128)(2,1)S(1)}, u32[]{:S(2)}, u32[]{:S(2)}) collective-permute-start(bf16[32,4096]{1,0:T(8,128)(2,1)S(1)} %collective-permute-done.5), channel_id=1, source_target_pairs={{8,0},{16,8},{24,16},{28,24},{20,28},{12,20},{4,12},{0,4},{9,1},{1... | collective-permute-start | bytes 786440 | tf_op jit(solution)/shard_map/ppermute | solution.py:44
  24.8 6.4 %collective-permute-start.3 = (bf16[32,4096]{1,0:T(8,128)(2,1)S(1)}, bf16[32,4096]{1,0:T(8,128)(2,1)S(1)}, u32[]{:S(2)}, u32[]{:S(2)}) collective-permute-start(bf16[32,4096]{1,0:T(8,128)(2,1)S(1)} %collective-permute-done.2), channel_id=1, source_target_pairs={{0,8},{8,16},{16,24},{24,28},{28,20},{20,12},{12,4},{4,0},{1,9},{9... | collective-permute-start | bytes 786440 | tf_op jit(solution)/shard_map/ppermute | solution.py:41
  39.4 7.3 %collective-permute-start.7 = (f32[80,1024]{1,0:T(8,128)S(1)}, f32[80,1024]{1,0:T(8,128)S(1)}, u32[]{:S(2)}, u32[]{:S(2)}) collective-permute-start(f32[80,1024]{1,0:T(8,128)S(1)} %select_bitcast_fusion.1), channel_id=1, source_target_pairs={{0,1},{1,0},{2,3},{3,2},{4,5},{5,4},{6,7},{7,6},{8,9},{9,8},{10,11... | collective-permute-start | bytes 983048 | tf_op jit(solution)/shard_map/ppermute | solution.py:84
  39.5 7.2 %copy-start.3 = (f32[160,1024]{1,0:T(8,128)S(1)}, f32[160,1024]{1,0:T(8,128)}, u32[]{:S(2)}) copy-start(f32[160,1024]{1,0:T(8,128)} %shard_map.86) | copy-start | bytes 1966084
  45.0 3.2 %copy-start.2 = (f32[160,1024]{1,0:T(8,128)S(1)}, f32[160,1024]{1,0:T(8,128)}, u32[]{:S(2)}) copy-start(f32[160,1024]{1,0:T(8,128)} %shard_map.87) | copy-start | bytes 1966084
  46.1 25.9 %copy-start.1 = (s32[8]{0:T(128)S(1)}, s32[8]{0:T(128)}, u32[]{:S(2)}) copy-start(s32[8]{0:T(128)} %param.17) | copy-start | bytes 100
  46.1 2.1 %collective-permute-start.9 = (f32[80,1024]{1,0:T(8,128)S(1)}, f32[80,1024]{1,0:T(8,128)S(1)}, u32[]{:S(2)}, u32[]{:S(2)}) collective-permute-start(f32[80,1024]{1,0:T(8,128)S(1)} %select_bitcast_fusion), channel_id=1, source_target_pairs={{0,1},{1,0},{2,3},{3,2},{4,5},{5,4},{6,7},{7,6},{8,9},{9,8},{10,11... | collective-permute-start | bytes 983048 | tf_op jit(solution)/shard_map/ppermute | solution.py:84
  46.7 28.0 %copy-start.4 = (f32[32]{0:T(128)S(1)}, f32[32]{0:T(128)}, u32[]{:S(2)}) copy-start(f32[32]{0:T(128)} %param.19) | copy-start | bytes 388
  46.8 7.1 %collective-permute-start.8 = (f32[40,1024]{1,0:T(8,128)S(1)}, f32[40,1024]{1,0:T(8,128)S(1)}, u32[]{:S(2)}, u32[]{:S(2)}) collective-permute-start(f32[40,1024]{1,0:T(8,128)S(1)} %select_bitcast_fusion.3), channel_id=1, source_target_pairs={{0,2},{1,3},{2,0},{3,1},{4,6},{5,7},{6,4},{7,5},{8,10},{9,11},{10,... | collective-permute-start | bytes 491528 | tf_op jit(solution)/shard_map/ppermute | solution.py:84
  48.3 8.2 %collective-permute-start.10 = (f32[40,1024]{1,0:T(8,128)S(1)}, f32[40,1024]{1,0:T(8,128)S(1)}, u32[]{:S(2)}, u32[]{:S(2)}) collective-permute-start(f32[40,1024]{1,0:T(8,128)S(1)} %select_bitcast_fusion.2), channel_id=1, source_target_pairs={{0,2},{1,3},{2,0},{3,1},{4,6},{5,7},{6,4},{7,5},{8,10},{9,11},{10,... | collective-permute-start | bytes 491528 | tf_op jit(solution)/shard_map/ppermute | solution.py:84
  56.9 3.7 %collective-permute-start.11 = (f32[3,40]{1,0:T(4,128)S(1)}, f32[3,40]{1,0:T(4,128)S(1)}, u32[]{:S(2)}, u32[]{:S(2)}) collective-permute-start(f32[3,40]{1,0:T(4,128)S(1)} %pad_maximum_fusion), channel_id=1, source_target_pairs={{0,4},{4,0},{8,12},{12,8},{16,20},{20,16},{24,28},{28,24},{1,5},{5... | collective-permute-start | bytes 1448 | tf_op jit(solution)/shard_map/ppermute | solution.py:101
  58.3 3.6 %collective-permute-start.12 = (f32[3,40]{1,0:T(4,128)S(1)}, f32[3,40]{1,0:T(4,128)S(1)}, u32[]{:S(2)}, u32[]{:S(2)}) collective-permute-start(f32[3,40]{1,0:T(4,128)S(1)} %pad_maximum_fusion), channel_id=1, source_target_pairs={{0,8},{4,12},{8,0},{12,4},{16,24},{20,28},{24,16},{28,20},{1,9},{5... | collective-permute-start | bytes 1448 | tf_op jit(solution)/shard_map/ppermute | solution.py:101
  59.9 4.5 %collective-permute-start.13 = (f32[3,40]{1,0:T(4,128)S(1)}, f32[3,40]{1,0:T(4,128)S(1)}, u32[]{:S(2)}, u32[]{:S(2)}) collective-permute-start(f32[3,40]{1,0:T(4,128)S(1)} %pad_maximum_fusion), channel_id=1, source_target_pairs={{0,12},{4,8},{8,4},{12,0},{16,28},{20,24},{24,20},{28,16},{1,13},{... | collective-permute-start | bytes 1448 | tf_op jit(solution)/shard_map/ppermute | solution.py:101
  64.4 4.5 %collective-permute-start.14 = (f32[3,40]{1,0:T(4,128)S(1)}, f32[3,40]{1,0:T(4,128)S(1)}, u32[]{:S(2)}, u32[]{:S(2)}) collective-permute-start(f32[3,40]{1,0:T(4,128)S(1)} %pad_maximum_fusion.1), channel_id=1, source_target_pairs={{0,16},{4,20},{8,24},{12,28},{16,0},{20,4},{24,8},{28,12},{1,17},{... | collective-permute-start | bytes 1448 | tf_op jit(solution)/shard_map/ppermute | solution.py:105
  69.1 1.2 %collective-permute-start.15 = (f32[160]{0:T(256)S(1)}, f32[160]{0:T(256)S(1)}, u32[]{:S(2)}, u32[]{:S(2)}) collective-permute-start(f32[160]{0:T(256)S(1)} %get-tuple-element.34), channel_id=1, source_target_pairs={{0,1},{1,0},{2,3},{3,2},{4,5},{5,4},{6,7},{7,6},{8,9},{9,8},{10,11... | collective-permute-start | bytes 1928 | tf_op jit(solution)/shard_map/ppermute | solution.py:117
  70.4 3.6 %collective-permute-start.16 = (f32[160]{0:T(256)S(1)}, f32[160]{0:T(256)S(1)}, u32[]{:S(2)}, u32[]{:S(2)}) collective-permute-start(f32[160]{0:T(256)S(1)} %add_dynamic-update-slice_fusion), channel_id=1, source_target_pairs={{0,2},{1,3},{2,0},{3,1},{4,6},{5,7},{6,4},{7,5},{8,10},{9,11},{10,... | collective-permute-start | bytes 1928 | tf_op jit(solution)/shard_map/ppermute | solution.py:117

commit v12 on v5

--- a/solution.py
+++ b/solution.py
@@ -48,6 +48,7 @@
     owner = rows // count
     hit = owner[None, :] == jnp.arange(size, dtype=jnp.int32)[:, None]
     where = jnp.sum(jnp.where(hit, slot_of[:, None], 0), axis=0) * count + rows % count
+    where = jnp.where(rows < 0, -1, where)
     choose = lax.broadcasted_iota(jnp.int32, (stacked.shape[0], where.shape[0]), 0) == where[None, :]
     picked = lax.dot_general(choose.astype(stacked.dtype), stacked, (((0,), (0,)), ((), ())), preferred_element_type=jnp.float32)
     return picked.astype(stacked.dtype)
@@ -121,16 +122,21 @@
         batch_of = jnp.sum(batch_hit.astype(jnp.int32), axis=0)
         in_batch = packed - jnp.sum(jnp.where(batch_of[None, :] == jnp.arange(MB, dtype=jnp.int32)[:, None], starts[:, None], 0), axis=0)
         live_rows = batch_of * slot_count + in_batch
-        full_rows = ring_gather(hidden, ring, live_rows)
+        is_own = (live_rows >= lax.axis_index("dp") * row_count) & (live_rows < lax.axis_index("dp") * row_count + row_count)
+        full_rows = ring_gather(hidden, ring, jnp.where(is_own, -1, live_rows))
         share = live_count // vocab_size
         row_targets = lax.dynamic_slice_in_dim(live_rows, live_count - share, share)
         row_targets = jnp.take(targets, row_targets)
+        own_first = lax.axis_index("dp") * row_count
+        own_partial = jnp.dot(hidden, head_weight, preferred_element_type=jnp.float32)
+        own_pick = (live_rows - own_first)[:, None] == lax.broadcasted_iota(jnp.int32, (live_count, row_count), 1)
+        own_spread = jnp.dot(own_pick.astype(jnp.float32), own_partial, precision=lax.Precision.HIGHEST, preferred_element_type=jnp.float32)
         pieces = 2 if tile_width % 256 == 0 else 1
         width = tile_width // pieces
         parts = []
         for piece in range(pieces):
             partial = jnp.dot(full_rows, head_weight[:, piece * width:(piece + 1) * width], preferred_element_type=jnp.float32)
-            logits = halving_scatter(partial, vocab_size)
+            logits = halving_scatter(partial + own_spread[:, piece * width:(piece + 1) * width], vocab_size)
             highest = jnp.max(logits, axis=1)
             exp_total = jnp.sum(jnp.exp(logits - highest[:, None]), axis=1)
             columns = col_start + piece * width + lax.broadcasted_iota(jnp.int32, logits.shape, 1)

time: 70.2 us -> 80.9 us (1.15)
  matrix products: 7.3 us -> 20.1 us
  local copies, waits for them, and re-layouts: 7.65 us -> 5.39 us
    dot_general x0 -> x2, matrix products: none -> 9.56 us  [the longest x1 8.85 us: on_device(): jnp.dot(hidden, head_weight, preferred_element_type=jnp.float32)]
    dot_general x2, matrix products: 6.75 us -> 9.96 us  [on_device(): jnp.dot(full_rows, head_weight[:, piece * width:(piece + 1) * width], pre...]
    unnamed x15 -> x13, local copies, waits for them, and re-layouts: 3.43 us -> 1.16 us
  transfers between devices with their start and end apart: 16 -> 16, of which waited for: 11 -> 10; matrix products, arithmetic and copies ran while one was open for 14% -> 28% of each run, Pallas kernels for 0% -> 0%
where the time goes in v12:
time: 80.9 us; the launch traced here: 80.6 us
  waiting for transfers between devices  30.7 us (38%)
  matrix products  20.1 us (25%)
  starting transfers between devices  18.7 us (23%)
  local copies, waits for them, and re-layouts  5.39 us (7%)
  other arithmetic  4.8 us (6%)
  between operations  0.91 us (1%)
    ppermute x4, waiting for transfers between devices, ring_gather(): ahead = lax.ppermute(ahead, 'dp', fwd)  15.4 us
    dot_general x2, matrix products, on_device(): jnp.dot(full_rows, head_weight[:, piece * width:(piece + 1) * width], pre...  9.96 us
    dot_general x1, matrix products, on_device(): jnp.dot(hidden, head_weight, preferred_element_type=jnp.float32)  8.85 us
    ppermute x4, starting transfers between devices, ring_gather(): ahead = lax.ppermute(ahead, 'dp', fwd)  8.29 us
    ppermute x4, waiting for transfers between devices, halving_scatter(): lax.ppermute(partial[:half], 'vocab', [(i, i ^ bit) for i in range(size)])  6.97 us
    ppermute x3, waiting for transfers between devices, merge_stats(): other = lax.ppermute(stats, 'dp', [(i, i ^ bit) for i in range(size)])  5.71 us
    ppermute x3, starting transfers between devices, merge_stats(): other = lax.ppermute(stats, 'dp', [(i, i ^ bit) for i in range(size)])  5.42 us
    ppermute x4, starting transfers between devices, halving_scatter(): lax.ppermute(partial[:half], 'vocab', [(i, i ^ bit) for i in range(size)])  3.16 us
  transfers between devices with their start and end apart: 16, of which 10 were waited for; matrix products, arithmetic and copies ran while one was open for 28% of the time, Pallas kernels for 0%

profile of v12, /device:TPU:0, one launch (start us, length us, event | category | flops | bytes accessed | tf_op | source)
XLA Modules:
  0.0 80.6 jit_solution(9548664634504525698)
XLA Ops:
  0.6 3.1 %collective-permute-start = (bf16[32,4096]{1,0:T(8,128)(2,1)}, bf16[32,4096]{1,0:T(8,128)(2,1)S(1)}, u32[]{:S(2)}, u32[]{:S(2)}) collective-permute-start(bf16[32,4096]{1,0:T(8,128)(2,1)} %param.9), channel_id=1, source_target_pairs={{0,8},{8,16},{16,24},{24,28},{28,20},{20,12},{12,4},{4,0},{1,9},{9... | collective-permute-start | bytes 786440 | tf_op jit(solution)/shard_map/ppermute | solution.py:39
  6.6 1.2 %dynamic_slice.7 = s32[1]{0:T(128)} dynamic-slice(s32[8]{0:T(128)} %constant.212.clone, s32[]{:T(128)S(6)} %select_n.228), dynamic_slice_sizes={1} | dynamic-slice | bytes 12 | tf_op jit(solution)/shard_map/dynamic_slice | solution.py:46
  7.9 1.3 %and_select_fusion.1 = s32[8]{0:T(128)S(1)} fusion(s32[8]{0:T(128)} %constant.213, s32[]{:T(128)} %bitcast.2), kind=kLoop, calls=%fused_computation.59 | loop fusion | flops 96 | bytes 68 | tf_op jit(solution)/shard_map/jit(remainder)/select_n | solution.py:47
  9.3 8.8 %fusion.59 = f32[32,2048]{1,0:T(8,128)S(1)} fusion(bf16[32,4096]{1,0:T(8,128)(2,1)} %param.9, bf16[4096,2048]{1,0:T(8,128)(2,1)} %param.10), kind=kOutput, calls=%fused_computation.157 | convolution fusion | flops 536870912 | bytes 17301504 | tf_op jit(solution)/shard_map/dot_general | solution.py:131
  19.7 2.0 %collective-permute-start.1 = (bf16[32,4096]{1,0:T(8,128)(2,1)S(1)}, bf16[32,4096]{1,0:T(8,128)(2,1)S(1)}, u32[]{:S(2)}, u32[]{:S(2)}) collective-permute-start(bf16[32,4096]{1,0:T(8,128)(2,1)S(1)} %collective-permute-done), channel_id=1, source_target_pairs={{0,8},{8,16},{16,24},{24,28},{28,20},{20,12},{12,4},{4,0},{1,9},{9... | collective-permute-start | bytes 786440 | tf_op jit(solution)/shard_map/ppermute | solution.py:39
  21.8 5.7 %collective-permute-done.1 = bf16[32,4096]{1,0:T(8,128)(2,1)S(1)} collective-permute-done((bf16[32,4096]{1,0:T(8,128)(2,1)S(1)}, bf16[32,4096]{1,0:T(8,128)(2,1)S(1)}, u32[]{:S(2)}, u32[]{:S(2)}) %collective-permute-start.1) | collective-permute-done | bytes 262176 | tf_op jit(solution)/shard_map/ppermute | solution.py:39
  27.5 1.7 %collective-permute-start.2 = (bf16[32,4096]{1,0:T(8,128)(2,1)S(1)}, bf16[32,4096]{1,0:T(8,128)(2,1)S(1)}, u32[]{:S(2)}, u32[]{:S(2)}) collective-permute-start(bf16[32,4096]{1,0:T(8,128)(2,1)S(1)} %collective-permute-done.1), channel_id=1, source_target_pairs={{0,8},{8,16},{16,24},{24,28},{28,20},{20,12},{12,4},{4,0},{1,9},{9... | collective-permute-start | bytes 786440 | tf_op jit(solution)/shard_map/ppermute | solution.py:39
  29.6 4.8 %collective-permute-done.2 = bf16[32,4096]{1,0:T(8,128)(2,1)S(1)} collective-permute-done((bf16[32,4096]{1,0:T(8,128)(2,1)S(1)}, bf16[32,4096]{1,0:T(8,128)(2,1)S(1)}, u32[]{:S(2)}, u32[]{:S(2)}) %collective-permute-start.2) | collective-permute-done | bytes 262176 | tf_op jit(solution)/shard_map/ppermute | solution.py:39
  34.4 1.4 %collective-permute-start.3 = (bf16[32,4096]{1,0:T(8,128)(2,1)S(1)}, bf16[32,4096]{1,0:T(8,128)(2,1)S(1)}, u32[]{:S(2)}, u32[]{:S(2)}) collective-permute-start(bf16[32,4096]{1,0:T(8,128)(2,1)S(1)} %collective-permute-done.2), channel_id=1, source_target_pairs={{0,8},{8,16},{16,24},{24,28},{28,20},{20,12},{12,4},{4,0},{1,9},{9... | collective-permute-start | bytes 786440 | tf_op jit(solution)/shard_map/ppermute | solution.py:39
  35.8 4.9 %collective-permute-done.3 = bf16[32,4096]{1,0:T(8,128)(2,1)S(1)} collective-permute-done((bf16[32,4096]{1,0:T(8,128)(2,1)S(1)}, bf16[32,4096]{1,0:T(8,128)(2,1)S(1)}, u32[]{:S(2)}, u32[]{:S(2)}) %collective-permute-start.3) | collective-permute-done | bytes 262176 | tf_op jit(solution)/shard_map/ppermute | solution.py:39
  41.4 5.0 %fusion.4 = f32[160,1024]{1,0:T(8,128)S(1)} fusion(bf16[160,4096]{1,0:T(8,128)(2,1)S(1)} %convolution_convert_fusion, bf16[4096,2048]{1,0:T(8,128)(2,1)} %param.10, f32[160,2048]{1,0:T(8,128)S(1)} %fusion.11), kind=kOutput, calls=%fused_computation.9 | convolution fusion | flops 1342341120 | bytes 11010048 | tf_op jit(solution)/shard_map/dot_general | solution.py:138
  46.5 5.0 %fusion.7 = f32[160,1024]{1,0:T(8,128)S(1)} fusion(bf16[160,4096]{1,0:T(8,128)(2,1)S(1)} %convolution_convert_fusion, bf16[4096,2048]{1,0:T(8,128)(2,1)} %param.10, f32[160,2048]{1,0:T(8,128)S(1)} %fusion.11), kind=kOutput, calls=%fused_computation.10 | convolution fusion | flops 1342341120 | bytes 11010048 | tf_op jit(solution)/shard_map/dot_general | solution.py:138
  52.3 1.4 %collective-permute-start.8 = (f32[40,1024]{1,0:T(8,128)S(1)}, f32[40,1024]{1,0:T(8,128)S(1)}, u32[]{:S(2)}, u32[]{:S(2)}) collective-permute-start(f32[40,1024]{1,0:T(8,128)S(1)} %slice.99), channel_id=1, source_target_pairs={{0,2},{1,3},{2,0},{3,1},{4,6},{5,7},{6,4},{7,5},{8,10},{9,11},{10,... | collective-permute-start | bytes 491528 | tf_op jit(solution)/shard_map/ppermute | solution.py:61
  54.9 4.5 %collective-permute-done.8 = f32[40,1024]{1,0:T(8,128)S(1)} collective-permute-done((f32[40,1024]{1,0:T(8,128)S(1)}, f32[40,1024]{1,0:T(8,128)S(1)}, u32[]{:S(2)}, u32[]{:S(2)}) %collective-permute-start.8) | collective-permute-done | bytes 163872 | tf_op jit(solution)/shard_map/ppermute | solution.py:61
  59.5 2.4 %collective-permute-done.10 = f32[40,1024]{1,0:T(8,128)S(1)} collective-permute-done((f32[40,1024]{1,0:T(8,128)S(1)}, f32[40,1024]{1,0:T(8,128)S(1)}, u32[]{:S(2)}, u32[]{:S(2)}) %collective-permute-start.10) | collective-permute-done | bytes 163872 | tf_op jit(solution)/shard_map/ppermute | solution.py:61
  62.4 1.4 %collective-permute-start.11 = (f32[3,40]{1,0:T(4,128)S(1)}, f32[3,40]{1,0:T(4,128)S(1)}, u32[]{:S(2)}, u32[]{:S(2)}) collective-permute-start(f32[3,40]{1,0:T(4,128)S(1)} %pad_maximum_fusion), channel_id=1, source_target_pairs={{0,4},{4,0},{8,12},{12,8},{16,20},{20,16},{24,28},{28,24},{1,5},{5... | collective-permute-start | bytes 1448 | tf_op jit(solution)/shard_map/ppermute | solution.py:87
  63.8 2.2 %collective-permute-done.11 = f32[3,40]{1,0:T(4,128)S(1)} collective-permute-done((f32[3,40]{1,0:T(4,128)S(1)}, f32[3,40]{1,0:T(4,128)S(1)}, u32[]{:S(2)}, u32[]{:S(2)}) %collective-permute-start.11) | collective-permute-done | bytes 512 | tf_op jit(solution)/shard_map/ppermute | solution.py:87
  66.1 1.5 %collective-permute-start.12 = (f32[3,40]{1,0:T(4,128)S(1)}, f32[3,40]{1,0:T(4,128)S(1)}, u32[]{:S(2)}, u32[]{:S(2)}) collective-permute-start(f32[3,40]{1,0:T(4,128)S(1)} %pad_maximum_fusion.1), channel_id=1, source_target_pairs={{0,8},{4,12},{8,0},{12,4},{16,24},{20,28},{24,16},{28,20},{1,9},{5... | collective-permute-start | bytes 1448 | tf_op jit(solution)/shard_map/ppermute | solution.py:87
  67.6 2.1 %collective-permute-done.12 = f32[3,40]{1,0:T(4,128)S(1)} collective-permute-done((f32[3,40]{1,0:T(4,128)S(1)}, f32[3,40]{1,0:T(4,128)S(1)}, u32[]{:S(2)}, u32[]{:S(2)}) %collective-permute-start.12) | collective-permute-done | bytes 512 | tf_op jit(solution)/shard_map/ppermute | solution.py:87
  69.7 2.5 %collective-permute-start.13 = (f32[3,40]{1,0:T(4,128)S(1)}, f32[3,40]{1,0:T(4,128)S(1)}, u32[]{:S(2)}, u32[]{:S(2)}) collective-permute-start(f32[3,40]{1,0:T(4,128)S(1)} %pad_maximum_fusion.2), channel_id=1, source_target_pairs={{0,16},{4,20},{8,24},{12,28},{16,0},{20,4},{24,8},{28,12},{1,17},{... | collective-permute-start | bytes 1448 | tf_op jit(solution)/shard_map/ppermute | solution.py:87
  73.0 1.3 %collective-permute-done.13 = f32[3,40]{1,0:T(4,128)S(1)} collective-permute-done((f32[3,40]{1,0:T(4,128)S(1)}, f32[3,40]{1,0:T(4,128)S(1)}, u32[]{:S(2)}, u32[]{:S(2)}) %collective-permute-start.13) | collective-permute-done | bytes 512 | tf_op jit(solution)/shard_map/ppermute | solution.py:87
  74.4 1.1 %collective-permute-done.14 = f32[160]{0:T(256)S(1)} collective-permute-done((f32[160]{0:T(256)S(1)}, f32[160]{0:T(256)S(1)}, u32[]{:S(2)}, u32[]{:S(2)}) %collective-permute-start.14) | collective-permute-done | bytes 672 | tf_op jit(solution)/shard_map/ppermute | solution.py:102
  75.7 1.4 %collective-permute-start.15 = (f32[160]{0:T(256)S(1)}, f32[160]{0:T(256)S(1)}, u32[]{:S(2)}, u32[]{:S(2)}) collective-permute-start(f32[160]{0:T(256)S(1)} %add_dynamic-update-slice_fusion), channel_id=1, source_target_pairs={{0,2},{1,3},{2,0},{3,1},{4,6},{5,7},{6,4},{7,5},{8,10},{9,11},{10,... | collective-permute-start | bytes 1928 | tf_op jit(solution)/shard_map/ppermute | solution.py:102
  77.8 1.5 %collective-permute-done.15 = f32[160]{0:T(256)S(1)} collective-permute-done((f32[160]{0:T(256)S(1)}, f32[160]{0:T(256)S(1)}, u32[]{:S(2)}, u32[]{:S(2)}) %collective-permute-start.15) | collective-permute-done | bytes 672 | tf_op jit(solution)/shard_map/ppermute | solution.py:102
  (71 shorter events, 11.1 us)
Async XLA Ops:
  0.6 17.5 %copy-start = (s32[256]{0:T(256)S(1)}, s32[256]{0:T(256)}, u32[]{:S(2)}) copy-start(s32[256]{0:T(256)} %param.12) | copy-start | bytes 3076
  0.6 19.0 %collective-permute-start = (bf16[32,4096]{1,0:T(8,128)(2,1)}, bf16[32,4096]{1,0:T(8,128)(2,1)S(1)}, u32[]{:S(2)}, u32[]{:S(2)}) collective-permute-start(bf16[32,4096]{1,0:T(8,128)(2,1)} %param.9), channel_id=1, source_target_pairs={{0,8},{8,16},{16,24},{24,28},{28,20},{20,12},{12,4},{4,0},{1,9},{9... | collective-permute-start | bytes 786440 | tf_op jit(solution)/shard_map/ppermute | solution.py:39
  3.7 18.0 %collective-permute-start.4 = (bf16[32,4096]{1,0:T(8,128)(2,1)}, bf16[32,4096]{1,0:T(8,128)(2,1)S(1)}, u32[]{:S(2)}, u32[]{:S(2)}) collective-permute-start(bf16[32,4096]{1,0:T(8,128)(2,1)} %param.9), channel_id=1, source_target_pairs={{8,0},{16,8},{24,16},{28,24},{20,28},{12,20},{4,12},{0,4},{9,1},{1... | collective-permute-start | bytes 786440 | tf_op jit(solution)/shard_map/ppermute | solution.py:42
  19.7 7.8 %collective-permute-start.1 = (bf16[32,4096]{1,0:T(8,128)(2,1)S(1)}, bf16[32,4096]{1,0:T(8,128)(2,1)S(1)}, u32[]{:S(2)}, u32[]{:S(2)}) collective-permute-start(bf16[32,4096]{1,0:T(8,128)(2,1)S(1)} %collective-permute-done), channel_id=1, source_target_pairs={{0,8},{8,16},{16,24},{24,28},{28,20},{20,12},{12,4},{4,0},{1,9},{9... | collective-permute-start | bytes 786440 | tf_op jit(solution)/shard_map/ppermute | solution.py:39
  21.7 7.5 %collective-permute-start.5 = (bf16[32,4096]{1,0:T(8,128)(2,1)S(1)}, bf16[32,4096]{1,0:T(8,128)(2,1)S(1)}, u32[]{:S(2)}, u32[]{:S(2)}) collective-permute-start(bf16[32,4096]{1,0:T(8,128)(2,1)S(1)} %collective-permute-done.4), channel_id=1, source_target_pairs={{8,0},{16,8},{24,16},{28,24},{20,28},{12,20},{4,12},{0,4},{9,1},{1... | collective-permute-start | bytes 786440 | tf_op jit(solution)/shard_map/ppermute | solution.py:42
  27.5 6.9 %collective-permute-start.2 = (bf16[32,4096]{1,0:T(8,128)(2,1)S(1)}, bf16[32,4096]{1,0:T(8,128)(2,1)S(1)}, u32[]{:S(2)}, u32[]{:S(2)}) collective-permute-start(bf16[32,4096]{1,0:T(8,128)(2,1)S(1)} %collective-permute-done.1), channel_id=1, source_target_pairs={{0,8},{8,16},{16,24},{24,28},{28,20},{20,12},{12,4},{4,0},{1,9},{9... | collective-permute-start | bytes 786440 | tf_op jit(solution)/shard_map/ppermute | solution.py:39
  29.2 11.6 %collective-permute-start.6 = (bf16[32,4096]{1,0:T(8,128)(2,1)S(1)}, bf16[32,4096]{1,0:T(8,128)(2,1)S(1)}, u32[]{:S(2)}, u32[]{:S(2)}) collective-permute-start(bf16[32,4096]{1,0:T(8,128)(2,1)S(1)} %collective-permute-done.5), channel_id=1, source_target_pairs={{8,0},{16,8},{24,16},{28,24},{20,28},{12,20},{4,12},{0,4},{9,1},{1... | collective-permute-start | bytes 786440 | tf_op jit(solution)/shard_map/ppermute | solution.py:42
  34.4 6.4 %collective-permute-start.3 = (bf16[32,4096]{1,0:T(8,128)(2,1)S(1)}, bf16[32,4096]{1,0:T(8,128)(2,1)S(1)}, u32[]{:S(2)}, u32[]{:S(2)}) collective-permute-start(bf16[32,4096]{1,0:T(8,128)(2,1)S(1)} %collective-permute-done.2), channel_id=1, source_target_pairs={{0,8},{8,16},{16,24},{24,28},{28,20},{20,12},{12,4},{4,0},{1,9},{9... | collective-permute-start | bytes 786440 | tf_op jit(solution)/shard_map/ppermute | solution.py:39
  46.4 5.7 %collective-permute-start.7 = (f32[80,1024]{1,0:T(8,128)S(1)}, f32[80,1024]{1,0:T(8,128)S(1)}, u32[]{:S(2)}, u32[]{:S(2)}) collective-permute-start(f32[80,1024]{1,0:T(8,128)S(1)} %slice.97), channel_id=1, source_target_pairs={{0,1},{1,0},{2,3},{3,2},{4,5},{5,4},{6,7},{7,6},{8,9},{9,8},{10,11... | collective-permute-start | bytes 983048 | tf_op jit(solution)/shard_map/ppermute | solution.py:61
  51.5 2.2 %collective-permute-start.9 = (f32[80,1024]{1,0:T(8,128)S(1)}, f32[80,1024]{1,0:T(8,128)S(1)}, u32[]{:S(2)}, u32[]{:S(2)}) collective-permute-start(f32[80,1024]{1,0:T(8,128)S(1)} %slice.102), channel_id=1, source_target_pairs={{0,1},{1,0},{2,3},{3,2},{4,5},{5,4},{6,7},{7,6},{8,9},{9,8},{10,11... | collective-permute-start | bytes 983048 | tf_op jit(solution)/shard_map/ppermute | solution.py:61
  52.2 24.9 %copy-start.1 = (s32[8]{0:T(128)S(1)}, s32[8]{0:T(128)}, u32[]{:S(2)}) copy-start(s32[8]{0:T(128)} %param.11) | copy-start | bytes 100
  52.2 27.8 %copy-start.2 = (f32[32]{0:T(128)S(1)}, f32[32]{0:T(128)}, u32[]{:S(2)}) copy-start(f32[32]{0:T(128)} %param.13) | copy-start | bytes 388
  52.3 7.1 %collective-permute-start.8 = (f32[40,1024]{1,0:T(8,128)S(1)}, f32[40,1024]{1,0:T(8,128)S(1)}, u32[]{:S(2)}, u32[]{:S(2)}) collective-permute-start(f32[40,1024]{1,0:T(8,128)S(1)} %slice.99), channel_id=1, source_target_pairs={{0,2},{1,3},{2,0},{3,1},{4,6},{5,7},{6,4},{7,5},{8,10},{9,11},{10,... | collective-permute-start | bytes 491528 | tf_op jit(solution)/shard_map/ppermute | solution.py:61
  53.8 8.2 %collective-permute-start.10 = (f32[40,1024]{1,0:T(8,128)S(1)}, f32[40,1024]{1,0:T(8,128)S(1)}, u32[]{:S(2)}, u32[]{:S(2)}) collective-permute-start(f32[40,1024]{1,0:T(8,128)S(1)} %slice.104), channel_id=1, source_target_pairs={{0,2},{1,3},{2,0},{3,1},{4,6},{5,7},{6,4},{7,5},{8,10},{9,11},{10,... | collective-permute-start | bytes 491528 | tf_op jit(solution)/shard_map/ppermute | solution.py:61
  62.4 3.7 %collective-permute-start.11 = (f32[3,40]{1,0:T(4,128)S(1)}, f32[3,40]{1,0:T(4,128)S(1)}, u32[]{:S(2)}, u32[]{:S(2)}) collective-permute-start(f32[3,40]{1,0:T(4,128)S(1)} %pad_maximum_fusion), channel_id=1, source_target_pairs={{0,4},{4,0},{8,12},{12,8},{16,20},{20,16},{24,28},{28,24},{1,5},{5... | collective-permute-start | bytes 1448 | tf_op jit(solution)/shard_map/ppermute | solution.py:87
  66.1 3.7 %collective-permute-start.12 = (f32[3,40]{1,0:T(4,128)S(1)}, f32[3,40]{1,0:T(4,128)S(1)}, u32[]{:S(2)}, u32[]{:S(2)}) collective-permute-start(f32[3,40]{1,0:T(4,128)S(1)} %pad_maximum_fusion.1), channel_id=1, source_target_pairs={{0,8},{4,12},{8,0},{12,4},{16,24},{20,28},{24,16},{28,20},{1,9},{5... | collective-permute-start | bytes 1448 | tf_op jit(solution)/shard_map/ppermute | solution.py:87
  69.7 4.5 %collective-permute-start.13 = (f32[3,40]{1,0:T(4,128)S(1)}, f32[3,40]{1,0:T(4,128)S(1)}, u32[]{:S(2)}, u32[]{:S(2)}) collective-permute-start(f32[3,40]{1,0:T(4,128)S(1)} %pad_maximum_fusion.2), channel_id=1, source_target_pairs={{0,16},{4,20},{8,24},{12,28},{16,0},{20,4},{24,8},{28,12},{1,17},{... | collective-permute-start | bytes 1448 | tf_op jit(solution)/shard_map/ppermute | solution.py:87
  74.4 1.2 %collective-permute-start.14 = (f32[160]{0:T(256)S(1)}, f32[160]{0:T(256)S(1)}, u32[]{:S(2)}, u32[]{:S(2)}) collective-permute-start(f32[160]{0:T(256)S(1)} %get-tuple-element.9), channel_id=1, source_target_pairs={{0,1},{1,0},{2,3},{3,2},{4,5},{5,4},{6,7},{7,6},{8,9},{9,8},{10,11... | collective-permute-start | bytes 1928 | tf_op jit(solution)/shard_map/ppermute | solution.py:102
  75.7 3.6 %collective-permute-start.15 = (f32[160]{0:T(256)S(1)}, f32[160]{0:T(256)S(1)}, u32[]{:S(2)}, u32[]{:S(2)}) collective-permute-start(f32[160]{0:T(256)S(1)} %add_dynamic-update-slice_fusion), channel_id=1, source_target_pairs={{0,2},{1,3},{2,0},{3,1},{4,6},{5,7},{6,4},{7,5},{8,10},{9,11},{10,... | collective-permute-start | bytes 1928 | tf_op jit(solution)/shard_map/ppermute | solution.py:102

commit v13 on v7

--- a/solution.py
+++ b/solution.py
@@ -77,15 +77,20 @@
 
 
 def merge_stats(stats, size):
+    bits = []
     bit = 1
     while bit < size:
-        if bit * 4 <= size:
-            got = [lax.ppermute(stats, "dp", [(i, i ^ (bit * k)) for i in range(size)]) for k in (1, 2, 3)]
+        bits.append(bit)
+        bit *= 2
+    while bits:
+        if len(bits) >= 2:
+            low, high = bits[-2], bits[-1]
+            bits = bits[:-2]
+            got = [lax.ppermute(stats, "dp", [(i, i ^ flip) for i in range(size)]) for flip in (low, high, low | high)]
             stats = merge_pair(merge_pair(stats, got[0]), merge_pair(got[1], got[2]))
-            bit *= 4
         else:
-            stats = merge_pair(stats, lax.ppermute(stats, "dp", [(i, i ^ bit) for i in range(size)]))
-            bit *= 2
+            stats = merge_pair(stats, lax.ppermute(stats, "dp", [(i, i ^ bits[0]) for i in range(size)]))
+            bits = []
     return stats
 
 

time: 69.1 us -> 69.6 us (level)
  waiting for transfers between devices: 31.5 us -> 32.3 us
    ppermute x4, waiting for transfers between devices: 4.39 us -> 5.19 us  [the longest x3 3.79 us: merge_stats(): lax.ppermute(stats, 'dp', [(i, i ^ flip) for i in range(size)])]
  transfers between devices with their start and end apart: 15 -> 15, of which waited for: 12 -> 11; matrix products, arithmetic and copies ran while one was open for 11% -> 11% of each run, Pallas kernels for 0% -> 0%
where the time goes in v13:
time: 69.6 us; the launch traced here: 69.5 us
  waiting for transfers between devices  32.3 us (46%)
  starting transfers between devices  18.3 us (26%)
  matrix products  7.93 us (11%)
  local copies, waits for them, and re-layouts  5.32 us (8%)
  other arithmetic  4.72 us (7%)
  between operations  0.92 us (1%)
    ppermute x4, waiting for transfers between devices, ring_gather(): ahead = lax.ppermute(ahead, 'dp', fwd)  15.5 us
    ppermute x2, waiting for transfers between devices, halving_scatter(): got = lax.ppermute(send, 'vocab', [(i, i ^ bit) for i in range(size)])  9.12 us
    ppermute x4, starting transfers between devices, ring_gather(): ahead = lax.ppermute(ahead, 'dp', fwd)  8.21 us
    dot_general x1, matrix products, on_device(): jnp.dot(full_rows, head_weight, preferred_element_type=jnp.float32)  7.37 us
    ppermute x3, starting transfers between devices, merge_stats(): lax.ppermute(stats, 'dp', [(i, i ^ flip) for i in range(size)])  4.39 us
    ppermute x3, waiting for transfers between devices, merge_stats(): lax.ppermute(stats, 'dp', [(i, i ^ flip) for i in range(size)])  3.79 us
    ppermute x2, waiting for transfers between devices, doubling_gather(): other = lax.ppermute(out, 'vocab', [(i, i ^ bit) for i in range(size)])  2.47 us
    ppermute x2, starting transfers between devices, halving_scatter(): got = lax.ppermute(send, 'vocab', [(i, i ^ bit) for i in range(size)])  1.81 us
  transfers between devices with their start and end apart: 15, of which 11 were waited for; matrix products, arithmetic and copies ran while one was open for 11% of the time, Pallas kernels for 0%

profile of v13, /device:TPU:0, one launch (start us, length us, event | category | flops | bytes accessed | tf_op | source)
XLA Modules:
  0.0 69.5 jit_solution(3213102800470965799)
XLA Ops:
  0.6 3.1 %collective-permute-start = (bf16[32,4096]{1,0:T(8,128)(2,1)}, bf16[32,4096]{1,0:T(8,128)(2,1)S(1)}, u32[]{:S(2)}, u32[]{:S(2)}) collective-permute-start(bf16[32,4096]{1,0:T(8,128)(2,1)} %param.13), channel_id=1, source_target_pairs={{0,8},{8,16},{16,24},{24,28},{28,20},{20,12},{12,4},{4,0},{1,9},{9... | collective-permute-start | bytes 786440 | tf_op jit(solution)/shard_map/ppermute | solution.py:39
  3.8 1.0 %bitcast_dynamic-update-slice_fusion.7 = bf16[8,32,4096]{2,1,0:T(8,128)(2,1)S(1)} fusion(bf16[32,4096]{1,0:T(8,128)(2,1)} %param.13), kind=kLoop, calls=%fused_computation.18 | loop fusion | bytes 524288
  4.8 0.8 %reduce-window.8 = s32[8,1]{0,1:T(1,128)S(1)} reduce-window(s32[8,1]{0,1:T(1,128)} %bitcast.166, s32[]{:T(128)} %constant.172.clone.1), window={size=8x1 pad=7_0x0_0}, to_apply=%region_0.2 | reduce-window | flops 56 | bytes 68 | tf_op jit(solution)/shard_map/reduce-window.3
  6.5 1.2 %dynamic_slice.7 = s32[1]{0:T(128)} dynamic-slice(s32[8]{0:T(128)} %constant.196.clone, s32[]{:T(128)S(6)} %select_n.127), dynamic_slice_sizes={1} | dynamic-slice | bytes 12 | tf_op jit(solution)/shard_map/dynamic_slice | solution.py:46
  7.7 1.3 %and_select_fusion.1 = s32[8]{0:T(128)S(1)} fusion(s32[8]{0:T(128)} %constant.235, s32[]{:T(128)} %bitcast.2), kind=kLoop, calls=%fused_computation.40 | loop fusion | flops 96 | bytes 68 | tf_op jit(solution)/shard_map/jit(remainder)/select_n | solution.py:47
  9.2 1.0 %collective-permute-done = bf16[32,4096]{1,0:T(8,128)(2,1)S(1)} collective-permute-done((bf16[32,4096]{1,0:T(8,128)(2,1)}, bf16[32,4096]{1,0:T(8,128)(2,1)S(1)}, u32[]{:S(2)}, u32[]{:S(2)}) %collective-permute-start) | collective-permute-done | bytes 262176 | tf_op jit(solution)/shard_map/ppermute | solution.py:39
  10.2 1.8 %collective-permute-start.1 = (bf16[32,4096]{1,0:T(8,128)(2,1)S(1)}, bf16[32,4096]{1,0:T(8,128)(2,1)S(1)}, u32[]{:S(2)}, u32[]{:S(2)}) collective-permute-start(bf16[32,4096]{1,0:T(8,128)(2,1)S(1)} %collective-permute-done), channel_id=1, source_target_pairs={{0,8},{8,16},{16,24},{24,28},{28,20},{20,12},{12,4},{4,0},{1,9},{9... | collective-permute-start | bytes 786440 | tf_op jit(solution)/shard_map/ppermute | solution.py:39
  12.3 5.4 %collective-permute-done.1 = bf16[32,4096]{1,0:T(8,128)(2,1)S(1)} collective-permute-done((bf16[32,4096]{1,0:T(8,128)(2,1)S(1)}, bf16[32,4096]{1,0:T(8,128)(2,1)S(1)}, u32[]{:S(2)}, u32[]{:S(2)}) %collective-permute-start.1) | collective-permute-done | bytes 262176 | tf_op jit(solution)/shard_map/ppermute | solution.py:39
  17.7 1.5 %collective-permute-start.2 = (bf16[32,4096]{1,0:T(8,128)(2,1)S(1)}, bf16[32,4096]{1,0:T(8,128)(2,1)S(1)}, u32[]{:S(2)}, u32[]{:S(2)}) collective-permute-start(bf16[32,4096]{1,0:T(8,128)(2,1)S(1)} %collective-permute-done.1), channel_id=1, source_target_pairs={{0,8},{8,16},{16,24},{24,28},{28,20},{20,12},{12,4},{4,0},{1,9},{9... | collective-permute-start | bytes 786440 | tf_op jit(solution)/shard_map/ppermute | solution.py:39
  19.8 4.5 %collective-permute-done.2 = bf16[32,4096]{1,0:T(8,128)(2,1)S(1)} collective-permute-done((bf16[32,4096]{1,0:T(8,128)(2,1)S(1)}, bf16[32,4096]{1,0:T(8,128)(2,1)S(1)}, u32[]{:S(2)}, u32[]{:S(2)}) %collective-permute-start.2) | collective-permute-done | bytes 262176 | tf_op jit(solution)/shard_map/ppermute | solution.py:39
  24.3 1.7 %collective-permute-start.3 = (bf16[32,4096]{1,0:T(8,128)(2,1)S(1)}, bf16[32,4096]{1,0:T(8,128)(2,1)S(1)}, u32[]{:S(2)}, u32[]{:S(2)}) collective-permute-start(bf16[32,4096]{1,0:T(8,128)(2,1)S(1)} %collective-permute-done.2), channel_id=1, source_target_pairs={{0,8},{8,16},{16,24},{24,28},{28,20},{20,12},{12,4},{4,0},{1,9},{9... | collective-permute-start | bytes 786440 | tf_op jit(solution)/shard_map/ppermute | solution.py:39
  26.0 4.6 %collective-permute-done.3 = bf16[32,4096]{1,0:T(8,128)(2,1)S(1)} collective-permute-done((bf16[32,4096]{1,0:T(8,128)(2,1)S(1)}, bf16[32,4096]{1,0:T(8,128)(2,1)S(1)}, u32[]{:S(2)}, u32[]{:S(2)}) %collective-permute-start.3) | collective-permute-done | bytes 262176 | tf_op jit(solution)/shard_map/ppermute | solution.py:39
  31.3 7.4 %fusion.30 = f32[160,2048]{1,0:T(8,128)S(1)} fusion(bf16[160,4096]{1,0:T(8,128)(2,1)S(1)} %convolution_convert_fusion, bf16[4096,2048]{1,0:T(8,128)(2,1)} %param.14), kind=kOutput, calls=%fused_computation.107 | convolution fusion | flops 2684354560 | bytes 19398656 | tf_op jit(solution)/shard_map/dot_general | solution.py:128
  39.8 1.1 %collective-permute-done.7 = f32[80,2048]{1,0:T(8,128)S(1)} collective-permute-done((f32[80,2048]{1,0:T(8,128)S(1)}, f32[80,2048]{1,0:T(8,128)S(1)}, u32[]{:S(2)}, u32[]{:S(2)}) %collective-permute-start.7) | collective-permute-done | bytes 655392 | tf_op jit(solution)/shard_map/ppermute | solution.py:66
  41.1 1.7 %collective-permute-start.8 = (f32[40,2048]{1,0:T(8,128)S(1)}, f32[40,2048]{1,0:T(8,128)S(1)}, u32[]{:S(2)}, u32[]{:S(2)}) collective-permute-start(f32[40,2048]{1,0:T(8,128)S(1)} %select_bitcast_fusion.1), channel_id=1, source_target_pairs={{0,2},{1,3},{2,0},{3,1},{4,6},{5,7},{6,4},{7,5},{8,10},{9,11},{10,... | collective-permute-start | bytes 983048 | tf_op jit(solution)/shard_map/ppermute | solution.py:66
  42.9 8.0 %collective-permute-done.8 = f32[40,2048]{1,0:T(8,128)S(1)} collective-permute-done((f32[40,2048]{1,0:T(8,128)S(1)}, f32[40,2048]{1,0:T(8,128)S(1)}, u32[]{:S(2)}, u32[]{:S(2)}) %collective-permute-start.8) | collective-permute-done | bytes 327712 | tf_op jit(solution)/shard_map/ppermute | solution.py:66
  51.3 2.8 %collective-permute-start.10 = (f32[3,40]{1,0:T(4,128)S(1)}, f32[3,40]{1,0:T(4,128)S(1)}, u32[]{:S(2)}, u32[]{:S(2)}) collective-permute-start(f32[3,40]{1,0:T(4,128)S(1)} %pad_maximum_fusion), channel_id=1, source_target_pairs={{0,16},{4,20},{8,24},{12,28},{16,0},{20,4},{24,8},{28,12},{1,17},{... | collective-permute-start | bytes 1448 | tf_op jit(solution)/shard_map/ppermute | solution.py:89
  54.1 1.3 %collective-permute-start.11 = (f32[3,40]{1,0:T(4,128)S(1)}, f32[3,40]{1,0:T(4,128)S(1)}, u32[]{:S(2)}, u32[]{:S(2)}) collective-permute-start(f32[3,40]{1,0:T(4,128)S(1)} %pad_maximum_fusion), channel_id=1, source_target_pairs={{0,24},{4,28},{8,16},{12,20},{16,8},{20,12},{24,0},{28,4},{1,25},{... | collective-permute-start | bytes 1448 | tf_op jit(solution)/shard_map/ppermute | solution.py:89
  55.8 3.6 %collective-permute-done.11 = f32[3,40]{1,0:T(4,128)S(1)} collective-permute-done((f32[3,40]{1,0:T(4,128)S(1)}, f32[3,40]{1,0:T(4,128)S(1)}, u32[]{:S(2)}, u32[]{:S(2)}) %collective-permute-start.11) | collective-permute-done | bytes 512 | tf_op jit(solution)/shard_map/ppermute | solution.py:89
  59.5 1.6 %collective-permute-start.12 = (f32[3,40]{1,0:T(4,128)S(1)}, f32[3,40]{1,0:T(4,128)S(1)}, u32[]{:S(2)}, u32[]{:S(2)}) collective-permute-start(f32[3,40]{1,0:T(4,128)S(1)} %pad_maximum_fusion.1), channel_id=1, source_target_pairs={{0,4},{4,0},{8,12},{12,8},{16,20},{20,16},{24,28},{28,24},{1,5},{5... | collective-permute-start | bytes 1448 | tf_op jit(solution)/shard_map/ppermute | solution.py:92
  61.8 1.4 %collective-permute-done.12 = f32[3,40]{1,0:T(4,128)S(1)} collective-permute-done((f32[3,40]{1,0:T(4,128)S(1)}, f32[3,40]{1,0:T(4,128)S(1)}, u32[]{:S(2)}, u32[]{:S(2)}) %collective-permute-start.12) | collective-permute-done | bytes 512 | tf_op jit(solution)/shard_map/ppermute | solution.py:92
  63.3 1.1 %collective-permute-done.13 = f32[160]{0:T(256)S(1)} collective-permute-done((f32[160]{0:T(256)S(1)}, f32[160]{0:T(256)S(1)}, u32[]{:S(2)}, u32[]{:S(2)}) %collective-permute-start.13) | collective-permute-done | bytes 672 | tf_op jit(solution)/shard_map/ppermute | solution.py:104
  64.6 1.5 %collective-permute-start.14 = (f32[160]{0:T(256)S(1)}, f32[160]{0:T(256)S(1)}, u32[]{:S(2)}, u32[]{:S(2)}) collective-permute-start(f32[160]{0:T(256)S(1)} %add_dynamic-update-slice_fusion), channel_id=1, source_target_pairs={{0,2},{1,3},{2,0},{3,1},{4,6},{5,7},{6,4},{7,5},{8,10},{9,11},{10,... | collective-permute-start | bytes 1928 | tf_op jit(solution)/shard_map/ppermute | solution.py:104
  66.8 1.3 %collective-permute-done.14 = f32[160]{0:T(256)S(1)} collective-permute-done((f32[160]{0:T(256)S(1)}, f32[160]{0:T(256)S(1)}, u32[]{:S(2)}, u32[]{:S(2)}) %collective-permute-start.14) | collective-permute-done | bytes 672 | tf_op jit(solution)/shard_map/ppermute | solution.py:104
  (56 shorter events, 7.4 us)
Async XLA Ops:
  0.6 38.4 %copy-start = (s32[256]{0:T(256)S(1)}, s32[256]{0:T(256)}, u32[]{:S(2)}) copy-start(s32[256]{0:T(256)} %param.16) | copy-start | bytes 3076
  0.6 9.5 %collective-permute-start = (bf16[32,4096]{1,0:T(8,128)(2,1)}, bf16[32,4096]{1,0:T(8,128)(2,1)S(1)}, u32[]{:S(2)}, u32[]{:S(2)}) collective-permute-start(bf16[32,4096]{1,0:T(8,128)(2,1)} %param.13), channel_id=1, source_target_pairs={{0,8},{8,16},{16,24},{24,28},{28,20},{20,12},{12,4},{4,0},{1,9},{9... | collective-permute-start | bytes 786440 | tf_op jit(solution)/shard_map/ppermute | solution.py:39
  3.7 8.3 %collective-permute-start.4 = (bf16[32,4096]{1,0:T(8,128)(2,1)}, bf16[32,4096]{1,0:T(8,128)(2,1)S(1)}, u32[]{:S(2)}, u32[]{:S(2)}) collective-permute-start(bf16[32,4096]{1,0:T(8,128)(2,1)} %param.13), channel_id=1, source_target_pairs={{8,0},{16,8},{24,16},{28,24},{20,28},{12,20},{4,12},{0,4},{9,1},{1... | collective-permute-start | bytes 786440 | tf_op jit(solution)/shard_map/ppermute | solution.py:42
  10.2 7.5 %collective-permute-start.1 = (bf16[32,4096]{1,0:T(8,128)(2,1)S(1)}, bf16[32,4096]{1,0:T(8,128)(2,1)S(1)}, u32[]{:S(2)}, u32[]{:S(2)}) collective-permute-start(bf16[32,4096]{1,0:T(8,128)(2,1)S(1)} %collective-permute-done), channel_id=1, source_target_pairs={{0,8},{8,16},{16,24},{24,28},{28,20},{20,12},{12,4},{4,0},{1,9},{9... | collective-permute-start | bytes 786440 | tf_op jit(solution)/shard_map/ppermute | solution.py:39
  12.0 7.2 %collective-permute-start.5 = (bf16[32,4096]{1,0:T(8,128)(2,1)S(1)}, bf16[32,4096]{1,0:T(8,128)(2,1)S(1)}, u32[]{:S(2)}, u32[]{:S(2)}) collective-permute-start(bf16[32,4096]{1,0:T(8,128)(2,1)S(1)} %collective-permute-done.4), channel_id=1, source_target_pairs={{8,0},{16,8},{24,16},{28,24},{20,28},{12,20},{4,12},{0,4},{9,1},{1... | collective-permute-start | bytes 786440 | tf_op jit(solution)/shard_map/ppermute | solution.py:42
  17.7 6.6 %collective-permute-start.2 = (bf16[32,4096]{1,0:T(8,128)(2,1)S(1)}, bf16[32,4096]{1,0:T(8,128)(2,1)S(1)}, u32[]{:S(2)}, u32[]{:S(2)}) collective-permute-start(bf16[32,4096]{1,0:T(8,128)(2,1)S(1)} %collective-permute-done.1), channel_id=1, source_target_pairs={{0,8},{8,16},{16,24},{24,28},{28,20},{20,12},{12,4},{4,0},{1,9},{9... | collective-permute-start | bytes 786440 | tf_op jit(solution)/shard_map/ppermute | solution.py:39
  19.2 11.4 %collective-permute-start.6 = (bf16[32,4096]{1,0:T(8,128)(2,1)S(1)}, bf16[32,4096]{1,0:T(8,128)(2,1)S(1)}, u32[]{:S(2)}, u32[]{:S(2)}) collective-permute-start(bf16[32,4096]{1,0:T(8,128)(2,1)S(1)} %collective-permute-done.5), channel_id=1, source_target_pairs={{8,0},{16,8},{24,16},{28,24},{20,28},{12,20},{4,12},{0,4},{9,1},{1... | collective-permute-start | bytes 786440 | tf_op jit(solution)/shard_map/ppermute | solution.py:42
  24.3 6.4 %collective-permute-start.3 = (bf16[32,4096]{1,0:T(8,128)(2,1)S(1)}, bf16[32,4096]{1,0:T(8,128)(2,1)S(1)}, u32[]{:S(2)}, u32[]{:S(2)}) collective-permute-start(bf16[32,4096]{1,0:T(8,128)(2,1)S(1)} %collective-permute-done.2), channel_id=1, source_target_pairs={{0,8},{8,16},{16,24},{24,28},{28,20},{20,12},{12,4},{4,0},{1,9},{9... | collective-permute-start | bytes 786440 | tf_op jit(solution)/shard_map/ppermute | solution.py:39
  38.8 2.2 %collective-permute-start.7 = (f32[80,2048]{1,0:T(8,128)S(1)}, f32[80,2048]{1,0:T(8,128)S(1)}, u32[]{:S(2)}, u32[]{:S(2)}) collective-permute-start(f32[80,2048]{1,0:T(8,128)S(1)} %select_bitcast_fusion), channel_id=1, source_target_pairs={{0,1},{1,0},{2,3},{3,2},{4,5},{5,4},{6,7},{7,6},{8,9},{9,8},{10,11... | collective-permute-start | bytes 1966088 | tf_op jit(solution)/shard_map/ppermute | solution.py:66
  39.8 26.4 %copy-start.1 = (s32[8]{0:T(128)S(1)}, s32[8]{0:T(128)}, u32[]{:S(2)}) copy-start(s32[8]{0:T(128)} %param.15) | copy-start | bytes 100
  41.0 27.9 %copy-start.2 = (f32[32]{0:T(128)S(1)}, f32[32]{0:T(128)}, u32[]{:S(2)}) copy-start(f32[32]{0:T(128)} %param.17) | copy-start | bytes 388
  41.1 9.8 %collective-permute-start.8 = (f32[40,2048]{1,0:T(8,128)S(1)}, f32[40,2048]{1,0:T(8,128)S(1)}, u32[]{:S(2)}, u32[]{:S(2)}) collective-permute-start(f32[40,2048]{1,0:T(8,128)S(1)} %select_bitcast_fusion.1), channel_id=1, source_target_pairs={{0,2},{1,3},{2,0},{3,1},{4,6},{5,7},{6,4},{7,5},{8,10},{9,11},{10,... | collective-permute-start | bytes 983048 | tf_op jit(solution)/shard_map/ppermute | solution.py:66
  51.3 4.5 %collective-permute-start.10 = (f32[3,40]{1,0:T(4,128)S(1)}, f32[3,40]{1,0:T(4,128)S(1)}, u32[]{:S(2)}, u32[]{:S(2)}) collective-permute-start(f32[3,40]{1,0:T(4,128)S(1)} %pad_maximum_fusion), channel_id=1, source_target_pairs={{0,16},{4,20},{8,24},{12,28},{16,0},{20,4},{24,8},{28,12},{1,17},{... | collective-permute-start | bytes 1448 | tf_op jit(solution)/shard_map/ppermute | solution.py:89
  54.1 5.4 %collective-permute-start.11 = (f32[3,40]{1,0:T(4,128)S(1)}, f32[3,40]{1,0:T(4,128)S(1)}, u32[]{:S(2)}, u32[]{:S(2)}) collective-permute-start(f32[3,40]{1,0:T(4,128)S(1)} %pad_maximum_fusion), channel_id=1, source_target_pairs={{0,24},{4,28},{8,16},{12,20},{16,8},{20,12},{24,0},{28,4},{1,25},{... | collective-permute-start | bytes 1448 | tf_op jit(solution)/shard_map/ppermute | solution.py:89
  55.5 4.0 %collective-permute-start.9 = (f32[3,40]{1,0:T(4,128)S(1)}, f32[3,40]{1,0:T(4,128)S(1)}, u32[]{:S(2)}, u32[]{:S(2)}) collective-permute-start(f32[3,40]{1,0:T(4,128)S(1)} %pad_maximum_fusion), channel_id=1, source_target_pairs={{0,8},{4,12},{8,0},{12,4},{16,24},{20,28},{24,16},{28,20},{1,9},{5... | collective-permute-start | bytes 1448 | tf_op jit(solution)/shard_map/ppermute | solution.py:89
  59.5 3.7 %collective-permute-start.12 = (f32[3,40]{1,0:T(4,128)S(1)}, f32[3,40]{1,0:T(4,128)S(1)}, u32[]{:S(2)}, u32[]{:S(2)}) collective-permute-start(f32[3,40]{1,0:T(4,128)S(1)} %pad_maximum_fusion.1), channel_id=1, source_target_pairs={{0,4},{4,0},{8,12},{12,8},{16,20},{20,16},{24,28},{28,24},{1,5},{5... | collective-permute-start | bytes 1448 | tf_op jit(solution)/shard_map/ppermute | solution.py:92
  63.3 1.2 %collective-permute-start.13 = (f32[160]{0:T(256)S(1)}, f32[160]{0:T(256)S(1)}, u32[]{:S(2)}, u32[]{:S(2)}) collective-permute-start(f32[160]{0:T(256)S(1)} %get-tuple-element.31), channel_id=1, source_target_pairs={{0,1},{1,0},{2,3},{3,2},{4,5},{5,4},{6,7},{7,6},{8,9},{9,8},{10,11... | collective-permute-start | bytes 1928 | tf_op jit(solution)/shard_map/ppermute | solution.py:104
  64.6 3.6 %collective-permute-start.14 = (f32[160]{0:T(256)S(1)}, f32[160]{0:T(256)S(1)}, u32[]{:S(2)}, u32[]{:S(2)}) collective-permute-start(f32[160]{0:T(256)S(1)} %add_dynamic-update-slice_fusion), channel_id=1, source_target_pairs={{0,2},{1,3},{2,0},{3,1},{4,6},{5,7},{6,4},{7,5},{8,10},{9,11},{10,... | collective-permute-start | bytes 1928 | tf_op jit(solution)/shard_map/ppermute | solution.py:104

commit v14 on v7

--- a/solution.py
+++ b/solution.py
@@ -50,7 +50,7 @@
     where = jnp.sum(jnp.where(hit, slot_of[:, None], 0), axis=0) * count + rows % count
     choose = lax.broadcasted_iota(jnp.int32, (stacked.shape[0], where.shape[0]), 0) == where[None, :]
     picked = lax.dot_general(choose.astype(stacked.dtype), stacked, (((0,), (0,)), ((), ())), preferred_element_type=jnp.float32)
-    return lax.optimization_barrier(picked.astype(stacked.dtype))
+    return picked.astype(stacked.dtype)
 
 
 def halving_scatter(partial, size):

time: 69.1 us -> 68.9 us (level)
  no operation moved by 1% of the time
where the time goes in v14:
time: 68.9 us; the launch traced here: 68.7 us
  waiting for transfers between devices  31.5 us (46%)
  starting transfers between devices  18.5 us (27%)
  matrix products  7.71 us (11%)
  local copies, waits for them, and re-layouts  5.32 us (8%)
  other arithmetic  4.71 us (7%)
  between operations  0.91 us (1%)
    ppermute x4, waiting for transfers between devices, ring_gather(): ahead = lax.ppermute(ahead, 'dp', fwd)  15.5 us
    ppermute x2, waiting for transfers between devices, halving_scatter(): got = lax.ppermute(send, 'vocab', [(i, i ^ bit) for i in range(size)])  9.12 us
    ppermute x4, starting transfers between devices, ring_gather(): ahead = lax.ppermute(ahead, 'dp', fwd)  8.21 us
    dot_general x1, matrix products, on_device(): jnp.dot(full_rows, head_weight, preferred_element_type=jnp.float32)  7.71 us
    ppermute x3, starting transfers between devices, merge_stats(): lax.ppermute(stats, 'dp', [(i, i ^ bit * k) for i in range(size)])  3.55 us
    ppermute x3, waiting for transfers between devices, merge_stats(): lax.ppermute(stats, 'dp', [(i, i ^ bit * k) for i in range(size)])  3.19 us
    ppermute x1, starting transfers between devices, merge_stats(): lax.ppermute(stats, 'dp', [(i, i ^ bit) for i in range(size)])  2.65 us
    ppermute x2, waiting for transfers between devices, doubling_gather(): other = lax.ppermute(out, 'vocab', [(i, i ^ bit) for i in range(size)])  2.47 us
  transfers between devices with their start and end apart: 15, of which 12 were waited for; matrix products, arithmetic and copies ran while one was open for 11% of the time, Pallas kernels for 0%

profile of v14, /device:TPU:0, one launch (start us, length us, event | category | flops | bytes accessed | tf_op | source)
XLA Modules:
  0.0 68.7 jit_solution(2281900366203907917)
XLA Ops:
  0.6 3.1 %collective-permute-start = (bf16[32,4096]{1,0:T(8,128)(2,1)}, bf16[32,4096]{1,0:T(8,128)(2,1)S(1)}, u32[]{:S(2)}, u32[]{:S(2)}) collective-permute-start(bf16[32,4096]{1,0:T(8,128)(2,1)} %param.13), channel_id=1, source_target_pairs={{0,8},{8,16},{16,24},{24,28},{28,20},{20,12},{12,4},{4,0},{1,9},{9... | collective-permute-start | bytes 786440 | tf_op jit(solution)/shard_map/ppermute | solution.py:39
  3.8 1.0 %bitcast_dynamic-update-slice_fusion.7 = bf16[8,32,4096]{2,1,0:T(8,128)(2,1)S(1)} fusion(bf16[32,4096]{1,0:T(8,128)(2,1)} %param.13), kind=kLoop, calls=%fused_computation.19 | loop fusion | bytes 524288
  4.8 0.8 %reduce-window.8 = s32[8,1]{0,1:T(1,128)S(1)} reduce-window(s32[8,1]{0,1:T(1,128)} %bitcast.165, s32[]{:T(128)} %constant.172.clone.1), window={size=8x1 pad=7_0x0_0}, to_apply=%region_0.2 | reduce-window | flops 56 | bytes 68 | tf_op jit(solution)/shard_map/reduce-window.3
  6.5 1.2 %dynamic_slice.7 = s32[1]{0:T(128)} dynamic-slice(s32[8]{0:T(128)} %constant.196.clone, s32[]{:T(128)S(6)} %select_n.127), dynamic_slice_sizes={1} | dynamic-slice | bytes 12 | tf_op jit(solution)/shard_map/dynamic_slice | solution.py:46
  7.7 1.3 %and_select_fusion.1 = s32[8]{0:T(128)S(1)} fusion(s32[8]{0:T(128)} %constant.235, s32[]{:T(128)} %bitcast.2), kind=kLoop, calls=%fused_computation.41 | loop fusion | flops 96 | bytes 68 | tf_op jit(solution)/shard_map/jit(remainder)/select_n | solution.py:47
  9.2 1.0 %collective-permute-done = bf16[32,4096]{1,0:T(8,128)(2,1)S(1)} collective-permute-done((bf16[32,4096]{1,0:T(8,128)(2,1)}, bf16[32,4096]{1,0:T(8,128)(2,1)S(1)}, u32[]{:S(2)}, u32[]{:S(2)}) %collective-permute-start) | collective-permute-done | bytes 262176 | tf_op jit(solution)/shard_map/ppermute | solution.py:39
  10.2 1.8 %collective-permute-start.1 = (bf16[32,4096]{1,0:T(8,128)(2,1)S(1)}, bf16[32,4096]{1,0:T(8,128)(2,1)S(1)}, u32[]{:S(2)}, u32[]{:S(2)}) collective-permute-start(bf16[32,4096]{1,0:T(8,128)(2,1)S(1)} %collective-permute-done), channel_id=1, source_target_pairs={{0,8},{8,16},{16,24},{24,28},{28,20},{20,12},{12,4},{4,0},{1,9},{9... | collective-permute-start | bytes 786440 | tf_op jit(solution)/shard_map/ppermute | solution.py:39
  12.3 5.4 %collective-permute-done.1 = bf16[32,4096]{1,0:T(8,128)(2,1)S(1)} collective-permute-done((bf16[32,4096]{1,0:T(8,128)(2,1)S(1)}, bf16[32,4096]{1,0:T(8,128)(2,1)S(1)}, u32[]{:S(2)}, u32[]{:S(2)}) %collective-permute-start.1) | collective-permute-done | bytes 262176 | tf_op jit(solution)/shard_map/ppermute | solution.py:39
  17.7 1.5 %collective-permute-start.2 = (bf16[32,4096]{1,0:T(8,128)(2,1)S(1)}, bf16[32,4096]{1,0:T(8,128)(2,1)S(1)}, u32[]{:S(2)}, u32[]{:S(2)}) collective-permute-start(bf16[32,4096]{1,0:T(8,128)(2,1)S(1)} %collective-permute-done.1), channel_id=1, source_target_pairs={{0,8},{8,16},{16,24},{24,28},{28,20},{20,12},{12,4},{4,0},{1,9},{9... | collective-permute-start | bytes 786440 | tf_op jit(solution)/shard_map/ppermute | solution.py:39
  19.8 4.5 %collective-permute-done.2 = bf16[32,4096]{1,0:T(8,128)(2,1)S(1)} collective-permute-done((bf16[32,4096]{1,0:T(8,128)(2,1)S(1)}, bf16[32,4096]{1,0:T(8,128)(2,1)S(1)}, u32[]{:S(2)}, u32[]{:S(2)}) %collective-permute-start.2) | collective-permute-done | bytes 262176 | tf_op jit(solution)/shard_map/ppermute | solution.py:39
  24.3 1.7 %collective-permute-start.3 = (bf16[32,4096]{1,0:T(8,128)(2,1)S(1)}, bf16[32,4096]{1,0:T(8,128)(2,1)S(1)}, u32[]{:S(2)}, u32[]{:S(2)}) collective-permute-start(bf16[32,4096]{1,0:T(8,128)(2,1)S(1)} %collective-permute-done.2), channel_id=1, source_target_pairs={{0,8},{8,16},{16,24},{24,28},{28,20},{20,12},{12,4},{4,0},{1,9},{9... | collective-permute-start | bytes 786440 | tf_op jit(solution)/shard_map/ppermute | solution.py:39
  26.0 4.6 %collective-permute-done.3 = bf16[32,4096]{1,0:T(8,128)(2,1)S(1)} collective-permute-done((bf16[32,4096]{1,0:T(8,128)(2,1)S(1)}, bf16[32,4096]{1,0:T(8,128)(2,1)S(1)}, u32[]{:S(2)}, u32[]{:S(2)}) %collective-permute-start.3) | collective-permute-done | bytes 262176 | tf_op jit(solution)/shard_map/ppermute | solution.py:39
  30.8 7.7 %fusion = f32[160,2048]{1,0:T(8,128)S(1)} fusion(bf16[4096,2048]{1,0:T(8,128)(2,1)} %param.14, bf16[256,4096]{1,0:T(8,128)(2,1)S(1)} %bitcast.170, s32[160]{0:T(256)S(1)} %fusion.3), kind=kOutput, calls=%fused_computation.5 | convolution fusion | flops 3020595200 | bytes 20185728 | tf_op jit(solution)/shard_map/dot_general | solution.py:123
  39.6 1.1 %collective-permute-done.7 = f32[80,2048]{1,0:T(8,128)S(1)} collective-permute-done((f32[80,2048]{1,0:T(8,128)S(1)}, f32[80,2048]{1,0:T(8,128)S(1)}, u32[]{:S(2)}, u32[]{:S(2)}) %collective-permute-start.7) | collective-permute-done | bytes 655392 | tf_op jit(solution)/shard_map/ppermute | solution.py:66
  40.8 1.7 %collective-permute-start.8 = (f32[40,2048]{1,0:T(8,128)S(1)}, f32[40,2048]{1,0:T(8,128)S(1)}, u32[]{:S(2)}, u32[]{:S(2)}) collective-permute-start(f32[40,2048]{1,0:T(8,128)S(1)} %select_bitcast_fusion.1), channel_id=1, source_target_pairs={{0,2},{1,3},{2,0},{3,1},{4,6},{5,7},{6,4},{7,5},{8,10},{9,11},{10,... | collective-permute-start | bytes 983048 | tf_op jit(solution)/shard_map/ppermute | solution.py:66
  42.6 8.0 %collective-permute-done.8 = f32[40,2048]{1,0:T(8,128)S(1)} collective-permute-done((f32[40,2048]{1,0:T(8,128)S(1)}, f32[40,2048]{1,0:T(8,128)S(1)}, u32[]{:S(2)}, u32[]{:S(2)}) %collective-permute-start.8) | collective-permute-done | bytes 327712 | tf_op jit(solution)/shard_map/ppermute | solution.py:66
  51.1 1.8 %collective-permute-start.10 = (f32[3,40]{1,0:T(4,128)S(1)}, f32[3,40]{1,0:T(4,128)S(1)}, u32[]{:S(2)}, u32[]{:S(2)}) collective-permute-start(f32[3,40]{1,0:T(4,128)S(1)} %pad_maximum_fusion), channel_id=1, source_target_pairs={{0,8},{4,12},{8,0},{12,4},{16,24},{20,28},{24,16},{28,20},{1,9},{5... | collective-permute-start | bytes 1448 | tf_op jit(solution)/shard_map/ppermute | solution.py:83
  52.9 1.4 %collective-permute-start.11 = (f32[3,40]{1,0:T(4,128)S(1)}, f32[3,40]{1,0:T(4,128)S(1)}, u32[]{:S(2)}, u32[]{:S(2)}) collective-permute-start(f32[3,40]{1,0:T(4,128)S(1)} %pad_maximum_fusion), channel_id=1, source_target_pairs={{0,12},{4,8},{8,4},{12,0},{16,28},{20,24},{24,20},{28,16},{1,13},{... | collective-permute-start | bytes 1448 | tf_op jit(solution)/shard_map/ppermute | solution.py:83
  54.7 2.6 %collective-permute-done.11 = f32[3,40]{1,0:T(4,128)S(1)} collective-permute-done((f32[3,40]{1,0:T(4,128)S(1)}, f32[3,40]{1,0:T(4,128)S(1)}, u32[]{:S(2)}, u32[]{:S(2)}) %collective-permute-start.11) | collective-permute-done | bytes 512 | tf_op jit(solution)/shard_map/ppermute | solution.py:83
  57.9 2.7 %collective-permute-start.12 = (f32[3,40]{1,0:T(4,128)S(1)}, f32[3,40]{1,0:T(4,128)S(1)}, u32[]{:S(2)}, u32[]{:S(2)}) collective-permute-start(f32[3,40]{1,0:T(4,128)S(1)} %pad_maximum_fusion.1), channel_id=1, source_target_pairs={{0,16},{4,20},{8,24},{12,28},{16,0},{20,4},{24,8},{28,12},{1,17},{... | collective-permute-start | bytes 1448 | tf_op jit(solution)/shard_map/ppermute | solution.py:87
  61.2 1.2 %collective-permute-done.12 = f32[3,40]{1,0:T(4,128)S(1)} collective-permute-done((f32[3,40]{1,0:T(4,128)S(1)}, f32[3,40]{1,0:T(4,128)S(1)}, u32[]{:S(2)}, u32[]{:S(2)}) %collective-permute-start.12) | collective-permute-done | bytes 512 | tf_op jit(solution)/shard_map/ppermute | solution.py:87
  62.6 1.1 %collective-permute-done.13 = f32[160]{0:T(256)S(1)} collective-permute-done((f32[160]{0:T(256)S(1)}, f32[160]{0:T(256)S(1)}, u32[]{:S(2)}, u32[]{:S(2)}) %collective-permute-start.13) | collective-permute-done | bytes 672 | tf_op jit(solution)/shard_map/ppermute | solution.py:99
  63.8 1.5 %collective-permute-start.14 = (f32[160]{0:T(256)S(1)}, f32[160]{0:T(256)S(1)}, u32[]{:S(2)}, u32[]{:S(2)}) collective-permute-start(f32[160]{0:T(256)S(1)} %add_dynamic-update-slice_fusion), channel_id=1, source_target_pairs={{0,2},{1,3},{2,0},{3,1},{4,6},{5,7},{6,4},{7,5},{8,10},{9,11},{10,... | collective-permute-start | bytes 1928 | tf_op jit(solution)/shard_map/ppermute | solution.py:99
  66.1 1.3 %collective-permute-done.14 = f32[160]{0:T(256)S(1)} collective-permute-done((f32[160]{0:T(256)S(1)}, f32[160]{0:T(256)S(1)}, u32[]{:S(2)}, u32[]{:S(2)}) %collective-permute-start.14) | collective-permute-done | bytes 672 | tf_op jit(solution)/shard_map/ppermute | solution.py:99
  (55 shorter events, 7.4 us)
Async XLA Ops:
  0.6 38.1 %copy-start = (s32[256]{0:T(256)S(1)}, s32[256]{0:T(256)}, u32[]{:S(2)}) copy-start(s32[256]{0:T(256)} %param.16) | copy-start | bytes 3076
  0.6 9.5 %collective-permute-start = (bf16[32,4096]{1,0:T(8,128)(2,1)}, bf16[32,4096]{1,0:T(8,128)(2,1)S(1)}, u32[]{:S(2)}, u32[]{:S(2)}) collective-permute-start(bf16[32,4096]{1,0:T(8,128)(2,1)} %param.13), channel_id=1, source_target_pairs={{0,8},{8,16},{16,24},{24,28},{28,20},{20,12},{12,4},{4,0},{1,9},{9... | collective-permute-start | bytes 786440 | tf_op jit(solution)/shard_map/ppermute | solution.py:39
  3.7 8.3 %collective-permute-start.4 = (bf16[32,4096]{1,0:T(8,128)(2,1)}, bf16[32,4096]{1,0:T(8,128)(2,1)S(1)}, u32[]{:S(2)}, u32[]{:S(2)}) collective-permute-start(bf16[32,4096]{1,0:T(8,128)(2,1)} %param.13), channel_id=1, source_target_pairs={{8,0},{16,8},{24,16},{28,24},{20,28},{12,20},{4,12},{0,4},{9,1},{1... | collective-permute-start | bytes 786440 | tf_op jit(solution)/shard_map/ppermute | solution.py:42
  10.2 7.5 %collective-permute-start.1 = (bf16[32,4096]{1,0:T(8,128)(2,1)S(1)}, bf16[32,4096]{1,0:T(8,128)(2,1)S(1)}, u32[]{:S(2)}, u32[]{:S(2)}) collective-permute-start(bf16[32,4096]{1,0:T(8,128)(2,1)S(1)} %collective-permute-done), channel_id=1, source_target_pairs={{0,8},{8,16},{16,24},{24,28},{28,20},{20,12},{12,4},{4,0},{1,9},{9... | collective-permute-start | bytes 786440 | tf_op jit(solution)/shard_map/ppermute | solution.py:39
  12.0 7.2 %collective-permute-start.5 = (bf16[32,4096]{1,0:T(8,128)(2,1)S(1)}, bf16[32,4096]{1,0:T(8,128)(2,1)S(1)}, u32[]{:S(2)}, u32[]{:S(2)}) collective-permute-start(bf16[32,4096]{1,0:T(8,128)(2,1)S(1)} %collective-permute-done.4), channel_id=1, source_target_pairs={{8,0},{16,8},{24,16},{28,24},{20,28},{12,20},{4,12},{0,4},{9,1},{1... | collective-permute-start | bytes 786440 | tf_op jit(solution)/shard_map/ppermute | solution.py:42
  17.7 6.6 %collective-permute-start.2 = (bf16[32,4096]{1,0:T(8,128)(2,1)S(1)}, bf16[32,4096]{1,0:T(8,128)(2,1)S(1)}, u32[]{:S(2)}, u32[]{:S(2)}) collective-permute-start(bf16[32,4096]{1,0:T(8,128)(2,1)S(1)} %collective-permute-done.1), channel_id=1, source_target_pairs={{0,8},{8,16},{16,24},{24,28},{28,20},{20,12},{12,4},{4,0},{1,9},{9... | collective-permute-start | bytes 786440 | tf_op jit(solution)/shard_map/ppermute | solution.py:39
  19.2 11.4 %collective-permute-start.6 = (bf16[32,4096]{1,0:T(8,128)(2,1)S(1)}, bf16[32,4096]{1,0:T(8,128)(2,1)S(1)}, u32[]{:S(2)}, u32[]{:S(2)}) collective-permute-start(bf16[32,4096]{1,0:T(8,128)(2,1)S(1)} %collective-permute-done.5), channel_id=1, source_target_pairs={{8,0},{16,8},{24,16},{28,24},{20,28},{12,20},{4,12},{0,4},{9,1},{1... | collective-permute-start | bytes 786440 | tf_op jit(solution)/shard_map/ppermute | solution.py:42
  24.3 6.4 %collective-permute-start.3 = (bf16[32,4096]{1,0:T(8,128)(2,1)S(1)}, bf16[32,4096]{1,0:T(8,128)(2,1)S(1)}, u32[]{:S(2)}, u32[]{:S(2)}) collective-permute-start(bf16[32,4096]{1,0:T(8,128)(2,1)S(1)} %collective-permute-done.2), channel_id=1, source_target_pairs={{0,8},{8,16},{16,24},{24,28},{28,20},{20,12},{12,4},{4,0},{1,9},{9... | collective-permute-start | bytes 786440 | tf_op jit(solution)/shard_map/ppermute | solution.py:39
  38.5 2.2 %collective-permute-start.7 = (f32[80,2048]{1,0:T(8,128)S(1)}, f32[80,2048]{1,0:T(8,128)S(1)}, u32[]{:S(2)}, u32[]{:S(2)}) collective-permute-start(f32[80,2048]{1,0:T(8,128)S(1)} %select_bitcast_fusion), channel_id=1, source_target_pairs={{0,1},{1,0},{2,3},{3,2},{4,5},{5,4},{6,7},{7,6},{8,9},{9,8},{10,11... | collective-permute-start | bytes 1966088 | tf_op jit(solution)/shard_map/ppermute | solution.py:66
  39.6 25.8 %copy-start.1 = (s32[8]{0:T(128)S(1)}, s32[8]{0:T(128)}, u32[]{:S(2)}) copy-start(s32[8]{0:T(128)} %param.15) | copy-start | bytes 100
  40.8 27.4 %copy-start.2 = (f32[32]{0:T(128)S(1)}, f32[32]{0:T(128)}, u32[]{:S(2)}) copy-start(f32[32]{0:T(128)} %param.17) | copy-start | bytes 388
  40.8 9.8 %collective-permute-start.8 = (f32[40,2048]{1,0:T(8,128)S(1)}, f32[40,2048]{1,0:T(8,128)S(1)}, u32[]{:S(2)}, u32[]{:S(2)}) collective-permute-start(f32[40,2048]{1,0:T(8,128)S(1)} %select_bitcast_fusion.1), channel_id=1, source_target_pairs={{0,2},{1,3},{2,0},{3,1},{4,6},{5,7},{6,4},{7,5},{8,10},{9,11},{10,... | collective-permute-start | bytes 983048 | tf_op jit(solution)/shard_map/ppermute | solution.py:66
  51.1 3.7 %collective-permute-start.10 = (f32[3,40]{1,0:T(4,128)S(1)}, f32[3,40]{1,0:T(4,128)S(1)}, u32[]{:S(2)}, u32[]{:S(2)}) collective-permute-start(f32[3,40]{1,0:T(4,128)S(1)} %pad_maximum_fusion), channel_id=1, source_target_pairs={{0,8},{4,12},{8,0},{12,4},{16,24},{20,28},{24,16},{28,20},{1,9},{5... | collective-permute-start | bytes 1448 | tf_op jit(solution)/shard_map/ppermute | solution.py:83
  52.9 4.5 %collective-permute-start.11 = (f32[3,40]{1,0:T(4,128)S(1)}, f32[3,40]{1,0:T(4,128)S(1)}, u32[]{:S(2)}, u32[]{:S(2)}) collective-permute-start(f32[3,40]{1,0:T(4,128)S(1)} %pad_maximum_fusion), channel_id=1, source_target_pairs={{0,12},{4,8},{8,4},{12,0},{16,28},{20,24},{24,20},{28,16},{1,13},{... | collective-permute-start | bytes 1448 | tf_op jit(solution)/shard_map/ppermute | solution.py:83
  54.2 3.6 %collective-permute-start.9 = (f32[3,40]{1,0:T(4,128)S(1)}, f32[3,40]{1,0:T(4,128)S(1)}, u32[]{:S(2)}, u32[]{:S(2)}) collective-permute-start(f32[3,40]{1,0:T(4,128)S(1)} %pad_maximum_fusion), channel_id=1, source_target_pairs={{0,4},{4,0},{8,12},{12,8},{16,20},{20,16},{24,28},{28,24},{1,5},{5... | collective-permute-start | bytes 1448 | tf_op jit(solution)/shard_map/ppermute | solution.py:83
  57.9 4.5 %collective-permute-start.12 = (f32[3,40]{1,0:T(4,128)S(1)}, f32[3,40]{1,0:T(4,128)S(1)}, u32[]{:S(2)}, u32[]{:S(2)}) collective-permute-start(f32[3,40]{1,0:T(4,128)S(1)} %pad_maximum_fusion.1), channel_id=1, source_target_pairs={{0,16},{4,20},{8,24},{12,28},{16,0},{20,4},{24,8},{28,12},{1,17},{... | collective-permute-start | bytes 1448 | tf_op jit(solution)/shard_map/ppermute | solution.py:87
  62.5 1.2 %collective-permute-start.13 = (f32[160]{0:T(256)S(1)}, f32[160]{0:T(256)S(1)}, u32[]{:S(2)}, u32[]{:S(2)}) collective-permute-start(f32[160]{0:T(256)S(1)} %get-tuple-element.31), channel_id=1, source_target_pairs={{0,1},{1,0},{2,3},{3,2},{4,5},{5,4},{6,7},{7,6},{8,9},{9,8},{10,11... | collective-permute-start | bytes 1928 | tf_op jit(solution)/shard_map/ppermute | solution.py:99
  63.8 3.6 %collective-permute-start.14 = (f32[160]{0:T(256)S(1)}, f32[160]{0:T(256)S(1)}, u32[]{:S(2)}, u32[]{:S(2)}) collective-permute-start(f32[160]{0:T(256)S(1)} %add_dynamic-update-slice_fusion), channel_id=1, source_target_pairs={{0,2},{1,3},{2,0},{3,1},{4,6},{5,7},{6,4},{7,5},{8,10},{9,11},{10,... | collective-permute-start | bytes 1928 | tf_op jit(solution)/shard_map/ppermute | solution.py:99

commit v15 on v5

--- a/solution.py
+++ b/solution.py
@@ -80,14 +80,22 @@
     return canon + place % span, first
 
 
+def merge_pair(stats, other):
+    top = jnp.maximum(stats[0], other[0])
+    total = stats[1] * jnp.exp(stats[0] - top) + other[1] * jnp.exp(other[0] - top)
+    return jnp.stack([top, total, stats[2] + other[2]])
+
+
 def merge_stats(stats, size):
     bit = 1
     while bit < size:
-        other = lax.ppermute(stats, "dp", [(i, i ^ bit) for i in range(size)])
-        top = jnp.maximum(stats[0], other[0])
-        total = stats[1] * jnp.exp(stats[0] - top) + other[1] * jnp.exp(other[0] - top)
-        stats = jnp.stack([top, total, stats[2] + other[2]])
-        bit *= 2
+        if bit * 4 <= size:
+            got = [lax.ppermute(stats, "dp", [(i, i ^ (bit * k)) for i in range(size)]) for k in (1, 2, 3)]
+            stats = merge_pair(merge_pair(stats, got[0]), merge_pair(got[1], got[2]))
+            bit *= 4
+        else:
+            stats = merge_pair(stats, lax.ppermute(stats, "dp", [(i, i ^ bit) for i in range(size)]))
+            bit *= 2
     return stats
 
 
@@ -127,9 +135,10 @@
         row_targets = jnp.take(targets, row_targets)
         pieces = 2 if tile_width % 256 == 0 else 1
         width = tile_width // pieces
+        halves = lax.optimization_barrier(tuple(head_weight[:, piece * width:(piece + 1) * width] for piece in range(pieces)))
         parts = []
         for piece in range(pieces):
-            partial = jnp.dot(full_rows, head_weight[:, piece * width:(piece + 1) * width], preferred_element_type=jnp.float32)
+            partial = jnp.dot(full_rows, halves[piece], preferred_element_type=jnp.float32)
             logits = halving_scatter(partial, vocab_size)
             highest = jnp.max(logits, axis=1)
             exp_total = jnp.sum(jnp.exp(logits - highest[:, None]), axis=1)

time: 70.2 us -> 78.6 us (1.12)
  local copies, waits for them, and re-layouts: 7.65 us -> 16.4 us
  starting transfers between devices: 18.9 us -> 19.7 us
    slice x0 -> x1, local copies, waits for them, and re-layouts: none -> 11.6 us  [on_device(): head_weight[:, piece * width:(piece + 1) * width]]
    unnamed x15 -> x21, local copies, waits for them, and re-layouts: 3.43 us -> 1.23 us
    ppermute x3 -> x4, starting transfers between devices: 5.59 us -> 6.21 us  [the longest x3 3.55 us: merge_stats(): lax.ppermute(stats, 'dp', [(i, i ^ bit * k) for i in range(size)])]
    ppermute x3 -> x4, waiting for transfers between devices: 5.55 us -> 5.1 us  [the longest x3 3.91 us: merge_stats(): lax.ppermute(stats, 'dp', [(i, i ^ bit * k) for i in range(size)])]
  transfers between devices with their start and end apart: 16 -> 17, of which waited for: 11 -> 11; matrix products, arithmetic and copies ran while one was open for 14% -> 25% of each run, Pallas kernels for 0% -> 0%
where the time goes in v15:
time: 78.6 us; the launch traced here: 78.4 us
  waiting for transfers between devices  29.9 us (38%)
  starting transfers between devices  19.7 us (25%)
  local copies, waits for them, and re-layouts  16.4 us (21%)
  matrix products  7.37 us (9%)
  other arithmetic  4.12 us (5%)
  between operations  0.94 us (1%)
    ppermute x4, waiting for transfers between devices, ring_gather(): ahead = lax.ppermute(ahead, 'dp', fwd)  15.4 us
    slice x1, local copies, waits for them, and re-layouts, on_device(): head_weight[:, piece * width:(piece + 1) * width]  11.6 us
    ppermute x4, starting transfers between devices, ring_gather(): ahead = lax.ppermute(ahead, 'dp', fwd)  8.28 us
    ppermute x4, waiting for transfers between devices, halving_scatter(): lax.ppermute(partial[:half], 'vocab', [(i, i ^ bit) for i in range(size)])  6.94 us
    dot_general x2, matrix products, on_device(): jnp.dot(full_rows, halves[piece], preferred_element_type=jnp.float32)  6.81 us
    ppermute x3, waiting for transfers between devices, merge_stats(): lax.ppermute(stats, 'dp', [(i, i ^ bit * k) for i in range(size)])  3.91 us
    ppermute x3, starting transfers between devices, merge_stats(): lax.ppermute(stats, 'dp', [(i, i ^ bit * k) for i in range(size)])  3.55 us
    ppermute x4, starting transfers between devices, halving_scatter(): lax.ppermute(partial[:half], 'vocab', [(i, i ^ bit) for i in range(size)])  3.19 us
  transfers between devices with their start and end apart: 17, of which 11 were waited for; matrix products, arithmetic and copies ran while one was open for 25% of the time, Pallas kernels for 0%

profile of v15, /device:TPU:0, one launch (start us, length us, event | category | flops | bytes accessed | tf_op | source)
XLA Modules:
  0.0 78.4 jit_solution(3396823617012410056)
XLA Ops:
  0.6 3.1 %collective-permute-start = (bf16[32,4096]{1,0:T(8,128)(2,1)}, bf16[32,4096]{1,0:T(8,128)(2,1)S(1)}, u32[]{:S(2)}, u32[]{:S(2)}) collective-permute-start(bf16[32,4096]{1,0:T(8,128)(2,1)} %param.9), channel_id=1, source_target_pairs={{0,8},{8,16},{16,24},{24,28},{28,20},{20,12},{12,4},{4,0},{1,9},{9... | collective-permute-start | bytes 786440 | tf_op jit(solution)/shard_map/ppermute | solution.py:39
  3.8 1.0 %bitcast_dynamic-update-slice_fusion.7 = bf16[8,32,4096]{2,1,0:T(8,128)(2,1)S(1)} fusion(bf16[32,4096]{1,0:T(8,128)(2,1)} %param.9), kind=kLoop, calls=%fused_computation.14 | loop fusion | bytes 524288
  6.6 11.6 %fusion.46 = (bf16[4096,1024]{1,0:T(8,128)(2,1)}, bf16[4096,1024]{1,0:T(8,128)(2,1)}) fusion(bf16[4096,2048]{1,0:T(8,128)(2,1)} %param.10), kind=kLoop, calls=%fused_computation.145 | loop fusion | bytes 33554432 | tf_op jit(solution)/shard_map/slice | solution.py:138
  20.5 2.0 %collective-permute-start.1 = (bf16[32,4096]{1,0:T(8,128)(2,1)S(1)}, bf16[32,4096]{1,0:T(8,128)(2,1)S(1)}, u32[]{:S(2)}, u32[]{:S(2)}) collective-permute-start(bf16[32,4096]{1,0:T(8,128)(2,1)S(1)} %collective-permute-done), channel_id=1, source_target_pairs={{0,8},{8,16},{16,24},{24,28},{28,20},{20,12},{12,4},{4,0},{1,9},{9... | collective-permute-start | bytes 786440 | tf_op jit(solution)/shard_map/ppermute | solution.py:39
  22.6 5.7 %collective-permute-done.1 = bf16[32,4096]{1,0:T(8,128)(2,1)S(1)} collective-permute-done((bf16[32,4096]{1,0:T(8,128)(2,1)S(1)}, bf16[32,4096]{1,0:T(8,128)(2,1)S(1)}, u32[]{:S(2)}, u32[]{:S(2)}) %collective-permute-start.1) | collective-permute-done | bytes 262176 | tf_op jit(solution)/shard_map/ppermute | solution.py:39
  28.3 1.7 %collective-permute-start.2 = (bf16[32,4096]{1,0:T(8,128)(2,1)S(1)}, bf16[32,4096]{1,0:T(8,128)(2,1)S(1)}, u32[]{:S(2)}, u32[]{:S(2)}) collective-permute-start(bf16[32,4096]{1,0:T(8,128)(2,1)S(1)} %collective-permute-done.1), channel_id=1, source_target_pairs={{0,8},{8,16},{16,24},{24,28},{28,20},{20,12},{12,4},{4,0},{1,9},{9... | collective-permute-start | bytes 786440 | tf_op jit(solution)/shard_map/ppermute | solution.py:39
  30.4 4.8 %collective-permute-done.2 = bf16[32,4096]{1,0:T(8,128)(2,1)S(1)} collective-permute-done((bf16[32,4096]{1,0:T(8,128)(2,1)S(1)}, bf16[32,4096]{1,0:T(8,128)(2,1)S(1)}, u32[]{:S(2)}, u32[]{:S(2)}) %collective-permute-start.2) | collective-permute-done | bytes 262176 | tf_op jit(solution)/shard_map/ppermute | solution.py:39
  35.2 1.4 %collective-permute-start.3 = (bf16[32,4096]{1,0:T(8,128)(2,1)S(1)}, bf16[32,4096]{1,0:T(8,128)(2,1)S(1)}, u32[]{:S(2)}, u32[]{:S(2)}) collective-permute-start(bf16[32,4096]{1,0:T(8,128)(2,1)S(1)} %collective-permute-done.2), channel_id=1, source_target_pairs={{0,8},{8,16},{16,24},{24,28},{28,20},{20,12},{12,4},{4,0},{1,9},{9... | collective-permute-start | bytes 786440 | tf_op jit(solution)/shard_map/ppermute | solution.py:39
  36.7 4.9 %collective-permute-done.3 = bf16[32,4096]{1,0:T(8,128)(2,1)S(1)} collective-permute-done((bf16[32,4096]{1,0:T(8,128)(2,1)S(1)}, bf16[32,4096]{1,0:T(8,128)(2,1)S(1)}, u32[]{:S(2)}, u32[]{:S(2)}) %collective-permute-start.3) | collective-permute-done | bytes 262176 | tf_op jit(solution)/shard_map/ppermute | solution.py:39
  42.3 5.2 %fusion.47 = f32[160,1024]{1,0:T(8,128)S(1)} fusion(bf16[160,4096]{1,0:T(8,128)(2,1)S(1)} %convolution_convert_fusion, bf16[4096,1024]{1,0:T(8,128)(2,1)} %get-tuple-element.5), kind=kOutput, calls=%fused_computation.146 | convolution fusion | flops 1342177280 | bytes 10354688 | tf_op jit(solution)/shard_map/dot_general | solution.py:141
  47.7 1.6 %fusion.48 = f32[160,1024]{1,0:T(8,128)S(1)} fusion(bf16[160,4096]{1,0:T(8,128)(2,1)S(1)} %convolution_convert_fusion, bf16[4096,1024]{1,0:T(8,128)(2,1)S(1)} %bitcast.177), kind=kOutput, calls=%fused_computation.147 | convolution fusion | flops 1342177280 | bytes 10354688 | tf_op jit(solution)/shard_map/dot_general | solution.py:141
  49.9 1.4 %collective-permute-start.8 = (f32[40,1024]{1,0:T(8,128)S(1)}, f32[40,1024]{1,0:T(8,128)S(1)}, u32[]{:S(2)}, u32[]{:S(2)}) collective-permute-start(f32[40,1024]{1,0:T(8,128)S(1)} %slice.103), channel_id=1, source_target_pairs={{0,2},{1,3},{2,0},{3,1},{4,6},{5,7},{6,4},{7,5},{8,10},{9,11},{10,... | collective-permute-start | bytes 491528 | tf_op jit(solution)/shard_map/ppermute | solution.py:60
  51.4 1.2 %collective-permute-start.10 = (f32[40,1024]{1,0:T(8,128)S(1)}, f32[40,1024]{1,0:T(8,128)S(1)}, u32[]{:S(2)}, u32[]{:S(2)}) collective-permute-start(f32[40,1024]{1,0:T(8,128)S(1)} %slice.107), channel_id=1, source_target_pairs={{0,2},{1,3},{2,0},{3,1},{4,6},{5,7},{6,4},{7,5},{8,10},{9,11},{10,... | collective-permute-start | bytes 491528 | tf_op jit(solution)/shard_map/ppermute | solution.py:60
  52.6 4.4 %collective-permute-done.8 = f32[40,1024]{1,0:T(8,128)S(1)} collective-permute-done((f32[40,1024]{1,0:T(8,128)S(1)}, f32[40,1024]{1,0:T(8,128)S(1)}, u32[]{:S(2)}, u32[]{:S(2)}) %collective-permute-start.8) | collective-permute-done | bytes 163872 | tf_op jit(solution)/shard_map/ppermute | solution.py:60
  57.2 2.5 %collective-permute-done.10 = f32[40,1024]{1,0:T(8,128)S(1)} collective-permute-done((f32[40,1024]{1,0:T(8,128)S(1)}, f32[40,1024]{1,0:T(8,128)S(1)}, u32[]{:S(2)}, u32[]{:S(2)}) %collective-permute-start.10) | collective-permute-done | bytes 163872 | tf_op jit(solution)/shard_map/ppermute | solution.py:60
  60.1 1.4 %collective-permute-start.11 = (f32[3,40]{1,0:T(4,128)S(1)}, f32[3,40]{1,0:T(4,128)S(1)}, u32[]{:S(2)}, u32[]{:S(2)}) collective-permute-start(f32[3,40]{1,0:T(4,128)S(1)} %pad_maximum_fusion), channel_id=1, source_target_pairs={{0,4},{4,0},{8,12},{12,8},{16,20},{20,16},{24,28},{28,24},{1,5},{5... | collective-permute-start | bytes 1448 | tf_op jit(solution)/shard_map/ppermute | solution.py:93
  61.5 1.6 %collective-permute-start.12 = (f32[3,40]{1,0:T(4,128)S(1)}, f32[3,40]{1,0:T(4,128)S(1)}, u32[]{:S(2)}, u32[]{:S(2)}) collective-permute-start(f32[3,40]{1,0:T(4,128)S(1)} %pad_maximum_fusion), channel_id=1, source_target_pairs={{0,8},{4,12},{8,0},{12,4},{16,24},{20,28},{24,16},{28,20},{1,9},{5... | collective-permute-start | bytes 1448 | tf_op jit(solution)/shard_map/ppermute | solution.py:93
  63.7 1.3 %collective-permute-done.12 = f32[3,40]{1,0:T(4,128)S(1)} collective-permute-done((f32[3,40]{1,0:T(4,128)S(1)}, f32[3,40]{1,0:T(4,128)S(1)}, u32[]{:S(2)}, u32[]{:S(2)}) %collective-permute-start.12) | collective-permute-done | bytes 512 | tf_op jit(solution)/shard_map/ppermute | solution.py:93
  65.1 2.5 %collective-permute-done.13 = f32[3,40]{1,0:T(4,128)S(1)} collective-permute-done((f32[3,40]{1,0:T(4,128)S(1)}, f32[3,40]{1,0:T(4,128)S(1)}, u32[]{:S(2)}, u32[]{:S(2)}) %collective-permute-start.13) | collective-permute-done | bytes 512 | tf_op jit(solution)/shard_map/ppermute | solution.py:93
  67.6 2.7 %collective-permute-start.14 = (f32[3,40]{1,0:T(4,128)S(1)}, f32[3,40]{1,0:T(4,128)S(1)}, u32[]{:S(2)}, u32[]{:S(2)}) collective-permute-start(f32[3,40]{1,0:T(4,128)S(1)} %pad_maximum_fusion.1), channel_id=1, source_target_pairs={{0,16},{4,20},{8,24},{12,28},{16,0},{20,4},{24,8},{28,12},{1,17},{... | collective-permute-start | bytes 1448 | tf_op jit(solution)/shard_map/ppermute | solution.py:97
  70.9 1.2 %collective-permute-done.14 = f32[3,40]{1,0:T(4,128)S(1)} collective-permute-done((f32[3,40]{1,0:T(4,128)S(1)}, f32[3,40]{1,0:T(4,128)S(1)}, u32[]{:S(2)}, u32[]{:S(2)}) %collective-permute-start.14) | collective-permute-done | bytes 512 | tf_op jit(solution)/shard_map/ppermute | solution.py:97
  72.3 1.1 %collective-permute-done.15 = f32[160]{0:T(256)S(1)} collective-permute-done((f32[160]{0:T(256)S(1)}, f32[160]{0:T(256)S(1)}, u32[]{:S(2)}, u32[]{:S(2)}) %collective-permute-start.15) | collective-permute-done | bytes 672 | tf_op jit(solution)/shard_map/ppermute | solution.py:109
  73.6 1.5 %collective-permute-start.16 = (f32[160]{0:T(256)S(1)}, f32[160]{0:T(256)S(1)}, u32[]{:S(2)}, u32[]{:S(2)}) collective-permute-start(f32[160]{0:T(256)S(1)} %add_dynamic-update-slice_fusion), channel_id=1, source_target_pairs={{0,2},{1,3},{2,0},{3,1},{4,6},{5,7},{6,4},{7,5},{8,10},{9,11},{10,... | collective-permute-start | bytes 1928 | tf_op jit(solution)/shard_map/ppermute | solution.py:109
  75.8 1.3 %collective-permute-done.16 = f32[160]{0:T(256)S(1)} collective-permute-done((f32[160]{0:T(256)S(1)}, f32[160]{0:T(256)S(1)}, u32[]{:S(2)}, u32[]{:S(2)}) %collective-permute-start.16) | collective-permute-done | bytes 672 | tf_op jit(solution)/shard_map/ppermute | solution.py:109
  (78 shorter events, 10.2 us)
Async XLA Ops:
  0.6 17.6 %copy-start = (s32[256]{0:T(256)S(1)}, s32[256]{0:T(256)}, u32[]{:S(2)}) copy-start(s32[256]{0:T(256)} %param.12) | copy-start | bytes 3076
  0.6 19.8 %collective-permute-start = (bf16[32,4096]{1,0:T(8,128)(2,1)}, bf16[32,4096]{1,0:T(8,128)(2,1)S(1)}, u32[]{:S(2)}, u32[]{:S(2)}) collective-permute-start(bf16[32,4096]{1,0:T(8,128)(2,1)} %param.9), channel_id=1, source_target_pairs={{0,8},{8,16},{16,24},{24,28},{28,20},{20,12},{12,4},{4,0},{1,9},{9... | collective-permute-start | bytes 786440 | tf_op jit(solution)/shard_map/ppermute | solution.py:39
  3.7 18.8 %collective-permute-start.4 = (bf16[32,4096]{1,0:T(8,128)(2,1)}, bf16[32,4096]{1,0:T(8,128)(2,1)S(1)}, u32[]{:S(2)}, u32[]{:S(2)}) collective-permute-start(bf16[32,4096]{1,0:T(8,128)(2,1)} %param.9), channel_id=1, source_target_pairs={{8,0},{16,8},{24,16},{28,24},{20,28},{12,20},{4,12},{0,4},{9,1},{1... | collective-permute-start | bytes 786440 | tf_op jit(solution)/shard_map/ppermute | solution.py:42
  6.5 12.6 %copy-start.4 = (s32[8]{0:T(128)S(1)}, s32[8]{0:T(128)}, u32[]{:S(2)}) copy-start(s32[8]{0:T(128)} %constant.206.clone) | copy-start | bytes 100
  6.5 13.2 %copy-start.3 = (s32[8]{0:T(128)S(1)}, s32[8]{0:T(128)}, u32[]{:S(2)}) copy-start(s32[8]{0:T(128)} %constant.207) | copy-start | bytes 100
  20.5 7.8 %collective-permute-start.1 = (bf16[32,4096]{1,0:T(8,128)(2,1)S(1)}, bf16[32,4096]{1,0:T(8,128)(2,1)S(1)}, u32[]{:S(2)}, u32[]{:S(2)}) collective-permute-start(bf16[32,4096]{1,0:T(8,128)(2,1)S(1)} %collective-permute-done), channel_id=1, source_target_pairs={{0,8},{8,16},{16,24},{24,28},{28,20},{20,12},{12,4},{4,0},{1,9},{9... | collective-permute-start | bytes 786440 | tf_op jit(solution)/shard_map/ppermute | solution.py:39
  22.6 7.5 %collective-permute-start.5 = (bf16[32,4096]{1,0:T(8,128)(2,1)S(1)}, bf16[32,4096]{1,0:T(8,128)(2,1)S(1)}, u32[]{:S(2)}, u32[]{:S(2)}) collective-permute-start(bf16[32,4096]{1,0:T(8,128)(2,1)S(1)} %collective-permute-done.4), channel_id=1, source_target_pairs={{8,0},{16,8},{24,16},{28,24},{20,28},{12,20},{4,12},{0,4},{9,1},{1... | collective-permute-start | bytes 786440 | tf_op jit(solution)/shard_map/ppermute | solution.py:42
  28.3 6.9 %collective-permute-start.2 = (bf16[32,4096]{1,0:T(8,128)(2,1)S(1)}, bf16[32,4096]{1,0:T(8,128)(2,1)S(1)}, u32[]{:S(2)}, u32[]{:S(2)}) collective-permute-start(bf16[32,4096]{1,0:T(8,128)(2,1)S(1)} %collective-permute-done.1), channel_id=1, source_target_pairs={{0,8},{8,16},{16,24},{24,28},{28,20},{20,12},{12,4},{4,0},{1,9},{9... | collective-permute-start | bytes 786440 | tf_op jit(solution)/shard_map/ppermute | solution.py:39
  30.0 11.6 %collective-permute-start.6 = (bf16[32,4096]{1,0:T(8,128)(2,1)S(1)}, bf16[32,4096]{1,0:T(8,128)(2,1)S(1)}, u32[]{:S(2)}, u32[]{:S(2)}) collective-permute-start(bf16[32,4096]{1,0:T(8,128)(2,1)S(1)} %collective-permute-done.5), channel_id=1, source_target_pairs={{8,0},{16,8},{24,16},{28,24},{20,28},{12,20},{4,12},{0,4},{9,1},{1... | collective-permute-start | bytes 786440 | tf_op jit(solution)/shard_map/ppermute | solution.py:42
  35.2 6.4 %collective-permute-start.3 = (bf16[32,4096]{1,0:T(8,128)(2,1)S(1)}, bf16[32,4096]{1,0:T(8,128)(2,1)S(1)}, u32[]{:S(2)}, u32[]{:S(2)}) collective-permute-start(bf16[32,4096]{1,0:T(8,128)(2,1)S(1)} %collective-permute-done.2), channel_id=1, source_target_pairs={{0,8},{8,16},{16,24},{24,28},{28,20},{20,12},{12,4},{4,0},{1,9},{9... | collective-permute-start | bytes 786440 | tf_op jit(solution)/shard_map/ppermute | solution.py:39
  41.7 5.9 %slice-start = ((s8[8388608]{0:T(1024)(128)(4,1)}), s8[4194304]{0:T(1024)(128)(4,1)S(1)}, s32[]{:S(2)}) async-start(s8[8388608]{0:T(1024)(128)(4,1)} %bitcast.176), calls=%async_computation | async-start | bytes 8388608
  42.3 5.4 %slice-start.1 = ((s8[8388608]{0:T(1024)(128)(4,1)}), s8[4194304]{0:T(1024)(128)(4,1)S(1)}, s32[]{:S(2)}) async-start(s8[8388608]{0:T(1024)(128)(4,1)} %bitcast.176), calls=%async_computation.1 | async-start | bytes 8388608
  47.6 2.3 %collective-permute-start.7 = (f32[80,1024]{1,0:T(8,128)S(1)}, f32[80,1024]{1,0:T(8,128)S(1)}, u32[]{:S(2)}, u32[]{:S(2)}) collective-permute-start(f32[80,1024]{1,0:T(8,128)S(1)} %slice.101), channel_id=1, source_target_pairs={{0,1},{1,0},{2,3},{3,2},{4,5},{5,4},{6,7},{7,6},{8,9},{9,8},{10,11... | collective-permute-start | bytes 983048 | tf_op jit(solution)/shard_map/ppermute | solution.py:60
  49.3 2.1 %collective-permute-start.9 = (f32[80,1024]{1,0:T(8,128)S(1)}, f32[80,1024]{1,0:T(8,128)S(1)}, u32[]{:S(2)}, u32[]{:S(2)}) collective-permute-start(f32[80,1024]{1,0:T(8,128)S(1)} %slice.105), channel_id=1, source_target_pairs={{0,1},{1,0},{2,3},{3,2},{4,5},{5,4},{6,7},{7,6},{8,9},{9,8},{10,11... | collective-permute-start | bytes 983048 | tf_op jit(solution)/shard_map/ppermute | solution.py:60
  49.8 25.3 %copy-start.1 = (s32[8]{0:T(128)S(1)}, s32[8]{0:T(128)}, u32[]{:S(2)}) copy-start(s32[8]{0:T(128)} %param.11) | copy-start | bytes 100
  49.9 28.0 %copy-start.2 = (f32[32]{0:T(128)S(1)}, f32[32]{0:T(128)}, u32[]{:S(2)}) copy-start(f32[32]{0:T(128)} %param.13) | copy-start | bytes 388
  49.9 7.1 %collective-permute-start.8 = (f32[40,1024]{1,0:T(8,128)S(1)}, f32[40,1024]{1,0:T(8,128)S(1)}, u32[]{:S(2)}, u32[]{:S(2)}) collective-permute-start(f32[40,1024]{1,0:T(8,128)S(1)} %slice.103), channel_id=1, source_target_pairs={{0,2},{1,3},{2,0},{3,1},{4,6},{5,7},{6,4},{7,5},{8,10},{9,11},{10,... | collective-permute-start | bytes 491528 | tf_op jit(solution)/shard_map/ppermute | solution.py:60
  51.4 8.2 %collective-permute-start.10 = (f32[40,1024]{1,0:T(8,128)S(1)}, f32[40,1024]{1,0:T(8,128)S(1)}, u32[]{:S(2)}, u32[]{:S(2)}) collective-permute-start(f32[40,1024]{1,0:T(8,128)S(1)} %slice.107), channel_id=1, source_target_pairs={{0,2},{1,3},{2,0},{3,1},{4,6},{5,7},{6,4},{7,5},{8,10},{9,11},{10,... | collective-permute-start | bytes 491528 | tf_op jit(solution)/shard_map/ppermute | solution.py:60
  60.1 3.7 %collective-permute-start.11 = (f32[3,40]{1,0:T(4,128)S(1)}, f32[3,40]{1,0:T(4,128)S(1)}, u32[]{:S(2)}, u32[]{:S(2)}) collective-permute-start(f32[3,40]{1,0:T(4,128)S(1)} %pad_maximum_fusion), channel_id=1, source_target_pairs={{0,4},{4,0},{8,12},{12,8},{16,20},{20,16},{24,28},{28,24},{1,5},{5... | collective-permute-start | bytes 1448 | tf_op jit(solution)/shard_map/ppermute | solution.py:93
  61.5 3.6 %collective-permute-start.12 = (f32[3,40]{1,0:T(4,128)S(1)}, f32[3,40]{1,0:T(4,128)S(1)}, u32[]{:S(2)}, u32[]{:S(2)}) collective-permute-start(f32[3,40]{1,0:T(4,128)S(1)} %pad_maximum_fusion), channel_id=1, source_target_pairs={{0,8},{4,12},{8,0},{12,4},{16,24},{20,28},{24,16},{28,20},{1,9},{5... | collective-permute-start | bytes 1448 | tf_op jit(solution)/shard_map/ppermute | solution.py:93
  63.1 4.5 %collective-permute-start.13 = (f32[3,40]{1,0:T(4,128)S(1)}, f32[3,40]{1,0:T(4,128)S(1)}, u32[]{:S(2)}, u32[]{:S(2)}) collective-permute-start(f32[3,40]{1,0:T(4,128)S(1)} %pad_maximum_fusion), channel_id=1, source_target_pairs={{0,12},{4,8},{8,4},{12,0},{16,28},{20,24},{24,20},{28,16},{1,13},{... | collective-permute-start | bytes 1448 | tf_op jit(solution)/shard_map/ppermute | solution.py:93
  67.6 4.5 %collective-permute-start.14 = (f32[3,40]{1,0:T(4,128)S(1)}, f32[3,40]{1,0:T(4,128)S(1)}, u32[]{:S(2)}, u32[]{:S(2)}) collective-permute-start(f32[3,40]{1,0:T(4,128)S(1)} %pad_maximum_fusion.1), channel_id=1, source_target_pairs={{0,16},{4,20},{8,24},{12,28},{16,0},{20,4},{24,8},{28,12},{1,17},{... | collective-permute-start | bytes 1448 | tf_op jit(solution)/shard_map/ppermute | solution.py:97
  72.2 1.2 %collective-permute-start.15 = (f32[160]{0:T(256)S(1)}, f32[160]{0:T(256)S(1)}, u32[]{:S(2)}, u32[]{:S(2)}) collective-permute-start(f32[160]{0:T(256)S(1)} %get-tuple-element.13), channel_id=1, source_target_pairs={{0,1},{1,0},{2,3},{3,2},{4,5},{5,4},{6,7},{7,6},{8,9},{9,8},{10,11... | collective-permute-start | bytes 1928 | tf_op jit(solution)/shard_map/ppermute | solution.py:109
  73.6 3.6 %collective-permute-start.16 = (f32[160]{0:T(256)S(1)}, f32[160]{0:T(256)S(1)}, u32[]{:S(2)}, u32[]{:S(2)}) collective-permute-start(f32[160]{0:T(256)S(1)} %add_dynamic-update-slice_fusion), channel_id=1, source_target_pairs={{0,2},{1,3},{2,0},{3,1},{4,6},{5,7},{6,4},{7,5},{8,10},{9,11},{10,... | collective-permute-start | bytes 1928 | tf_op jit(solution)/shard_map/ppermute | solution.py:109

commit v16 on v7

--- a/solution.py
+++ b/solution.py
@@ -135,7 +135,7 @@
         own_batch = own_rows // slot_count
         is_live = own_rows % slot_count < jnp.take(lengths, own_batch)
         own_slot = jnp.clip(jnp.take(starts, own_batch) + own_rows % slot_count, 0, live_count - 1)
-        own_values = jnp.take(all_values, own_slot)
+        own_values = jnp.sum(jnp.where(own_slot[:, None] == jnp.arange(live_count, dtype=jnp.int32)[None, :], all_values[None, :], 0.0), axis=1)
         ref_logprob = jnp.where(is_live, own_values, 0.0)
         ratio_log = jnp.clip(ref_logprob - policy_logprobs, -20.0, 20.0)
         kl_value = jnp.where(is_live, jnp.minimum(jnp.exp(ratio_log) - ratio_log - 1.0, 10.0), 0.0)

time: 69.1 us -> 68.6 us (level)
  local copies, waits for them, and re-layouts: 5.32 us -> 4.61 us
    gather x1 -> x0, local copies, waits for them, and re-layouts: 0.71 us -> none  [on_device(): own_values = jnp.take(all_values, own_slot)]
    ppermute x2, waiting for transfers between devices: 2.47 us -> 1.77 us  [doubling_gather(): other = lax.ppermute(out, 'vocab', [(i, i ^ bit) for i in range(size)])]
where the time goes in v16:
time: 68.6 us; the launch traced here: 68.4 us
  waiting for transfers between devices  31.5 us (46%)
  starting transfers between devices  18.5 us (27%)
  matrix products  7.93 us (12%)
  other arithmetic  4.88 us (7%)
  local copies, waits for them, and re-layouts  4.61 us (7%)
  between operations  0.92 us (1%)
    ppermute x4, waiting for transfers between devices, ring_gather(): ahead = lax.ppermute(ahead, 'dp', fwd)  15.5 us
    ppermute x2, waiting for transfers between devices, halving_scatter(): got = lax.ppermute(send, 'vocab', [(i, i ^ bit) for i in range(size)])  9.12 us
    ppermute x4, starting transfers between devices, ring_gather(): ahead = lax.ppermute(ahead, 'dp', fwd)  8.21 us
    dot_general x1, matrix products, on_device(): jnp.dot(full_rows, head_weight, preferred_element_type=jnp.float32)  7.37 us
    ppermute x3, starting transfers between devices, merge_stats(): lax.ppermute(stats, 'dp', [(i, i ^ bit * k) for i in range(size)])  3.55 us
    ppermute x3, waiting for transfers between devices, merge_stats(): lax.ppermute(stats, 'dp', [(i, i ^ bit * k) for i in range(size)])  3.2 us
    ppermute x1, starting transfers between devices, merge_stats(): lax.ppermute(stats, 'dp', [(i, i ^ bit) for i in range(size)])  2.65 us
    ppermute x1, waiting for transfers between devices, merge_stats(): lax.ppermute(stats, 'dp', [(i, i ^ bit) for i in range(size)])  1.89 us
  transfers between devices with their start and end apart: 15, of which 12 were waited for; matrix products, arithmetic and copies ran while one was open for 11% of the time, Pallas kernels for 0%

profile of v16, /device:TPU:0, one launch (start us, length us, event | category | flops | bytes accessed | tf_op | source)
XLA Modules:
  0.0 68.4 jit_solution(7296836779825313175)
XLA Ops:
  0.6 3.1 %collective-permute-start = (bf16[32,4096]{1,0:T(8,128)(2,1)}, bf16[32,4096]{1,0:T(8,128)(2,1)S(1)}, u32[]{:S(2)}, u32[]{:S(2)}) collective-permute-start(bf16[32,4096]{1,0:T(8,128)(2,1)} %param.13), channel_id=1, source_target_pairs={{0,8},{8,16},{16,24},{24,28},{28,20},{20,12},{12,4},{4,0},{1,9},{9... | collective-permute-start | bytes 786440 | tf_op jit(solution)/shard_map/ppermute | solution.py:39
  3.8 1.0 %bitcast_dynamic-update-slice_fusion.7 = bf16[8,32,4096]{2,1,0:T(8,128)(2,1)S(1)} fusion(bf16[32,4096]{1,0:T(8,128)(2,1)} %param.13), kind=kLoop, calls=%fused_computation.17 | loop fusion | bytes 524288
  4.8 0.8 %reduce-window.8 = s32[8,1]{0,1:T(1,128)S(1)} reduce-window(s32[8,1]{0,1:T(1,128)} %bitcast.166, s32[]{:T(128)} %constant.160.clone.1), window={size=8x1 pad=7_0x0_0}, to_apply=%region_0.2 | reduce-window | flops 56 | bytes 68 | tf_op jit(solution)/shard_map/reduce-window.3
  6.5 1.2 %dynamic_slice.7 = s32[1]{0:T(128)} dynamic-slice(s32[8]{0:T(128)} %constant.183.clone, s32[]{:T(128)S(6)} %select_n.122), dynamic_slice_sizes={1} | dynamic-slice | bytes 12 | tf_op jit(solution)/shard_map/dynamic_slice | solution.py:46
  7.7 1.3 %and_select_fusion.1 = s32[8]{0:T(128)S(1)} fusion(s32[8]{0:T(128)} %constant.222, s32[]{:T(128)} %bitcast.2), kind=kLoop, calls=%fused_computation.39 | loop fusion | flops 96 | bytes 68 | tf_op jit(solution)/shard_map/jit(remainder)/select_n | solution.py:47
  9.2 1.0 %collective-permute-done = bf16[32,4096]{1,0:T(8,128)(2,1)S(1)} collective-permute-done((bf16[32,4096]{1,0:T(8,128)(2,1)}, bf16[32,4096]{1,0:T(8,128)(2,1)S(1)}, u32[]{:S(2)}, u32[]{:S(2)}) %collective-permute-start) | collective-permute-done | bytes 262176 | tf_op jit(solution)/shard_map/ppermute | solution.py:39
  10.2 1.8 %collective-permute-start.1 = (bf16[32,4096]{1,0:T(8,128)(2,1)S(1)}, bf16[32,4096]{1,0:T(8,128)(2,1)S(1)}, u32[]{:S(2)}, u32[]{:S(2)}) collective-permute-start(bf16[32,4096]{1,0:T(8,128)(2,1)S(1)} %collective-permute-done), channel_id=1, source_target_pairs={{0,8},{8,16},{16,24},{24,28},{28,20},{20,12},{12,4},{4,0},{1,9},{9... | collective-permute-start | bytes 786440 | tf_op jit(solution)/shard_map/ppermute | solution.py:39
  12.3 5.4 %collective-permute-done.1 = bf16[32,4096]{1,0:T(8,128)(2,1)S(1)} collective-permute-done((bf16[32,4096]{1,0:T(8,128)(2,1)S(1)}, bf16[32,4096]{1,0:T(8,128)(2,1)S(1)}, u32[]{:S(2)}, u32[]{:S(2)}) %collective-permute-start.1) | collective-permute-done | bytes 262176 | tf_op jit(solution)/shard_map/ppermute | solution.py:39
  17.7 1.5 %collective-permute-start.2 = (bf16[32,4096]{1,0:T(8,128)(2,1)S(1)}, bf16[32,4096]{1,0:T(8,128)(2,1)S(1)}, u32[]{:S(2)}, u32[]{:S(2)}) collective-permute-start(bf16[32,4096]{1,0:T(8,128)(2,1)S(1)} %collective-permute-done.1), channel_id=1, source_target_pairs={{0,8},{8,16},{16,24},{24,28},{28,20},{20,12},{12,4},{4,0},{1,9},{9... | collective-permute-start | bytes 786440 | tf_op jit(solution)/shard_map/ppermute | solution.py:39
  19.8 4.5 %collective-permute-done.2 = bf16[32,4096]{1,0:T(8,128)(2,1)S(1)} collective-permute-done((bf16[32,4096]{1,0:T(8,128)(2,1)S(1)}, bf16[32,4096]{1,0:T(8,128)(2,1)S(1)}, u32[]{:S(2)}, u32[]{:S(2)}) %collective-permute-start.2) | collective-permute-done | bytes 262176 | tf_op jit(solution)/shard_map/ppermute | solution.py:39
  24.3 1.7 %collective-permute-start.3 = (bf16[32,4096]{1,0:T(8,128)(2,1)S(1)}, bf16[32,4096]{1,0:T(8,128)(2,1)S(1)}, u32[]{:S(2)}, u32[]{:S(2)}) collective-permute-start(bf16[32,4096]{1,0:T(8,128)(2,1)S(1)} %collective-permute-done.2), channel_id=1, source_target_pairs={{0,8},{8,16},{16,24},{24,28},{28,20},{20,12},{12,4},{4,0},{1,9},{9... | collective-permute-start | bytes 786440 | tf_op jit(solution)/shard_map/ppermute | solution.py:39
  26.0 4.6 %collective-permute-done.3 = bf16[32,4096]{1,0:T(8,128)(2,1)S(1)} collective-permute-done((bf16[32,4096]{1,0:T(8,128)(2,1)S(1)}, bf16[32,4096]{1,0:T(8,128)(2,1)S(1)}, u32[]{:S(2)}, u32[]{:S(2)}) %collective-permute-start.3) | collective-permute-done | bytes 262176 | tf_op jit(solution)/shard_map/ppermute | solution.py:39
  31.3 7.4 %fusion.28 = f32[160,2048]{1,0:T(8,128)S(1)} fusion(bf16[160,4096]{1,0:T(8,128)(2,1)S(1)} %convolution_convert_fusion, bf16[4096,2048]{1,0:T(8,128)(2,1)} %param.14), kind=kOutput, calls=%fused_computation.105 | convolution fusion | flops 2684354560 | bytes 19398656 | tf_op jit(solution)/shard_map/dot_general | solution.py:123
  39.0 0.8 %gather_fusion = s32[40]{0:T(128)S(1)} fusion(s32[256]{0:T(256)S(1)} %copy-done, s32[1024]{0:T(1024)S(1)} %pad_clamp_fusion), kind=kCustom, calls=%fused_computation.2 | custom fusion | bytes 480 | tf_op jit(solution)/shard_map/jit(_take)/gather | solution.py:126
  39.8 1.1 %collective-permute-done.7 = f32[80,2048]{1,0:T(8,128)S(1)} collective-permute-done((f32[80,2048]{1,0:T(8,128)S(1)}, f32[80,2048]{1,0:T(8,128)S(1)}, u32[]{:S(2)}, u32[]{:S(2)}) %collective-permute-start.7) | collective-permute-done | bytes 655392 | tf_op jit(solution)/shard_map/ppermute | solution.py:66
  41.0 1.7 %collective-permute-start.8 = (f32[40,2048]{1,0:T(8,128)S(1)}, f32[40,2048]{1,0:T(8,128)S(1)}, u32[]{:S(2)}, u32[]{:S(2)}) collective-permute-start(f32[40,2048]{1,0:T(8,128)S(1)} %select_bitcast_fusion.1), channel_id=1, source_target_pairs={{0,2},{1,3},{2,0},{3,1},{4,6},{5,7},{6,4},{7,5},{8,10},{9,11},{10,... | collective-permute-start | bytes 983048 | tf_op jit(solution)/shard_map/ppermute | solution.py:66
  42.9 8.0 %collective-permute-done.8 = f32[40,2048]{1,0:T(8,128)S(1)} collective-permute-done((f32[40,2048]{1,0:T(8,128)S(1)}, f32[40,2048]{1,0:T(8,128)S(1)}, u32[]{:S(2)}, u32[]{:S(2)}) %collective-permute-start.8) | collective-permute-done | bytes 327712 | tf_op jit(solution)/shard_map/ppermute | solution.py:66
  51.3 1.8 %collective-permute-start.10 = (f32[3,40]{1,0:T(4,128)S(1)}, f32[3,40]{1,0:T(4,128)S(1)}, u32[]{:S(2)}, u32[]{:S(2)}) collective-permute-start(f32[3,40]{1,0:T(4,128)S(1)} %pad_maximum_fusion), channel_id=1, source_target_pairs={{0,8},{4,12},{8,0},{12,4},{16,24},{20,28},{24,16},{28,20},{1,9},{5... | collective-permute-start | bytes 1448 | tf_op jit(solution)/shard_map/ppermute | solution.py:83
  53.1 1.4 %collective-permute-start.11 = (f32[3,40]{1,0:T(4,128)S(1)}, f32[3,40]{1,0:T(4,128)S(1)}, u32[]{:S(2)}, u32[]{:S(2)}) collective-permute-start(f32[3,40]{1,0:T(4,128)S(1)} %pad_maximum_fusion), channel_id=1, source_target_pairs={{0,12},{4,8},{8,4},{12,0},{16,28},{20,24},{24,20},{28,16},{1,13},{... | collective-permute-start | bytes 1448 | tf_op jit(solution)/shard_map/ppermute | solution.py:83
  54.9 2.6 %collective-permute-done.11 = f32[3,40]{1,0:T(4,128)S(1)} collective-permute-done((f32[3,40]{1,0:T(4,128)S(1)}, f32[3,40]{1,0:T(4,128)S(1)}, u32[]{:S(2)}, u32[]{:S(2)}) %collective-permute-start.11) | collective-permute-done | bytes 512 | tf_op jit(solution)/shard_map/ppermute | solution.py:83
  58.1 2.6 %collective-permute-start.12 = (f32[3,40]{1,0:T(4,128)S(1)}, f32[3,40]{1,0:T(4,128)S(1)}, u32[]{:S(2)}, u32[]{:S(2)}) collective-permute-start(f32[3,40]{1,0:T(4,128)S(1)} %pad_maximum_fusion.1), channel_id=1, source_target_pairs={{0,16},{4,20},{8,24},{12,28},{16,0},{20,4},{24,8},{28,12},{1,17},{... | collective-permute-start | bytes 1448 | tf_op jit(solution)/shard_map/ppermute | solution.py:87
  60.7 1.9 %collective-permute-done.12 = f32[3,40]{1,0:T(4,128)S(1)} collective-permute-done((f32[3,40]{1,0:T(4,128)S(1)}, f32[3,40]{1,0:T(4,128)S(1)}, u32[]{:S(2)}, u32[]{:S(2)}) %collective-permute-start.12) | collective-permute-done | bytes 512 | tf_op jit(solution)/shard_map/ppermute | solution.py:87
  64.1 1.5 %collective-permute-start.14 = (f32[160]{0:T(256)S(1)}, f32[160]{0:T(256)S(1)}, u32[]{:S(2)}, u32[]{:S(2)}) collective-permute-start(f32[160]{0:T(256)S(1)} %add_dynamic-update-slice_fusion), channel_id=1, source_target_pairs={{0,2},{1,3},{2,0},{3,1},{4,6},{5,7},{6,4},{7,5},{8,10},{9,11},{10,... | collective-permute-start | bytes 1928 | tf_op jit(solution)/shard_map/ppermute | solution.py:99
  66.3 1.3 %collective-permute-done.14 = f32[160]{0:T(256)S(1)} collective-permute-done((f32[160]{0:T(256)S(1)}, f32[160]{0:T(256)S(1)}, u32[]{:S(2)}, u32[]{:S(2)}) %collective-permute-start.14) | collective-permute-done | bytes 672 | tf_op jit(solution)/shard_map/ppermute | solution.py:99
  (55 shorter events, 7.1 us)
Async XLA Ops:
  0.6 38.4 %copy-start = (s32[256]{0:T(256)S(1)}, s32[256]{0:T(256)}, u32[]{:S(2)}) copy-start(s32[256]{0:T(256)} %param.16) | copy-start | bytes 3076
  0.6 9.5 %collective-permute-start = (bf16[32,4096]{1,0:T(8,128)(2,1)}, bf16[32,4096]{1,0:T(8,128)(2,1)S(1)}, u32[]{:S(2)}, u32[]{:S(2)}) collective-permute-start(bf16[32,4096]{1,0:T(8,128)(2,1)} %param.13), channel_id=1, source_target_pairs={{0,8},{8,16},{16,24},{24,28},{28,20},{20,12},{12,4},{4,0},{1,9},{9... | collective-permute-start | bytes 786440 | tf_op jit(solution)/shard_map/ppermute | solution.py:39
  3.7 8.3 %collective-permute-start.4 = (bf16[32,4096]{1,0:T(8,128)(2,1)}, bf16[32,4096]{1,0:T(8,128)(2,1)S(1)}, u32[]{:S(2)}, u32[]{:S(2)}) collective-permute-start(bf16[32,4096]{1,0:T(8,128)(2,1)} %param.13), channel_id=1, source_target_pairs={{8,0},{16,8},{24,16},{28,24},{20,28},{12,20},{4,12},{0,4},{9,1},{1... | collective-permute-start | bytes 786440 | tf_op jit(solution)/shard_map/ppermute | solution.py:42
  10.2 7.5 %collective-permute-start.1 = (bf16[32,4096]{1,0:T(8,128)(2,1)S(1)}, bf16[32,4096]{1,0:T(8,128)(2,1)S(1)}, u32[]{:S(2)}, u32[]{:S(2)}) collective-permute-start(bf16[32,4096]{1,0:T(8,128)(2,1)S(1)} %collective-permute-done), channel_id=1, source_target_pairs={{0,8},{8,16},{16,24},{24,28},{28,20},{20,12},{12,4},{4,0},{1,9},{9... | collective-permute-start | bytes 786440 | tf_op jit(solution)/shard_map/ppermute | solution.py:39
  12.0 7.2 %collective-permute-start.5 = (bf16[32,4096]{1,0:T(8,128)(2,1)S(1)}, bf16[32,4096]{1,0:T(8,128)(2,1)S(1)}, u32[]{:S(2)}, u32[]{:S(2)}) collective-permute-start(bf16[32,4096]{1,0:T(8,128)(2,1)S(1)} %collective-permute-done.4), channel_id=1, source_target_pairs={{8,0},{16,8},{24,16},{28,24},{20,28},{12,20},{4,12},{0,4},{9,1},{1... | collective-permute-start | bytes 786440 | tf_op jit(solution)/shard_map/ppermute | solution.py:42
  17.7 6.6 %collective-permute-start.2 = (bf16[32,4096]{1,0:T(8,128)(2,1)S(1)}, bf16[32,4096]{1,0:T(8,128)(2,1)S(1)}, u32[]{:S(2)}, u32[]{:S(2)}) collective-permute-start(bf16[32,4096]{1,0:T(8,128)(2,1)S(1)} %collective-permute-done.1), channel_id=1, source_target_pairs={{0,8},{8,16},{16,24},{24,28},{28,20},{20,12},{12,4},{4,0},{1,9},{9... | collective-permute-start | bytes 786440 | tf_op jit(solution)/shard_map/ppermute | solution.py:39
  19.2 11.4 %collective-permute-start.6 = (bf16[32,4096]{1,0:T(8,128)(2,1)S(1)}, bf16[32,4096]{1,0:T(8,128)(2,1)S(1)}, u32[]{:S(2)}, u32[]{:S(2)}) collective-permute-start(bf16[32,4096]{1,0:T(8,128)(2,1)S(1)} %collective-permute-done.5), channel_id=1, source_target_pairs={{8,0},{16,8},{24,16},{28,24},{20,28},{12,20},{4,12},{0,4},{9,1},{1... | collective-permute-start | bytes 786440 | tf_op jit(solution)/shard_map/ppermute | solution.py:42
  24.3 6.4 %collective-permute-start.3 = (bf16[32,4096]{1,0:T(8,128)(2,1)S(1)}, bf16[32,4096]{1,0:T(8,128)(2,1)S(1)}, u32[]{:S(2)}, u32[]{:S(2)}) collective-permute-start(bf16[32,4096]{1,0:T(8,128)(2,1)S(1)} %collective-permute-done.2), channel_id=1, source_target_pairs={{0,8},{8,16},{16,24},{24,28},{28,20},{20,12},{12,4},{4,0},{1,9},{9... | collective-permute-start | bytes 786440 | tf_op jit(solution)/shard_map/ppermute | solution.py:39
  38.8 2.2 %collective-permute-start.7 = (f32[80,2048]{1,0:T(8,128)S(1)}, f32[80,2048]{1,0:T(8,128)S(1)}, u32[]{:S(2)}, u32[]{:S(2)}) collective-permute-start(f32[80,2048]{1,0:T(8,128)S(1)} %select_bitcast_fusion), channel_id=1, source_target_pairs={{0,1},{1,0},{2,3},{3,2},{4,5},{5,4},{6,7},{7,6},{8,9},{9,8},{10,11... | collective-permute-start | bytes 1966088 | tf_op jit(solution)/shard_map/ppermute | solution.py:66
  39.8 25.8 %copy-start.1 = (s32[8]{0:T(128)S(1)}, s32[8]{0:T(128)}, u32[]{:S(2)}) copy-start(s32[8]{0:T(128)} %param.15) | copy-start | bytes 100
  39.8 28.0 %copy-start.2 = (f32[32]{0:T(128)S(1)}, f32[32]{0:T(128)}, u32[]{:S(2)}) copy-start(f32[32]{0:T(128)} %param.17) | copy-start | bytes 388
  41.0 9.8 %collective-permute-start.8 = (f32[40,2048]{1,0:T(8,128)S(1)}, f32[40,2048]{1,0:T(8,128)S(1)}, u32[]{:S(2)}, u32[]{:S(2)}) collective-permute-start(f32[40,2048]{1,0:T(8,128)S(1)} %select_bitcast_fusion.1), channel_id=1, source_target_pairs={{0,2},{1,3},{2,0},{3,1},{4,6},{5,7},{6,4},{7,5},{8,10},{9,11},{10,... | collective-permute-start | bytes 983048 | tf_op jit(solution)/shard_map/ppermute | solution.py:66
  51.3 3.7 %collective-permute-start.10 = (f32[3,40]{1,0:T(4,128)S(1)}, f32[3,40]{1,0:T(4,128)S(1)}, u32[]{:S(2)}, u32[]{:S(2)}) collective-permute-start(f32[3,40]{1,0:T(4,128)S(1)} %pad_maximum_fusion), channel_id=1, source_target_pairs={{0,8},{4,12},{8,0},{12,4},{16,24},{20,28},{24,16},{28,20},{1,9},{5... | collective-permute-start | bytes 1448 | tf_op jit(solution)/shard_map/ppermute | solution.py:83
  53.1 4.5 %collective-permute-start.11 = (f32[3,40]{1,0:T(4,128)S(1)}, f32[3,40]{1,0:T(4,128)S(1)}, u32[]{:S(2)}, u32[]{:S(2)}) collective-permute-start(f32[3,40]{1,0:T(4,128)S(1)} %pad_maximum_fusion), channel_id=1, source_target_pairs={{0,12},{4,8},{8,4},{12,0},{16,28},{20,24},{24,20},{28,16},{1,13},{... | collective-permute-start | bytes 1448 | tf_op jit(solution)/shard_map/ppermute | solution.py:83
  54.5 3.6 %collective-permute-start.9 = (f32[3,40]{1,0:T(4,128)S(1)}, f32[3,40]{1,0:T(4,128)S(1)}, u32[]{:S(2)}, u32[]{:S(2)}) collective-permute-start(f32[3,40]{1,0:T(4,128)S(1)} %pad_maximum_fusion), channel_id=1, source_target_pairs={{0,4},{4,0},{8,12},{12,8},{16,20},{20,16},{24,28},{28,24},{1,5},{5... | collective-permute-start | bytes 1448 | tf_op jit(solution)/shard_map/ppermute | solution.py:83
  58.1 4.5 %collective-permute-start.12 = (f32[3,40]{1,0:T(4,128)S(1)}, f32[3,40]{1,0:T(4,128)S(1)}, u32[]{:S(2)}, u32[]{:S(2)}) collective-permute-start(f32[3,40]{1,0:T(4,128)S(1)} %pad_maximum_fusion.1), channel_id=1, source_target_pairs={{0,16},{4,20},{8,24},{12,28},{16,0},{20,4},{24,8},{28,12},{1,17},{... | collective-permute-start | bytes 1448 | tf_op jit(solution)/shard_map/ppermute | solution.py:87
  62.7 1.2 %collective-permute-start.13 = (f32[160]{0:T(256)S(1)}, f32[160]{0:T(256)S(1)}, u32[]{:S(2)}, u32[]{:S(2)}) collective-permute-start(f32[160]{0:T(256)S(1)} %get-tuple-element.31), channel_id=1, source_target_pairs={{0,1},{1,0},{2,3},{3,2},{4,5},{5,4},{6,7},{7,6},{8,9},{9,8},{10,11... | collective-permute-start | bytes 1928 | tf_op jit(solution)/shard_map/ppermute | solution.py:99
  64.1 3.6 %collective-permute-start.14 = (f32[160]{0:T(256)S(1)}, f32[160]{0:T(256)S(1)}, u32[]{:S(2)}, u32[]{:S(2)}) collective-permute-start(f32[160]{0:T(256)S(1)} %add_dynamic-update-slice_fusion), channel_id=1, source_target_pairs={{0,2},{1,3},{2,0},{3,1},{4,6},{5,7},{6,4},{7,5},{8,10},{9,11},{10,... | collective-permute-start | bytes 1928 | tf_op jit(solution)/shard_map/ppermute | solution.py:99

commit v17 on v16

--- a/solution.py
+++ b/solution.py
@@ -90,16 +90,18 @@
 
 
 def doubling_gather(values, first, size):
-    me = lax.axis_index("vocab")
     total = values.shape[0] * size
     out = jnp.zeros((total,), values.dtype)
     out = lax.dynamic_update_slice(out, values, (first,))
     bit = 1
+    other = jnp.zeros_like(out)
     while bit < size:
-        other = lax.ppermute(out, "vocab", [(i, i ^ bit) for i in range(size)])
-        out = out + other
+        if bit * 2 >= size:
+            other = lax.ppermute(out, "vocab", [(i, i ^ bit) for i in range(size)])
+        else:
+            out = out + lax.ppermute(out, "vocab", [(i, i ^ bit) for i in range(size)])
         bit *= 2
-    return out
+    return out, other
 
 
 def make_body(ring):
@@ -130,12 +132,13 @@
         picked = jnp.sum(jnp.where(columns == row_targets[:, None], logits, 0.0), axis=1)
         stats = merge_stats(jnp.stack([highest, exp_total, picked]), dp_size)
         logprob = stats[2] - (stats[0] + jnp.log(stats[1]))
-        all_values = doubling_gather(logprob, first, vocab_size)
+        mine, theirs = doubling_gather(logprob, first, vocab_size)
         own_rows = lax.axis_index("dp") * row_count + jnp.arange(row_count, dtype=jnp.int32)
         own_batch = own_rows // slot_count
         is_live = own_rows % slot_count < jnp.take(lengths, own_batch)
         own_slot = jnp.clip(jnp.take(starts, own_batch) + own_rows % slot_count, 0, live_count - 1)
-        own_values = jnp.sum(jnp.where(own_slot[:, None] == jnp.arange(live_count, dtype=jnp.int32)[None, :], all_values[None, :], 0.0), axis=1)
+        own_hit = own_slot[:, None] == jnp.arange(live_count, dtype=jnp.int32)[None, :]
+        own_values = jnp.sum(jnp.where(own_hit, mine[None, :], 0.0), axis=1) + jnp.sum(jnp.where(own_hit, theirs[None, :], 0.0), axis=1)
         ref_logprob = jnp.where(is_live, own_values, 0.0)
         ratio_log = jnp.clip(ref_logprob - policy_logprobs, -20.0, 20.0)
         kl_value = jnp.where(is_live, jnp.minimum(jnp.exp(ratio_log) - ratio_log - 1.0, 10.0), 0.0)

time: 68.6 us -> 68.6 us (level)
    ppermute x2 -> x1, waiting for transfers between devices: 1.77 us -> 1.33 us  [doubling_gather(): other = lax.ppermute(out, 'vocab', [(i, i ^ bit) for i in range(size)])]
    ppermute x2 -> x1, starting transfers between devices: 1.53 us -> 1.52 us  [doubling_gather(): other = lax.ppermute(out, 'vocab', [(i, i ^ bit) for i in range(size)])]
where the time goes in v17:
time: 68.6 us; the launch traced here: 68.4 us
  waiting for transfers between devices  31.5 us (46%)
  starting transfers between devices  18.5 us (27%)
  matrix products  7.93 us (12%)
  other arithmetic  4.88 us (7%)
  local copies, waits for them, and re-layouts  4.61 us (7%)
  between operations  0.92 us (1%)
    ppermute x4, waiting for transfers between devices, ring_gather(): ahead = lax.ppermute(ahead, 'dp', fwd)  15.5 us
    ppermute x2, waiting for transfers between devices, halving_scatter(): got = lax.ppermute(send, 'vocab', [(i, i ^ bit) for i in range(size)])  9.12 us
    ppermute x4, starting transfers between devices, ring_gather(): ahead = lax.ppermute(ahead, 'dp', fwd)  8.21 us
    dot_general x1, matrix products, on_device(): jnp.dot(full_rows, head_weight, preferred_element_type=jnp.float32)  7.37 us
    ppermute x3, starting transfers between devices, merge_stats(): lax.ppermute(stats, 'dp', [(i, i ^ bit * k) for i in range(size)])  3.55 us
    ppermute x3, waiting for transfers between devices, merge_stats(): lax.ppermute(stats, 'dp', [(i, i ^ bit * k) for i in range(size)])  3.2 us
    ppermute x1, starting transfers between devices, merge_stats(): lax.ppermute(stats, 'dp', [(i, i ^ bit) for i in range(size)])  2.65 us
    ppermute x1, waiting for transfers between devices, merge_stats(): lax.ppermute(stats, 'dp', [(i, i ^ bit) for i in range(size)])  1.89 us
  transfers between devices with their start and end apart: 15, of which 12 were waited for; matrix products, arithmetic and copies ran while one was open for 11% of the time, Pallas kernels for 0%

profile of v17, /device:TPU:0, one launch (start us, length us, event | category | flops | bytes accessed | tf_op | source)
XLA Modules:
  0.0 68.4 jit_solution(9183245994132872859)
XLA Ops:
  0.6 3.1 %collective-permute-start = (bf16[32,4096]{1,0:T(8,128)(2,1)}, bf16[32,4096]{1,0:T(8,128)(2,1)S(1)}, u32[]{:S(2)}, u32[]{:S(2)}) collective-permute-start(bf16[32,4096]{1,0:T(8,128)(2,1)} %param.13), channel_id=1, source_target_pairs={{0,8},{8,16},{16,24},{24,28},{28,20},{20,12},{12,4},{4,0},{1,9},{9... | collective-permute-start | bytes 786440 | tf_op jit(solution)/shard_map/ppermute | solution.py:39
  3.8 1.0 %bitcast_dynamic-update-slice_fusion.7 = bf16[8,32,4096]{2,1,0:T(8,128)(2,1)S(1)} fusion(bf16[32,4096]{1,0:T(8,128)(2,1)} %param.13), kind=kLoop, calls=%fused_computation.17 | loop fusion | bytes 524288
  4.8 0.8 %reduce-window.8 = s32[8,1]{0,1:T(1,128)S(1)} reduce-window(s32[8,1]{0,1:T(1,128)} %bitcast.166, s32[]{:T(128)} %constant.160.clone.1), window={size=8x1 pad=7_0x0_0}, to_apply=%region_0.2 | reduce-window | flops 56 | bytes 68 | tf_op jit(solution)/shard_map/reduce-window.3
  6.5 1.2 %dynamic_slice.7 = s32[1]{0:T(128)} dynamic-slice(s32[8]{0:T(128)} %constant.183.clone, s32[]{:T(128)S(6)} %select_n.125), dynamic_slice_sizes={1} | dynamic-slice | bytes 12 | tf_op jit(solution)/shard_map/dynamic_slice | solution.py:46
  7.7 1.3 %and_select_fusion.1 = s32[8]{0:T(128)S(1)} fusion(s32[8]{0:T(128)} %constant.222, s32[]{:T(128)} %bitcast.2), kind=kLoop, calls=%fused_computation.40 | loop fusion | flops 96 | bytes 68 | tf_op jit(solution)/shard_map/jit(remainder)/select_n | solution.py:47
  9.2 1.0 %collective-permute-done = bf16[32,4096]{1,0:T(8,128)(2,1)S(1)} collective-permute-done((bf16[32,4096]{1,0:T(8,128)(2,1)}, bf16[32,4096]{1,0:T(8,128)(2,1)S(1)}, u32[]{:S(2)}, u32[]{:S(2)}) %collective-permute-start) | collective-permute-done | bytes 262176 | tf_op jit(solution)/shard_map/ppermute | solution.py:39
  10.2 1.8 %collective-permute-start.1 = (bf16[32,4096]{1,0:T(8,128)(2,1)S(1)}, bf16[32,4096]{1,0:T(8,128)(2,1)S(1)}, u32[]{:S(2)}, u32[]{:S(2)}) collective-permute-start(bf16[32,4096]{1,0:T(8,128)(2,1)S(1)} %collective-permute-done), channel_id=1, source_target_pairs={{0,8},{8,16},{16,24},{24,28},{28,20},{20,12},{12,4},{4,0},{1,9},{9... | collective-permute-start | bytes 786440 | tf_op jit(solution)/shard_map/ppermute | solution.py:39
  12.3 5.4 %collective-permute-done.1 = bf16[32,4096]{1,0:T(8,128)(2,1)S(1)} collective-permute-done((bf16[32,4096]{1,0:T(8,128)(2,1)S(1)}, bf16[32,4096]{1,0:T(8,128)(2,1)S(1)}, u32[]{:S(2)}, u32[]{:S(2)}) %collective-permute-start.1) | collective-permute-done | bytes 262176 | tf_op jit(solution)/shard_map/ppermute | solution.py:39
  17.7 1.5 %collective-permute-start.2 = (bf16[32,4096]{1,0:T(8,128)(2,1)S(1)}, bf16[32,4096]{1,0:T(8,128)(2,1)S(1)}, u32[]{:S(2)}, u32[]{:S(2)}) collective-permute-start(bf16[32,4096]{1,0:T(8,128)(2,1)S(1)} %collective-permute-done.1), channel_id=1, source_target_pairs={{0,8},{8,16},{16,24},{24,28},{28,20},{20,12},{12,4},{4,0},{1,9},{9... | collective-permute-start | bytes 786440 | tf_op jit(solution)/shard_map/ppermute | solution.py:39
  19.8 4.5 %collective-permute-done.2 = bf16[32,4096]{1,0:T(8,128)(2,1)S(1)} collective-permute-done((bf16[32,4096]{1,0:T(8,128)(2,1)S(1)}, bf16[32,4096]{1,0:T(8,128)(2,1)S(1)}, u32[]{:S(2)}, u32[]{:S(2)}) %collective-permute-start.2) | collective-permute-done | bytes 262176 | tf_op jit(solution)/shard_map/ppermute | solution.py:39
  24.3 1.7 %collective-permute-start.3 = (bf16[32,4096]{1,0:T(8,128)(2,1)S(1)}, bf16[32,4096]{1,0:T(8,128)(2,1)S(1)}, u32[]{:S(2)}, u32[]{:S(2)}) collective-permute-start(bf16[32,4096]{1,0:T(8,128)(2,1)S(1)} %collective-permute-done.2), channel_id=1, source_target_pairs={{0,8},{8,16},{16,24},{24,28},{28,20},{20,12},{12,4},{4,0},{1,9},{9... | collective-permute-start | bytes 786440 | tf_op jit(solution)/shard_map/ppermute | solution.py:39
  26.0 4.6 %collective-permute-done.3 = bf16[32,4096]{1,0:T(8,128)(2,1)S(1)} collective-permute-done((bf16[32,4096]{1,0:T(8,128)(2,1)S(1)}, bf16[32,4096]{1,0:T(8,128)(2,1)S(1)}, u32[]{:S(2)}, u32[]{:S(2)}) %collective-permute-start.3) | collective-permute-done | bytes 262176 | tf_op jit(solution)/shard_map/ppermute | solution.py:39
  31.3 7.4 %fusion.28 = f32[160,2048]{1,0:T(8,128)S(1)} fusion(bf16[160,4096]{1,0:T(8,128)(2,1)S(1)} %convolution_convert_fusion, bf16[4096,2048]{1,0:T(8,128)(2,1)} %param.14), kind=kOutput, calls=%fused_computation.106 | convolution fusion | flops 2684354560 | bytes 19398656 | tf_op jit(solution)/shard_map/dot_general | solution.py:125
  39.0 0.8 %gather_fusion = s32[40]{0:T(128)S(1)} fusion(s32[256]{0:T(256)S(1)} %copy-done, s32[1024]{0:T(1024)S(1)} %pad_clamp_fusion), kind=kCustom, calls=%fused_computation.2 | custom fusion | bytes 480 | tf_op jit(solution)/shard_map/jit(_take)/gather | solution.py:128
  39.8 1.1 %collective-permute-done.7 = f32[80,2048]{1,0:T(8,128)S(1)} collective-permute-done((f32[80,2048]{1,0:T(8,128)S(1)}, f32[80,2048]{1,0:T(8,128)S(1)}, u32[]{:S(2)}, u32[]{:S(2)}) %collective-permute-start.7) | collective-permute-done | bytes 655392 | tf_op jit(solution)/shard_map/ppermute | solution.py:66
  41.0 1.7 %collective-permute-start.8 = (f32[40,2048]{1,0:T(8,128)S(1)}, f32[40,2048]{1,0:T(8,128)S(1)}, u32[]{:S(2)}, u32[]{:S(2)}) collective-permute-start(f32[40,2048]{1,0:T(8,128)S(1)} %select_bitcast_fusion.1), channel_id=1, source_target_pairs={{0,2},{1,3},{2,0},{3,1},{4,6},{5,7},{6,4},{7,5},{8,10},{9,11},{10,... | collective-permute-start | bytes 983048 | tf_op jit(solution)/shard_map/ppermute | solution.py:66
  42.9 8.0 %collective-permute-done.8 = f32[40,2048]{1,0:T(8,128)S(1)} collective-permute-done((f32[40,2048]{1,0:T(8,128)S(1)}, f32[40,2048]{1,0:T(8,128)S(1)}, u32[]{:S(2)}, u32[]{:S(2)}) %collective-permute-start.8) | collective-permute-done | bytes 327712 | tf_op jit(solution)/shard_map/ppermute | solution.py:66
  51.3 1.8 %collective-permute-start.10 = (f32[3,40]{1,0:T(4,128)S(1)}, f32[3,40]{1,0:T(4,128)S(1)}, u32[]{:S(2)}, u32[]{:S(2)}) collective-permute-start(f32[3,40]{1,0:T(4,128)S(1)} %pad_maximum_fusion), channel_id=1, source_target_pairs={{0,8},{4,12},{8,0},{12,4},{16,24},{20,28},{24,16},{28,20},{1,9},{5... | collective-permute-start | bytes 1448 | tf_op jit(solution)/shard_map/ppermute | solution.py:83
  53.1 1.4 %collective-permute-start.11 = (f32[3,40]{1,0:T(4,128)S(1)}, f32[3,40]{1,0:T(4,128)S(1)}, u32[]{:S(2)}, u32[]{:S(2)}) collective-permute-start(f32[3,40]{1,0:T(4,128)S(1)} %pad_maximum_fusion), channel_id=1, source_target_pairs={{0,12},{4,8},{8,4},{12,0},{16,28},{20,24},{24,20},{28,16},{1,13},{... | collective-permute-start | bytes 1448 | tf_op jit(solution)/shard_map/ppermute | solution.py:83
  54.9 2.6 %collective-permute-done.11 = f32[3,40]{1,0:T(4,128)S(1)} collective-permute-done((f32[3,40]{1,0:T(4,128)S(1)}, f32[3,40]{1,0:T(4,128)S(1)}, u32[]{:S(2)}, u32[]{:S(2)}) %collective-permute-start.11) | collective-permute-done | bytes 512 | tf_op jit(solution)/shard_map/ppermute | solution.py:83
  58.1 2.6 %collective-permute-start.12 = (f32[3,40]{1,0:T(4,128)S(1)}, f32[3,40]{1,0:T(4,128)S(1)}, u32[]{:S(2)}, u32[]{:S(2)}) collective-permute-start(f32[3,40]{1,0:T(4,128)S(1)} %pad_maximum_fusion.1), channel_id=1, source_target_pairs={{0,16},{4,20},{8,24},{12,28},{16,0},{20,4},{24,8},{28,12},{1,17},{... | collective-permute-start | bytes 1448 | tf_op jit(solution)/shard_map/ppermute | solution.py:87
  60.7 1.9 %collective-permute-done.12 = f32[3,40]{1,0:T(4,128)S(1)} collective-permute-done((f32[3,40]{1,0:T(4,128)S(1)}, f32[3,40]{1,0:T(4,128)S(1)}, u32[]{:S(2)}, u32[]{:S(2)}) %collective-permute-start.12) | collective-permute-done | bytes 512 | tf_op jit(solution)/shard_map/ppermute | solution.py:87
  64.1 1.5 %collective-permute-start.14 = (f32[160]{0:T(256)S(1)}, f32[160]{0:T(256)S(1)}, u32[]{:S(2)}, u32[]{:S(2)}) collective-permute-start(f32[160]{0:T(256)S(1)} %add_dynamic-update-slice_fusion), channel_id=1, source_target_pairs={{0,2},{1,3},{2,0},{3,1},{4,6},{5,7},{6,4},{7,5},{8,10},{9,11},{10,... | collective-permute-start | bytes 1928 | tf_op jit(solution)/shard_map/ppermute | solution.py:100
  66.3 1.3 %collective-permute-done.14 = f32[160]{0:T(256)S(1)} collective-permute-done((f32[160]{0:T(256)S(1)}, f32[160]{0:T(256)S(1)}, u32[]{:S(2)}, u32[]{:S(2)}) %collective-permute-start.14) | collective-permute-done | bytes 672 | tf_op jit(solution)/shard_map/ppermute | solution.py:100
  (54 shorter events, 7.1 us)
Async XLA Ops:
  0.6 38.4 %copy-start = (s32[256]{0:T(256)S(1)}, s32[256]{0:T(256)}, u32[]{:S(2)}) copy-start(s32[256]{0:T(256)} %param.16) | copy-start | bytes 3076
  0.6 9.5 %collective-permute-start = (bf16[32,4096]{1,0:T(8,128)(2,1)}, bf16[32,4096]{1,0:T(8,128)(2,1)S(1)}, u32[]{:S(2)}, u32[]{:S(2)}) collective-permute-start(bf16[32,4096]{1,0:T(8,128)(2,1)} %param.13), channel_id=1, source_target_pairs={{0,8},{8,16},{16,24},{24,28},{28,20},{20,12},{12,4},{4,0},{1,9},{9... | collective-permute-start | bytes 786440 | tf_op jit(solution)/shard_map/ppermute | solution.py:39
  3.7 8.3 %collective-permute-start.4 = (bf16[32,4096]{1,0:T(8,128)(2,1)}, bf16[32,4096]{1,0:T(8,128)(2,1)S(1)}, u32[]{:S(2)}, u32[]{:S(2)}) collective-permute-start(bf16[32,4096]{1,0:T(8,128)(2,1)} %param.13), channel_id=1, source_target_pairs={{8,0},{16,8},{24,16},{28,24},{20,28},{12,20},{4,12},{0,4},{9,1},{1... | collective-permute-start | bytes 786440 | tf_op jit(solution)/shard_map/ppermute | solution.py:42
  10.2 7.5 %collective-permute-start.1 = (bf16[32,4096]{1,0:T(8,128)(2,1)S(1)}, bf16[32,4096]{1,0:T(8,128)(2,1)S(1)}, u32[]{:S(2)}, u32[]{:S(2)}) collective-permute-start(bf16[32,4096]{1,0:T(8,128)(2,1)S(1)} %collective-permute-done), channel_id=1, source_target_pairs={{0,8},{8,16},{16,24},{24,28},{28,20},{20,12},{12,4},{4,0},{1,9},{9... | collective-permute-start | bytes 786440 | tf_op jit(solution)/shard_map/ppermute | solution.py:39
  12.0 7.2 %collective-permute-start.5 = (bf16[32,4096]{1,0:T(8,128)(2,1)S(1)}, bf16[32,4096]{1,0:T(8,128)(2,1)S(1)}, u32[]{:S(2)}, u32[]{:S(2)}) collective-permute-start(bf16[32,4096]{1,0:T(8,128)(2,1)S(1)} %collective-permute-done.4), channel_id=1, source_target_pairs={{8,0},{16,8},{24,16},{28,24},{20,28},{12,20},{4,12},{0,4},{9,1},{1... | collective-permute-start | bytes 786440 | tf_op jit(solution)/shard_map/ppermute | solution.py:42
  17.7 6.6 %collective-permute-start.2 = (bf16[32,4096]{1,0:T(8,128)(2,1)S(1)}, bf16[32,4096]{1,0:T(8,128)(2,1)S(1)}, u32[]{:S(2)}, u32[]{:S(2)}) collective-permute-start(bf16[32,4096]{1,0:T(8,128)(2,1)S(1)} %collective-permute-done.1), channel_id=1, source_target_pairs={{0,8},{8,16},{16,24},{24,28},{28,20},{20,12},{12,4},{4,0},{1,9},{9... | collective-permute-start | bytes 786440 | tf_op jit(solution)/shard_map/ppermute | solution.py:39
  19.2 11.4 %collective-permute-start.6 = (bf16[32,4096]{1,0:T(8,128)(2,1)S(1)}, bf16[32,4096]{1,0:T(8,128)(2,1)S(1)}, u32[]{:S(2)}, u32[]{:S(2)}) collective-permute-start(bf16[32,4096]{1,0:T(8,128)(2,1)S(1)} %collective-permute-done.5), channel_id=1, source_target_pairs={{8,0},{16,8},{24,16},{28,24},{20,28},{12,20},{4,12},{0,4},{9,1},{1... | collective-permute-start | bytes 786440 | tf_op jit(solution)/shard_map/ppermute | solution.py:42
  24.3 6.4 %collective-permute-start.3 = (bf16[32,4096]{1,0:T(8,128)(2,1)S(1)}, bf16[32,4096]{1,0:T(8,128)(2,1)S(1)}, u32[]{:S(2)}, u32[]{:S(2)}) collective-permute-start(bf16[32,4096]{1,0:T(8,128)(2,1)S(1)} %collective-permute-done.2), channel_id=1, source_target_pairs={{0,8},{8,16},{16,24},{24,28},{28,20},{20,12},{12,4},{4,0},{1,9},{9... | collective-permute-start | bytes 786440 | tf_op jit(solution)/shard_map/ppermute | solution.py:39
  38.8 2.2 %collective-permute-start.7 = (f32[80,2048]{1,0:T(8,128)S(1)}, f32[80,2048]{1,0:T(8,128)S(1)}, u32[]{:S(2)}, u32[]{:S(2)}) collective-permute-start(f32[80,2048]{1,0:T(8,128)S(1)} %select_bitcast_fusion), channel_id=1, source_target_pairs={{0,1},{1,0},{2,3},{3,2},{4,5},{5,4},{6,7},{7,6},{8,9},{9,8},{10,11... | collective-permute-start | bytes 1966088 | tf_op jit(solution)/shard_map/ppermute | solution.py:66
  39.8 25.8 %copy-start.1 = (s32[8]{0:T(128)S(1)}, s32[8]{0:T(128)}, u32[]{:S(2)}) copy-start(s32[8]{0:T(128)} %param.15) | copy-start | bytes 100
  39.8 28.0 %copy-start.2 = (f32[32]{0:T(128)S(1)}, f32[32]{0:T(128)}, u32[]{:S(2)}) copy-start(f32[32]{0:T(128)} %param.17) | copy-start | bytes 388
  41.0 9.8 %collective-permute-start.8 = (f32[40,2048]{1,0:T(8,128)S(1)}, f32[40,2048]{1,0:T(8,128)S(1)}, u32[]{:S(2)}, u32[]{:S(2)}) collective-permute-start(f32[40,2048]{1,0:T(8,128)S(1)} %select_bitcast_fusion.1), channel_id=1, source_target_pairs={{0,2},{1,3},{2,0},{3,1},{4,6},{5,7},{6,4},{7,5},{8,10},{9,11},{10,... | collective-permute-start | bytes 983048 | tf_op jit(solution)/shard_map/ppermute | solution.py:66
  51.3 3.7 %collective-permute-start.10 = (f32[3,40]{1,0:T(4,128)S(1)}, f32[3,40]{1,0:T(4,128)S(1)}, u32[]{:S(2)}, u32[]{:S(2)}) collective-permute-start(f32[3,40]{1,0:T(4,128)S(1)} %pad_maximum_fusion), channel_id=1, source_target_pairs={{0,8},{4,12},{8,0},{12,4},{16,24},{20,28},{24,16},{28,20},{1,9},{5... | collective-permute-start | bytes 1448 | tf_op jit(solution)/shard_map/ppermute | solution.py:83
  53.1 4.5 %collective-permute-start.11 = (f32[3,40]{1,0:T(4,128)S(1)}, f32[3,40]{1,0:T(4,128)S(1)}, u32[]{:S(2)}, u32[]{:S(2)}) collective-permute-start(f32[3,40]{1,0:T(4,128)S(1)} %pad_maximum_fusion), channel_id=1, source_target_pairs={{0,12},{4,8},{8,4},{12,0},{16,28},{20,24},{24,20},{28,16},{1,13},{... | collective-permute-start | bytes 1448 | tf_op jit(solution)/shard_map/ppermute | solution.py:83
  54.5 3.6 %collective-permute-start.9 = (f32[3,40]{1,0:T(4,128)S(1)}, f32[3,40]{1,0:T(4,128)S(1)}, u32[]{:S(2)}, u32[]{:S(2)}) collective-permute-start(f32[3,40]{1,0:T(4,128)S(1)} %pad_maximum_fusion), channel_id=1, source_target_pairs={{0,4},{4,0},{8,12},{12,8},{16,20},{20,16},{24,28},{28,24},{1,5},{5... | collective-permute-start | bytes 1448 | tf_op jit(solution)/shard_map/ppermute | solution.py:83
  58.1 4.5 %collective-permute-start.12 = (f32[3,40]{1,0:T(4,128)S(1)}, f32[3,40]{1,0:T(4,128)S(1)}, u32[]{:S(2)}, u32[]{:S(2)}) collective-permute-start(f32[3,40]{1,0:T(4,128)S(1)} %pad_maximum_fusion.1), channel_id=1, source_target_pairs={{0,16},{4,20},{8,24},{12,28},{16,0},{20,4},{24,8},{28,12},{1,17},{... | collective-permute-start | bytes 1448 | tf_op jit(solution)/shard_map/ppermute | solution.py:87
  62.7 1.2 %collective-permute-start.13 = (f32[160]{0:T(256)S(1)}, f32[160]{0:T(256)S(1)}, u32[]{:S(2)}, u32[]{:S(2)}) collective-permute-start(f32[160]{0:T(256)S(1)} %get-tuple-element.33), channel_id=1, source_target_pairs={{0,1},{1,0},{2,3},{3,2},{4,5},{5,4},{6,7},{7,6},{8,9},{9,8},{10,11... | collective-permute-start | bytes 1928 | tf_op jit(solution)/shard_map/ppermute | solution.py:102
  64.1 3.6 %collective-permute-start.14 = (f32[160]{0:T(256)S(1)}, f32[160]{0:T(256)S(1)}, u32[]{:S(2)}, u32[]{:S(2)}) collective-permute-start(f32[160]{0:T(256)S(1)} %add_dynamic-update-slice_fusion), channel_id=1, source_target_pairs={{0,2},{1,3},{2,0},{3,1},{4,6},{5,7},{6,4},{7,5},{8,10},{9,11},{10,... | collective-permute-start | bytes 1928 | tf_op jit(solution)/shard_map/ppermute | solution.py:100
